TPU v7x, 32 devices: a whole 2x2x4 slice. The times are simulated.
32 devices in a mesh: rec: 4 (over y, x), seq: 8 (over z, core).
Axes of the slice: x: 2, y: 2, z: 4, core: 2. Of those that a mesh axis runs over, the one named last changes fastest.
Arguments:
- owned_rows: bfloat16 [4, 2048, 1024], P('rec', 'seq'), may hold values from -20 to 20
- seq_position: int32 [4, 2048], P('rec', 'seq'), may hold values from 0 to 2047, as said below
- head_weights: bfloat16 [1024, 8, 128], replicated, may hold values from -0.1875 to 0.1875
- key_blocks: int32 [1, 16, 8], replicated, may hold values from 0 to 15, as said below
- key_counts: int32 [1, 16], replicated, may hold values from 1 to 8, as said below
- out_grad: bfloat16 [4, 8, 2048, 64], P('rec', None, 'seq'), may hold values from -6 to 6
Outputs:
- attention: bfloat16 [4, 8, 2048, 64], P('rec', None, 'seq')
- seq_grad: bfloat16 [4, 2048, 1024], P('rec', 'seq')
- weight_grad: float32 [1024, 8, 128], P(('rec', 'seq'))
Inputs may be any that keep to these rules, and one draw needn't show every extreme that they name: `seq_position`: in each recording every position appears once. The rows of one index of seq go to each index of seq (positions p with the same p // 256) between 1 and 63 times, and in every recording some index sends exactly 63 rows to some index. `key_blocks`: each list holds 8 different block numbers of the same spatial group, the query block's own number first; only the first key_counts entries are used. `key_counts`: every spatial group has a query block that uses all 8 listed blocks.
All inputs are finite; a program needn't handle non-finite values.
Results may differ from a plain program's by a relative error of at most 0.012.
Values may be sent and summed in bfloat16 or wider, within the bound.
No kernel may reach another device: no remote copies, remote signals or barrier semaphores. Data moves between devices by JAX's collectives and lax.ppermute only.
A program may use at most 64 MiB of HBM per device.

v0:
```python
import jax
import jax.numpy as jnp
from jax import lax
from jax.sharding import PartitionSpec as P
from jax.experimental import pallas as pl
from jax.experimental.pallas import tpu as pltpu

BLOCK = 128


def attention_kernel(lists_ref, counts_ref, both_ref, grad_ref, out_ref, back_ref, acc_ref):
    nblocks, listed = lists_ref.shape
    depth = grad_ref.shape[1]
    scale = depth ** (-0.5)
    acc_ref[...] = jnp.zeros(acc_ref.shape, jnp.float32)
    col_block = lax.broadcasted_iota(jnp.int32, (BLOCK, listed * BLOCK), 1) // BLOCK
    trans_a = (((0,), (0,)), ((), ()))
    trans_b = (((1,), (1,)), ((), ()))

    def one_block(a, carry):
        start = pl.multiple_of(a * BLOCK, BLOCK)
        own = both_ref[pl.ds(start, BLOCK), :]
        query = own[:, :depth]
        upstream = grad_ref[pl.ds(start, BLOCK), :]
        active = counts_ref[a]
        picks = [jnp.clip(lists_ref[a, j], 0, nblocks - 1) for j in range(listed)]
        tiles = [both_ref[pl.ds(pl.multiple_of(b * BLOCK, BLOCK), BLOCK), :] for b in picks]
        keys = [t[:, :depth] for t in tiles]
        values = [t[:, depth:] for t in tiles]
        scores = jnp.concatenate(
            [lax.dot_general(query, k, trans_b, preferred_element_type=jnp.float32) for k in keys],
            axis=1,
        ) * scale
        usable = col_block < active
        scores = jnp.where(usable, scores, -jnp.inf)
        peak = jnp.max(scores, axis=1, keepdims=True)
        weights = jnp.where(usable, jnp.exp(scores - peak), 0.0)
        probs = weights / jnp.sum(weights, axis=1, keepdims=True)
        probs_low = probs.astype(jnp.bfloat16)
        dprobs = jnp.concatenate(
            [lax.dot_general(upstream, v, trans_b, preferred_element_type=jnp.float32) for v in values],
            axis=1,
        )
        inner = jnp.sum(probs * dprobs, axis=1, keepdims=True)
        dscores = (scale * probs * (dprobs - inner)).astype(jnp.bfloat16)
        mixed = jnp.zeros((BLOCK, depth), jnp.float32)
        dquery = jnp.zeros((BLOCK, depth), jnp.float32)
        for j in range(listed):
            cols = slice(j * BLOCK, (j + 1) * BLOCK)
            mixed = mixed + jnp.dot(probs_low[:, cols], values[j], preferred_element_type=jnp.float32)
            dquery = dquery + jnp.dot(dscores[:, cols], keys[j], preferred_element_type=jnp.float32)
        out_ref[pl.ds(start, BLOCK), :] = mixed.astype(out_ref.dtype)
        for j in range(listed):
            cols = slice(j * BLOCK, (j + 1) * BLOCK)
            dkeys = lax.dot_general(dscores[:, cols], query, trans_a, preferred_element_type=jnp.float32)
            dvalues = lax.dot_general(probs_low[:, cols], upstream, trans_a, preferred_element_type=jnp.float32)
            if j == 0:
                dkeys = dkeys + dquery

            @pl.when(j < active)
            def _():
                rows = pl.ds(pl.multiple_of(picks[j] * BLOCK, BLOCK), BLOCK)
                acc_ref[rows, :] += jnp.concatenate([dkeys, dvalues], axis=1)

        return carry

    lax.fori_loop(0, nblocks, one_block, 0)
    back_ref[...] = acc_ref[...].astype(back_ref.dtype)


def attend_group(both, grad_rows, lists, counts):
    total, width = both.shape
    depth = grad_rows.shape[1]
    smem = pltpu.MemorySpace.SMEM
    vmem = pltpu.MemorySpace.VMEM
    return pl.pallas_call(
        attention_kernel,
        out_shape=(
            jax.ShapeDtypeStruct((total, depth), jnp.bfloat16),
            jax.ShapeDtypeStruct((total, width), jnp.bfloat16),
        ),
        in_specs=[
            pl.BlockSpec(memory_space=smem),
            pl.BlockSpec(memory_space=smem),
            pl.BlockSpec(memory_space=vmem),
            pl.BlockSpec(memory_space=vmem),
        ],
        out_specs=(pl.BlockSpec(memory_space=vmem), pl.BlockSpec(memory_space=vmem)),
        scratch_shapes=[pltpu.VMEM((total, width), jnp.float32)],
    )(lists, counts, both, grad_rows)


def local(owned_rows, seq_position, head_weights, key_blocks, key_counts, out_grad):
    seq_count = lax.axis_size("seq")
    my_index = lax.axis_index("seq")
    tokens_here = owned_rows.shape[1]
    width = owned_rows.shape[2]
    heads = head_weights.shape[1]
    depth = head_weights.shape[2] // 2
    groups = seq_count // heads
    portion = tokens_here // groups
    room = 2 * tokens_here // seq_count - 1
    rows_here = owned_rows[0]
    targets = seq_position[0]
    holders = targets // tokens_here
    order_ids = jnp.arange(tokens_here)
    earlier = order_ids[None, :] < order_ids[:, None]
    same_holder = holders[:, None] == holders[None, :]
    ranked = jnp.sum((earlier & same_holder).astype(jnp.int32), axis=1)
    slot_ids = holders * room + ranked
    outgoing = jnp.zeros((seq_count * room, width), rows_here.dtype).at[slot_ids].set(rows_here)
    outgoing = outgoing.reshape(seq_count, room, width)
    labels = (
        jnp.full((seq_count * room,), -1, jnp.int32)
        .at[slot_ids]
        .set(targets)
        .reshape(seq_count, room)
    )
    arrived, arrived_pos = (
        lax.all_to_all(outgoing, "seq", split_axis=0, concat_axis=0, tiled=True),
        lax.all_to_all(labels, "seq", split_axis=0, concat_axis=0, tiled=True),
    )
    local_ids = jnp.where(
        arrived_pos >= 0, arrived_pos - my_index * tokens_here, tokens_here
    ).reshape(-1)
    tokens = (
        jnp.zeros((tokens_here, width), rows_here.dtype)
        .at[local_ids]
        .set(arrived.reshape(-1, width), mode="drop")
    )
    proj = jnp.einsum(
        "td,dhc->htc", tokens, head_weights, preferred_element_type=jnp.float32
    ).astype(jnp.bfloat16)
    sending = proj.reshape(seq_count, portion * 2 * depth)
    upstream = out_grad[0].reshape(seq_count, portion * depth)
    got, got_grad = (
        lax.all_to_all(sending, "seq", split_axis=0, concat_axis=0, tiled=True),
        lax.all_to_all(upstream, "seq", split_axis=0, concat_axis=0, tiled=True),
    )
    gathered = got.reshape(seq_count * portion, 2 * depth)
    grad_rows = got_grad.reshape(seq_count * portion, depth)
    group = my_index % groups
    mixed, grad_both = attend_group(gathered, grad_rows, key_blocks[group], key_counts[group])
    back_out, back_grad = (
        lax.all_to_all(
            mixed.reshape(seq_count, portion * depth),
            "seq",
            split_axis=0,
            concat_axis=0,
            tiled=True,
        ),
        lax.all_to_all(
            grad_both.reshape(seq_count, portion * 2 * depth),
            "seq",
            split_axis=0,
            concat_axis=0,
            tiled=True,
        ),
    )
    attention = back_out.reshape(heads, tokens_here, depth)[None]
    grad_proj = back_grad.reshape(heads, tokens_here, 2 * depth)
    seq_grad = jnp.einsum(
        "htc,dhc->td", grad_proj, head_weights, preferred_element_type=jnp.float32
    ).astype(jnp.bfloat16)[None]
    weight_grad = lax.psum_scatter(
        jnp.einsum("td,htc->dhc", tokens, grad_proj, preferred_element_type=jnp.float32),
        ("rec", "seq"),
        scatter_dimension=0,
        tiled=True,
    )
    return (attention, seq_grad, weight_grad)


def solution(mesh):
    placed = (P("rec", "seq", None), P("rec", "seq"), P(), P(), P(), P("rec", None, "seq", None))
    return jax.shard_map(
        local,
        mesh=mesh,
        in_specs=placed,
        out_specs=(
            P("rec", None, "seq", None),
            P("rec", "seq", None),
            P(("rec", "seq"), None, None),
        ),
        check_vma=False,
    )
```

profile of v0, /device:TPU:0, one launch (start us, length us, event | category | flops | bytes accessed | tf_op | source)
XLA Modules:
  0.0 331.2 jit_solution(13382838427989020583)
XLA Ops:
  7.2 0.0 copy-start
  7.2 0.8 and_select_fusion
  8.0 0.7 and_select_fusion.2
  8.7 0.2 convert_reduce_fusion
  8.9 0.7 compare_select_fusion.2
  9.6 1.6 scatter_custom_fusion
  11.1 0.7 all_to_all.33
  11.8 6.3 %all-to-all-start = ((s32[8,1,63]{2,1,0:T(1,128)}), s32[8,1,63]{2,1,0:T(1,128)S(1)}, u32[]{:S(2)}, u32[]{:S(2)}) async-start(s32[8,1,63]{2,1,0:T(1,128)} %all_to_all.33), calls=%async_computation | async-start | bytes 8192 | tf_op jit(solution)/shard_map/all_to_all | solution.py:121
  18.2 2.5 scatter_custom_fusion.1
  20.6 0.0 copy-start.4
  20.7 1.3 reshape.181
  22.0 1.7 all-to-all-done
  23.6 3.6 %all-to-all-start.1 = ((bf16[8,63,1024]{2,1,0:T(8,128)(2,1)}), bf16[8,63,1024]{2,1,0:T(8,128)(2,1)S(1)}, u32[]{:S(2)}, u32[]{:S(2)}) async-start(bf16[8,63,1024]{2,1,0:T(8,128)(2,1)} %reshape.181), calls=%async_computation.1 | async-start | bytes 2097152 | tf_op jit(solution)/shard_map/all_to_all | solution.py:120
  27.2 0.0 copy-done.4
  27.2 1.0 copy.45
  28.2 2.0 all_to_all.45
  30.3 0.5 broadcast.165
  30.8 3.2 reduce.9
  34.0 0.9 reshape.232
  34.9 0.1 select_n.77
  35.0 18.7 %all-to-all-done.1 = bf16[8,63,1024]{2,1,0:T(8,128)(2,1)S(1)} async-done(((bf16[8,63,1024]{2,1,0:T(8,128)(2,1)}), bf16[8,63,1024]{2,1,0:T(8,128)(2,1)S(1)}, u32[]{:S(2)}, u32[]{:S(2)}) %all-to-all-start.1) | async-done | bytes 1032224 | tf_op jit(solution)/shard_map/all_to_all | solution.py:120
  53.7 3.4 %all-to-all-start.3 = ((bf16[8,2,8192]{2,1,0:T(2,128)(2,1)}), bf16[8,2,8192]{2,1,0:T(2,128)(2,1)S(1)}, u32[]{:S(2)}, u32[]{:S(2)}) async-start(bf16[8,2,8192]{2,1,0:T(2,128)(2,1)} %reshape.232), calls=%async_computation.3 | async-start | bytes 524288 | tf_op jit(solution)/shard_map/all_to_all | solution.py:138
  57.1 1.3 reshape.206
  58.5 3.6 %scatter_custom_fusion.2 = bf16[256,1024]{1,0:T(8,128)(2,1)S(1)} fusion(s32[504]{0:T(512)S(1)} %bitcast.51, bf16[504,1024]{1,0:T(8,128)(2,1)} %reshape.206, bf16[]{:T(256)} %constant.14.clone.1), kind=kCustom, calls=%fused_computation.24 | custom fusion | bytes 524800 | tf_op jit(solution)/shard_map/scatter | solution.py:129
  62.1 0.0 copy-start.2
  62.1 0.8 copy-done.2
  62.9 1.5 fusion.13
  64.4 2.0 all_to_all.44
  66.4 0.0 copy-start.5
  66.4 4.6 %reduce.8 = bf16[8,32768]{1,0:T(8,128)(2,1)} reduce(bf16[8,1,32768]{2,1,0:T(2,128)(2,1)S(1)} %all_to_all.44, bf16[]{:T(256)} %broadcast.165), dimensions={1}, to_apply=%all_to_all.44.reduce_sub_computation | reduce | bytes 1048578 | tf_op jit(solution)/shard_map/all_to_all | solution.py:137
  71.0 2.2 reshape.230
  73.2 0.0 all-to-all-done.3
  73.2 5.0 %all-to-all-start.2 = ((bf16[8,2,16384]{2,1,0:T(2,128)(2,1)}), bf16[8,2,16384]{2,1,0:T(2,128)(2,1)}, u32[]{:S(2)}, u32[]{:S(2)}) async-start(bf16[8,2,16384]{2,1,0:T(2,128)(2,1)} %reshape.230), calls=%async_computation.2 | async-start | bytes 1048576 | tf_op jit(solution)/shard_map/all_to_all | solution.py:137
  78.3 0.0 reduce-scatter.2.cloned.1.call-start
  78.3 0.7 copy.47.lists_ref
  79.0 0.3 reshape.233
  79.3 1.6 reduce.2
  80.8 1.3 reshape.184.grad_ref
  82.2 11.6 %all-to-all-done.2 = bf16[8,2,16384]{2,1,0:T(2,128)(2,1)} async-done(((bf16[8,2,16384]{2,1,0:T(2,128)(2,1)}), bf16[8,2,16384]{2,1,0:T(2,128)(2,1)}, u32[]{:S(2)}, u32[]{:S(2)}) %all-to-all-start.2) | async-done | bytes 524320 | tf_op jit(solution)/shard_map/all_to_all | solution.py:137
  93.7 2.2 reshape.231
  96.0 4.0 %reduce.1 = bf16[8,32768]{1,0:T(8,128)(2,1)} reduce(bf16[8,1,32768]{2,1,0:T(2,128)(2,1)S(1)} %reshape.231, bf16[]{:T(256)} %constant.46), dimensions={1}, to_apply=%all_to_all.37.reduce_sub_computation | reduce | bytes 1048578 | tf_op jit(solution)/shard_map/all_to_all | solution.py:137
  99.9 2.1 reshape.183.both_ref
  102.0 42.0 %shard_map.85 = (bf16[2048,64]{1,0:T(8,128)(2,1)}, bf16[2048,128]{1,0:T(8,128)(2,1)}) custom-call(s32[16,8]{1,0:T(8,128)} %copy.47.lists_ref, s32[16]{0:T(128)} %bitcast.54, bf16[2048,128]{1,0:T(8,128)(2,1)} %reshape.183.both_ref, bf16[2048,64]{1,0:T(8,128)(2,1)} %reshape.184.grad_ref), custom_call_target="tpu_custom_call" | custom-call | tf_op jit(solution)/shard_map/pallas_call | solution.py:76
  144.0 2.0 all_to_all.47
  146.1 4.6 %reduce.11 = bf16[8,32768]{1,0:T(8,128)(2,1)} reduce(bf16[8,1,32768]{2,1,0:T(2,128)(2,1)S(1)} %all_to_all.47, bf16[]{:T(256)} %broadcast.165), dimensions={1}, to_apply=%all_to_all.47.reduce_sub_computation | reduce | bytes 1048578 | tf_op jit(solution)/shard_map/all_to_all | solution.py:152
  150.6 1.4 reshape.236
  152.1 18.4 %all_to_all.54 = bf16[8,2,16384]{2,1,0:T(2,128)(2,1)} all-to-all(bf16[8,2,16384]{2,1,0:T(2,128)(2,1)S(1)} %reshape.236), channel_id=1, replica_groups=mesh['rec'=4,'seq'=8] {'seq'}, dimensions={0} | all-to-all | bytes 1048576 | tf_op jit(solution)/shard_map/all_to_all | solution.py:152
  170.5 2.2 reshape.237
  172.7 4.0 %reduce.4 = bf16[8,32768]{1,0:T(8,128)(2,1)} reduce(bf16[8,1,32768]{2,1,0:T(2,128)(2,1)S(1)} %reshape.237, bf16[]{:T(256)} %constant.46), dimensions={1}, to_apply=%all_to_all.43.reduce_sub_computation | reduce | bytes 1048578 | tf_op jit(solution)/shard_map/all_to_all | solution.py:152
  176.7 3.9 %fusion.19 = f32[1024,8,128]{2,0,1:T(8,128)} fusion(bf16[256,1024]{1,0:T(8,128)(2,1)} %copy-done.2, bf16[1,8,256,128]{3,1,2,0:T(8,128)(2,1)} %bitcast.44), kind=kOutput, calls=%fused_computation.12 | convolution fusion | flops 536870912 | bytes 5242880 | tf_op jit(solution)/shard_map/td,htc->dhc/dot_general | solution.py:166
  180.6 0.0 reduce-scatter.2.cloned.1.call-update
  180.6 1.0 copy-done.3
  181.7 0.3 all_to_all.46
  182.0 2.2 reduce.10
  184.2 0.0 copy-start.1
  184.2 0.2 reshape.234
  184.4 14.6 %all_to_all.55 = bf16[8,2,8192]{2,1,0:T(2,128)(2,1)S(1)} all-to-all(bf16[8,2,8192]{2,1,0:T(2,128)(2,1)S(1)} %reshape.234), channel_id=1, replica_groups=mesh['rec'=4,'seq'=8] {'seq'}, dimensions={0} | all-to-all | bytes 524288 | tf_op jit(solution)/shard_map/all_to_all | solution.py:145
  199.0 0.3 reshape.235
  199.3 1.6 reduce.3
  200.8 0.5 broadcast_in_dim_reshape.3
  201.4 0.9 copy.52
  202.3 1.5 fusion.16
  203.8 118.9 %reduce-scatter.2.cloned.1.call-done = f32[32,8,128]{2,0,1:T(8,128)} async-done(((f32[1024,8,128]{2,0,1:T(8,128)}), f32[32,8,128]{2,0,1:T(8,128)}) %reduce-scatter.2.cloned.1.call-update) | async-done | bytes 131088 | tf_op jit(solution)/shard_map/reduce_scatter | solution.py:165
  322.7 1.6 copy.53
  (6 shorter events, 0.0 us)
Async XLA Ops:
  7.2 55.7 %copy-start = (bf16[1024,8,128]{2,1,0:T(8,128)(2,1)S(1)}, bf16[1024,8,128]{2,1,0:T(8,128)(2,1)}, u32[]{:S(2)}) copy-start(bf16[1024,8,128]{2,1,0:T(8,128)(2,1)} %param.8) | copy-start | bytes 6291460
  11.8 11.8 %all-to-all-start = ((s32[8,1,63]{2,1,0:T(1,128)}), s32[8,1,63]{2,1,0:T(1,128)S(1)}, u32[]{:S(2)}, u32[]{:S(2)}) async-start(s32[8,1,63]{2,1,0:T(1,128)} %all_to_all.33), calls=%async_computation | async-start | bytes 8192 | tf_op jit(solution)/shard_map/all_to_all | solution.py:121
  20.6 6.6 %copy-start.4 = (bf16[1,8,256,64]{2,3,1,0:T(8,128)(2,1)S(1)}, bf16[1,8,256,64]{2,3,1,0:T(8,128)(2,1)}, u32[]{:S(2)}) copy-start(bf16[1,8,256,64]{2,3,1,0:T(8,128)(2,1)} %param.11) | copy-start | bytes 786436
  23.6 30.1 %all-to-all-start.1 = ((bf16[8,63,1024]{2,1,0:T(8,128)(2,1)}), bf16[8,63,1024]{2,1,0:T(8,128)(2,1)S(1)}, u32[]{:S(2)}, u32[]{:S(2)}) async-start(bf16[8,63,1024]{2,1,0:T(8,128)(2,1)} %reshape.181), calls=%async_computation.1 | async-start | bytes 2097152 | tf_op jit(solution)/shard_map/all_to_all | solution.py:120
  53.7 19.5 %all-to-all-start.3 = ((bf16[8,2,8192]{2,1,0:T(2,128)(2,1)}), bf16[8,2,8192]{2,1,0:T(2,128)(2,1)S(1)}, u32[]{:S(2)}, u32[]{:S(2)}) async-start(bf16[8,2,8192]{2,1,0:T(2,128)(2,1)} %reshape.232), calls=%async_computation.3 | async-start | bytes 524288 | tf_op jit(solution)/shard_map/all_to_all | solution.py:138
  62.1 0.8 copy-start.2
  66.4 11.9 %copy-start.5 = (s32[1,16,8]{1,2,0:T(8,128)S(1)}, s32[1,16,8]{1,2,0:T(8,128)}, u32[]{:S(2)}) copy-start(s32[1,16,8]{1,2,0:T(8,128)} %param.9) | copy-start | bytes 1540
  73.2 20.5 %all-to-all-start.2 = ((bf16[8,2,16384]{2,1,0:T(2,128)(2,1)}), bf16[8,2,16384]{2,1,0:T(2,128)(2,1)}, u32[]{:S(2)}, u32[]{:S(2)}) async-start(bf16[8,2,16384]{2,1,0:T(2,128)(2,1)} %reshape.230), calls=%async_computation.2 | async-start | bytes 1048576 | tf_op jit(solution)/shard_map/all_to_all | solution.py:137
  78.3 244.4 %reduce-scatter.2.cloned.1.call-start = ((), (), s32[]{:S(2)}) async-start(), calls=%async_computation.7 | async-start | bytes 4325376 | tf_op jit(solution)/shard_map/reduce_scatter | solution.py:165
  180.6 1.0 copy-start.3
  184.2 18.1 %copy-start.1 = (bf16[8,32768]{1,0:T(8,128)(2,1)S(1)}, bf16[8,32768]{1,0:T(8,128)(2,1)}, u32[]{:S(2)}) copy-start(bf16[8,32768]{1,0:T(8,128)(2,1)} %reduce.4) | copy-start | bytes 1572868
Sparse Core Ops, SparseCore 0:
  180.8 141.8 reduce-scatter.1
where the time goes:
time: 332 us; the launch traced here: 331 us
  waiting for transfers between devices  151 us (45%)
  Pallas kernels  42 us (13%)
  local copies, waits for them, and re-layouts  37.7 us (11%)
  blocking collectives  33 us (10%)
  other arithmetic  28.1 us (8%)
  starting transfers between devices  18.4 us (6%)
  between operations  14.3 us (4%)
  matrix products  6.92 us (2%)
    reduce_scatter x1, waiting for transfers between devices, local(): lax.psum_scatter(jnp.einsum('td,htc->dhc', tokens, grad_proj, preferred_e...  119 us
    pallas_call x1, Pallas kernels, attend_group(): pl.pallas_call(attention_kernel, out_shape=(jax.ShapeDtypeStruct((total,...  42 us
    all_to_all x1, waiting for transfers between devices, local(): lax.all_to_all(outgoing, 'seq', split_axis=0, concat_axis=0, tiled=True)  18.7 us
    all_to_all x1, blocking collectives, local(): lax.all_to_all(grad_both.reshape(seq_count, portion * 2 * depth), 'seq',...  18.4 us
    unnamed x23, local copies, waits for them, and re-layouts  15.1 us
    all_to_all x1, blocking collectives, local(): lax.all_to_all(mixed.reshape(seq_count, portion * depth), 'seq', split_ax...  14.6 us
    all_to_all x1, waiting for transfers between devices, local(): lax.all_to_all(sending, 'seq', split_axis=0, concat_axis=0, tiled=True)  11.6 us
    all_to_all x2, other arithmetic, local(): lax.all_to_all(grad_both.reshape(seq_count, portion * 2 * depth), 'seq',...  8.57 us
  transfers between devices with their start and end apart: 5, of which 4 were waited for; matrix products, arithmetic and copies ran while one was open for 10% of the time, Pallas kernels for 0%

commit v1 on v0

--- a/solution.py
+++ b/solution.py
@@ -102,6 +102,9 @@
     room = 2 * tokens_here // seq_count - 1
     rows_here = owned_rows[0]
     targets = seq_position[0]
+    if groups == 1:
+        owned_all = lax.all_gather(rows_here, "seq", axis=0, tiled=True)
+        places_all = lax.all_gather(targets, "seq", axis=0, tiled=True)
     holders = targets // tokens_here
     order_ids = jnp.arange(tokens_here)
     earlier = order_ids[None, :] < order_ids[:, None]
@@ -162,12 +165,29 @@
     seq_grad = jnp.einsum(
         "htc,dhc->td", grad_proj, head_weights, preferred_element_type=jnp.float32
     ).astype(jnp.bfloat16)[None]
-    weight_grad = lax.psum_scatter(
-        jnp.einsum("td,htc->dhc", tokens, grad_proj, preferred_element_type=jnp.float32),
-        ("rec", "seq"),
-        scatter_dimension=0,
-        tiled=True,
-    )
+    if groups == 1:
+        rec_count = lax.axis_size("rec")
+        rows_out = width // (rec_count * seq_count)
+        head_grad = grad_both[places_all]
+        partial = jnp.einsum(
+            "od,oc->dc", owned_all, head_grad, preferred_element_type=jnp.float32
+        )
+        summed = lax.psum_scatter(partial, "rec", scatter_dimension=0, tiled=True)
+        spread = lax.all_to_all(
+            summed.reshape(seq_count, rows_out, 2 * depth),
+            "seq",
+            split_axis=0,
+            concat_axis=0,
+            tiled=True,
+        )
+        weight_grad = jnp.transpose(spread, (1, 0, 2))
+    else:
+        weight_grad = lax.psum_scatter(
+            jnp.einsum("td,htc->dhc", tokens, grad_proj, preferred_element_type=jnp.float32),
+            ("rec", "seq"),
+            scatter_dimension=0,
+            tiled=True,
+        )
     return (attention, seq_grad, weight_grad)
 
 

time: 332 us -> 246 us (0.74)
  waiting for transfers between devices: 151 us -> 61.5 us
  blocking collectives: 33 us -> 15.6 us
  starting transfers between devices: 18.4 us -> 31.6 us
  local copies, waits for them, and re-layouts: 37.7 us -> 44 us
    reduce_scatter x1, waiting for transfers between devices: 119 us -> 0.01 us  [local(): summed = lax.psum_scatter(partial, 'rec', scatter_dimension=0, tiled=True)]
    all_to_all x2 -> x0, blocking collectives: 33 us -> none  [the longest x1 18.4 us: local(): lax.all_to_all(grad_both.reshape(seq_count, portion * 2 * depth), 'seq',...]
    all_to_all x1, waiting for transfers between devices: 18.7 us -> 42.8 us  [local(): lax.all_to_all(outgoing, 'seq', split_axis=0, concat_axis=0, tiled=True)]
    all_to_all x0 -> x3, waiting for transfers between devices: none -> 16.3 us  [the longest x1 12.2 us: local(): lax.all_to_all(grad_both.reshape(seq_count, portion * 2 * depth), 'seq',...]
    all_gather x0 -> x1, blocking collectives: none -> 15.6 us  [local(): places_all = lax.all_gather(targets, 'seq', axis=0, tiled=True)]
    all_to_all x0 -> x3, starting transfers between devices: none -> 13 us  [the longest x1 4.84 us: local(): lax.all_to_all(mixed.reshape(seq_count, portion * depth), 'seq', split_ax...]
    all_to_all x1, waiting for transfers between devices: 11.6 us -> 0.01 us  [local(): lax.all_to_all(sending, 'seq', split_axis=0, concat_axis=0, tiled=True)]
    gather x0 -> x1, local copies, waits for them, and re-layouts: none -> 6.19 us  [local(): head_grad = grad_both[places_all]]
  transfers between devices with their start and end apart: 5 -> 9, of which waited for: 4 -> 4; matrix products, arithmetic and copies ran while one was open for 10% -> 29% of each run, Pallas kernels for 0% -> 17%
where the time goes in v1:
time: 246 us; the launch traced here: 245 us
  waiting for transfers between devices  61.5 us (25%)
  local copies, waits for them, and re-layouts  44 us (18%)
  Pallas kernels  41.9 us (17%)
  starting transfers between devices  31.6 us (13%)
  other arithmetic  28.4 us (12%)
  blocking collectives  15.6 us (6%)
  between operations  14.3 us (6%)
  matrix products  7.82 us (3%)
    all_to_all x1, waiting for transfers between devices, local(): lax.all_to_all(outgoing, 'seq', split_axis=0, concat_axis=0, tiled=True)  42.8 us
    pallas_call x1, Pallas kernels, attend_group(): pl.pallas_call(attention_kernel, out_shape=(jax.ShapeDtypeStruct((total,...  41.9 us
    all_gather x1, blocking collectives, local(): places_all = lax.all_gather(targets, 'seq', axis=0, tiled=True)  15.6 us
    unnamed x21, local copies, waits for them, and re-layouts  12.8 us
    all_to_all x1, waiting for transfers between devices, local(): lax.all_to_all(grad_both.reshape(seq_count, portion * 2 * depth), 'seq',...  12.2 us
    all_to_all x2, other arithmetic, local(): lax.all_to_all(grad_both.reshape(seq_count, portion * 2 * depth), 'seq',...  8.93 us
    all_to_all x2, other arithmetic, local(): lax.all_to_all(sending, 'seq', split_axis=0, concat_axis=0, tiled=True)  8.61 us
    all_to_all x1, starting transfers between devices, local(): lax.all_to_all(labels, 'seq', split_axis=0, concat_axis=0, tiled=True)  6.33 us
  transfers between devices with their start and end apart: 9, of which 4 were waited for; matrix products, arithmetic and copies ran while one was open for 29% of the time, Pallas kernels for 17%

profile of v1, /device:TPU:0, one launch (start us, length us, event | category | flops | bytes accessed | tf_op | source)
XLA Modules:
  0.0 245.2 jit_solution(2552092605210385936)
XLA Ops:
  7.2 0.0 copy-start
  7.2 0.0 all-gather.4.cloned.1.call-start
  7.2 0.7 all-gather.4.cloned.1.call-update
  7.9 0.7 and_select_fusion
  8.6 0.7 and_select_fusion.2
  9.3 0.2 convert_reduce_fusion
  9.5 0.7 compare_select_fusion.3
  10.2 1.6 scatter_custom_fusion
  11.7 0.7 all_to_all.36
  12.4 6.3 %all-to-all-start = ((s32[8,1,63]{2,1,0:T(1,128)}), s32[8,1,63]{2,1,0:T(1,128)S(1)}, u32[]{:S(2)}, u32[]{:S(2)}) async-start(s32[8,1,63]{2,1,0:T(1,128)} %all_to_all.36), calls=%async_computation | async-start | bytes 8192 | tf_op jit(solution)/shard_map/all_to_all | solution.py:124
  18.7 2.5 %scatter_custom_fusion.1 = bf16[504,1024]{1,0:T(8,128)(2,1)S(1)} fusion(s32[256]{0:T(256)S(1)} %bitcast.60, bf16[1,256,1024]{2,1,0:T(8,128)(2,1)} %param.6, bf16[]{:T(256)} %constant.14.clone.1), kind=kCustom, calls=%fused_computation.19 | custom fusion | bytes 1556482 | tf_op jit(solution)/shard_map/scatter | solution.py:114
  21.3 0.0 copy-start.2
  21.3 1.3 reshape.184
  22.6 1.7 all-to-all-done
  24.3 3.6 %all-to-all-start.1 = ((bf16[8,63,1024]{2,1,0:T(8,128)(2,1)}), bf16[8,63,1024]{2,1,0:T(8,128)(2,1)S(1)}, u32[]{:S(2)}, u32[]{:S(2)}) async-start(bf16[8,63,1024]{2,1,0:T(8,128)(2,1)} %reshape.184), calls=%async_computation.1 | async-start | bytes 2097152 | tf_op jit(solution)/shard_map/all_to_all | solution.py:123
  27.8 1.0 copy.44
  28.8 2.0 all_to_all.49
  30.9 0.6 broadcast.169
  31.5 3.2 %reduce.9 = bf16[8,16384]{1,0:T(8,128)(2,1)S(1)} reduce(bf16[8,1,16384]{2,1,0:T(2,128)(2,1)} %all_to_all.49, bf16[]{:T(256)} %broadcast.169), dimensions={1}, to_apply=%all_to_all.49.reduce_sub_computation | reduce | bytes 524290 | tf_op jit(solution)/shard_map/all_to_all | solution.py:141
  34.7 0.9 reshape.246
  35.6 0.1 select_n.80
  35.7 42.8 %all-to-all-done.1 = bf16[8,63,1024]{2,1,0:T(8,128)(2,1)S(1)} async-done(((bf16[8,63,1024]{2,1,0:T(8,128)(2,1)}), bf16[8,63,1024]{2,1,0:T(8,128)(2,1)S(1)}, u32[]{:S(2)}, u32[]{:S(2)}) %all-to-all-start.1) | async-done | bytes 1032224 | tf_op jit(solution)/shard_map/all_to_all | solution.py:123
  78.5 3.4 %all-to-all-start.3 = ((bf16[8,2,8192]{2,1,0:T(2,128)(2,1)}), bf16[8,2,8192]{2,1,0:T(2,128)(2,1)S(1)}, u32[]{:S(2)}, u32[]{:S(2)}) async-start(bf16[8,2,8192]{2,1,0:T(2,128)(2,1)} %reshape.246), calls=%async_computation.3 | async-start | bytes 524288 | tf_op jit(solution)/shard_map/all_to_all | solution.py:141
  82.0 1.3 reshape.218
  83.3 3.6 %scatter_custom_fusion.2 = bf16[256,1024]{1,0:T(8,128)(2,1)S(1)} fusion(s32[504]{0:T(512)S(1)} %bitcast.58, bf16[504,1024]{1,0:T(8,128)(2,1)} %reshape.218, bf16[]{:T(256)} %constant.14.clone.1), kind=kCustom, calls=%fused_computation.24 | custom fusion | bytes 524800 | tf_op jit(solution)/shard_map/scatter | solution.py:132
  86.9 1.5 fusion.15
  88.4 2.0 all_to_all.48
  90.4 4.7 %reduce.8 = bf16[8,32768]{1,0:T(8,128)(2,1)} reduce(bf16[8,1,32768]{2,1,0:T(2,128)(2,1)S(1)} %all_to_all.48, bf16[]{:T(256)} %broadcast.169), dimensions={1}, to_apply=%all_to_all.48.reduce_sub_computation | reduce | bytes 1048578 | tf_op jit(solution)/shard_map/all_to_all | solution.py:140
  95.1 2.2 reshape.244
  97.3 5.0 %all-to-all-start.2 = ((bf16[8,2,16384]{2,1,0:T(2,128)(2,1)}), bf16[8,2,16384]{2,1,0:T(2,128)(2,1)}, u32[]{:S(2)}, u32[]{:S(2)}) async-start(bf16[8,2,16384]{2,1,0:T(2,128)(2,1)} %reshape.244), calls=%async_computation.2 | async-start | bytes 1048576 | tf_op jit(solution)/shard_map/all_to_all | solution.py:140
  102.3 0.7 copy.46.lists_ref
  103.0 15.6 %all-gather = s32[1,2048]{1,0:T(1,128)S(1)} all-gather(s32[1,256]{1,0:T(1,128)S(1)} %copy-done.3), channel_id=2, replica_groups=mesh['rec'=4,'seq'=8] {'seq'}, dimensions={1}, use_global_device_ids=true | all-gather | bytes 9216 | tf_op jit(solution)/shard_map/all_gather | solution.py:107
  118.6 0.3 reshape.247
  118.9 1.6 reduce.2
  120.4 1.3 reshape.187.grad_ref
  121.8 2.2 reshape.245
  124.0 4.0 %reduce.1 = bf16[8,32768]{1,0:T(8,128)(2,1)} reduce(bf16[8,1,32768]{2,1,0:T(2,128)(2,1)S(1)} %reshape.245, bf16[]{:T(256)} %constant.49), dimensions={1}, to_apply=%all_to_all.40.reduce_sub_computation | reduce | bytes 1048578 | tf_op jit(solution)/shard_map/all_to_all | solution.py:140
  128.0 2.1 reshape.186.both_ref
  130.1 41.9 %shard_map.85 = (bf16[2048,64]{1,0:T(8,128)(2,1)}, bf16[2048,128]{1,0:T(8,128)(2,1)}) custom-call(s32[16,8]{1,0:T(8,128)} %copy.46.lists_ref, s32[16]{0:T(128)} %bitcast.61, bf16[2048,128]{1,0:T(8,128)(2,1)} %reshape.186.both_ref, bf16[2048,64]{1,0:T(8,128)(2,1)} %reshape.187.grad_ref), custom_call_target="tpu_custom_call" | custom-call | tf_op jit(solution)/shard_map/pallas_call | solution.py:76
  172.0 1.4 all_to_all.50
  173.4 2.2 reduce.10
  175.6 0.9 reshape.248
  176.5 4.8 %all-to-all-start.4 = ((bf16[8,2,8192]{2,1,0:T(2,128)(2,1)}), bf16[8,2,8192]{2,1,0:T(2,128)(2,1)S(1)}, u32[]{:S(2)}, u32[]{:S(2)}) async-start(bf16[8,2,8192]{2,1,0:T(2,128)(2,1)} %reshape.248), calls=%async_computation.4 | async-start | bytes 524288 | tf_op jit(solution)/shard_map/all_to_all | solution.py:148
  181.4 0.3 reduce-scatter.2.cloned.1.call-start
  181.6 6.2 %gather_fusion = bf16[2048,128]{1,0:T(8,128)(2,1)S(1)} fusion(bf16[2048,128]{1,0:T(8,128)(2,1)S(1)} %copy-done.1, s32[2048]{0:T(1024)S(1)} %fusion.33), kind=kCustom, calls=%fused_computation | custom fusion | bytes 1056768 | tf_op jit(solution)/shard_map/gather | solution.py:171
  187.8 0.0 all-gather.4.cloned.1.call-done
  187.9 3.7 %fusion.21 = f32[1024,128]{0,1:T(8,128)} fusion(bf16[2048,128]{1,0:T(8,128)(2,1)S(1)} %gather_fusion, bf16[1,2048,1024]{2,1,0:T(8,128)(2,1)} %all-gather.4.cloned.1.call-done), kind=kOutput, calls=%fused_computation.15 | convolution fusion | flops 536870912 | bytes 5242880 | tf_op jit(solution)/shard_map/od,oc->dc/dot_general | solution.py:172
  191.6 0.0 reduce-scatter.2.cloned.1.call-update
  191.6 1.6 all_to_all.51
  193.2 5.0 %reduce.11 = bf16[8,32768]{1,0:T(8,128)(2,1)S(1)} reduce(bf16[8,1,32768]{2,1,0:T(2,128)(2,1)} %all_to_all.51, bf16[]{:T(256)} %broadcast.169), dimensions={1}, to_apply=%all_to_all.51.reduce_sub_computation | reduce | bytes 1048578 | tf_op jit(solution)/shard_map/all_to_all | solution.py:155
  198.2 1.2 reshape.250
  199.4 4.8 %all-to-all-start.5 = ((bf16[8,2,16384]{2,1,0:T(2,128)(2,1)}), bf16[8,2,16384]{2,1,0:T(2,128)(2,1)}, u32[]{:S(2)}, u32[]{:S(2)}) async-start(bf16[8,2,16384]{2,1,0:T(2,128)(2,1)} %reshape.250), calls=%async_computation.5 | async-start | bytes 1048576 | tf_op jit(solution)/shard_map/all_to_all | solution.py:155
  204.2 0.3 reshape.249
  204.5 1.6 reduce.3
  206.1 0.5 broadcast_in_dim_reshape.3
  206.6 0.9 copy.51
  207.5 12.2 %all-to-all-done.5 = bf16[8,2,16384]{2,1,0:T(2,128)(2,1)} async-done(((bf16[8,2,16384]{2,1,0:T(2,128)(2,1)}), bf16[8,2,16384]{2,1,0:T(2,128)(2,1)}, u32[]{:S(2)}, u32[]{:S(2)}) %all-to-all-start.5) | async-done | bytes 524320 | tf_op jit(solution)/shard_map/all_to_all | solution.py:155
  219.7 2.2 reshape.251
  221.9 4.0 %reduce.4 = bf16[8,32768]{1,0:T(8,128)(2,1)} reduce(bf16[8,1,32768]{2,1,0:T(2,128)(2,1)S(1)} %reshape.251, bf16[]{:T(256)} %constant.49), dimensions={1}, to_apply=%all_to_all.46.reduce_sub_computation | reduce | bytes 1048578 | tf_op jit(solution)/shard_map/all_to_all | solution.py:155
  225.9 1.7 copy.50
  227.5 3.4 %all-to-all-start.6 = ((f32[8,32,128]{2,1,0:T(8,128)}), f32[8,32,128]{2,1,0:T(8,128)S(1)}, u32[]{:S(2)}, u32[]{:S(2)}) async-start(f32[8,32,128]{2,1,0:T(8,128)} %bitcast.16), calls=%async_computation.7 | async-start | bytes 262144 | tf_op jit(solution)/shard_map/all_to_all | solution.py:176
  230.9 2.6 %fusion.18 = bf16[1,256,1024]{2,1,0:T(8,128)(2,1)} fusion(bf16[1024,8,128]{2,1,0:T(8,128)(2,1)S(1)} %copy-done, bf16[1,8,256,128]{3,1,2,0:T(8,128)(2,1)} %bitcast.50), kind=kOutput, calls=%fused_computation.14 | convolution fusion | flops 537133056 | bytes 3145728 | tf_op jit(solution)/shard_map/htc,dhc->td/dot_general | solution.py:165
  233.5 4.1 %all-to-all-done.6 = f32[8,32,128]{2,1,0:T(8,128)S(1)} async-done(((f32[8,32,128]{2,1,0:T(8,128)}), f32[8,32,128]{2,1,0:T(8,128)S(1)}, u32[]{:S(2)}, u32[]{:S(2)}) %all-to-all-start.6) | async-done | bytes 131104 | tf_op jit(solution)/shard_map/all_to_all | solution.py:176
  237.6 0.7 copy.52
  (15 shorter events, 0.1 us)
Async XLA Ops:
  7.2 79.7 %copy-start = (bf16[1024,8,128]{2,1,0:T(8,128)(2,1)S(1)}, bf16[1024,8,128]{2,1,0:T(8,128)(2,1)}, u32[]{:S(2)}) copy-start(bf16[1024,8,128]{2,1,0:T(8,128)(2,1)} %param.8) | copy-start | bytes 6291460
  7.2 180.7 %all-gather.4.cloned.1.call-start = ((), (), s32[]{:S(2)}) async-start(), calls=%async_computation.9 | async-start | bytes 4718592 | tf_op jit(solution)/shard_map/all_gather | solution.py:106
  12.4 11.8 %all-to-all-start = ((s32[8,1,63]{2,1,0:T(1,128)}), s32[8,1,63]{2,1,0:T(1,128)S(1)}, u32[]{:S(2)}, u32[]{:S(2)}) async-start(s32[8,1,63]{2,1,0:T(1,128)} %all_to_all.36), calls=%async_computation | async-start | bytes 8192 | tf_op jit(solution)/shard_map/all_to_all | solution.py:124
  21.3 6.6 %copy-start.2 = (bf16[1,8,256,64]{2,3,1,0:T(8,128)(2,1)S(1)}, bf16[1,8,256,64]{2,3,1,0:T(8,128)(2,1)}, u32[]{:S(2)}) copy-start(bf16[1,8,256,64]{2,3,1,0:T(8,128)(2,1)} %param.11) | copy-start | bytes 786436
  24.3 54.3 %all-to-all-start.1 = ((bf16[8,63,1024]{2,1,0:T(8,128)(2,1)}), bf16[8,63,1024]{2,1,0:T(8,128)(2,1)S(1)}, u32[]{:S(2)}, u32[]{:S(2)}) async-start(bf16[8,63,1024]{2,1,0:T(8,128)(2,1)} %reshape.184), calls=%async_computation.1 | async-start | bytes 2097152 | tf_op jit(solution)/shard_map/all_to_all | solution.py:123
  78.5 18.8 %all-to-all-start.3 = ((bf16[8,2,8192]{2,1,0:T(2,128)(2,1)}), bf16[8,2,8192]{2,1,0:T(2,128)(2,1)S(1)}, u32[]{:S(2)}, u32[]{:S(2)}) async-start(bf16[8,2,8192]{2,1,0:T(2,128)(2,1)} %reshape.246), calls=%async_computation.3 | async-start | bytes 524288 | tf_op jit(solution)/shard_map/all_to_all | solution.py:141
  90.4 11.9 %copy-start.4 = (s32[1,16,8]{1,2,0:T(8,128)S(1)}, s32[1,16,8]{1,2,0:T(8,128)}, u32[]{:S(2)}) copy-start(s32[1,16,8]{1,2,0:T(8,128)} %param.9) | copy-start | bytes 1540
  90.4 12.6 %copy-start.3 = (s32[1,256]{1,0:T(1,128)S(1)}, s32[1,256]{1,0:T(1,128)}, u32[]{:S(2)}) copy-start(s32[1,256]{1,0:T(1,128)} %param.7) | copy-start | bytes 3076
  97.3 24.4 %all-to-all-start.2 = ((bf16[8,2,16384]{2,1,0:T(2,128)(2,1)}), bf16[8,2,16384]{2,1,0:T(2,128)(2,1)}, u32[]{:S(2)}, u32[]{:S(2)}) async-start(bf16[8,2,16384]{2,1,0:T(2,128)(2,1)} %reshape.244), calls=%async_computation.2 | async-start | bytes 1048576 | tf_op jit(solution)/shard_map/all_to_all | solution.py:140
  172.0 9.6 %copy-start.1 = (bf16[2048,128]{1,0:T(8,128)(2,1)S(1)}, bf16[2048,128]{1,0:T(8,128)(2,1)}, u32[]{:S(2)}) copy-start(bf16[2048,128]{1,0:T(8,128)(2,1)} %get-tuple-element.6) | copy-start | bytes 1572868
  176.5 22.9 %all-to-all-start.4 = ((bf16[8,2,8192]{2,1,0:T(2,128)(2,1)}), bf16[8,2,8192]{2,1,0:T(2,128)(2,1)S(1)}, u32[]{:S(2)}, u32[]{:S(2)}) async-start(bf16[8,2,8192]{2,1,0:T(2,128)(2,1)} %reshape.248), calls=%async_computation.4 | async-start | bytes 524288 | tf_op jit(solution)/shard_map/all_to_all | solution.py:148
  181.4 44.5 %reduce-scatter.2.cloned.1.call-start = ((), (), s32[]{:S(2)}) async-start(), calls=%async_computation.8 | async-start | bytes 655360 | tf_op jit(solution)/shard_map/reduce_scatter | solution.py:175
  199.4 20.3 %all-to-all-start.5 = ((bf16[8,2,16384]{2,1,0:T(2,128)(2,1)}), bf16[8,2,16384]{2,1,0:T(2,128)(2,1)}, u32[]{:S(2)}, u32[]{:S(2)}) async-start(bf16[8,2,16384]{2,1,0:T(2,128)(2,1)} %reshape.250), calls=%async_computation.5 | async-start | bytes 1048576 | tf_op jit(solution)/shard_map/all_to_all | solution.py:155
  227.5 10.1 %all-to-all-start.6 = ((f32[8,32,128]{2,1,0:T(8,128)}), f32[8,32,128]{2,1,0:T(8,128)S(1)}, u32[]{:S(2)}, u32[]{:S(2)}) async-start(f32[8,32,128]{2,1,0:T(8,128)} %bitcast.16), calls=%async_computation.7 | async-start | bytes 262144 | tf_op jit(solution)/shard_map/all_to_all | solution.py:176
Sparse Core Ops, SparseCore 0:
  9.6 72.1 all-gather.3
  191.7 26.0 reduce-scatter.1

commit v2 on v1

--- a/solution.py
+++ b/solution.py
@@ -90,21 +90,9 @@
     )(lists, counts, both, grad_rows)
 
 
-def local(owned_rows, seq_position, head_weights, key_blocks, key_counts, out_grad):
-    seq_count = lax.axis_size("seq")
-    my_index = lax.axis_index("seq")
-    tokens_here = owned_rows.shape[1]
-    width = owned_rows.shape[2]
-    heads = head_weights.shape[1]
-    depth = head_weights.shape[2] // 2
-    groups = seq_count // heads
-    portion = tokens_here // groups
+def route_tokens(rows_here, targets, seq_count, my_index):
+    tokens_here, width = rows_here.shape
     room = 2 * tokens_here // seq_count - 1
-    rows_here = owned_rows[0]
-    targets = seq_position[0]
-    if groups == 1:
-        owned_all = lax.all_gather(rows_here, "seq", axis=0, tiled=True)
-        places_all = lax.all_gather(targets, "seq", axis=0, tiled=True)
     holders = targets // tokens_here
     order_ids = jnp.arange(tokens_here)
     earlier = order_ids[None, :] < order_ids[:, None]
@@ -126,23 +114,49 @@
     local_ids = jnp.where(
         arrived_pos >= 0, arrived_pos - my_index * tokens_here, tokens_here
     ).reshape(-1)
-    tokens = (
+    return (
         jnp.zeros((tokens_here, width), rows_here.dtype)
         .at[local_ids]
         .set(arrived.reshape(-1, width), mode="drop")
     )
-    proj = jnp.einsum(
-        "td,dhc->htc", tokens, head_weights, preferred_element_type=jnp.float32
-    ).astype(jnp.bfloat16)
-    sending = proj.reshape(seq_count, portion * 2 * depth)
+
+
+def local(owned_rows, seq_position, head_weights, key_blocks, key_counts, out_grad):
+    seq_count = lax.axis_size("seq")
+    rec_count = lax.axis_size("rec")
+    my_index = lax.axis_index("seq")
+    tokens_here = owned_rows.shape[1]
+    width = owned_rows.shape[2]
+    heads = head_weights.shape[1]
+    depth = head_weights.shape[2] // 2
+    groups = seq_count // heads
+    portion = tokens_here // groups
+    rows_here = owned_rows[0]
+    targets = seq_position[0]
+    group = my_index % groups
     upstream = out_grad[0].reshape(seq_count, portion * depth)
-    got, got_grad = (
-        lax.all_to_all(sending, "seq", split_axis=0, concat_axis=0, tiled=True),
-        lax.all_to_all(upstream, "seq", split_axis=0, concat_axis=0, tiled=True),
-    )
-    gathered = got.reshape(seq_count * portion, 2 * depth)
+    got_grad = lax.all_to_all(upstream, "seq", split_axis=0, concat_axis=0, tiled=True)
     grad_rows = got_grad.reshape(seq_count * portion, depth)
-    group = my_index % groups
+    if groups == 1:
+        owned_all = lax.all_gather(rows_here, "seq", axis=0, tiled=True)
+        places_all = lax.all_gather(targets, "seq", axis=0, tiled=True)
+        head_w = lax.dynamic_index_in_dim(head_weights, my_index // groups, axis=1, keepdims=False)
+        proj_owned = jnp.dot(owned_all, head_w, preferred_element_type=jnp.float32).astype(
+            jnp.bfloat16
+        )
+        gathered = (
+            jnp.zeros(proj_owned.shape, proj_owned.dtype)
+            .at[places_all]
+            .set(proj_owned, unique_indices=True)
+        )
+    else:
+        tokens = route_tokens(rows_here, targets, seq_count, my_index)
+        proj = jnp.einsum(
+            "td,dhc->htc", tokens, head_weights, preferred_element_type=jnp.float32
+        ).astype(jnp.bfloat16)
+        sending = proj.reshape(seq_count, portion * 2 * depth)
+        got = lax.all_to_all(sending, "seq", split_axis=0, concat_axis=0, tiled=True)
+        gathered = got.reshape(seq_count * portion, 2 * depth)
     mixed, grad_both = attend_group(gathered, grad_rows, key_blocks[group], key_counts[group])
     back_out, back_grad = (
         lax.all_to_all(
@@ -166,7 +180,6 @@
         "htc,dhc->td", grad_proj, head_weights, preferred_element_type=jnp.float32
     ).astype(jnp.bfloat16)[None]
     if groups == 1:
-        rec_count = lax.axis_size("rec")
         rows_out = width // (rec_count * seq_count)
         head_grad = grad_both[places_all]
         partial = jnp.einsum(

time: 246 us -> 185 us (0.75)
  waiting for transfers between devices: 61.5 us -> 42.4 us
  local copies, waits for them, and re-layouts: 44 us -> 28.7 us
  other arithmetic: 28.4 us -> 14.6 us
  starting transfers between devices: 31.6 us -> 18.2 us
  matrix products: 7.82 us -> 10.6 us
    all_to_all x3 -> x0, waiting for transfers between devices: 44.5 us -> none  [the longest x1 42.8 us: local(): lax.all_to_all(outgoing, 'seq', split_axis=0, concat_axis=0, tiled=True)]
    all_gather x1, waiting for transfers between devices: 0.02 us -> 25.4 us  [local(): owned_all = lax.all_gather(rows_here, 'seq', axis=0, tiled=True)]
    all_to_all x3 -> x0, starting transfers between devices: 14.9 us -> none  [the longest x1 6.33 us: local(): lax.all_to_all(labels, 'seq', split_axis=0, concat_axis=0, tiled=True)]
    all_to_all x2 -> x0, other arithmetic: 8.61 us -> none  [local(): lax.all_to_all(sending, 'seq', split_axis=0, concat_axis=0, tiled=True)]
    reshape x3 -> x0, local copies, waits for them, and re-layouts: 4.68 us -> none  [the longest x1 2.1 us: local(): gathered = got.reshape(seq_count * portion, 2 * depth)]
    unnamed x21 -> x16, local copies, waits for them, and re-layouts: 12.8 us -> 8.94 us
    all_to_all x3 -> x0, local copies, waits for them, and re-layouts: 3.28 us -> none  [the longest x2 2.6 us: local(): lax.all_to_all(sending, 'seq', split_axis=0, concat_axis=0, tiled=True)]
    all_to_all x1, starting transfers between devices: 3.41 us -> 6.33 us  [local(): lax.all_to_all(upstream, 'seq', split_axis=0, concat_axis=0, tiled=True)]
  transfers between devices with their start and end apart: 9 -> 6, of which waited for: 4 -> 4; matrix products, arithmetic and copies ran while one was open for 29% -> 20% of each run, Pallas kernels for 17% -> 0%
where the time goes in v2:
time: 185 us; the launch traced here: 184 us
  waiting for transfers between devices  42.4 us (23%)
  Pallas kernels  41.5 us (22%)
  local copies, waits for them, and re-layouts  28.7 us (16%)
  starting transfers between devices  18.2 us (10%)
  other arithmetic  14.6 us (8%)
  between operations  14.2 us (8%)
  blocking collectives  13.5 us (7%)
  matrix products  10.6 us (6%)
    pallas_call x1, Pallas kernels, attend_group(): pl.pallas_call(attention_kernel, out_shape=(jax.ShapeDtypeStruct((total,...  41.5 us
    all_gather x1, waiting for transfers between devices, local(): owned_all = lax.all_gather(rows_here, 'seq', axis=0, tiled=True)  25.4 us
    all_gather x1, blocking collectives, local(): places_all = lax.all_gather(targets, 'seq', axis=0, tiled=True)  13.5 us
    all_to_all x1, waiting for transfers between devices, local(): lax.all_to_all(grad_both.reshape(seq_count, portion * 2 * depth), 'seq',...  12.1 us
    unnamed x16, local copies, waits for them, and re-layouts  8.94 us
    all_to_all x2, other arithmetic, local(): lax.all_to_all(grad_both.reshape(seq_count, portion * 2 * depth), 'seq',...  7.02 us
    scatter x1, local copies, waits for them, and re-layouts, local(): gathered = jnp.zeros(proj_owned.shape, proj_owned.dtype).at[places_all].s...  6.51 us
    all_to_all x1, starting transfers between devices, local(): lax.all_to_all(upstream, 'seq', split_axis=0, concat_axis=0, tiled=True)  6.33 us
  transfers between devices with their start and end apart: 6, of which 4 were waited for; matrix products, arithmetic and copies ran while one was open for 20% of the time, Pallas kernels for 0%

profile of v2, /device:TPU:0, one launch (start us, length us, event | category | flops | bytes accessed | tf_op | source)
XLA Modules:
  0.0 183.7 jit_solution(16073279523506381790)
XLA Ops:
  7.2 0.0 all-gather.4.cloned.1.call-start
  7.2 0.7 all-gather.4.cloned.1.call-update
  7.9 1.2 copy.34
  9.1 0.3 all_to_all.28
  9.5 0.6 broadcast.23
  10.1 2.2 %reduce.3 = bf16[8,16384]{1,0:T(8,128)(2,1)S(1)} reduce(bf16[8,1,16384]{2,1,0:T(2,128)(2,1)S(1)} %all_to_all.28, bf16[]{:T(256)} %broadcast.23), dimensions={1}, to_apply=%all_to_all.28.reduce_sub_computation | reduce | bytes 524290 | tf_op jit(solution)/shard_map/all_to_all | solution.py:138
  12.3 0.9 reshape.58
  13.2 6.3 %all-to-all-start = ((bf16[8,2,8192]{2,1,0:T(2,128)(2,1)}), bf16[8,2,8192]{2,1,0:T(2,128)(2,1)S(1)}, u32[]{:S(2)}, u32[]{:S(2)}) async-start(bf16[8,2,8192]{2,1,0:T(2,128)(2,1)} %reshape.58), calls=%async_computation | async-start | bytes 524288 | tf_op jit(solution)/shard_map/all_to_all | solution.py:138
  19.5 0.0 copy-start.1
  19.5 0.0 copy-start.2
  19.6 2.1 %copy.32 = bf16[1024,8,128]{2,0,1:T(8,128)(2,1)S(1)} copy(bf16[1024,8,128]{2,1,0:T(8,128)(2,1)} %param.8) | data formatting | bytes 4194304 | tf_op args[2]
  21.6 0.0 copy-done.1
  21.6 0.7 copy.36.lists_ref
  22.3 0.0 copy-done.2
  22.3 13.5 %all-gather = s32[1,2048]{1,0:T(1,128)S(1)} all-gather(s32[1,256]{1,0:T(1,128)S(1)} %copy-done.2), channel_id=2, replica_groups=mesh['rec'=4,'seq'=8] {'seq'}, dimensions={1}, use_global_device_ids=true | all-gather | bytes 9216 | tf_op jit(solution)/shard_map/all_gather | solution.py:142
  35.8 0.7 all-to-all-done
  36.5 0.3 reshape.59
  36.8 1.6 reduce
  38.3 1.3 reshape.29.grad_ref
  39.7 25.4 %all-gather.4.cloned.1.call-done = bf16[1,2048,1024]{2,1,0:T(8,128)(2,1)} async-done(((bf16[1,256,1024]{2,1,0:T(8,128)(2,1)}), bf16[1,2048,1024]{2,1,0:T(8,128)(2,1)}) %all-gather.4.cloned.1.call-update) | async-done | bytes 4194320 | tf_op jit(solution)/shard_map/all_gather | solution.py:141
  65.0 3.7 %fusion.7 = bf16[2048,128]{0,1:T(8,128)(2,1)S(1)} fusion(bf16[1,2048,1024]{2,1,0:T(8,128)(2,1)} %all-gather.4.cloned.1.call-done, bf16[1024,8,128]{2,0,1:T(8,128)(2,1)S(1)} %copy.32, s32[]{:T(128)S(6)} %select_n.18), kind=kOutput, calls=%fused_computation.7 | convolution fusion | flops 537133056 | bytes 4980740 | tf_op jit(solution)/shard_map/dot_general | solution.py:144
  68.7 0.3 copy.33
  69.0 6.5 %scatter_custom_fusion.both_ref = bf16[2048,128]{1,0:T(8,128)(2,1)} fusion(s32[2048]{0:T(1024)S(1)} %get-tuple-element.17, bf16[2048,128]{1,0:T(8,128)(2,1)S(1)} %copy.33, bf16[]{:T(256)} %constant.29.clone.1), kind=kCustom, calls=%fused_computation.16 | custom fusion | bytes 524290 | tf_op jit(solution)/shard_map/scatter | solution.py:150
  75.5 41.5 %shard_map.85 = (bf16[2048,64]{1,0:T(8,128)(2,1)}, bf16[2048,128]{1,0:T(8,128)(2,1)}) custom-call(s32[16,8]{1,0:T(8,128)} %copy.36.lists_ref, s32[16]{0:T(128)} %bitcast.42, bf16[2048,128]{1,0:T(8,128)(2,1)} %scatter_custom_fusion.both_ref, bf16[2048,64]{1,0:T(8,128)(2,1)} %reshape.29.grad_ref), custom_call_target="tpu_custom_call" | custom-call | tf_op jit(solution)/shard_map/pallas_call | solution.py:76
  117.0 0.0 copy-start
  117.0 1.4 all_to_all.29
  118.4 2.2 %reduce.4 = bf16[8,16384]{1,0:T(8,128)(2,1)S(1)} reduce(bf16[8,1,16384]{2,1,0:T(2,128)(2,1)S(1)} %all_to_all.29, bf16[]{:T(256)} %broadcast.23), dimensions={1}, to_apply=%all_to_all.29.reduce_sub_computation | reduce | bytes 524290 | tf_op jit(solution)/shard_map/all_to_all | solution.py:162
  120.6 0.9 reshape.60
  121.5 3.4 %all-to-all-start.1 = ((bf16[8,2,8192]{2,1,0:T(2,128)(2,1)}), bf16[8,2,8192]{2,1,0:T(2,128)(2,1)S(1)}, u32[]{:S(2)}, u32[]{:S(2)}) async-start(bf16[8,2,8192]{2,1,0:T(2,128)(2,1)} %reshape.60), calls=%async_computation.1 | async-start | bytes 524288 | tf_op jit(solution)/shard_map/all_to_all | solution.py:162
  124.9 0.2 reduce-scatter.2.cloned.1.call-start
  125.2 0.0 copy-done
  125.2 6.2 %gather_fusion = bf16[2048,128]{1,0:T(8,128)(2,1)S(1)} fusion(bf16[2048,128]{1,0:T(8,128)(2,1)S(1)} %copy-done, s32[2048]{0:T(1024)S(1)} %get-tuple-element.16), kind=kCustom, calls=%fused_computation | custom fusion | bytes 1056768 | tf_op jit(solution)/shard_map/gather | solution.py:184
  131.4 3.7 %fusion.12 = f32[1024,128]{0,1:T(8,128)} fusion(bf16[2048,128]{1,0:T(8,128)(2,1)S(1)} %gather_fusion, bf16[1,2048,1024]{2,1,0:T(8,128)(2,1)} %all-gather.4.cloned.1.call-done), kind=kOutput, calls=%fused_computation.11 | convolution fusion | flops 536870912 | bytes 5242880 | tf_op jit(solution)/shard_map/od,oc->dc/dot_general | solution.py:185
  135.1 0.0 reduce-scatter.2.cloned.1.call-update
  135.1 0.3 all_to_all.30
  135.4 3.9 %reduce.5 = bf16[8,32768]{1,0:T(8,128)(2,1)S(1)} reduce(bf16[8,1,32768]{2,1,0:T(2,128)(2,1)S(1)} %all_to_all.30, bf16[]{:T(256)} %broadcast.23), dimensions={1}, to_apply=%all_to_all.30.reduce_sub_computation | reduce | bytes 1048578 | tf_op jit(solution)/shard_map/all_to_all | solution.py:169
  139.3 1.2 reshape.62
  140.4 0.0 all-to-all-done.1
  140.4 4.8 %all-to-all-start.2 = ((bf16[8,2,16384]{2,1,0:T(2,128)(2,1)}), bf16[8,2,16384]{2,1,0:T(2,128)(2,1)S(1)}, u32[]{:S(2)}, u32[]{:S(2)}) async-start(bf16[8,2,16384]{2,1,0:T(2,128)(2,1)} %reshape.62), calls=%async_computation.2 | async-start | bytes 1048576 | tf_op jit(solution)/shard_map/all_to_all | solution.py:169
  145.2 0.3 reshape.61
  145.5 1.6 reduce.1
  147.1 0.5 broadcast_in_dim_reshape.3
  147.6 0.9 copy.41
  148.5 12.1 %all-to-all-done.2 = bf16[8,2,16384]{2,1,0:T(2,128)(2,1)S(1)} async-done(((bf16[8,2,16384]{2,1,0:T(2,128)(2,1)}), bf16[8,2,16384]{2,1,0:T(2,128)(2,1)S(1)}, u32[]{:S(2)}, u32[]{:S(2)}) %all-to-all-start.2) | async-done | bytes 524320 | tf_op jit(solution)/shard_map/all_to_all | solution.py:169
  160.6 0.5 reshape.63
  161.1 3.2 %reduce.2 = bf16[8,32768]{1,0:T(8,128)(2,1)S(1)} reduce(bf16[8,1,32768]{2,1,0:T(2,128)(2,1)S(1)} %reshape.63, bf16[]{:T(256)} %constant.37), dimensions={1}, to_apply=%all_to_all.26.reduce_sub_computation | reduce | bytes 1048578 | tf_op jit(solution)/shard_map/all_to_all | solution.py:169
  164.3 0.0 reduce-scatter.2.cloned.1.call-done
  164.3 1.7 copy.40
  166.0 3.4 %all-to-all-start.3 = ((f32[8,32,128]{2,1,0:T(8,128)}), f32[8,32,128]{2,1,0:T(8,128)S(1)}, u32[]{:S(2)}, u32[]{:S(2)}) async-start(f32[8,32,128]{2,1,0:T(8,128)} %bitcast.9), calls=%async_computation.4 | async-start | bytes 262144 | tf_op jit(solution)/shard_map/all_to_all | solution.py:189
  169.4 3.1 %fusion.11 = bf16[1,256,1024]{2,1,0:T(8,128)(2,1)} fusion(bf16[1,8,256,128]{3,1,2,0:T(8,128)(2,1)S(1)} %bitcast.38, bf16[1024,8,128]{2,1,0:T(8,128)(2,1)} %param.8), kind=kOutput, calls=%fused_computation.10 | convolution fusion | flops 537133056 | bytes 3145728 | tf_op jit(solution)/shard_map/htc,dhc->td/dot_general | solution.py:179
  172.5 3.6 %all-to-all-done.3 = f32[8,32,128]{2,1,0:T(8,128)S(1)} async-done(((f32[8,32,128]{2,1,0:T(8,128)}), f32[8,32,128]{2,1,0:T(8,128)S(1)}, u32[]{:S(2)}, u32[]{:S(2)}) %all-to-all-start.3) | async-done | bytes 131104 | tf_op jit(solution)/shard_map/all_to_all | solution.py:189
  176.1 0.7 copy.42
  (1 shorter events, 0.0 us)
Async XLA Ops:
  7.2 57.9 %all-gather.4.cloned.1.call-start = ((), (), s32[]{:S(2)}) async-start(), calls=%async_computation.6 | async-start | bytes 4718592 | tf_op jit(solution)/shard_map/all_gather | solution.py:141
  13.2 23.3 %all-to-all-start = ((bf16[8,2,8192]{2,1,0:T(2,128)(2,1)}), bf16[8,2,8192]{2,1,0:T(2,128)(2,1)S(1)}, u32[]{:S(2)}, u32[]{:S(2)}) async-start(bf16[8,2,8192]{2,1,0:T(2,128)(2,1)} %reshape.58), calls=%async_computation | async-start | bytes 524288 | tf_op jit(solution)/shard_map/all_to_all | solution.py:138
  19.5 2.1 %copy-start.1 = (s32[1,16,8]{1,2,0:T(8,128)S(1)}, s32[1,16,8]{1,2,0:T(8,128)}, u32[]{:S(2)}) copy-start(s32[1,16,8]{1,2,0:T(8,128)} %param.9) | copy-start | bytes 1540
  19.5 2.8 %copy-start.2 = (s32[1,256]{1,0:T(1,128)S(1)}, s32[1,256]{1,0:T(1,128)}, u32[]{:S(2)}) copy-start(s32[1,256]{1,0:T(1,128)} %param.7) | copy-start | bytes 3076
  117.0 8.2 %copy-start = (bf16[2048,128]{1,0:T(8,128)(2,1)S(1)}, bf16[2048,128]{1,0:T(8,128)(2,1)}, u32[]{:S(2)}) copy-start(bf16[2048,128]{1,0:T(8,128)(2,1)} %get-tuple-element.6) | copy-start | bytes 1572868
  121.5 18.9 %all-to-all-start.1 = ((bf16[8,2,8192]{2,1,0:T(2,128)(2,1)}), bf16[8,2,8192]{2,1,0:T(2,128)(2,1)S(1)}, u32[]{:S(2)}, u32[]{:S(2)}) async-start(bf16[8,2,8192]{2,1,0:T(2,128)(2,1)} %reshape.60), calls=%async_computation.1 | async-start | bytes 524288 | tf_op jit(solution)/shard_map/all_to_all | solution.py:162
  124.9 39.4 %reduce-scatter.2.cloned.1.call-start = ((), (), s32[]{:S(2)}) async-start(), calls=%async_computation.5 | async-start | bytes 655360 | tf_op jit(solution)/shard_map/reduce_scatter | solution.py:188
  140.4 20.2 %all-to-all-start.2 = ((bf16[8,2,16384]{2,1,0:T(2,128)(2,1)}), bf16[8,2,16384]{2,1,0:T(2,128)(2,1)S(1)}, u32[]{:S(2)}, u32[]{:S(2)}) async-start(bf16[8,2,16384]{2,1,0:T(2,128)(2,1)} %reshape.62), calls=%async_computation.2 | async-start | bytes 1048576 | tf_op jit(solution)/shard_map/all_to_all | solution.py:169
  166.0 10.1 %all-to-all-start.3 = ((f32[8,32,128]{2,1,0:T(8,128)}), f32[8,32,128]{2,1,0:T(8,128)S(1)}, u32[]{:S(2)}, u32[]{:S(2)}) async-start(f32[8,32,128]{2,1,0:T(8,128)} %bitcast.9), calls=%async_computation.4 | async-start | bytes 262144 | tf_op jit(solution)/shard_map/all_to_all | solution.py:189
Sparse Core Ops, SparseCore 0:
  9.6 55.3 all-gather.3
  135.2 25.9 reduce-scatter.1

commit v3 on v2

--- a/solution.py
+++ b/solution.py
@@ -139,11 +139,19 @@
     grad_rows = got_grad.reshape(seq_count * portion, depth)
     if groups == 1:
         owned_all = lax.all_gather(rows_here, "seq", axis=0, tiled=True)
-        places_all = lax.all_gather(targets, "seq", axis=0, tiled=True)
-        head_w = lax.dynamic_index_in_dim(head_weights, my_index // groups, axis=1, keepdims=False)
-        proj_owned = jnp.dot(owned_all, head_w, preferred_element_type=jnp.float32).astype(
-            jnp.bfloat16
-        )
+        places_all = lax.all_to_all(
+            jnp.broadcast_to(targets[None], (seq_count, tokens_here)),
+            "seq",
+            split_axis=0,
+            concat_axis=0,
+            tiled=True,
+        ).reshape(-1)
+        proj_mine = jnp.einsum(
+            "td,dhc->htc", rows_here, head_weights, preferred_element_type=jnp.float32
+        ).astype(jnp.bfloat16)
+        proj_owned = lax.all_to_all(
+            proj_mine, "seq", split_axis=0, concat_axis=0, tiled=True
+        ).reshape(seq_count * tokens_here, 2 * depth)
         gathered = (
             jnp.zeros(proj_owned.shape, proj_owned.dtype)
             .at[places_all]

time: 185 us -> 189 us (1.022)
  blocking collectives: 13.5 us -> 0 us
  waiting for transfers between devices: 42.4 us -> 53.3 us
  starting transfers between devices: 18.2 us -> 26.5 us
    all_gather x1, waiting for transfers between devices: 25.4 us -> 0.02 us  [local(): owned_all = lax.all_gather(rows_here, 'seq', axis=0, tiled=True)]
    all_to_all x0 -> x2, waiting for transfers between devices: none -> 23.1 us  [the longest x1 22.9 us: local(): lax.all_to_all(proj_mine, 'seq', split_axis=0, concat_axis=0, tiled=True)]
    all_gather x1 -> x0, blocking collectives: 13.5 us -> none  [local(): places_all = lax.all_gather(targets, 'seq', axis=0, tiled=True)]
    all_to_all x1, waiting for transfers between devices: 0.69 us -> 13.8 us  [local(): lax.all_to_all(upstream, 'seq', split_axis=0, concat_axis=0, tiled=True)]
    all_to_all x0 -> x2, starting transfers between devices: none -> 9.82 us  [the longest x1 6.33 us: local(): lax.all_to_all(jnp.broadcast_to(targets[None], (seq_count, tokens_here)),...]
    unnamed x16 -> x15, local copies, waits for them, and re-layouts: 8.94 us -> 6.9 us
  transfers between devices with their start and end apart: 6 -> 8, of which waited for: 4 -> 5; matrix products, arithmetic and copies ran while one was open for 20% -> 26% of each run, Pallas kernels for 0% -> 22%
where the time goes in v3:
time: 189 us; the launch traced here: 188 us
  waiting for transfers between devices  53.3 us (28%)
  Pallas kernels  41.3 us (22%)
  local copies, waits for them, and re-layouts  27.9 us (15%)
  starting transfers between devices  26.5 us (14%)
  other arithmetic  14.8 us (8%)
  between operations  14.2 us (8%)
  matrix products  10.1 us (5%)
    pallas_call x1, Pallas kernels, attend_group(): pl.pallas_call(attention_kernel, out_shape=(jax.ShapeDtypeStruct((total,...  41.3 us
    all_to_all x1, waiting for transfers between devices, local(): lax.all_to_all(proj_mine, 'seq', split_axis=0, concat_axis=0, tiled=True)  22.9 us
    all_to_all x1, waiting for transfers between devices, local(): lax.all_to_all(upstream, 'seq', split_axis=0, concat_axis=0, tiled=True)  13.8 us
    all_to_all x1, waiting for transfers between devices, local(): lax.all_to_all(grad_both.reshape(seq_count, portion * 2 * depth), 'seq',...  12.1 us
    all_to_all x2, other arithmetic, local(): lax.all_to_all(grad_both.reshape(seq_count, portion * 2 * depth), 'seq',...  7.02 us
    unnamed x15, local copies, waits for them, and re-layouts  6.9 us
    scatter x1, local copies, waits for them, and re-layouts, local(): gathered = jnp.zeros(proj_owned.shape, proj_owned.dtype).at[places_all].s...  6.51 us
    all_to_all x1, starting transfers between devices, local(): lax.all_to_all(jnp.broadcast_to(targets[None], (seq_count, tokens_here)),...  6.33 us
  transfers between devices with their start and end apart: 8, of which 5 were waited for; matrix products, arithmetic and copies ran while one was open for 26% of the time, Pallas kernels for 22%

profile of v3, /device:TPU:0, one launch (start us, length us, event | category | flops | bytes accessed | tf_op | source)
XLA Modules:
  0.0 188.2 jit_solution(17178184406927479499)
XLA Ops:
  7.2 0.0 copy-start.1
  7.2 0.0 all-gather.3.cloned.1.call-start
  7.2 0.7 all-gather.3.cloned.1.call-update
  7.9 1.3 broadcast_in_dim.14
  9.2 6.3 %all-to-all-start = ((s32[8,1,256]{2,1,0:T(1,128)}), s32[8,1,256]{2,1,0:T(1,128)S(1)}, u32[]{:S(2)}, u32[]{:S(2)}) async-start(s32[8,1,256]{2,1,0:T(1,128)} %broadcast_in_dim.14), calls=%async_computation | async-start | bytes 16384 | tf_op jit(solution)/shard_map/all_to_all | solution.py:142
  15.5 1.2 copy.35
  16.7 0.3 all_to_all.37
  17.1 0.6 broadcast.36
  17.7 2.3 %reduce.3 = bf16[8,16384]{1,0:T(8,128)(2,1)S(1)} reduce(bf16[8,1,16384]{2,1,0:T(2,128)(2,1)S(1)} %all_to_all.37, bf16[]{:T(256)} %broadcast.36), dimensions={1}, to_apply=%all_to_all.37.reduce_sub_computation | reduce | bytes 524290 | tf_op jit(solution)/shard_map/all_to_all | solution.py:138
  20.0 0.9 reshape.99
  20.9 0.2 all-to-all-done
  21.1 4.9 %all-to-all-start.2 = ((bf16[8,2,8192]{2,1,0:T(2,128)(2,1)}), bf16[8,2,8192]{2,1,0:T(2,128)(2,1)S(1)}, u32[]{:S(2)}, u32[]{:S(2)}) async-start(bf16[8,2,8192]{2,1,0:T(2,128)(2,1)} %reshape.99), calls=%async_computation.2 | async-start | bytes 524288 | tf_op jit(solution)/shard_map/all_to_all | solution.py:138
  26.0 0.0 copy-done.1
  26.0 0.0 copy-start.2
  26.0 3.2 %fusion.15 = bf16[8,256,128]{1,2,0:T(8,128)(2,1)} fusion(bf16[1024,8,128]{2,1,0:T(8,128)(2,1)} %param.8, bf16[1,256,1024]{2,1,0:T(8,128)(2,1)S(1)} %copy-done.1), kind=kOutput, calls=%fused_computation.11 | convolution fusion | flops 537133056 | bytes 3145728 | tf_op jit(solution)/shard_map/td,dhc->htc/dot_general | solution.py:149
  29.2 13.8 %all-to-all-done.2 = bf16[8,2,8192]{2,1,0:T(2,128)(2,1)S(1)} async-done(((bf16[8,2,8192]{2,1,0:T(2,128)(2,1)}), bf16[8,2,8192]{2,1,0:T(2,128)(2,1)S(1)}, u32[]{:S(2)}, u32[]{:S(2)}) %all-to-all-start.2) | async-done | bytes 262176 | tf_op jit(solution)/shard_map/all_to_all | solution.py:138
  43.0 3.5 %all-to-all-start.1 = ((bf16[8,256,128]{1,2,0:T(8,128)(2,1)}), bf16[8,256,128]{1,2,0:T(8,128)(2,1)S(1)}, u32[]{:S(2)}, u32[]{:S(2)}) async-start(bf16[8,256,128]{1,2,0:T(8,128)(2,1)} %fusion.15), calls=%async_computation.1 | async-start | bytes 1048576 | tf_op jit(solution)/shard_map/all_to_all | solution.py:152
  46.5 0.0 copy-done.2
  46.5 0.7 copy.37.lists_ref
  47.2 0.3 reshape.100
  47.5 1.6 reduce
  49.1 1.3 reshape.72.grad_ref
  50.4 22.9 %all-to-all-done.1 = bf16[8,256,128]{1,2,0:T(8,128)(2,1)S(1)} async-done(((bf16[8,256,128]{1,2,0:T(8,128)(2,1)}), bf16[8,256,128]{1,2,0:T(8,128)(2,1)S(1)}, u32[]{:S(2)}, u32[]{:S(2)}) %all-to-all-start.1) | async-done | bytes 524320 | tf_op jit(solution)/shard_map/all_to_all | solution.py:152
  73.3 0.3 copy.34
  73.6 6.5 %scatter_custom_fusion.both_ref = bf16[2048,128]{1,0:T(8,128)(2,1)} fusion(s32[2048]{0:T(1024)S(1)} %bitcast.41, bf16[2048,128]{1,0:T(8,128)(2,1)S(1)} %bitcast.37, bf16[]{:T(256)} %constant.6.clone.1), kind=kCustom, calls=%fused_computation.17 | custom fusion | bytes 524290 | tf_op jit(solution)/shard_map/scatter | solution.py:158
  80.1 41.3 %shard_map.88 = (bf16[2048,64]{1,0:T(8,128)(2,1)}, bf16[2048,128]{1,0:T(8,128)(2,1)}) custom-call(s32[16,8]{1,0:T(8,128)} %copy.37.lists_ref, s32[16]{0:T(128)} %bitcast.44, bf16[2048,128]{1,0:T(8,128)(2,1)} %scatter_custom_fusion.both_ref, bf16[2048,64]{1,0:T(8,128)(2,1)} %reshape.72.grad_ref), custom_call_target="tpu_custom_call" | custom-call | tf_op jit(solution)/shard_map/pallas_call | solution.py:76
  121.4 0.0 copy-start
  121.4 1.4 all_to_all.38
  122.8 2.3 %reduce.4 = bf16[8,16384]{1,0:T(8,128)(2,1)S(1)} reduce(bf16[8,1,16384]{2,1,0:T(2,128)(2,1)S(1)} %all_to_all.38, bf16[]{:T(256)} %broadcast.36), dimensions={1}, to_apply=%all_to_all.38.reduce_sub_computation | reduce | bytes 524290 | tf_op jit(solution)/shard_map/all_to_all | solution.py:170
  125.2 0.9 reshape.101
  126.1 3.4 %all-to-all-start.3 = ((bf16[8,2,8192]{2,1,0:T(2,128)(2,1)}), bf16[8,2,8192]{2,1,0:T(2,128)(2,1)S(1)}, u32[]{:S(2)}, u32[]{:S(2)}) async-start(bf16[8,2,8192]{2,1,0:T(2,128)(2,1)} %reshape.101), calls=%async_computation.3 | async-start | bytes 524288 | tf_op jit(solution)/shard_map/all_to_all | solution.py:170
  129.5 0.2 reduce-scatter.2.cloned.1.call-start
  129.7 0.0 copy-done
  129.7 6.2 %gather_fusion = bf16[2048,128]{1,0:T(8,128)(2,1)S(1)} fusion(bf16[2048,128]{1,0:T(8,128)(2,1)S(1)} %copy-done, s32[2048]{0:T(1024)S(1)} %broadcast_clamp_fusion), kind=kCustom, calls=%fused_computation | custom fusion | bytes 1056768 | tf_op jit(solution)/shard_map/gather | solution.py:192
  135.9 0.0 all-gather.3.cloned.1.call-done
  135.9 3.7 %fusion.21 = f32[1024,128]{0,1:T(8,128)} fusion(bf16[2048,128]{1,0:T(8,128)(2,1)S(1)} %gather_fusion, bf16[1,2048,1024]{2,1,0:T(8,128)(2,1)} %all-gather.3.cloned.1.call-done), kind=kOutput, calls=%fused_computation.13 | convolution fusion | flops 536870912 | bytes 5242880 | tf_op jit(solution)/shard_map/od,oc->dc/dot_general | solution.py:193
  139.7 0.0 reduce-scatter.2.cloned.1.call-update
  139.7 0.3 all_to_all.39
  140.0 3.9 %reduce.5 = bf16[8,32768]{1,0:T(8,128)(2,1)S(1)} reduce(bf16[8,1,32768]{2,1,0:T(2,128)(2,1)S(1)} %all_to_all.39, bf16[]{:T(256)} %broadcast.36), dimensions={1}, to_apply=%all_to_all.39.reduce_sub_computation | reduce | bytes 1048578 | tf_op jit(solution)/shard_map/all_to_all | solution.py:177
  143.8 1.2 reshape.103
  145.0 0.0 all-to-all-done.3
  145.0 4.8 %all-to-all-start.4 = ((bf16[8,2,16384]{2,1,0:T(2,128)(2,1)}), bf16[8,2,16384]{2,1,0:T(2,128)(2,1)S(1)}, u32[]{:S(2)}, u32[]{:S(2)}) async-start(bf16[8,2,16384]{2,1,0:T(2,128)(2,1)} %reshape.103), calls=%async_computation.4 | async-start | bytes 1048576 | tf_op jit(solution)/shard_map/all_to_all | solution.py:177
  149.8 0.3 reshape.102
  150.1 1.6 reduce.1
  151.6 0.5 broadcast_in_dim_reshape.3
  152.2 0.9 copy.42
  153.1 12.1 %all-to-all-done.4 = bf16[8,2,16384]{2,1,0:T(2,128)(2,1)S(1)} async-done(((bf16[8,2,16384]{2,1,0:T(2,128)(2,1)}), bf16[8,2,16384]{2,1,0:T(2,128)(2,1)S(1)}, u32[]{:S(2)}, u32[]{:S(2)}) %all-to-all-start.4) | async-done | bytes 524320 | tf_op jit(solution)/shard_map/all_to_all | solution.py:177
  165.2 0.5 reshape.104
  165.7 3.2 %reduce.2 = bf16[8,32768]{1,0:T(8,128)(2,1)S(1)} reduce(bf16[8,1,32768]{2,1,0:T(2,128)(2,1)S(1)} %reshape.104, bf16[]{:T(256)} %constant.21), dimensions={1}, to_apply=%all_to_all.35.reduce_sub_computation | reduce | bytes 1048578 | tf_op jit(solution)/shard_map/all_to_all | solution.py:177
  168.9 0.0 reduce-scatter.2.cloned.1.call-done
  168.9 1.7 copy.41
  170.6 3.4 %all-to-all-start.5 = ((f32[8,32,128]{2,1,0:T(8,128)}), f32[8,32,128]{2,1,0:T(8,128)S(1)}, u32[]{:S(2)}, u32[]{:S(2)}) async-start(f32[8,32,128]{2,1,0:T(8,128)} %bitcast.13), calls=%async_computation.6 | async-start | bytes 262144 | tf_op jit(solution)/shard_map/all_to_all | solution.py:197
  173.9 3.1 %fusion.18 = bf16[1,256,1024]{2,1,0:T(8,128)(2,1)} fusion(bf16[1024,8,128]{2,1,0:T(8,128)(2,1)} %param.8, bf16[1,8,256,128]{3,1,2,0:T(8,128)(2,1)S(1)} %bitcast.36), kind=kOutput, calls=%fused_computation.12 | convolution fusion | flops 537133056 | bytes 3145728 | tf_op jit(solution)/shard_map/htc,dhc->td/dot_general | solution.py:187
  177.1 3.6 %all-to-all-done.5 = f32[8,32,128]{2,1,0:T(8,128)S(1)} async-done(((f32[8,32,128]{2,1,0:T(8,128)}), f32[8,32,128]{2,1,0:T(8,128)S(1)}, u32[]{:S(2)}, u32[]{:S(2)}) %all-to-all-start.5) | async-done | bytes 131104 | tf_op jit(solution)/shard_map/all_to_all | solution.py:197
  180.7 0.7 copy.43
  (2 shorter events, 0.0 us)
Async XLA Ops:
  7.2 18.8 %copy-start.1 = (bf16[1,256,1024]{2,1,0:T(8,128)(2,1)S(1)}, bf16[1,256,1024]{2,1,0:T(8,128)(2,1)}, u32[]{:S(2)}) copy-start(bf16[1,256,1024]{2,1,0:T(8,128)(2,1)} %param.6) | copy-start | bytes 1572868
  7.2 128.8 %all-gather.3.cloned.1.call-start = ((), (), s32[]{:S(2)}) async-start(), calls=%async_computation.8 | async-start | bytes 4718592 | tf_op jit(solution)/shard_map/all_gather | solution.py:141
  9.2 11.9 %all-to-all-start = ((s32[8,1,256]{2,1,0:T(1,128)}), s32[8,1,256]{2,1,0:T(1,128)S(1)}, u32[]{:S(2)}, u32[]{:S(2)}) async-start(s32[8,1,256]{2,1,0:T(1,128)} %broadcast_in_dim.14), calls=%async_computation | async-start | bytes 16384 | tf_op jit(solution)/shard_map/all_to_all | solution.py:142
  21.1 21.9 %all-to-all-start.2 = ((bf16[8,2,8192]{2,1,0:T(2,128)(2,1)}), bf16[8,2,8192]{2,1,0:T(2,128)(2,1)S(1)}, u32[]{:S(2)}, u32[]{:S(2)}) async-start(bf16[8,2,8192]{2,1,0:T(2,128)(2,1)} %reshape.99), calls=%async_computation.2 | async-start | bytes 524288 | tf_op jit(solution)/shard_map/all_to_all | solution.py:138
  26.0 20.5 %copy-start.2 = (s32[1,16,8]{1,2,0:T(8,128)S(1)}, s32[1,16,8]{1,2,0:T(8,128)}, u32[]{:S(2)}) copy-start(s32[1,16,8]{1,2,0:T(8,128)} %param.9) | copy-start | bytes 1540
  43.0 30.3 %all-to-all-start.1 = ((bf16[8,256,128]{1,2,0:T(8,128)(2,1)}), bf16[8,256,128]{1,2,0:T(8,128)(2,1)S(1)}, u32[]{:S(2)}, u32[]{:S(2)}) async-start(bf16[8,256,128]{1,2,0:T(8,128)(2,1)} %fusion.15), calls=%async_computation.1 | async-start | bytes 1048576 | tf_op jit(solution)/shard_map/all_to_all | solution.py:152
  121.4 8.3 %copy-start = (bf16[2048,128]{1,0:T(8,128)(2,1)S(1)}, bf16[2048,128]{1,0:T(8,128)(2,1)}, u32[]{:S(2)}) copy-start(bf16[2048,128]{1,0:T(8,128)(2,1)} %get-tuple-element.6) | copy-start | bytes 1572868
  126.1 19.0 %all-to-all-start.3 = ((bf16[8,2,8192]{2,1,0:T(2,128)(2,1)}), bf16[8,2,8192]{2,1,0:T(2,128)(2,1)S(1)}, u32[]{:S(2)}, u32[]{:S(2)}) async-start(bf16[8,2,8192]{2,1,0:T(2,128)(2,1)} %reshape.101), calls=%async_computation.3 | async-start | bytes 524288 | tf_op jit(solution)/shard_map/all_to_all | solution.py:170
  129.5 39.4 %reduce-scatter.2.cloned.1.call-start = ((), (), s32[]{:S(2)}) async-start(), calls=%async_computation.7 | async-start | bytes 655360 | tf_op jit(solution)/shard_map/reduce_scatter | solution.py:196
  145.0 20.2 %all-to-all-start.4 = ((bf16[8,2,16384]{2,1,0:T(2,128)(2,1)}), bf16[8,2,16384]{2,1,0:T(2,128)(2,1)S(1)}, u32[]{:S(2)}, u32[]{:S(2)}) async-start(bf16[8,2,16384]{2,1,0:T(2,128)(2,1)} %reshape.103), calls=%async_computation.4 | async-start | bytes 1048576 | tf_op jit(solution)/shard_map/all_to_all | solution.py:177
  170.6 10.1 %all-to-all-start.5 = ((f32[8,32,128]{2,1,0:T(8,128)}), f32[8,32,128]{2,1,0:T(8,128)S(1)}, u32[]{:S(2)}, u32[]{:S(2)}) async-start(f32[8,32,128]{2,1,0:T(8,128)} %bitcast.13), calls=%async_computation.6 | async-start | bytes 262144 | tf_op jit(solution)/shard_map/all_to_all | solution.py:197
Sparse Core Ops, SparseCore 0:
  9.6 66.5 all-gather.2
  139.8 25.9 reduce-scatter.1

commit v4 on v3

--- a/solution.py
+++ b/solution.py
@@ -138,7 +138,6 @@
     got_grad = lax.all_to_all(upstream, "seq", split_axis=0, concat_axis=0, tiled=True)
     grad_rows = got_grad.reshape(seq_count * portion, depth)
     if groups == 1:
-        owned_all = lax.all_gather(rows_here, "seq", axis=0, tiled=True)
         places_all = lax.all_to_all(
             jnp.broadcast_to(targets[None], (seq_count, tokens_here)),
             "seq",
@@ -152,6 +151,10 @@
         proj_owned = lax.all_to_all(
             proj_mine, "seq", split_axis=0, concat_axis=0, tiled=True
         ).reshape(seq_count * tokens_here, 2 * depth)
+        later_rows, proj_owned, grad_rows, places_all = lax.optimization_barrier(
+            (rows_here, proj_owned, grad_rows, places_all)
+        )
+        owned_all = lax.all_gather(later_rows, "seq", axis=0, tiled=True)
         gathered = (
             jnp.zeros(proj_owned.shape, proj_owned.dtype)
             .at[places_all]

time: 189 us -> 171 us (0.905)
  waiting for transfers between devices: 53.3 us -> 25 us
  blocking collectives: 0 us -> 17.8 us
  starting transfers between devices: 26.5 us -> 21.5 us
  local copies, waits for them, and re-layouts: 27.9 us -> 25.7 us
    all_to_all x1 -> x0, waiting for transfers between devices: 22.9 us -> none  [local(): lax.all_to_all(proj_mine, 'seq', split_axis=0, concat_axis=0, tiled=True)]
    all_to_all x0 -> x1, blocking collectives: none -> 17.8 us  [local(): lax.all_to_all(proj_mine, 'seq', split_axis=0, concat_axis=0, tiled=True)]
    all_to_all x1, waiting for transfers between devices: 13.8 us -> 7.33 us  [local(): lax.all_to_all(upstream, 'seq', split_axis=0, concat_axis=0, tiled=True)]
    all_to_all x1 -> x0, starting transfers between devices: 3.49 us -> none  [local(): lax.all_to_all(proj_mine, 'seq', split_axis=0, concat_axis=0, tiled=True)]
    all_to_all x1, starting transfers between devices: 6.33 us -> 3.33 us  [local(): lax.all_to_all(jnp.broadcast_to(targets[None], (seq_count, tokens_here)),...]
    unnamed x15 -> x17, local copies, waits for them, and re-layouts: 6.9 us -> 6.96 us
  transfers between devices with their start and end apart: 8 -> 7, of which waited for: 5 -> 4; matrix products, arithmetic and copies ran while one was open for 26% -> 25% of each run, Pallas kernels for 22% -> 24%
where the time goes in v4:
time: 171 us; the launch traced here: 170 us
  Pallas kernels  41.3 us (24%)
  local copies, waits for them, and re-layouts  25.7 us (15%)
  waiting for transfers between devices  25 us (15%)
  starting transfers between devices  21.5 us (13%)
  blocking collectives  17.8 us (10%)
  other arithmetic  14.8 us (9%)
  between operations  14.2 us (8%)
  matrix products  9.79 us (6%)
    pallas_call x1, Pallas kernels, attend_group(): pl.pallas_call(attention_kernel, out_shape=(jax.ShapeDtypeStruct((total,...  41.3 us
    all_to_all x1, blocking collectives, local(): lax.all_to_all(proj_mine, 'seq', split_axis=0, concat_axis=0, tiled=True)  17.8 us
    all_to_all x1, waiting for transfers between devices, local(): lax.all_to_all(grad_both.reshape(seq_count, portion * 2 * depth), 'seq',...  12.1 us
    all_to_all x1, waiting for transfers between devices, local(): lax.all_to_all(upstream, 'seq', split_axis=0, concat_axis=0, tiled=True)  7.33 us
    all_to_all x2, other arithmetic, local(): lax.all_to_all(grad_both.reshape(seq_count, portion * 2 * depth), 'seq',...  7.02 us
    unnamed x17, local copies, waits for them, and re-layouts  6.96 us
    scatter x1, local copies, waits for them, and re-layouts, local(): gathered = jnp.zeros(proj_owned.shape, proj_owned.dtype).at[places_all].s...  6.51 us
    all_to_all x1, starting transfers between devices, local(): lax.all_to_all(upstream, 'seq', split_axis=0, concat_axis=0, tiled=True)  6.33 us
  transfers between devices with their start and end apart: 7, of which 4 were waited for; matrix products, arithmetic and copies ran while one was open for 25% of the time, Pallas kernels for 24%

profile of v4, /device:TPU:0, one launch (start us, length us, event | category | flops | bytes accessed | tf_op | source)
XLA Modules:
  0.0 170.0 jit_solution(10644872809675937299)
XLA Ops:
  7.2 0.0 copy-start.1
  7.2 1.3 copy.33
  8.5 0.3 all_to_all.37
  8.8 0.6 broadcast.26
  9.4 2.2 %reduce.3 = bf16[8,16384]{1,0:T(8,128)(2,1)S(1)} reduce(bf16[8,1,16384]{2,1,0:T(2,128)(2,1)S(1)} %all_to_all.37, bf16[]{:T(256)} %broadcast.26), dimensions={1}, to_apply=%all_to_all.37.reduce_sub_computation | reduce | bytes 524290 | tf_op jit(solution)/shard_map/all_to_all | solution.py:138
  11.7 0.9 reshape.72
  12.5 6.3 %all-to-all-start.1 = ((bf16[8,2,8192]{2,1,0:T(2,128)(2,1)}), bf16[8,2,8192]{2,1,0:T(2,128)(2,1)S(1)}, u32[]{:S(2)}, u32[]{:S(2)}) async-start(bf16[8,2,8192]{2,1,0:T(2,128)(2,1)} %reshape.72), calls=%async_computation.1 | async-start | bytes 524288 | tf_op jit(solution)/shard_map/all_to_all | solution.py:138
  18.9 0.0 copy-done.1
  18.9 0.0 copy-start.3
  18.9 2.4 %fusion.13 = bf16[8,256,128]{1,2,0:T(8,128)(2,1)S(1)} fusion(bf16[1024,8,128]{2,1,0:T(8,128)(2,1)} %param.8, bf16[1,256,1024]{2,1,0:T(8,128)(2,1)S(1)} %copy-done.1), kind=kOutput, calls=%fused_computation.9 | convolution fusion | flops 537133056 | bytes 3145728 | tf_op jit(solution)/shard_map/td,dhc->htc/dot_general | solution.py:148
  21.3 7.3 %all-to-all-done.1 = bf16[8,2,8192]{2,1,0:T(2,128)(2,1)S(1)} async-done(((bf16[8,2,8192]{2,1,0:T(2,128)(2,1)}), bf16[8,2,8192]{2,1,0:T(2,128)(2,1)S(1)}, u32[]{:S(2)}, u32[]{:S(2)}) %all-to-all-start.1) | async-done | bytes 262176 | tf_op jit(solution)/shard_map/all_to_all | solution.py:138
  28.6 17.8 %all_to_all.46 = bf16[8,256,128]{1,2,0:T(8,128)(2,1)S(1)} all-to-all(bf16[8,256,128]{1,2,0:T(8,128)(2,1)S(1)} %fusion.13), channel_id=1, replica_groups=mesh['rec'=4,'seq'=8] {'seq'}, dimensions={0} | all-to-all | bytes 1048576 | tf_op jit(solution)/shard_map/all_to_all | solution.py:151
  46.4 0.0 copy-start.2
  46.4 0.0 copy-done.3
  46.4 0.6 broadcast_in_dim.16
  47.0 3.3 %all-to-all-start.2 = ((s32[8,1,256]{2,1,0:T(1,128)}), s32[8,1,256]{2,1,0:T(1,128)S(1)}, u32[]{:S(2)}, u32[]{:S(2)}) async-start(s32[8,1,256]{2,1,0:T(1,128)} %broadcast_in_dim.16), calls=%async_computation.2 | async-start | bytes 16384 | tf_op jit(solution)/shard_map/all_to_all | solution.py:141
  50.3 0.0 all-gather.2.cloned.1.call-start
  50.4 0.3 reshape.73
  50.7 1.6 reduce
  52.3 1.3 reshape.43.grad_ref
  53.6 0.3 copy.32
  53.9 2.0 %all-to-all-done.2 = s32[8,1,256]{2,1,0:T(1,128)S(1)} async-done(((s32[8,1,256]{2,1,0:T(1,128)}), s32[8,1,256]{2,1,0:T(1,128)S(1)}, u32[]{:S(2)}, u32[]{:S(2)}) %all-to-all-start.2) | async-done | bytes 8224 | tf_op jit(solution)/shard_map/all_to_all | solution.py:141
  55.9 0.0 all-gather.2.cloned.1.call-update
  55.9 0.0 copy-done.2
  55.9 0.7 copy.35.lists_ref
  56.6 6.5 %scatter_custom_fusion.both_ref = bf16[2048,128]{1,0:T(8,128)(2,1)} fusion(s32[2048]{0:T(1024)S(1)} %get-tuple-element.25, bf16[2048,128]{1,0:T(8,128)(2,1)S(1)} %bitcast.30, bf16[]{:T(256)} %constant.6.clone.1), kind=kCustom, calls=%fused_computation.14 | custom fusion | bytes 524290 | tf_op jit(solution)/shard_map/scatter | solution.py:161
  63.1 41.3 %shard_map.88 = (bf16[2048,64]{1,0:T(8,128)(2,1)}, bf16[2048,128]{1,0:T(8,128)(2,1)}) custom-call(s32[16,8]{1,0:T(8,128)} %copy.35.lists_ref, s32[16]{0:T(128)} %bitcast.37, bf16[2048,128]{1,0:T(8,128)(2,1)} %scatter_custom_fusion.both_ref, bf16[2048,64]{1,0:T(8,128)(2,1)} %reshape.43.grad_ref), custom_call_target="tpu_custom_call" | custom-call | tf_op jit(solution)/shard_map/pallas_call | solution.py:76
  104.4 0.0 copy-start
  104.4 1.4 all_to_all.38
  105.8 2.3 %reduce.4 = bf16[8,16384]{1,0:T(8,128)(2,1)S(1)} reduce(bf16[8,1,16384]{2,1,0:T(2,128)(2,1)S(1)} %all_to_all.38, bf16[]{:T(256)} %broadcast.26), dimensions={1}, to_apply=%all_to_all.38.reduce_sub_computation | reduce | bytes 524290 | tf_op jit(solution)/shard_map/all_to_all | solution.py:173
  108.1 0.9 reshape.74
  109.0 3.4 %all-to-all-start.3 = ((bf16[8,2,8192]{2,1,0:T(2,128)(2,1)}), bf16[8,2,8192]{2,1,0:T(2,128)(2,1)S(1)}, u32[]{:S(2)}, u32[]{:S(2)}) async-start(bf16[8,2,8192]{2,1,0:T(2,128)(2,1)} %reshape.74), calls=%async_computation.3 | async-start | bytes 524288 | tf_op jit(solution)/shard_map/all_to_all | solution.py:173
  112.4 0.2 reduce-scatter.2.cloned.1.call-start
  112.6 0.0 copy-done
  112.6 6.2 %gather_fusion = bf16[2048,128]{1,0:T(8,128)(2,1)S(1)} fusion(bf16[2048,128]{1,0:T(8,128)(2,1)S(1)} %copy-done, s32[2048]{0:T(1024)S(1)} %get-tuple-element.24), kind=kCustom, calls=%fused_computation | custom fusion | bytes 1056768 | tf_op jit(solution)/shard_map/gather | solution.py:195
  118.8 0.0 all-gather.2.cloned.1.call-done
  118.9 4.3 %fusion.24 = f32[1024,128]{1,0:T(8,128)} fusion(bf16[2048,1024]{1,0:T(8,128)(2,1)} %all-gather.2.cloned.1.call-done, bf16[2048,128]{1,0:T(8,128)(2,1)S(1)} %gather_fusion), kind=kOutput, calls=%fused_computation.18 | convolution fusion | flops 536870912 | bytes 5242880 | tf_op jit(solution)/shard_map/od,oc->dc/dot_general | solution.py:196
  123.1 0.0 reduce-scatter.2.cloned.1.call-update
  123.2 0.3 all_to_all.39
  123.4 3.9 %reduce.5 = bf16[8,32768]{1,0:T(8,128)(2,1)S(1)} reduce(bf16[8,1,32768]{2,1,0:T(2,128)(2,1)S(1)} %all_to_all.39, bf16[]{:T(256)} %broadcast.26), dimensions={1}, to_apply=%all_to_all.39.reduce_sub_computation | reduce | bytes 1048578 | tf_op jit(solution)/shard_map/all_to_all | solution.py:180
  127.3 1.2 reshape.76
  128.5 0.0 all-to-all-done.3
  128.5 4.8 %all-to-all-start.4 = ((bf16[8,2,16384]{2,1,0:T(2,128)(2,1)}), bf16[8,2,16384]{2,1,0:T(2,128)(2,1)S(1)}, u32[]{:S(2)}, u32[]{:S(2)}) async-start(bf16[8,2,16384]{2,1,0:T(2,128)(2,1)} %reshape.76), calls=%async_computation.4 | async-start | bytes 1048576 | tf_op jit(solution)/shard_map/all_to_all | solution.py:180
  133.3 0.3 reshape.75
  133.5 1.6 reduce.1
  135.1 0.5 broadcast_in_dim_reshape.3
  135.6 0.9 copy.39
  136.5 12.1 %all-to-all-done.4 = bf16[8,2,16384]{2,1,0:T(2,128)(2,1)S(1)} async-done(((bf16[8,2,16384]{2,1,0:T(2,128)(2,1)}), bf16[8,2,16384]{2,1,0:T(2,128)(2,1)S(1)}, u32[]{:S(2)}, u32[]{:S(2)}) %all-to-all-start.4) | async-done | bytes 524320 | tf_op jit(solution)/shard_map/all_to_all | solution.py:180
  148.6 0.5 reshape.77
  149.2 3.2 %reduce.2 = bf16[8,32768]{1,0:T(8,128)(2,1)S(1)} reduce(bf16[8,1,32768]{2,1,0:T(2,128)(2,1)S(1)} %reshape.77, bf16[]{:T(256)} %constant.21), dimensions={1}, to_apply=%all_to_all.35.reduce_sub_computation | reduce | bytes 1048578 | tf_op jit(solution)/shard_map/all_to_all | solution.py:180
  152.3 0.0 reduce-scatter.2.cloned.1.call-done
  152.4 3.4 %all-to-all-start.5 = ((f32[8,32,128]{2,1,0:T(8,128)}), f32[8,32,128]{2,1,0:T(8,128)S(1)}, u32[]{:S(2)}, u32[]{:S(2)}) async-start(f32[8,32,128]{2,1,0:T(8,128)} %bitcast.33), calls=%async_computation.6 | async-start | bytes 262144 | tf_op jit(solution)/shard_map/all_to_all | solution.py:200
  155.8 3.1 %fusion.16 = bf16[1,256,1024]{2,1,0:T(8,128)(2,1)} fusion(bf16[1024,8,128]{2,1,0:T(8,128)(2,1)} %param.8, bf16[1,8,256,128]{3,1,2,0:T(8,128)(2,1)S(1)} %bitcast.31), kind=kOutput, calls=%fused_computation.10 | convolution fusion | flops 537133056 | bytes 3145728 | tf_op jit(solution)/shard_map/htc,dhc->td/dot_general | solution.py:190
  158.9 3.6 %all-to-all-done.5 = f32[8,32,128]{2,1,0:T(8,128)S(1)} async-done(((f32[8,32,128]{2,1,0:T(8,128)}), f32[8,32,128]{2,1,0:T(8,128)S(1)}, u32[]{:S(2)}, u32[]{:S(2)}) %all-to-all-start.5) | async-done | bytes 131104 | tf_op jit(solution)/shard_map/all_to_all | solution.py:200
  162.5 0.7 copy.40
  (1 shorter events, 0.0 us)
Async XLA Ops:
  7.2 11.7 %copy-start.1 = (bf16[1,256,1024]{2,1,0:T(8,128)(2,1)S(1)}, bf16[1,256,1024]{2,1,0:T(8,128)(2,1)}, u32[]{:S(2)}) copy-start(bf16[1,256,1024]{2,1,0:T(8,128)(2,1)} %param.6) | copy-start | bytes 1572868
  12.5 16.1 %all-to-all-start.1 = ((bf16[8,2,8192]{2,1,0:T(2,128)(2,1)}), bf16[8,2,8192]{2,1,0:T(2,128)(2,1)S(1)}, u32[]{:S(2)}, u32[]{:S(2)}) async-start(bf16[8,2,8192]{2,1,0:T(2,128)(2,1)} %reshape.72), calls=%async_computation.1 | async-start | bytes 524288 | tf_op jit(solution)/shard_map/all_to_all | solution.py:138
  18.9 27.5 %copy-start.3 = (s32[1,256]{1,0:T(1,128)S(1)}, s32[1,256]{1,0:T(1,128)}, u32[]{:S(2)}) copy-start(s32[1,256]{1,0:T(1,128)} %param.7) | copy-start | bytes 3076
  46.4 9.5 %copy-start.2 = (s32[1,16,8]{1,2,0:T(8,128)S(1)}, s32[1,16,8]{1,2,0:T(8,128)}, u32[]{:S(2)}) copy-start(s32[1,16,8]{1,2,0:T(8,128)} %param.9) | copy-start | bytes 1540
  47.0 8.9 %all-to-all-start.2 = ((s32[8,1,256]{2,1,0:T(1,128)}), s32[8,1,256]{2,1,0:T(1,128)S(1)}, u32[]{:S(2)}, u32[]{:S(2)}) async-start(s32[8,1,256]{2,1,0:T(1,128)} %broadcast_in_dim.16), calls=%async_computation.2 | async-start | bytes 16384 | tf_op jit(solution)/shard_map/all_to_all | solution.py:141
  50.3 68.5 %all-gather.2.cloned.1.call-start = ((), (), s32[]{:S(2)}) async-start(), calls=%async_computation.7 | async-start | bytes 4718592 | tf_op jit(solution)/shard_map/all_gather | solution.py:157
  104.4 8.3 %copy-start = (bf16[2048,128]{1,0:T(8,128)(2,1)S(1)}, bf16[2048,128]{1,0:T(8,128)(2,1)}, u32[]{:S(2)}) copy-start(bf16[2048,128]{1,0:T(8,128)(2,1)} %get-tuple-element.13) | copy-start | bytes 1572868
  109.0 19.5 %all-to-all-start.3 = ((bf16[8,2,8192]{2,1,0:T(2,128)(2,1)}), bf16[8,2,8192]{2,1,0:T(2,128)(2,1)S(1)}, u32[]{:S(2)}, u32[]{:S(2)}) async-start(bf16[8,2,8192]{2,1,0:T(2,128)(2,1)} %reshape.74), calls=%async_computation.3 | async-start | bytes 524288 | tf_op jit(solution)/shard_map/all_to_all | solution.py:173
  112.4 39.9 %reduce-scatter.2.cloned.1.call-start = ((), (), s32[]{:S(2)}) async-start(), calls=%async_computation.8 | async-start | bytes 655360 | tf_op jit(solution)/shard_map/reduce_scatter | solution.py:199
  128.5 20.2 %all-to-all-start.4 = ((bf16[8,2,16384]{2,1,0:T(2,128)(2,1)}), bf16[8,2,16384]{2,1,0:T(2,128)(2,1)S(1)}, u32[]{:S(2)}, u32[]{:S(2)}) async-start(bf16[8,2,16384]{2,1,0:T(2,128)(2,1)} %reshape.76), calls=%async_computation.4 | async-start | bytes 1048576 | tf_op jit(solution)/shard_map/all_to_all | solution.py:180
  152.4 10.1 %all-to-all-start.5 = ((f32[8,32,128]{2,1,0:T(8,128)}), f32[8,32,128]{2,1,0:T(8,128)S(1)}, u32[]{:S(2)}, u32[]{:S(2)}) async-start(f32[8,32,128]{2,1,0:T(8,128)} %bitcast.33), calls=%async_computation.6 | async-start | bytes 262144 | tf_op jit(solution)/shard_map/all_to_all | solution.py:200
Sparse Core Ops, SparseCore 0:
  56.0 46.6 all-gather.1
  123.3 25.8 reduce-scatter.1

commit v5 on v4

--- a/solution.py
+++ b/solution.py
@@ -134,7 +134,7 @@
     rows_here = owned_rows[0]
     targets = seq_position[0]
     group = my_index % groups
-    upstream = out_grad[0].reshape(seq_count, portion * depth)
+    upstream = out_grad[0].reshape(seq_count, portion, depth)
     got_grad = lax.all_to_all(upstream, "seq", split_axis=0, concat_axis=0, tiled=True)
     grad_rows = got_grad.reshape(seq_count * portion, depth)
     if groups == 1:
@@ -171,14 +171,14 @@
     mixed, grad_both = attend_group(gathered, grad_rows, key_blocks[group], key_counts[group])
     back_out, back_grad = (
         lax.all_to_all(
-            mixed.reshape(seq_count, portion * depth),
+            mixed.reshape(seq_count, portion, depth),
             "seq",
             split_axis=0,
             concat_axis=0,
             tiled=True,
         ),
         lax.all_to_all(
-            grad_both.reshape(seq_count, portion * 2 * depth),
+            grad_both.reshape(seq_count, portion, 2 * depth),
             "seq",
             split_axis=0,
             concat_axis=0,

time: 171 us -> 164 us (0.959)
  other arithmetic: 14.8 us -> 0.01 us
  waiting for transfers between devices: 25 us -> 38 us
  local copies, waits for them, and re-layouts: 25.7 us -> 19.2 us
  Pallas kernels: 41.3 us -> 43.1 us
    all_to_all x6 -> x0, other arithmetic: 14.7 us -> none  [the longest x2 7.02 us: local(): lax.all_to_all(grad_both.reshape(seq_count, portion * 2 * depth), 'seq',...]
    reduce_scatter x1, waiting for transfers between devices: 0.02 us -> 5.95 us  [local(): summed = lax.psum_scatter(partial, 'rec', scatter_dimension=0, tiled=True)]
    unnamed x17 -> x8, local copies, waits for them, and re-layouts: 6.96 us -> 1.45 us
    all_to_all x2, waiting for transfers between devices: 12.1 us -> 15.4 us  [the longest x1 15.4 us: local(): lax.all_to_all(grad_both.reshape(seq_count, portion, 2 * depth), 'seq', s...]
    all_to_all x1, waiting for transfers between devices: 1.96 us -> 4.2 us  [local(): lax.all_to_all(jnp.broadcast_to(targets[None], (seq_count, tokens_here)),...]
    pallas_call x1, Pallas kernels: 41.3 us -> 43.1 us  [attend_group(): pl.pallas_call(attention_kernel, out_shape=(jax.ShapeDtypeStruct((total,...]
  transfers between devices with their start and end apart: 7 -> 7, of which waited for: 4 -> 5; matrix products, arithmetic and copies ran while one was open for 25% -> 16% of each run, Pallas kernels for 24% -> 26%
where the time goes in v5:
time: 164 us; the launch traced here: 163 us
  Pallas kernels  43.1 us (26%)
  waiting for transfers between devices  38 us (23%)
  starting transfers between devices  22.8 us (14%)
  local copies, waits for them, and re-layouts  19.2 us (12%)
  blocking collectives  17.8 us (11%)
  between operations  14.1 us (9%)
  matrix products  8.44 us (5%)
    pallas_call x1, Pallas kernels, attend_group(): pl.pallas_call(attention_kernel, out_shape=(jax.ShapeDtypeStruct((total,...  43.1 us
    all_to_all x1, blocking collectives, local(): lax.all_to_all(proj_mine, 'seq', split_axis=0, concat_axis=0, tiled=True)  17.8 us
    all_to_all x1, waiting for transfers between devices, local(): lax.all_to_all(grad_both.reshape(seq_count, portion, 2 * depth), 'seq', s...  15.4 us
    all_to_all x1, waiting for transfers between devices, local(): lax.all_to_all(upstream, 'seq', split_axis=0, concat_axis=0, tiled=True)  7.25 us
    gather x1, local copies, waits for them, and re-layouts, local(): head_grad = grad_both[places_all]  6.7 us
    scatter x1, local copies, waits for them, and re-layouts, local(): gathered = jnp.zeros(proj_owned.shape, proj_owned.dtype).at[places_all].s...  6.51 us
    all_to_all x1, starting transfers between devices, local(): lax.all_to_all(upstream, 'seq', split_axis=0, concat_axis=0, tiled=True)  6.34 us
    reduce_scatter x1, waiting for transfers between devices, local(): summed = lax.psum_scatter(partial, 'rec', scatter_dimension=0, tiled=True)  5.95 us
  transfers between devices with their start and end apart: 7, of which 5 were waited for; matrix products, arithmetic and copies ran while one was open for 16% of the time, Pallas kernels for 26%

profile of v5, /device:TPU:0, one launch (start us, length us, event | category | flops | bytes accessed | tf_op | source)
XLA Modules:
  0.0 163.4 jit_solution(15838034658614201119)
XLA Ops:
  7.2 6.3 %all-to-all-start.1 = ((bf16[8,256,64]{1,2,0:T(8,128)(2,1)}), bf16[8,256,64]{1,2,0:T(8,128)(2,1)S(1)}, u32[]{:S(2)}, u32[]{:S(2)}) async-start(bf16[8,256,64]{1,2,0:T(8,128)(2,1)} %bitcast.35), calls=%async_computation.1 | async-start | bytes 524288 | tf_op jit(solution)/shard_map/all_to_all | solution.py:138
  13.5 0.0 copy-start.1
  13.5 2.5 %fusion.13 = bf16[8,256,128]{1,2,0:T(8,128)(2,1)S(1)} fusion(bf16[1024,8,128]{2,1,0:T(8,128)(2,1)} %param.8, bf16[1,256,1024]{2,1,0:T(8,128)(2,1)} %param.6), kind=kOutput, calls=%fused_computation.9 | convolution fusion | flops 537133056 | bytes 3145728 | tf_op jit(solution)/shard_map/td,dhc->htc/dot_general | solution.py:148
  16.0 0.0 copy-start
  16.0 7.2 %all-to-all-done.1 = bf16[8,256,64]{1,2,0:T(8,128)(2,1)S(1)} async-done(((bf16[8,256,64]{1,2,0:T(8,128)(2,1)}), bf16[8,256,64]{1,2,0:T(8,128)(2,1)S(1)}, u32[]{:S(2)}, u32[]{:S(2)}) %all-to-all-start.1) | async-done | bytes 262176 | tf_op jit(solution)/shard_map/all_to_all | solution.py:138
  23.2 17.8 %all_to_all.31 = bf16[8,256,128]{1,2,0:T(8,128)(2,1)S(1)} all-to-all(bf16[8,256,128]{1,2,0:T(8,128)(2,1)S(1)} %fusion.13), channel_id=1, replica_groups=mesh['rec'=4,'seq'=8] {'seq'}, dimensions={0} | all-to-all | bytes 1048576 | tf_op jit(solution)/shard_map/all_to_all | solution.py:151
  41.0 0.0 copy-done.1
  41.0 0.6 broadcast_in_dim.19
  41.6 3.3 %all-to-all-start.2 = ((s32[8,1,256]{2,1,0:T(1,128)}), s32[8,1,256]{2,1,0:T(1,128)S(1)}, u32[]{:S(2)}, u32[]{:S(2)}) async-start(s32[8,1,256]{2,1,0:T(1,128)} %broadcast_in_dim.19), calls=%async_computation.2 | async-start | bytes 16384 | tf_op jit(solution)/shard_map/all_to_all | solution.py:141
  45.0 0.0 all-gather.2.cloned.1.call-start
  45.0 1.0 copy.18
  46.0 0.3 copy.17
  46.3 4.2 %all-to-all-done.2 = s32[8,1,256]{2,1,0:T(1,128)S(1)} async-done(((s32[8,1,256]{2,1,0:T(1,128)}), s32[8,1,256]{2,1,0:T(1,128)S(1)}, u32[]{:S(2)}, u32[]{:S(2)}) %all-to-all-start.2) | async-done | bytes 8224 | tf_op jit(solution)/shard_map/all_to_all | solution.py:141
  50.5 0.0 all-gather.2.cloned.1.call-update
  50.5 0.0 copy-done
  50.5 0.7 copy.19.lists_ref
  51.2 6.5 %scatter_custom_fusion.both_ref = bf16[2048,128]{1,0:T(8,128)(2,1)} fusion(s32[2048]{0:T(1024)S(1)} %get-tuple-element.19, bf16[2048,128]{1,0:T(8,128)(2,1)S(1)} %bitcast.33, bf16[]{:T(256)} %constant.6.clone.1), kind=kCustom, calls=%fused_computation.12 | custom fusion | bytes 524290 | tf_op jit(solution)/shard_map/scatter | solution.py:161
  57.7 43.1 %shard_map.88 = (bf16[2048,64]{1,0:T(8,128)(2,1)}, bf16[2048,128]{1,0:T(8,128)(2,1)}) custom-call(s32[16,8]{1,0:T(8,128)} %copy.19.lists_ref, s32[16]{0:T(128)} %bitcast.40, bf16[2048,128]{1,0:T(8,128)(2,1)} %scatter_custom_fusion.both_ref, bf16[2048,64]{1,0:T(8,128)(2,1)} %bitcast.29), custom_call_target="tpu_custom_call" | custom-call | tf_op jit(solution)/shard_map/pallas_call | solution.py:76
  100.8 1.9 %copy.20 = bf16[8,256,64]{1,2,0:T(8,128)(2,1)} copy(bf16[8,256,64]{2,1,0:T(8,128)(2,1)} %bitcast.31) | data formatting | bytes 524288 | tf_op jit(solution)/shard_map/reshape | solution.py:174
  102.8 3.4 %all-to-all-start.3 = ((bf16[8,256,64]{1,2,0:T(8,128)(2,1)}), bf16[8,256,64]{1,2,0:T(8,128)(2,1)S(1)}, u32[]{:S(2)}, u32[]{:S(2)}) async-start(bf16[8,256,64]{1,2,0:T(8,128)(2,1)} %copy.20), calls=%async_computation.3 | async-start | bytes 524288 | tf_op jit(solution)/shard_map/all_to_all | solution.py:173
  106.2 0.0 reduce-scatter.2.cloned.1.call-start
  106.3 6.7 %gather_fusion = bf16[2048,128]{1,0:T(8,128)(2,1)S(1)} fusion(bf16[2048,128]{1,0:T(8,128)(2,1)} %get-tuple-element.13, s32[2048]{0:T(1024)S(1)} %get-tuple-element.18), kind=kCustom, calls=%fused_computation | custom fusion | bytes 1056768 | tf_op jit(solution)/shard_map/gather | solution.py:195
  113.0 0.0 copy-start.2
  113.0 0.0 all-gather.2.cloned.1.call-done
  113.0 4.4 %fusion.22 = f32[1024,128]{1,0:T(8,128)} fusion(bf16[2048,1024]{1,0:T(8,128)(2,1)} %all-gather.2.cloned.1.call-done, bf16[2048,128]{1,0:T(8,128)(2,1)S(1)} %gather_fusion), kind=kOutput, calls=%fused_computation.16 | convolution fusion | flops 536870912 | bytes 5242880 | tf_op jit(solution)/shard_map/od,oc->dc/dot_general | solution.py:196
  117.4 0.0 reduce-scatter.2.cloned.1.call-update
  117.4 0.0 all-to-all-done.3
  117.5 5.0 %all-to-all-start.4 = ((bf16[8,256,128]{2,1,0:T(8,128)(2,1)}), bf16[8,256,128]{2,1,0:T(8,128)(2,1)S(1)}, u32[]{:S(2)}, u32[]{:S(2)}) async-start(bf16[8,256,128]{2,1,0:T(8,128)(2,1)} %bitcast.12), calls=%async_computation.4 | async-start | bytes 1048576 | tf_op jit(solution)/shard_map/all_to_all | solution.py:180
  122.4 15.4 %all-to-all-done.4 = bf16[8,256,128]{2,1,0:T(8,128)(2,1)S(1)} async-done(((bf16[8,256,128]{2,1,0:T(8,128)(2,1)}), bf16[8,256,128]{2,1,0:T(8,128)(2,1)S(1)}, u32[]{:S(2)}, u32[]{:S(2)}) %all-to-all-start.4) | async-done | bytes 524320 | tf_op jit(solution)/shard_map/all_to_all | solution.py:180
  137.8 5.9 %reduce-scatter.2.cloned.1.call-done = f32[256,128]{1,0:T(8,128)} async-done(((f32[1024,128]{1,0:T(8,128)}), f32[256,128]{1,0:T(8,128)}) %reduce-scatter.2.cloned.1.call-update) | async-done | bytes 131088 | tf_op jit(solution)/shard_map/reduce_scatter | solution.py:199
  143.8 4.6 %all-to-all-start.5 = ((f32[8,32,128]{2,1,0:T(8,128)}), f32[8,32,128]{2,1,0:T(8,128)S(1)}, u32[]{:S(2)}, u32[]{:S(2)}) async-start(f32[8,32,128]{2,1,0:T(8,128)} %bitcast.36), calls=%async_computation.6 | async-start | bytes 262144 | tf_op jit(solution)/shard_map/all_to_all | solution.py:200
  148.4 0.0 copy-done.2
  148.4 1.6 fusion.16
  149.9 5.2 %all-to-all-done.5 = f32[8,32,128]{2,1,0:T(8,128)S(1)} async-done(((f32[8,32,128]{2,1,0:T(8,128)}), f32[8,32,128]{2,1,0:T(8,128)S(1)}, u32[]{:S(2)}, u32[]{:S(2)}) %all-to-all-start.5) | async-done | bytes 131104 | tf_op jit(solution)/shard_map/all_to_all | solution.py:200
  155.2 0.7 copy.22
  155.9 0.7 copy.38
  (1 shorter events, 0.0 us)
Async XLA Ops:
  7.2 16.1 %all-to-all-start.1 = ((bf16[8,256,64]{1,2,0:T(8,128)(2,1)}), bf16[8,256,64]{1,2,0:T(8,128)(2,1)S(1)}, u32[]{:S(2)}, u32[]{:S(2)}) async-start(bf16[8,256,64]{1,2,0:T(8,128)(2,1)} %bitcast.35), calls=%async_computation.1 | async-start | bytes 524288 | tf_op jit(solution)/shard_map/all_to_all | solution.py:138
  13.5 27.5 %copy-start.1 = (s32[1,256]{1,0:T(1,128)S(1)}, s32[1,256]{1,0:T(1,128)}, u32[]{:S(2)}) copy-start(s32[1,256]{1,0:T(1,128)} %param.7) | copy-start | bytes 3076
  16.0 34.5 %copy-start = (s32[1,16,8]{1,2,0:T(8,128)S(1)}, s32[1,16,8]{1,2,0:T(8,128)}, u32[]{:S(2)}) copy-start(s32[1,16,8]{1,2,0:T(8,128)} %param.9) | copy-start | bytes 1540
  41.6 8.9 %all-to-all-start.2 = ((s32[8,1,256]{2,1,0:T(1,128)}), s32[8,1,256]{2,1,0:T(1,128)S(1)}, u32[]{:S(2)}, u32[]{:S(2)}) async-start(s32[8,1,256]{2,1,0:T(1,128)} %broadcast_in_dim.19), calls=%async_computation.2 | async-start | bytes 16384 | tf_op jit(solution)/shard_map/all_to_all | solution.py:141
  45.0 68.0 %all-gather.2.cloned.1.call-start = ((), (), s32[]{:S(2)}) async-start(), calls=%async_computation.7 | async-start | bytes 4718592 | tf_op jit(solution)/shard_map/all_gather | solution.py:157
  102.8 14.7 %all-to-all-start.3 = ((bf16[8,256,64]{1,2,0:T(8,128)(2,1)}), bf16[8,256,64]{1,2,0:T(8,128)(2,1)S(1)}, u32[]{:S(2)}, u32[]{:S(2)}) async-start(bf16[8,256,64]{1,2,0:T(8,128)(2,1)} %copy.20), calls=%async_computation.3 | async-start | bytes 524288 | tf_op jit(solution)/shard_map/all_to_all | solution.py:173
  106.2 37.6 %reduce-scatter.2.cloned.1.call-start = ((), (), s32[]{:S(2)}) async-start(), calls=%async_computation.8 | async-start | bytes 655360 | tf_op jit(solution)/shard_map/reduce_scatter | solution.py:199
  113.0 35.4 %copy-start.2 = (bf16[1024,8,128]{2,1,0:T(8,128)(2,1)S(1)}, bf16[1024,8,128]{2,1,0:T(8,128)(2,1)}, u32[]{:S(2)}) copy-start(bf16[1024,8,128]{2,1,0:T(8,128)(2,1)} %param.8) | copy-start | bytes 6291460
  117.5 20.4 %all-to-all-start.4 = ((bf16[8,256,128]{2,1,0:T(8,128)(2,1)}), bf16[8,256,128]{2,1,0:T(8,128)(2,1)S(1)}, u32[]{:S(2)}, u32[]{:S(2)}) async-start(bf16[8,256,128]{2,1,0:T(8,128)(2,1)} %bitcast.12), calls=%async_computation.4 | async-start | bytes 1048576 | tf_op jit(solution)/shard_map/all_to_all | solution.py:180
  143.8 11.4 %all-to-all-start.5 = ((f32[8,32,128]{2,1,0:T(8,128)}), f32[8,32,128]{2,1,0:T(8,128)S(1)}, u32[]{:S(2)}, u32[]{:S(2)}) async-start(f32[8,32,128]{2,1,0:T(8,128)} %bitcast.36), calls=%async_computation.6 | async-start | bytes 262144 | tf_op jit(solution)/shard_map/all_to_all | solution.py:200
Sparse Core Ops, SparseCore 0:
  50.6 45.2 all-gather.1
  117.6 26.1 reduce-scatter.1

commit v6 on v5

--- a/solution.py
+++ b/solution.py
@@ -19,48 +19,40 @@
 
     def one_block(a, carry):
         start = pl.multiple_of(a * BLOCK, BLOCK)
-        own = both_ref[pl.ds(start, BLOCK), :]
-        query = own[:, :depth]
+        query = both_ref[pl.ds(start, BLOCK), :][:, :depth]
         upstream = grad_ref[pl.ds(start, BLOCK), :]
         active = counts_ref[a]
         picks = [jnp.clip(lists_ref[a, j], 0, nblocks - 1) for j in range(listed)]
-        tiles = [both_ref[pl.ds(pl.multiple_of(b * BLOCK, BLOCK), BLOCK), :] for b in picks]
-        keys = [t[:, :depth] for t in tiles]
-        values = [t[:, depth:] for t in tiles]
-        scores = jnp.concatenate(
-            [lax.dot_general(query, k, trans_b, preferred_element_type=jnp.float32) for k in keys],
-            axis=1,
-        ) * scale
+        near = jnp.concatenate(
+            [both_ref[pl.ds(pl.multiple_of(b * BLOCK, BLOCK), BLOCK), :] for b in picks], axis=0
+        )
+        keys = near[:, :depth]
+        values = near[:, depth:]
+        scores = lax.dot_general(query, keys, trans_b, preferred_element_type=jnp.float32) * scale
         usable = col_block < active
         scores = jnp.where(usable, scores, -jnp.inf)
         peak = jnp.max(scores, axis=1, keepdims=True)
         weights = jnp.where(usable, jnp.exp(scores - peak), 0.0)
         probs = weights / jnp.sum(weights, axis=1, keepdims=True)
         probs_low = probs.astype(jnp.bfloat16)
-        dprobs = jnp.concatenate(
-            [lax.dot_general(upstream, v, trans_b, preferred_element_type=jnp.float32) for v in values],
-            axis=1,
-        )
+        mixed = jnp.dot(probs_low, values, preferred_element_type=jnp.float32)
+        out_ref[pl.ds(start, BLOCK), :] = mixed.astype(out_ref.dtype)
+        dprobs = lax.dot_general(upstream, values, trans_b, preferred_element_type=jnp.float32)
         inner = jnp.sum(probs * dprobs, axis=1, keepdims=True)
         dscores = (scale * probs * (dprobs - inner)).astype(jnp.bfloat16)
-        mixed = jnp.zeros((BLOCK, depth), jnp.float32)
-        dquery = jnp.zeros((BLOCK, depth), jnp.float32)
+        dquery = jnp.dot(dscores, keys, preferred_element_type=jnp.float32)
+        dkeys = lax.dot_general(dscores, query, trans_a, preferred_element_type=jnp.float32)
+        dvalues = lax.dot_general(probs_low, upstream, trans_a, preferred_element_type=jnp.float32)
+        both_grads = jnp.concatenate([dkeys, dvalues], axis=1)
         for j in range(listed):
-            cols = slice(j * BLOCK, (j + 1) * BLOCK)
-            mixed = mixed + jnp.dot(probs_low[:, cols], values[j], preferred_element_type=jnp.float32)
-            dquery = dquery + jnp.dot(dscores[:, cols], keys[j], preferred_element_type=jnp.float32)
-        out_ref[pl.ds(start, BLOCK), :] = mixed.astype(out_ref.dtype)
-        for j in range(listed):
-            cols = slice(j * BLOCK, (j + 1) * BLOCK)
-            dkeys = lax.dot_general(dscores[:, cols], query, trans_a, preferred_element_type=jnp.float32)
-            dvalues = lax.dot_general(probs_low[:, cols], upstream, trans_a, preferred_element_type=jnp.float32)
+            part = both_grads[j * BLOCK:(j + 1) * BLOCK]
             if j == 0:
-                dkeys = dkeys + dquery
+                part = part + jnp.concatenate([dquery, jnp.zeros_like(dquery)], axis=1)
 
             @pl.when(j < active)
             def _():
                 rows = pl.ds(pl.multiple_of(picks[j] * BLOCK, BLOCK), BLOCK)
-                acc_ref[rows, :] += jnp.concatenate([dkeys, dvalues], axis=1)
+                acc_ref[rows, :] += part
 
         return carry
 

time: 164 us -> 150 us (0.915)
  Pallas kernels: 43.1 us -> 22.6 us
  waiting for transfers between devices: 38 us -> 46.1 us
    pallas_call x1, Pallas kernels: 43.1 us -> 22.6 us  [attend_group(): pl.pallas_call(attention_kernel, out_shape=(jax.ShapeDtypeStruct((total,...]
    all_gather x1, waiting for transfers between devices: 0.02 us -> 9.04 us  [local(): owned_all = lax.all_gather(later_rows, 'seq', axis=0, tiled=True)]
  transfers between devices with their start and end apart: 7 -> 7, of which waited for: 5 -> 6; matrix products, arithmetic and copies ran while one was open for 16% -> 17% of each run, Pallas kernels for 26% -> 15%
where the time goes in v6:
time: 150 us; the launch traced here: 149 us
  waiting for transfers between devices  46.1 us (31%)
  Pallas kernels  22.6 us (15%)
  starting transfers between devices  21.3 us (14%)
  local copies, waits for them, and re-layouts  19.2 us (13%)
  blocking collectives  17.8 us (12%)
  between operations  14.1 us (9%)
  matrix products  8.29 us (6%)
    pallas_call x1, Pallas kernels, attend_group(): pl.pallas_call(attention_kernel, out_shape=(jax.ShapeDtypeStruct((total,...  22.6 us
    all_to_all x1, blocking collectives, local(): lax.all_to_all(proj_mine, 'seq', split_axis=0, concat_axis=0, tiled=True)  17.8 us
    all_to_all x1, waiting for transfers between devices, local(): lax.all_to_all(grad_both.reshape(seq_count, portion, 2 * depth), 'seq', s...  15.3 us
    all_gather x1, waiting for transfers between devices, local(): owned_all = lax.all_gather(later_rows, 'seq', axis=0, tiled=True)  9.04 us
    all_to_all x1, waiting for transfers between devices, local(): lax.all_to_all(upstream, 'seq', split_axis=0, concat_axis=0, tiled=True)  7.25 us
    gather x1, local copies, waits for them, and re-layouts, local(): head_grad = grad_both[places_all]  6.7 us
    scatter x1, local copies, waits for them, and re-layouts, local(): gathered = jnp.zeros(proj_owned.shape, proj_owned.dtype).at[places_all].s...  6.51 us
    all_to_all x1, starting transfers between devices, local(): lax.all_to_all(upstream, 'seq', split_axis=0, concat_axis=0, tiled=True)  6.34 us
  transfers between devices with their start and end apart: 7, of which 6 were waited for; matrix products, arithmetic and copies ran while one was open for 17% of the time, Pallas kernels for 15%

profile of v6, /device:TPU:0, one launch (start us, length us, event | category | flops | bytes accessed | tf_op | source)
XLA Modules:
  0.0 149.3 jit_solution(11220669274979069021)
XLA Ops:
  7.2 6.3 %all-to-all-start.1 = ((bf16[8,256,64]{1,2,0:T(8,128)(2,1)}), bf16[8,256,64]{1,2,0:T(8,128)(2,1)S(1)}, u32[]{:S(2)}, u32[]{:S(2)}) async-start(bf16[8,256,64]{1,2,0:T(8,128)(2,1)} %bitcast.35), calls=%async_computation.1 | async-start | bytes 524288 | tf_op jit(solution)/shard_map/all_to_all | solution.py:130
  13.5 0.0 copy-start.1
  13.5 2.5 %fusion.13 = bf16[8,256,128]{1,2,0:T(8,128)(2,1)S(1)} fusion(bf16[1024,8,128]{2,1,0:T(8,128)(2,1)} %param.8, bf16[1,256,1024]{2,1,0:T(8,128)(2,1)} %param.6), kind=kOutput, calls=%fused_computation.9 | convolution fusion | flops 537133056 | bytes 3145728 | tf_op jit(solution)/shard_map/td,dhc->htc/dot_general | solution.py:140
  16.0 0.0 copy-start
  16.0 7.2 %all-to-all-done.1 = bf16[8,256,64]{1,2,0:T(8,128)(2,1)S(1)} async-done(((bf16[8,256,64]{1,2,0:T(8,128)(2,1)}), bf16[8,256,64]{1,2,0:T(8,128)(2,1)S(1)}, u32[]{:S(2)}, u32[]{:S(2)}) %all-to-all-start.1) | async-done | bytes 262176 | tf_op jit(solution)/shard_map/all_to_all | solution.py:130
  23.2 17.8 %all_to_all.31 = bf16[8,256,128]{1,2,0:T(8,128)(2,1)S(1)} all-to-all(bf16[8,256,128]{1,2,0:T(8,128)(2,1)S(1)} %fusion.13), channel_id=1, replica_groups=mesh['rec'=4,'seq'=8] {'seq'}, dimensions={0} | all-to-all | bytes 1048576 | tf_op jit(solution)/shard_map/all_to_all | solution.py:143
  41.0 0.0 copy-done.1
  41.0 0.6 broadcast_in_dim.19
  41.6 3.3 %all-to-all-start.2 = ((s32[8,1,256]{2,1,0:T(1,128)}), s32[8,1,256]{2,1,0:T(1,128)S(1)}, u32[]{:S(2)}, u32[]{:S(2)}) async-start(s32[8,1,256]{2,1,0:T(1,128)} %broadcast_in_dim.19), calls=%async_computation.2 | async-start | bytes 16384 | tf_op jit(solution)/shard_map/all_to_all | solution.py:133
  45.0 0.0 all-gather.2.cloned.1.call-start
  45.0 1.0 copy.18
  46.0 0.3 copy.17
  46.3 4.2 %all-to-all-done.2 = s32[8,1,256]{2,1,0:T(1,128)S(1)} async-done(((s32[8,1,256]{2,1,0:T(1,128)}), s32[8,1,256]{2,1,0:T(1,128)S(1)}, u32[]{:S(2)}, u32[]{:S(2)}) %all-to-all-start.2) | async-done | bytes 8224 | tf_op jit(solution)/shard_map/all_to_all | solution.py:133
  50.5 0.0 all-gather.2.cloned.1.call-update
  50.5 0.0 copy-done
  50.5 0.7 copy.19.lists_ref
  51.2 6.5 %scatter_custom_fusion.both_ref = bf16[2048,128]{1,0:T(8,128)(2,1)} fusion(s32[2048]{0:T(1024)S(1)} %get-tuple-element.19, bf16[2048,128]{1,0:T(8,128)(2,1)S(1)} %bitcast.33, bf16[]{:T(256)} %constant.6.clone.1), kind=kCustom, calls=%fused_computation.12 | custom fusion | bytes 524290 | tf_op jit(solution)/shard_map/scatter | solution.py:153
  57.7 22.6 %shard_map.88 = (bf16[2048,64]{1,0:T(8,128)(2,1)}, bf16[2048,128]{1,0:T(8,128)(2,1)}) custom-call(s32[16,8]{1,0:T(8,128)} %copy.19.lists_ref, s32[16]{0:T(128)} %bitcast.40, bf16[2048,128]{1,0:T(8,128)(2,1)} %scatter_custom_fusion.both_ref, bf16[2048,64]{1,0:T(8,128)(2,1)} %bitcast.29), custom_call_target="tpu_custom_call" | custom-call | tf_op jit(solution)/shard_map/pallas_call | solution.py:68
  80.3 1.9 %copy.20 = bf16[8,256,64]{1,2,0:T(8,128)(2,1)} copy(bf16[8,256,64]{2,1,0:T(8,128)(2,1)} %bitcast.31) | data formatting | bytes 524288 | tf_op jit(solution)/shard_map/reshape | solution.py:166
  82.2 3.4 %all-to-all-start.3 = ((bf16[8,256,64]{1,2,0:T(8,128)(2,1)}), bf16[8,256,64]{1,2,0:T(8,128)(2,1)S(1)}, u32[]{:S(2)}, u32[]{:S(2)}) async-start(bf16[8,256,64]{1,2,0:T(8,128)(2,1)} %copy.20), calls=%async_computation.3 | async-start | bytes 524288 | tf_op jit(solution)/shard_map/all_to_all | solution.py:165
  85.7 0.0 reduce-scatter.2.cloned.1.call-start
  85.7 6.7 %gather_fusion = bf16[2048,128]{1,0:T(8,128)(2,1)S(1)} fusion(bf16[2048,128]{1,0:T(8,128)(2,1)} %get-tuple-element.13, s32[2048]{0:T(1024)S(1)} %get-tuple-element.18), kind=kCustom, calls=%fused_computation | custom fusion | bytes 1056768 | tf_op jit(solution)/shard_map/gather | solution.py:187
  92.4 0.0 copy-start.2
  92.4 9.0 %all-gather.2.cloned.1.call-done = bf16[2048,1024]{1,0:T(8,128)(2,1)} async-done(((bf16[256,1024]{1,0:T(8,128)(2,1)}), bf16[2048,1024]{1,0:T(8,128)(2,1)}) %all-gather.2.cloned.1.call-update) | async-done | bytes 4194320 | tf_op jit(solution)/shard_map/all_gather | solution.py:149
  101.5 4.3 %fusion.22 = f32[1024,128]{1,0:T(8,128)} fusion(bf16[2048,1024]{1,0:T(8,128)(2,1)} %all-gather.2.cloned.1.call-done, bf16[2048,128]{1,0:T(8,128)(2,1)S(1)} %gather_fusion), kind=kOutput, calls=%fused_computation.16 | convolution fusion | flops 536870912 | bytes 5242880 | tf_op jit(solution)/shard_map/od,oc->dc/dot_general | solution.py:188
  105.7 0.0 reduce-scatter.2.cloned.1.call-update
  105.8 0.0 all-to-all-done.3
  105.8 3.5 %all-to-all-start.4 = ((bf16[8,256,128]{2,1,0:T(8,128)(2,1)}), bf16[8,256,128]{2,1,0:T(8,128)(2,1)S(1)}, u32[]{:S(2)}, u32[]{:S(2)}) async-start(bf16[8,256,128]{2,1,0:T(8,128)(2,1)} %bitcast.12), calls=%async_computation.4 | async-start | bytes 1048576 | tf_op jit(solution)/shard_map/all_to_all | solution.py:172
  109.3 15.3 %all-to-all-done.4 = bf16[8,256,128]{2,1,0:T(8,128)(2,1)S(1)} async-done(((bf16[8,256,128]{2,1,0:T(8,128)(2,1)}), bf16[8,256,128]{2,1,0:T(8,128)(2,1)S(1)}, u32[]{:S(2)}, u32[]{:S(2)}) %all-to-all-start.4) | async-done | bytes 524320 | tf_op jit(solution)/shard_map/all_to_all | solution.py:172
  124.6 5.0 %reduce-scatter.2.cloned.1.call-done = f32[256,128]{1,0:T(8,128)} async-done(((f32[1024,128]{1,0:T(8,128)}), f32[256,128]{1,0:T(8,128)}) %reduce-scatter.2.cloned.1.call-update) | async-done | bytes 131088 | tf_op jit(solution)/shard_map/reduce_scatter | solution.py:191
  129.6 4.6 %all-to-all-start.5 = ((f32[8,32,128]{2,1,0:T(8,128)}), f32[8,32,128]{2,1,0:T(8,128)S(1)}, u32[]{:S(2)}, u32[]{:S(2)}) async-start(f32[8,32,128]{2,1,0:T(8,128)} %bitcast.36), calls=%async_computation.6 | async-start | bytes 262144 | tf_op jit(solution)/shard_map/all_to_all | solution.py:192
  134.2 0.0 copy-done.2
  134.2 1.5 %fusion.16 = bf16[1,256,1024]{2,1,0:T(8,128)(2,1)} fusion(bf16[8,256,128]{2,1,0:T(8,128)(2,1)S(1)} %all-to-all-done.4, bf16[1024,8,128]{2,1,0:T(8,128)(2,1)S(1)} %copy-done.2), kind=kOutput, calls=%fused_computation.10 | convolution fusion | flops 537133056 | bytes 3145728 | tf_op jit(solution)/shard_map/htc,dhc->td/dot_general | solution.py:182
  135.8 5.2 %all-to-all-done.5 = f32[8,32,128]{2,1,0:T(8,128)S(1)} async-done(((f32[8,32,128]{2,1,0:T(8,128)}), f32[8,32,128]{2,1,0:T(8,128)S(1)}, u32[]{:S(2)}, u32[]{:S(2)}) %all-to-all-start.5) | async-done | bytes 131104 | tf_op jit(solution)/shard_map/all_to_all | solution.py:192
  141.0 0.7 copy.22
  141.7 0.7 copy.38
  (1 shorter events, 0.0 us)
Async XLA Ops:
  7.2 16.1 %all-to-all-start.1 = ((bf16[8,256,64]{1,2,0:T(8,128)(2,1)}), bf16[8,256,64]{1,2,0:T(8,128)(2,1)S(1)}, u32[]{:S(2)}, u32[]{:S(2)}) async-start(bf16[8,256,64]{1,2,0:T(8,128)(2,1)} %bitcast.35), calls=%async_computation.1 | async-start | bytes 524288 | tf_op jit(solution)/shard_map/all_to_all | solution.py:130
  13.5 27.5 %copy-start.1 = (s32[1,256]{1,0:T(1,128)S(1)}, s32[1,256]{1,0:T(1,128)}, u32[]{:S(2)}) copy-start(s32[1,256]{1,0:T(1,128)} %param.7) | copy-start | bytes 3076
  16.0 34.5 %copy-start = (s32[1,16,8]{1,2,0:T(8,128)S(1)}, s32[1,16,8]{1,2,0:T(8,128)}, u32[]{:S(2)}) copy-start(s32[1,16,8]{1,2,0:T(8,128)} %param.9) | copy-start | bytes 1540
  41.6 8.9 %all-to-all-start.2 = ((s32[8,1,256]{2,1,0:T(1,128)}), s32[8,1,256]{2,1,0:T(1,128)S(1)}, u32[]{:S(2)}, u32[]{:S(2)}) async-start(s32[8,1,256]{2,1,0:T(1,128)} %broadcast_in_dim.19), calls=%async_computation.2 | async-start | bytes 16384 | tf_op jit(solution)/shard_map/all_to_all | solution.py:133
  45.0 56.5 %all-gather.2.cloned.1.call-start = ((), (), s32[]{:S(2)}) async-start(), calls=%async_computation.7 | async-start | bytes 4718592 | tf_op jit(solution)/shard_map/all_gather | solution.py:149
  82.2 23.5 %all-to-all-start.3 = ((bf16[8,256,64]{1,2,0:T(8,128)(2,1)}), bf16[8,256,64]{1,2,0:T(8,128)(2,1)S(1)}, u32[]{:S(2)}, u32[]{:S(2)}) async-start(bf16[8,256,64]{1,2,0:T(8,128)(2,1)} %copy.20), calls=%async_computation.3 | async-start | bytes 524288 | tf_op jit(solution)/shard_map/all_to_all | solution.py:165
  85.7 44.0 %reduce-scatter.2.cloned.1.call-start = ((), (), s32[]{:S(2)}) async-start(), calls=%async_computation.8 | async-start | bytes 655360 | tf_op jit(solution)/shard_map/reduce_scatter | solution.py:191
  92.4 41.8 %copy-start.2 = (bf16[1024,8,128]{2,1,0:T(8,128)(2,1)S(1)}, bf16[1024,8,128]{2,1,0:T(8,128)(2,1)}, u32[]{:S(2)}) copy-start(bf16[1024,8,128]{2,1,0:T(8,128)(2,1)} %param.8) | copy-start | bytes 6291460
  105.8 18.8 %all-to-all-start.4 = ((bf16[8,256,128]{2,1,0:T(8,128)(2,1)}), bf16[8,256,128]{2,1,0:T(8,128)(2,1)S(1)}, u32[]{:S(2)}, u32[]{:S(2)}) async-start(bf16[8,256,128]{2,1,0:T(8,128)(2,1)} %bitcast.12), calls=%async_computation.4 | async-start | bytes 1048576 | tf_op jit(solution)/shard_map/all_to_all | solution.py:172
  129.6 11.4 %all-to-all-start.5 = ((f32[8,32,128]{2,1,0:T(8,128)}), f32[8,32,128]{2,1,0:T(8,128)S(1)}, u32[]{:S(2)}, u32[]{:S(2)}) async-start(f32[8,32,128]{2,1,0:T(8,128)} %bitcast.36), calls=%async_computation.6 | async-start | bytes 262144 | tf_op jit(solution)/shard_map/all_to_all | solution.py:192
Sparse Core Ops, SparseCore 0:
  50.6 50.7 all-gather.1
  105.9 23.6 reduce-scatter.1

commit v7 on v6

--- a/solution.py
+++ b/solution.py
@@ -143,8 +143,8 @@
         proj_owned = lax.all_to_all(
             proj_mine, "seq", split_axis=0, concat_axis=0, tiled=True
         ).reshape(seq_count * tokens_here, 2 * depth)
-        later_rows, proj_owned, grad_rows, places_all = lax.optimization_barrier(
-            (rows_here, proj_owned, grad_rows, places_all)
+        later_rows, proj_owned, grad_rows = lax.optimization_barrier(
+            (rows_here, proj_owned, grad_rows)
         )
         owned_all = lax.all_gather(later_rows, "seq", axis=0, tiled=True)
         gathered = (

time: 150 us -> 144 us (0.960)
  blocking collectives: 17.8 us -> 0 us
  waiting for transfers between devices: 46.1 us -> 52.2 us
  starting transfers between devices: 21.3 us -> 26.3 us
    all_to_all x1 -> x0, blocking collectives: 17.8 us -> none  [local(): lax.all_to_all(proj_mine, 'seq', split_axis=0, concat_axis=0, tiled=True)]
    all_to_all x0 -> x1, waiting for transfers between devices: none -> 14.2 us  [local(): lax.all_to_all(proj_mine, 'seq', split_axis=0, concat_axis=0, tiled=True)]
    all_gather x1, waiting for transfers between devices: 9.04 us -> 0.02 us  [local(): owned_all = lax.all_gather(later_rows, 'seq', axis=0, tiled=True)]
    all_to_all x0 -> x1, starting transfers between devices: none -> 3.49 us  [local(): lax.all_to_all(proj_mine, 'seq', split_axis=0, concat_axis=0, tiled=True)]
  transfers between devices with their start and end apart: 7 -> 8, of which waited for: 6 -> 6; matrix products, arithmetic and copies ran while one was open for 17% -> 19% of each run, Pallas kernels for 15% -> 16%
where the time goes in v7:
time: 144 us; the launch traced here: 143 us
  waiting for transfers between devices  52.2 us (36%)
  starting transfers between devices  26.3 us (18%)
  Pallas kernels  22.3 us (15%)
  local copies, waits for them, and re-layouts  19.2 us (13%)
  between operations  14.1 us (10%)
  matrix products  9.21 us (6%)
    pallas_call x1, Pallas kernels, attend_group(): pl.pallas_call(attention_kernel, out_shape=(jax.ShapeDtypeStruct((total,...  22.3 us
    all_to_all x1, waiting for transfers between devices, local(): lax.all_to_all(grad_both.reshape(seq_count, portion, 2 * depth), 'seq', s...  15.4 us
    all_to_all x1, waiting for transfers between devices, local(): lax.all_to_all(proj_mine, 'seq', split_axis=0, concat_axis=0, tiled=True)  14.2 us
    gather x1, local copies, waits for them, and re-layouts, local(): head_grad = grad_both[places_all]  6.7 us
    scatter x1, local copies, waits for them, and re-layouts, local(): gathered = jnp.zeros(proj_owned.shape, proj_owned.dtype).at[places_all].s...  6.51 us
    all_to_all x1, waiting for transfers between devices, local(): lax.all_to_all(upstream, 'seq', split_axis=0, concat_axis=0, tiled=True)  6.48 us
    all_to_all x1, starting transfers between devices, local(): lax.all_to_all(upstream, 'seq', split_axis=0, concat_axis=0, tiled=True)  6.34 us
    reduce_scatter x1, waiting for transfers between devices, local(): summed = lax.psum_scatter(partial, 'rec', scatter_dimension=0, tiled=True)  5.95 us
  transfers between devices with their start and end apart: 8, of which 6 were waited for; matrix products, arithmetic and copies ran while one was open for 19% of the time, Pallas kernels for 16%

profile of v7, /device:TPU:0, one launch (start us, length us, event | category | flops | bytes accessed | tf_op | source)
XLA Modules:
  0.0 143.3 jit_solution(607030080318795066)
XLA Ops:
  7.2 6.3 %all-to-all-start.2 = ((bf16[8,256,64]{1,2,0:T(8,128)(2,1)}), bf16[8,256,64]{1,2,0:T(8,128)(2,1)S(1)}, u32[]{:S(2)}, u32[]{:S(2)}) async-start(bf16[8,256,64]{1,2,0:T(8,128)(2,1)} %bitcast.37), calls=%async_computation.2 | async-start | bytes 524288 | tf_op jit(solution)/shard_map/all_to_all | solution.py:130
  13.5 3.3 %fusion.13 = bf16[8,256,128]{1,2,0:T(8,128)(2,1)} fusion(bf16[1024,8,128]{2,1,0:T(8,128)(2,1)} %param.8, bf16[1,256,1024]{2,1,0:T(8,128)(2,1)} %param.6), kind=kOutput, calls=%fused_computation.9 | convolution fusion | flops 537133056 | bytes 3145728 | tf_op jit(solution)/shard_map/td,dhc->htc/dot_general | solution.py:140
  16.8 0.0 copy-start.1
  16.8 0.0 copy-start
  16.8 6.5 %all-to-all-done.2 = bf16[8,256,64]{1,2,0:T(8,128)(2,1)S(1)} async-done(((bf16[8,256,64]{1,2,0:T(8,128)(2,1)}), bf16[8,256,64]{1,2,0:T(8,128)(2,1)S(1)}, u32[]{:S(2)}, u32[]{:S(2)}) %all-to-all-start.2) | async-done | bytes 262176 | tf_op jit(solution)/shard_map/all_to_all | solution.py:130
  23.2 3.5 %all-to-all-start.1 = ((bf16[8,256,128]{1,2,0:T(8,128)(2,1)}), bf16[8,256,128]{1,2,0:T(8,128)(2,1)S(1)}, u32[]{:S(2)}, u32[]{:S(2)}) async-start(bf16[8,256,128]{1,2,0:T(8,128)(2,1)} %fusion.13), calls=%async_computation.1 | async-start | bytes 1048576 | tf_op jit(solution)/shard_map/all_to_all | solution.py:143
  26.7 0.0 all-gather.2.cloned.1.call-start
  26.8 1.0 copy.18
  27.8 14.2 %all-to-all-done.1 = bf16[8,256,128]{1,2,0:T(8,128)(2,1)S(1)} async-done(((bf16[8,256,128]{1,2,0:T(8,128)(2,1)}), bf16[8,256,128]{1,2,0:T(8,128)(2,1)S(1)}, u32[]{:S(2)}, u32[]{:S(2)}) %all-to-all-start.1) | async-done | bytes 524320 | tf_op jit(solution)/shard_map/all_to_all | solution.py:143
  42.0 0.3 copy.17
  42.3 0.0 all-gather.2.cloned.1.call-update
  42.3 0.0 copy-done.1
  42.3 0.6 broadcast_in_dim.17
  42.9 3.3 %all-to-all-start = ((s32[8,1,256]{2,1,0:T(1,128)}), s32[8,1,256]{2,1,0:T(1,128)S(1)}, u32[]{:S(2)}, u32[]{:S(2)}) async-start(s32[8,1,256]{2,1,0:T(1,128)} %broadcast_in_dim.17), calls=%async_computation | async-start | bytes 16384 | tf_op jit(solution)/shard_map/all_to_all | solution.py:133
  46.3 0.0 copy-done
  46.3 0.7 copy.19.lists_ref
  47.0 4.9 %all-to-all-done = s32[8,1,256]{2,1,0:T(1,128)S(1)} async-done(((s32[8,1,256]{2,1,0:T(1,128)}), s32[8,1,256]{2,1,0:T(1,128)S(1)}, u32[]{:S(2)}, u32[]{:S(2)}) %all-to-all-start) | async-done | bytes 8224 | tf_op jit(solution)/shard_map/all_to_all | solution.py:133
  51.9 6.5 %scatter_custom_fusion.both_ref = bf16[2048,128]{1,0:T(8,128)(2,1)} fusion(s32[2048]{0:T(1024)S(1)} %bitcast.41, bf16[2048,128]{1,0:T(8,128)(2,1)S(1)} %bitcast.35, bf16[]{:T(256)} %constant.6.clone.1), kind=kCustom, calls=%fused_computation.12 | custom fusion | bytes 524290 | tf_op jit(solution)/shard_map/scatter | solution.py:153
  58.5 22.3 %shard_map.88 = (bf16[2048,64]{1,0:T(8,128)(2,1)}, bf16[2048,128]{1,0:T(8,128)(2,1)}) custom-call(s32[16,8]{1,0:T(8,128)} %copy.19.lists_ref, s32[16]{0:T(128)} %bitcast.44, bf16[2048,128]{1,0:T(8,128)(2,1)} %scatter_custom_fusion.both_ref, bf16[2048,64]{1,0:T(8,128)(2,1)} %bitcast.31), custom_call_target="tpu_custom_call" | custom-call | tf_op jit(solution)/shard_map/pallas_call | solution.py:68
  80.8 1.9 %copy.20 = bf16[8,256,64]{1,2,0:T(8,128)(2,1)} copy(bf16[8,256,64]{2,1,0:T(8,128)(2,1)} %bitcast.33) | data formatting | bytes 524288 | tf_op jit(solution)/shard_map/reshape | solution.py:166
  82.7 3.4 %all-to-all-start.3 = ((bf16[8,256,64]{1,2,0:T(8,128)(2,1)}), bf16[8,256,64]{1,2,0:T(8,128)(2,1)S(1)}, u32[]{:S(2)}, u32[]{:S(2)}) async-start(bf16[8,256,64]{1,2,0:T(8,128)(2,1)} %copy.20), calls=%async_computation.3 | async-start | bytes 524288 | tf_op jit(solution)/shard_map/all_to_all | solution.py:165
  86.1 0.0 reduce-scatter.2.cloned.1.call-start
  86.2 6.7 %gather_fusion = bf16[2048,128]{1,0:T(8,128)(2,1)S(1)} fusion(bf16[2048,128]{1,0:T(8,128)(2,1)} %get-tuple-element.11, s32[2048]{0:T(1024)S(1)} %broadcast_clamp_fusion), kind=kCustom, calls=%fused_computation | custom fusion | bytes 1056768 | tf_op jit(solution)/shard_map/gather | solution.py:187
  92.9 0.0 copy-start.2
  92.9 0.0 all-gather.2.cloned.1.call-done
  92.9 4.4 %fusion.22 = f32[1024,128]{1,0:T(8,128)} fusion(bf16[2048,1024]{1,0:T(8,128)(2,1)} %all-gather.2.cloned.1.call-done, bf16[2048,128]{1,0:T(8,128)(2,1)S(1)} %gather_fusion), kind=kOutput, calls=%fused_computation.16 | convolution fusion | flops 536870912 | bytes 5242880 | tf_op jit(solution)/shard_map/od,oc->dc/dot_general | solution.py:188
  97.3 0.0 reduce-scatter.2.cloned.1.call-update
  97.3 0.0 all-to-all-done.3
  97.4 5.0 %all-to-all-start.4 = ((bf16[8,256,128]{2,1,0:T(8,128)(2,1)}), bf16[8,256,128]{2,1,0:T(8,128)(2,1)S(1)}, u32[]{:S(2)}, u32[]{:S(2)}) async-start(bf16[8,256,128]{2,1,0:T(8,128)(2,1)} %bitcast.13), calls=%async_computation.4 | async-start | bytes 1048576 | tf_op jit(solution)/shard_map/all_to_all | solution.py:172
  102.3 15.4 %all-to-all-done.4 = bf16[8,256,128]{2,1,0:T(8,128)(2,1)S(1)} async-done(((bf16[8,256,128]{2,1,0:T(8,128)(2,1)}), bf16[8,256,128]{2,1,0:T(8,128)(2,1)S(1)}, u32[]{:S(2)}, u32[]{:S(2)}) %all-to-all-start.4) | async-done | bytes 524320 | tf_op jit(solution)/shard_map/all_to_all | solution.py:172
  117.7 5.9 %reduce-scatter.2.cloned.1.call-done = f32[256,128]{1,0:T(8,128)} async-done(((f32[1024,128]{1,0:T(8,128)}), f32[256,128]{1,0:T(8,128)}) %reduce-scatter.2.cloned.1.call-update) | async-done | bytes 131088 | tf_op jit(solution)/shard_map/reduce_scatter | solution.py:191
  123.6 4.6 %all-to-all-start.5 = ((f32[8,32,128]{2,1,0:T(8,128)}), f32[8,32,128]{2,1,0:T(8,128)S(1)}, u32[]{:S(2)}, u32[]{:S(2)}) async-start(f32[8,32,128]{2,1,0:T(8,128)} %bitcast.38), calls=%async_computation.6 | async-start | bytes 262144 | tf_op jit(solution)/shard_map/all_to_all | solution.py:192
  128.3 0.0 copy-done.2
  128.3 1.5 %fusion.16 = bf16[1,256,1024]{2,1,0:T(8,128)(2,1)} fusion(bf16[8,256,128]{2,1,0:T(8,128)(2,1)S(1)} %all-to-all-done.4, bf16[1024,8,128]{2,1,0:T(8,128)(2,1)S(1)} %copy-done.2), kind=kOutput, calls=%fused_computation.10 | convolution fusion | flops 537133056 | bytes 3145728 | tf_op jit(solution)/shard_map/htc,dhc->td/dot_general | solution.py:182
  129.8 5.2 %all-to-all-done.5 = f32[8,32,128]{2,1,0:T(8,128)S(1)} async-done(((f32[8,32,128]{2,1,0:T(8,128)}), f32[8,32,128]{2,1,0:T(8,128)S(1)}, u32[]{:S(2)}, u32[]{:S(2)}) %all-to-all-start.5) | async-done | bytes 131104 | tf_op jit(solution)/shard_map/all_to_all | solution.py:192
  135.0 0.7 copy.22
  135.8 0.7 copy.38
  (2 shorter events, 0.0 us)
Async XLA Ops:
  7.2 16.1 %all-to-all-start.2 = ((bf16[8,256,64]{1,2,0:T(8,128)(2,1)}), bf16[8,256,64]{1,2,0:T(8,128)(2,1)S(1)}, u32[]{:S(2)}, u32[]{:S(2)}) async-start(bf16[8,256,64]{1,2,0:T(8,128)(2,1)} %bitcast.37), calls=%async_computation.2 | async-start | bytes 524288 | tf_op jit(solution)/shard_map/all_to_all | solution.py:130
  16.8 25.6 %copy-start.1 = (s32[1,256]{1,0:T(1,128)S(1)}, s32[1,256]{1,0:T(1,128)}, u32[]{:S(2)}) copy-start(s32[1,256]{1,0:T(1,128)} %param.7) | copy-start | bytes 3076
  16.8 29.5 %copy-start = (s32[1,16,8]{1,2,0:T(8,128)S(1)}, s32[1,16,8]{1,2,0:T(8,128)}, u32[]{:S(2)}) copy-start(s32[1,16,8]{1,2,0:T(8,128)} %param.9) | copy-start | bytes 1540
  23.2 18.8 %all-to-all-start.1 = ((bf16[8,256,128]{1,2,0:T(8,128)(2,1)}), bf16[8,256,128]{1,2,0:T(8,128)(2,1)S(1)}, u32[]{:S(2)}, u32[]{:S(2)}) async-start(bf16[8,256,128]{1,2,0:T(8,128)(2,1)} %fusion.13), calls=%async_computation.1 | async-start | bytes 1048576 | tf_op jit(solution)/shard_map/all_to_all | solution.py:143
  26.7 66.2 %all-gather.2.cloned.1.call-start = ((), (), s32[]{:S(2)}) async-start(), calls=%async_computation.7 | async-start | bytes 4718592 | tf_op jit(solution)/shard_map/all_gather | solution.py:149
  42.9 9.0 %all-to-all-start = ((s32[8,1,256]{2,1,0:T(1,128)}), s32[8,1,256]{2,1,0:T(1,128)S(1)}, u32[]{:S(2)}, u32[]{:S(2)}) async-start(s32[8,1,256]{2,1,0:T(1,128)} %broadcast_in_dim.17), calls=%async_computation | async-start | bytes 16384 | tf_op jit(solution)/shard_map/all_to_all | solution.py:133
  82.7 14.7 %all-to-all-start.3 = ((bf16[8,256,64]{1,2,0:T(8,128)(2,1)}), bf16[8,256,64]{1,2,0:T(8,128)(2,1)S(1)}, u32[]{:S(2)}, u32[]{:S(2)}) async-start(bf16[8,256,64]{1,2,0:T(8,128)(2,1)} %copy.20), calls=%async_computation.3 | async-start | bytes 524288 | tf_op jit(solution)/shard_map/all_to_all | solution.py:165
  86.1 37.5 %reduce-scatter.2.cloned.1.call-start = ((), (), s32[]{:S(2)}) async-start(), calls=%async_computation.8 | async-start | bytes 655360 | tf_op jit(solution)/shard_map/reduce_scatter | solution.py:191
  92.9 35.4 %copy-start.2 = (bf16[1024,8,128]{2,1,0:T(8,128)(2,1)S(1)}, bf16[1024,8,128]{2,1,0:T(8,128)(2,1)}, u32[]{:S(2)}) copy-start(bf16[1024,8,128]{2,1,0:T(8,128)(2,1)} %param.8) | copy-start | bytes 6291460
  97.4 20.4 %all-to-all-start.4 = ((bf16[8,256,128]{2,1,0:T(8,128)(2,1)}), bf16[8,256,128]{2,1,0:T(8,128)(2,1)S(1)}, u32[]{:S(2)}, u32[]{:S(2)}) async-start(bf16[8,256,128]{2,1,0:T(8,128)(2,1)} %bitcast.13), calls=%async_computation.4 | async-start | bytes 1048576 | tf_op jit(solution)/shard_map/all_to_all | solution.py:172
  123.6 11.4 %all-to-all-start.5 = ((f32[8,32,128]{2,1,0:T(8,128)}), f32[8,32,128]{2,1,0:T(8,128)S(1)}, u32[]{:S(2)}, u32[]{:S(2)}) async-start(f32[8,32,128]{2,1,0:T(8,128)} %bitcast.38), calls=%async_computation.6 | async-start | bytes 262144 | tf_op jit(solution)/shard_map/all_to_all | solution.py:192
Sparse Core Ops, SparseCore 0:
  42.5 46.0 all-gather.1
  97.5 26.1 reduce-scatter.1

commit v8 on v7

--- a/solution.py
+++ b/solution.py
@@ -188,7 +188,14 @@
         partial = jnp.einsum(
             "od,oc->dc", owned_all, head_grad, preferred_element_type=jnp.float32
         )
-        summed = lax.psum_scatter(partial, "rec", scatter_dimension=0, tiled=True)
+        pieces = lax.all_to_all(
+            partial.reshape(rec_count, width // rec_count, 2 * depth),
+            "rec",
+            split_axis=0,
+            concat_axis=0,
+            tiled=True,
+        )
+        summed = jnp.sum(pieces, axis=0)
         spread = lax.all_to_all(
             summed.reshape(seq_count, rows_out, 2 * depth),
             "seq",

time: 144 us -> 149 us (1.035)
  blocking collectives: 0 us -> 12.7 us
  waiting for transfers between devices: 52.2 us -> 45.5 us
  starting transfers between devices: 26.3 us -> 24.8 us
    all_to_all x0 -> x1, blocking collectives: none -> 12.7 us  [local(): lax.all_to_all(partial.reshape(rec_count, width // rec_count, 2 * depth),...]
    reduce_scatter x1 -> x0, waiting for transfers between devices: 5.95 us -> none  [local(): summed = lax.psum_scatter(partial, 'rec', scatter_dimension=0, tiled=True)]
  transfers between devices with their start and end apart: 8 -> 7, of which waited for: 6 -> 5; matrix products, arithmetic and copies ran while one was open for 19% -> 18% of each run, Pallas kernels for 16% -> 15%
where the time goes in v8:
time: 149 us; the launch traced here: 148 us
  waiting for transfers between devices  45.5 us (31%)
  starting transfers between devices  24.8 us (17%)
  Pallas kernels  22.4 us (15%)
  local copies, waits for them, and re-layouts  19.2 us (13%)
  between operations  14.1 us (9%)
  blocking collectives  12.7 us (9%)
  matrix products  8.27 us (6%)
    pallas_call x1, Pallas kernels, attend_group(): pl.pallas_call(attention_kernel, out_shape=(jax.ShapeDtypeStruct((total,...  22.4 us
    all_to_all x1, waiting for transfers between devices, local(): lax.all_to_all(grad_both.reshape(seq_count, portion, 2 * depth), 'seq', s...  14.7 us
    all_to_all x1, waiting for transfers between devices, local(): lax.all_to_all(proj_mine, 'seq', split_axis=0, concat_axis=0, tiled=True)  14.2 us
    all_to_all x1, blocking collectives, local(): lax.all_to_all(partial.reshape(rec_count, width // rec_count, 2 * depth),...  12.7 us
    gather x1, local copies, waits for them, and re-layouts, local(): head_grad = grad_both[places_all]  6.7 us
    scatter x1, local copies, waits for them, and re-layouts, local(): gathered = jnp.zeros(proj_owned.shape, proj_owned.dtype).at[places_all].s...  6.51 us
    all_to_all x1, waiting for transfers between devices, local(): lax.all_to_all(upstream, 'seq', split_axis=0, concat_axis=0, tiled=True)  6.48 us
    all_to_all x1, starting transfers between devices, local(): lax.all_to_all(upstream, 'seq', split_axis=0, concat_axis=0, tiled=True)  6.34 us
  transfers between devices with their start and end apart: 7, of which 5 were waited for; matrix products, arithmetic and copies ran while one was open for 18% of the time, Pallas kernels for 15%

profile of v8, /device:TPU:0, one launch (start us, length us, event | category | flops | bytes accessed | tf_op | source)
XLA Modules:
  0.0 147.7 jit_solution(6844218636293339611)
XLA Ops:
  7.2 6.3 %all-to-all-start.2 = ((bf16[8,256,64]{1,2,0:T(8,128)(2,1)}), bf16[8,256,64]{1,2,0:T(8,128)(2,1)S(1)}, u32[]{:S(2)}, u32[]{:S(2)}) async-start(bf16[8,256,64]{1,2,0:T(8,128)(2,1)} %bitcast.39), calls=%async_computation.2 | async-start | bytes 524288 | tf_op jit(solution)/shard_map/all_to_all | solution.py:130
  13.5 3.3 %fusion.13 = bf16[8,256,128]{1,2,0:T(8,128)(2,1)} fusion(bf16[1024,8,128]{2,1,0:T(8,128)(2,1)} %param.8, bf16[1,256,1024]{2,1,0:T(8,128)(2,1)} %param.6), kind=kOutput, calls=%fused_computation.9 | convolution fusion | flops 537133056 | bytes 3145728 | tf_op jit(solution)/shard_map/td,dhc->htc/dot_general | solution.py:140
  16.8 0.0 copy-start.1
  16.8 0.0 copy-start
  16.8 6.5 %all-to-all-done.2 = bf16[8,256,64]{1,2,0:T(8,128)(2,1)S(1)} async-done(((bf16[8,256,64]{1,2,0:T(8,128)(2,1)}), bf16[8,256,64]{1,2,0:T(8,128)(2,1)S(1)}, u32[]{:S(2)}, u32[]{:S(2)}) %all-to-all-start.2) | async-done | bytes 262176 | tf_op jit(solution)/shard_map/all_to_all | solution.py:130
  23.2 3.5 %all-to-all-start.1 = ((bf16[8,256,128]{1,2,0:T(8,128)(2,1)}), bf16[8,256,128]{1,2,0:T(8,128)(2,1)S(1)}, u32[]{:S(2)}, u32[]{:S(2)}) async-start(bf16[8,256,128]{1,2,0:T(8,128)(2,1)} %fusion.13), calls=%async_computation.1 | async-start | bytes 1048576 | tf_op jit(solution)/shard_map/all_to_all | solution.py:143
  26.7 0.0 all-gather.2.cloned.1.call-start
  26.8 1.0 copy.17
  27.8 14.2 %all-to-all-done.1 = bf16[8,256,128]{1,2,0:T(8,128)(2,1)S(1)} async-done(((bf16[8,256,128]{1,2,0:T(8,128)(2,1)}), bf16[8,256,128]{1,2,0:T(8,128)(2,1)S(1)}, u32[]{:S(2)}, u32[]{:S(2)}) %all-to-all-start.1) | async-done | bytes 524320 | tf_op jit(solution)/shard_map/all_to_all | solution.py:143
  42.0 0.3 copy.16
  42.3 0.0 all-gather.2.cloned.1.call-update
  42.3 0.0 copy-done.1
  42.3 0.6 broadcast_in_dim.17
  42.9 3.3 %all-to-all-start = ((s32[8,1,256]{2,1,0:T(1,128)}), s32[8,1,256]{2,1,0:T(1,128)S(1)}, u32[]{:S(2)}, u32[]{:S(2)}) async-start(s32[8,1,256]{2,1,0:T(1,128)} %broadcast_in_dim.17), calls=%async_computation | async-start | bytes 16384 | tf_op jit(solution)/shard_map/all_to_all | solution.py:133
  46.3 0.0 copy-done
  46.3 0.7 copy.18.lists_ref
  47.0 4.9 %all-to-all-done = s32[8,1,256]{2,1,0:T(1,128)S(1)} async-done(((s32[8,1,256]{2,1,0:T(1,128)}), s32[8,1,256]{2,1,0:T(1,128)S(1)}, u32[]{:S(2)}, u32[]{:S(2)}) %all-to-all-start) | async-done | bytes 8224 | tf_op jit(solution)/shard_map/all_to_all | solution.py:133
  51.9 6.5 %scatter_custom_fusion.both_ref = bf16[2048,128]{1,0:T(8,128)(2,1)} fusion(s32[2048]{0:T(1024)S(1)} %bitcast.40, bf16[2048,128]{1,0:T(8,128)(2,1)S(1)} %bitcast.37, bf16[]{:T(256)} %constant.6.clone.1), kind=kCustom, calls=%fused_computation.12 | custom fusion | bytes 524290 | tf_op jit(solution)/shard_map/scatter | solution.py:153
  58.4 22.4 %shard_map.88 = (bf16[2048,64]{1,0:T(8,128)(2,1)}, bf16[2048,128]{1,0:T(8,128)(2,1)}) custom-call(s32[16,8]{1,0:T(8,128)} %copy.18.lists_ref, s32[16]{0:T(128)} %bitcast.45, bf16[2048,128]{1,0:T(8,128)(2,1)} %scatter_custom_fusion.both_ref, bf16[2048,64]{1,0:T(8,128)(2,1)} %bitcast.33), custom_call_target="tpu_custom_call" | custom-call | tf_op jit(solution)/shard_map/pallas_call | solution.py:68
  80.9 1.9 %copy.19 = bf16[8,256,64]{1,2,0:T(8,128)(2,1)} copy(bf16[8,256,64]{2,1,0:T(8,128)(2,1)} %bitcast.35) | data formatting | bytes 524288 | tf_op jit(solution)/shard_map/reshape | solution.py:166
  82.8 3.4 %all-to-all-start.3 = ((bf16[8,256,64]{1,2,0:T(8,128)(2,1)}), bf16[8,256,64]{1,2,0:T(8,128)(2,1)S(1)}, u32[]{:S(2)}, u32[]{:S(2)}) async-start(bf16[8,256,64]{1,2,0:T(8,128)(2,1)} %copy.19), calls=%async_computation.3 | async-start | bytes 524288 | tf_op jit(solution)/shard_map/all_to_all | solution.py:165
  86.3 6.7 %gather_fusion = bf16[2048,128]{1,0:T(8,128)(2,1)S(1)} fusion(bf16[2048,128]{1,0:T(8,128)(2,1)} %get-tuple-element.11, s32[2048]{0:T(1024)S(1)} %broadcast_clamp_fusion), kind=kCustom, calls=%fused_computation | custom fusion | bytes 1056768 | tf_op jit(solution)/shard_map/gather | solution.py:187
  93.0 0.0 all-gather.2.cloned.1.call-done
  93.0 3.5 %fusion.22 = f32[1024,128]{1,0:T(8,128)S(1)} fusion(bf16[2048,1024]{1,0:T(8,128)(2,1)} %all-gather.2.cloned.1.call-done, bf16[2048,128]{1,0:T(8,128)(2,1)S(1)} %gather_fusion), kind=kOutput, calls=%fused_computation.16 | convolution fusion | flops 536870912 | bytes 5242880 | tf_op jit(solution)/shard_map/od,oc->dc/dot_general | solution.py:188
  96.5 0.0 copy-start.2
  96.5 0.0 all-to-all-done.3
  96.5 12.7 %all_to_all.36 = f32[4,256,128]{2,1,0:T(8,128)S(1)} all-to-all(f32[4,256,128]{2,1,0:T(8,128)S(1)} %bitcast.32), channel_id=1, replica_groups=mesh['rec'=4,'seq'=8] {'rec'}, dimensions={0} | all-to-all | bytes 1048576 | tf_op jit(solution)/shard_map/all_to_all | solution.py:191
  109.2 4.8 %all-to-all-start.4 = ((bf16[8,256,128]{2,1,0:T(8,128)(2,1)}), bf16[8,256,128]{2,1,0:T(8,128)(2,1)S(1)}, u32[]{:S(2)}, u32[]{:S(2)}) async-start(bf16[8,256,128]{2,1,0:T(8,128)(2,1)} %bitcast.13), calls=%async_computation.4 | async-start | bytes 1048576 | tf_op jit(solution)/shard_map/all_to_all | solution.py:172
  114.0 0.7 reduce_sum.9
  114.7 14.7 %all-to-all-done.4 = bf16[8,256,128]{2,1,0:T(8,128)(2,1)S(1)} async-done(((bf16[8,256,128]{2,1,0:T(8,128)(2,1)}), bf16[8,256,128]{2,1,0:T(8,128)(2,1)S(1)}, u32[]{:S(2)}, u32[]{:S(2)}) %all-to-all-start.4) | async-done | bytes 524320 | tf_op jit(solution)/shard_map/all_to_all | solution.py:172
  129.4 3.4 %all-to-all-start.6 = ((f32[8,32,128]{2,1,0:T(8,128)}), f32[8,32,128]{2,1,0:T(8,128)S(1)}, u32[]{:S(2)}, u32[]{:S(2)}) async-start(f32[8,32,128]{2,1,0:T(8,128)} %bitcast.17), calls=%async_computation.6 | async-start | bytes 262144 | tf_op jit(solution)/shard_map/all_to_all | solution.py:199
  132.7 0.0 copy-done.2
  132.8 1.5 %fusion.16 = bf16[1,256,1024]{2,1,0:T(8,128)(2,1)} fusion(bf16[8,256,128]{2,1,0:T(8,128)(2,1)S(1)} %all-to-all-done.4, bf16[1024,8,128]{2,1,0:T(8,128)(2,1)S(1)} %copy-done.2), kind=kOutput, calls=%fused_computation.10 | convolution fusion | flops 537133056 | bytes 3145728 | tf_op jit(solution)/shard_map/htc,dhc->td/dot_general | solution.py:182
  134.3 5.2 %all-to-all-done.6 = f32[8,32,128]{2,1,0:T(8,128)S(1)} async-done(((f32[8,32,128]{2,1,0:T(8,128)}), f32[8,32,128]{2,1,0:T(8,128)S(1)}, u32[]{:S(2)}, u32[]{:S(2)}) %all-to-all-start.6) | async-done | bytes 131104 | tf_op jit(solution)/shard_map/all_to_all | solution.py:199
  139.5 0.7 copy.21
  140.2 0.7 copy.37
  (2 shorter events, 0.0 us)
Async XLA Ops:
  7.2 16.1 %all-to-all-start.2 = ((bf16[8,256,64]{1,2,0:T(8,128)(2,1)}), bf16[8,256,64]{1,2,0:T(8,128)(2,1)S(1)}, u32[]{:S(2)}, u32[]{:S(2)}) async-start(bf16[8,256,64]{1,2,0:T(8,128)(2,1)} %bitcast.39), calls=%async_computation.2 | async-start | bytes 524288 | tf_op jit(solution)/shard_map/all_to_all | solution.py:130
  16.8 25.6 %copy-start.1 = (s32[1,256]{1,0:T(1,128)S(1)}, s32[1,256]{1,0:T(1,128)}, u32[]{:S(2)}) copy-start(s32[1,256]{1,0:T(1,128)} %param.7) | copy-start | bytes 3076
  16.8 29.5 %copy-start = (s32[1,16,8]{1,2,0:T(8,128)S(1)}, s32[1,16,8]{1,2,0:T(8,128)}, u32[]{:S(2)}) copy-start(s32[1,16,8]{1,2,0:T(8,128)} %param.9) | copy-start | bytes 1540
  23.2 18.8 %all-to-all-start.1 = ((bf16[8,256,128]{1,2,0:T(8,128)(2,1)}), bf16[8,256,128]{1,2,0:T(8,128)(2,1)S(1)}, u32[]{:S(2)}, u32[]{:S(2)}) async-start(bf16[8,256,128]{1,2,0:T(8,128)(2,1)} %fusion.13), calls=%async_computation.1 | async-start | bytes 1048576 | tf_op jit(solution)/shard_map/all_to_all | solution.py:143
  26.7 66.2 %all-gather.2.cloned.1.call-start = ((), (), s32[]{:S(2)}) async-start(), calls=%async_computation.7 | async-start | bytes 4718592 | tf_op jit(solution)/shard_map/all_gather | solution.py:149
  42.9 9.0 %all-to-all-start = ((s32[8,1,256]{2,1,0:T(1,128)}), s32[8,1,256]{2,1,0:T(1,128)S(1)}, u32[]{:S(2)}, u32[]{:S(2)}) async-start(s32[8,1,256]{2,1,0:T(1,128)} %broadcast_in_dim.17), calls=%async_computation | async-start | bytes 16384 | tf_op jit(solution)/shard_map/all_to_all | solution.py:133
  82.8 13.7 %all-to-all-start.3 = ((bf16[8,256,64]{1,2,0:T(8,128)(2,1)}), bf16[8,256,64]{1,2,0:T(8,128)(2,1)S(1)}, u32[]{:S(2)}, u32[]{:S(2)}) async-start(bf16[8,256,64]{1,2,0:T(8,128)(2,1)} %copy.19), calls=%async_computation.3 | async-start | bytes 524288 | tf_op jit(solution)/shard_map/all_to_all | solution.py:165
  96.5 36.3 %copy-start.2 = (bf16[1024,8,128]{2,1,0:T(8,128)(2,1)S(1)}, bf16[1024,8,128]{2,1,0:T(8,128)(2,1)}, u32[]{:S(2)}) copy-start(bf16[1024,8,128]{2,1,0:T(8,128)(2,1)} %param.8) | copy-start | bytes 6291460
  109.2 20.1 %all-to-all-start.4 = ((bf16[8,256,128]{2,1,0:T(8,128)(2,1)}), bf16[8,256,128]{2,1,0:T(8,128)(2,1)S(1)}, u32[]{:S(2)}, u32[]{:S(2)}) async-start(bf16[8,256,128]{2,1,0:T(8,128)(2,1)} %bitcast.13), calls=%async_computation.4 | async-start | bytes 1048576 | tf_op jit(solution)/shard_map/all_to_all | solution.py:172
  129.4 10.1 %all-to-all-start.6 = ((f32[8,32,128]{2,1,0:T(8,128)}), f32[8,32,128]{2,1,0:T(8,128)S(1)}, u32[]{:S(2)}, u32[]{:S(2)}) async-start(f32[8,32,128]{2,1,0:T(8,128)} %bitcast.17), calls=%async_computation.6 | async-start | bytes 262144 | tf_op jit(solution)/shard_map/all_to_all | solution.py:199
Sparse Core Ops, SparseCore 0:
  42.5 46.0 all-gather.1

commit v9 on v7

--- a/solution.py
+++ b/solution.py
@@ -137,8 +137,9 @@
             concat_axis=0,
             tiled=True,
         ).reshape(-1)
+        rows_ready, places_all = lax.optimization_barrier((rows_here, places_all))
         proj_mine = jnp.einsum(
-            "td,dhc->htc", rows_here, head_weights, preferred_element_type=jnp.float32
+            "td,dhc->htc", rows_ready, head_weights, preferred_element_type=jnp.float32
         ).astype(jnp.bfloat16)
         proj_owned = lax.all_to_all(
             proj_mine, "seq", split_axis=0, concat_axis=0, tiled=True

time: 144 us -> 152 us (1.056)
  blocking collectives: 0 us -> 11.7 us
  starting transfers between devices: 26.3 us -> 18.5 us
  waiting for transfers between devices: 52.2 us -> 56.5 us
    all_to_all x0 -> x1, blocking collectives: none -> 11.7 us  [local(): lax.all_to_all(jnp.broadcast_to(targets[None], (seq_count, tokens_here)),...]
    all_gather x1, waiting for transfers between devices: 0.02 us -> 9.8 us  [local(): owned_all = lax.all_gather(later_rows, 'seq', axis=0, tiled=True)]
    all_to_all x1 -> x0, waiting for transfers between devices: 4.95 us -> none  [local(): lax.all_to_all(jnp.broadcast_to(targets[None], (seq_count, tokens_here)),...]
    all_to_all x1 -> x0, starting transfers between devices: 3.33 us -> none  [local(): lax.all_to_all(jnp.broadcast_to(targets[None], (seq_count, tokens_here)),...]
    all_to_all x1, starting transfers between devices: 6.34 us -> 3.41 us  [local(): lax.all_to_all(upstream, 'seq', split_axis=0, concat_axis=0, tiled=True)]
  transfers between devices with their start and end apart: 8 -> 7, of which waited for: 6 -> 6; matrix products, arithmetic and copies ran while one was open for 19% -> 17% of each run, Pallas kernels for 16% -> 15%
where the time goes in v9:
time: 152 us; the launch traced here: 151 us
  waiting for transfers between devices  56.5 us (37%)
  Pallas kernels  22.6 us (15%)
  local copies, waits for them, and re-layouts  19.1 us (13%)
  starting transfers between devices  18.5 us (12%)
  between operations  14.1 us (9%)
  blocking collectives  11.7 us (8%)
  matrix products  8.35 us (5%)
    pallas_call x1, Pallas kernels, attend_group(): pl.pallas_call(attention_kernel, out_shape=(jax.ShapeDtypeStruct((total,...  22.6 us
    all_to_all x1, waiting for transfers between devices, local(): lax.all_to_all(grad_both.reshape(seq_count, portion, 2 * depth), 'seq', s...  15.3 us
    all_to_all x1, waiting for transfers between devices, local(): lax.all_to_all(proj_mine, 'seq', split_axis=0, concat_axis=0, tiled=True)  14.2 us
    all_to_all x1, blocking collectives, local(): lax.all_to_all(jnp.broadcast_to(targets[None], (seq_count, tokens_here)),...  11.7 us
    all_gather x1, waiting for transfers between devices, local(): owned_all = lax.all_gather(later_rows, 'seq', axis=0, tiled=True)  9.8 us
    all_to_all x1, waiting for transfers between devices, local(): lax.all_to_all(upstream, 'seq', split_axis=0, concat_axis=0, tiled=True)  7.1 us
    gather x1, local copies, waits for them, and re-layouts, local(): head_grad = grad_both[places_all]  6.71 us
    scatter x1, local copies, waits for them, and re-layouts, local(): gathered = jnp.zeros(proj_owned.shape, proj_owned.dtype).at[places_all].s...  6.51 us
  transfers between devices with their start and end apart: 7, of which 6 were waited for; matrix products, arithmetic and copies ran while one was open for 17% of the time, Pallas kernels for 15%

profile of v9, /device:TPU:0, one launch (start us, length us, event | category | flops | bytes accessed | tf_op | source)
XLA Modules:
  0.0 151.0 jit_solution(1764734067515224609)
XLA Ops:
  7.2 0.0 copy-start
  7.2 0.8 broadcast_in_dim.19
  8.0 11.7 %all_to_all.31 = s32[8,1,256]{2,1,0:T(1,128)S(1)} all-to-all(s32[8,1,256]{2,1,0:T(1,128)S(1)} %broadcast_in_dim.19), channel_id=1, replica_groups=mesh['rec'=4,'seq'=8] {'seq'}, dimensions={0} | all-to-all | bytes 16384 | tf_op jit(solution)/shard_map/all_to_all | solution.py:133
  19.7 3.4 %all-to-all-start.2 = ((bf16[8,256,64]{1,2,0:T(8,128)(2,1)}), bf16[8,256,64]{1,2,0:T(8,128)(2,1)S(1)}, u32[]{:S(2)}, u32[]{:S(2)}) async-start(bf16[8,256,64]{1,2,0:T(8,128)(2,1)} %bitcast.37), calls=%async_computation.2 | async-start | bytes 524288 | tf_op jit(solution)/shard_map/all_to_all | solution.py:130
  23.1 0.0 copy-done
  23.2 2.5 %fusion.13 = bf16[8,256,128]{2,1,0:T(8,128)(2,1)} fusion(bf16[1024,8,128]{2,1,0:T(8,128)(2,1)S(1)} %copy-done, bf16[256,1024]{1,0:T(8,128)(2,1)} %bitcast.33), kind=kOutput, calls=%fused_computation.9 | convolution fusion | flops 537133056 | bytes 3145728 | tf_op jit(solution)/shard_map/td,dhc->htc/dot_general | solution.py:141
  25.7 0.0 copy-start.1
  25.7 7.1 %all-to-all-done.2 = bf16[8,256,64]{1,2,0:T(8,128)(2,1)S(1)} async-done(((bf16[8,256,64]{1,2,0:T(8,128)(2,1)}), bf16[8,256,64]{1,2,0:T(8,128)(2,1)S(1)}, u32[]{:S(2)}, u32[]{:S(2)}) %all-to-all-start.2) | async-done | bytes 262176 | tf_op jit(solution)/shard_map/all_to_all | solution.py:130
  32.8 3.5 %all-to-all-start.1 = ((bf16[8,256,128]{2,1,0:T(8,128)(2,1)}), bf16[8,256,128]{2,1,0:T(8,128)(2,1)S(1)}, u32[]{:S(2)}, u32[]{:S(2)}) async-start(bf16[8,256,128]{2,1,0:T(8,128)(2,1)} %fusion.13), calls=%async_computation.1 | async-start | bytes 1048576 | tf_op jit(solution)/shard_map/all_to_all | solution.py:144
  36.3 0.0 all-gather.2.cloned.1.call-start
  36.4 1.0 copy.16
  37.4 14.2 %all-to-all-done.1 = bf16[8,256,128]{2,1,0:T(8,128)(2,1)S(1)} async-done(((bf16[8,256,128]{2,1,0:T(8,128)(2,1)}), bf16[8,256,128]{2,1,0:T(8,128)(2,1)S(1)}, u32[]{:S(2)}, u32[]{:S(2)}) %all-to-all-start.1) | async-done | bytes 524320 | tf_op jit(solution)/shard_map/all_to_all | solution.py:144
  51.6 0.0 all-gather.2.cloned.1.call-update
  51.6 0.0 copy-done.1
  51.6 0.7 copy.17.lists_ref
  52.3 6.5 %scatter_custom_fusion.both_ref = bf16[2048,128]{1,0:T(8,128)(2,1)} fusion(s32[2048]{0:T(1024)S(1)} %get-tuple-element.21, bf16[2048,128]{1,0:T(8,128)(2,1)S(1)} %bitcast.35, bf16[]{:T(256)} %constant.6.clone.1), kind=kCustom, calls=%fused_computation.12 | custom fusion | bytes 524290 | tf_op jit(solution)/shard_map/scatter | solution.py:154
  58.8 22.6 %shard_map.88 = (bf16[2048,64]{1,0:T(8,128)(2,1)}, bf16[2048,128]{1,0:T(8,128)(2,1)}) custom-call(s32[16,8]{1,0:T(8,128)} %copy.17.lists_ref, s32[16]{0:T(128)} %bitcast.42, bf16[2048,128]{1,0:T(8,128)(2,1)} %scatter_custom_fusion.both_ref, bf16[2048,64]{1,0:T(8,128)(2,1)} %bitcast.30), custom_call_target="tpu_custom_call" | custom-call | tf_op jit(solution)/shard_map/pallas_call | solution.py:68
  81.5 1.9 %copy.18 = bf16[8,256,64]{1,2,0:T(8,128)(2,1)} copy(bf16[8,256,64]{2,1,0:T(8,128)(2,1)} %bitcast.32) | data formatting | bytes 524288 | tf_op jit(solution)/shard_map/reshape | solution.py:167
  83.4 3.4 %all-to-all-start.3 = ((bf16[8,256,64]{1,2,0:T(8,128)(2,1)}), bf16[8,256,64]{1,2,0:T(8,128)(2,1)S(1)}, u32[]{:S(2)}, u32[]{:S(2)}) async-start(bf16[8,256,64]{1,2,0:T(8,128)(2,1)} %copy.18), calls=%async_computation.3 | async-start | bytes 524288 | tf_op jit(solution)/shard_map/all_to_all | solution.py:166
  86.8 0.0 reduce-scatter.2.cloned.1.call-start
  86.9 6.7 %gather_fusion = bf16[2048,128]{1,0:T(8,128)(2,1)S(1)} fusion(bf16[2048,128]{1,0:T(8,128)(2,1)} %get-tuple-element.15, s32[2048]{0:T(1024)S(1)} %get-tuple-element.20), kind=kCustom, calls=%fused_computation | custom fusion | bytes 1056768 | tf_op jit(solution)/shard_map/gather | solution.py:188
  93.6 9.8 %all-gather.2.cloned.1.call-done = bf16[2048,1024]{1,0:T(8,128)(2,1)} async-done(((bf16[256,1024]{1,0:T(8,128)(2,1)}), bf16[2048,1024]{1,0:T(8,128)(2,1)}) %all-gather.2.cloned.1.call-update) | async-done | bytes 4194320 | tf_op jit(solution)/shard_map/all_gather | solution.py:150
  103.4 4.3 %fusion.22 = f32[1024,128]{1,0:T(8,128)} fusion(bf16[2048,1024]{1,0:T(8,128)(2,1)} %all-gather.2.cloned.1.call-done, bf16[2048,128]{1,0:T(8,128)(2,1)S(1)} %gather_fusion), kind=kOutput, calls=%fused_computation.16 | convolution fusion | flops 536870912 | bytes 5242880 | tf_op jit(solution)/shard_map/od,oc->dc/dot_general | solution.py:189
  107.6 0.0 reduce-scatter.2.cloned.1.call-update
  107.7 0.0 all-to-all-done.3
  107.7 3.5 %all-to-all-start.4 = ((bf16[8,256,128]{2,1,0:T(8,128)(2,1)}), bf16[8,256,128]{2,1,0:T(8,128)(2,1)S(1)}, u32[]{:S(2)}, u32[]{:S(2)}) async-start(bf16[8,256,128]{2,1,0:T(8,128)(2,1)} %bitcast.12), calls=%async_computation.4 | async-start | bytes 1048576 | tf_op jit(solution)/shard_map/all_to_all | solution.py:173
  111.2 15.3 %all-to-all-done.4 = bf16[8,256,128]{2,1,0:T(8,128)(2,1)S(1)} async-done(((bf16[8,256,128]{2,1,0:T(8,128)(2,1)}), bf16[8,256,128]{2,1,0:T(8,128)(2,1)S(1)}, u32[]{:S(2)}, u32[]{:S(2)}) %all-to-all-start.4) | async-done | bytes 524320 | tf_op jit(solution)/shard_map/all_to_all | solution.py:173
  126.5 4.9 %reduce-scatter.2.cloned.1.call-done = f32[256,128]{1,0:T(8,128)} async-done(((f32[1024,128]{1,0:T(8,128)}), f32[256,128]{1,0:T(8,128)}) %reduce-scatter.2.cloned.1.call-update) | async-done | bytes 131088 | tf_op jit(solution)/shard_map/reduce_scatter | solution.py:192
  131.3 4.6 %all-to-all-start.5 = ((f32[8,32,128]{2,1,0:T(8,128)}), f32[8,32,128]{2,1,0:T(8,128)S(1)}, u32[]{:S(2)}, u32[]{:S(2)}) async-start(f32[8,32,128]{2,1,0:T(8,128)} %bitcast.38), calls=%async_computation.6 | async-start | bytes 262144 | tf_op jit(solution)/shard_map/all_to_all | solution.py:193
  135.9 1.5 %fusion.16 = bf16[1,256,1024]{2,1,0:T(8,128)(2,1)} fusion(bf16[8,256,128]{2,1,0:T(8,128)(2,1)S(1)} %all-to-all-done.4, bf16[1024,8,128]{2,1,0:T(8,128)(2,1)S(1)} %copy-done), kind=kOutput, calls=%fused_computation.10 | convolution fusion | flops 537133056 | bytes 3145728 | tf_op jit(solution)/shard_map/htc,dhc->td/dot_general | solution.py:183
  137.5 5.2 %all-to-all-done.5 = f32[8,32,128]{2,1,0:T(8,128)S(1)} async-done(((f32[8,32,128]{2,1,0:T(8,128)}), f32[8,32,128]{2,1,0:T(8,128)S(1)}, u32[]{:S(2)}, u32[]{:S(2)}) %all-to-all-start.5) | async-done | bytes 131104 | tf_op jit(solution)/shard_map/all_to_all | solution.py:193
  142.7 0.7 copy.20
  143.5 0.7 copy.36
  (1 shorter events, 0.0 us)
Async XLA Ops:
  7.2 16.0 %copy-start = (bf16[1024,8,128]{2,1,0:T(8,128)(2,1)S(1)}, bf16[1024,8,128]{2,1,0:T(8,128)(2,1)}, u32[]{:S(2)}) copy-start(bf16[1024,8,128]{2,1,0:T(8,128)(2,1)} %param.8) | copy-start | bytes 6291460
  19.7 13.1 %all-to-all-start.2 = ((bf16[8,256,64]{1,2,0:T(8,128)(2,1)}), bf16[8,256,64]{1,2,0:T(8,128)(2,1)S(1)}, u32[]{:S(2)}, u32[]{:S(2)}) async-start(bf16[8,256,64]{1,2,0:T(8,128)(2,1)} %bitcast.37), calls=%async_computation.2 | async-start | bytes 524288 | tf_op jit(solution)/shard_map/all_to_all | solution.py:130
  25.7 25.9 %copy-start.1 = (s32[1,16,8]{1,2,0:T(8,128)S(1)}, s32[1,16,8]{1,2,0:T(8,128)}, u32[]{:S(2)}) copy-start(s32[1,16,8]{1,2,0:T(8,128)} %param.9) | copy-start | bytes 1540
  32.8 18.8 %all-to-all-start.1 = ((bf16[8,256,128]{2,1,0:T(8,128)(2,1)}), bf16[8,256,128]{2,1,0:T(8,128)(2,1)S(1)}, u32[]{:S(2)}, u32[]{:S(2)}) async-start(bf16[8,256,128]{2,1,0:T(8,128)(2,1)} %fusion.13), calls=%async_computation.1 | async-start | bytes 1048576 | tf_op jit(solution)/shard_map/all_to_all | solution.py:144
  36.3 67.1 %all-gather.2.cloned.1.call-start = ((), (), s32[]{:S(2)}) async-start(), calls=%async_computation.7 | async-start | bytes 4718592 | tf_op jit(solution)/shard_map/all_gather | solution.py:150
  83.4 24.3 %all-to-all-start.3 = ((bf16[8,256,64]{1,2,0:T(8,128)(2,1)}), bf16[8,256,64]{1,2,0:T(8,128)(2,1)S(1)}, u32[]{:S(2)}, u32[]{:S(2)}) async-start(bf16[8,256,64]{1,2,0:T(8,128)(2,1)} %copy.18), calls=%async_computation.3 | async-start | bytes 524288 | tf_op jit(solution)/shard_map/all_to_all | solution.py:166
  86.8 44.5 %reduce-scatter.2.cloned.1.call-start = ((), (), s32[]{:S(2)}) async-start(), calls=%async_computation.8 | async-start | bytes 655360 | tf_op jit(solution)/shard_map/reduce_scatter | solution.py:192
  107.7 18.8 %all-to-all-start.4 = ((bf16[8,256,128]{2,1,0:T(8,128)(2,1)}), bf16[8,256,128]{2,1,0:T(8,128)(2,1)S(1)}, u32[]{:S(2)}, u32[]{:S(2)}) async-start(bf16[8,256,128]{2,1,0:T(8,128)(2,1)} %bitcast.12), calls=%async_computation.4 | async-start | bytes 1048576 | tf_op jit(solution)/shard_map/all_to_all | solution.py:173
  131.3 11.4 %all-to-all-start.5 = ((f32[8,32,128]{2,1,0:T(8,128)}), f32[8,32,128]{2,1,0:T(8,128)S(1)}, u32[]{:S(2)}, u32[]{:S(2)}) async-start(f32[8,32,128]{2,1,0:T(8,128)} %bitcast.38), calls=%async_computation.6 | async-start | bytes 262144 | tf_op jit(solution)/shard_map/all_to_all | solution.py:193
Sparse Core Ops, SparseCore 0:
  51.7 51.5 all-gather.1
  107.8 23.5 reduce-scatter.1

commit v10 on v7

--- a/solution.py
+++ b/solution.py
@@ -147,10 +147,10 @@
             (rows_here, proj_owned, grad_rows)
         )
         owned_all = lax.all_gather(later_rows, "seq", axis=0, tiled=True)
-        gathered = (
-            jnp.zeros(proj_owned.shape, proj_owned.dtype)
-            .at[places_all]
-            .set(proj_owned, unique_indices=True)
+        slots = jnp.arange(places_all.shape[0], dtype=places_all.dtype)
+        placing = (slots[:, None] == places_all[None, :]).astype(jnp.bfloat16)
+        gathered = jnp.dot(placing, proj_owned, preferred_element_type=jnp.float32).astype(
+            jnp.bfloat16
         )
     else:
         tokens = route_tokens(rows_here, targets, seq_count, my_index)
@@ -184,7 +184,9 @@
     ).astype(jnp.bfloat16)[None]
     if groups == 1:
         rows_out = width // (rec_count * seq_count)
-        head_grad = grad_both[places_all]
+        head_grad = lax.dot_general(
+            placing, grad_both, (((0,), (0,)), ((), ())), preferred_element_type=jnp.float32
+        ).astype(jnp.bfloat16)
         partial = jnp.einsum(
             "od,oc->dc", owned_all, head_grad, preferred_element_type=jnp.float32
         )

time: 144 us -> 142 us (0.986)
  local copies, waits for them, and re-layouts: 19.2 us -> 5.95 us
  matrix products: 9.21 us -> 18.1 us
  waiting for transfers between devices: 52.2 us -> 55.9 us
    gather x1 -> x0, local copies, waits for them, and re-layouts: 6.7 us -> none  [local(): head_grad = grad_both[places_all]]
    scatter x1 -> x0, local copies, waits for them, and re-layouts: 6.51 us -> none  [local(): gathered = jnp.zeros(proj_owned.shape, proj_owned.dtype).at[places_all].s...]
    dot_general x1, matrix products: 4.4 us -> 9.52 us  [local(): jnp.einsum('od,oc->dc', owned_all, head_grad, preferred_element_type=jnp....]
    all_gather x1, waiting for transfers between devices: 0.02 us -> 4.84 us  [local(): owned_all = lax.all_gather(later_rows, 'seq', axis=0, tiled=True)]
    dot_general x0 -> x1, matrix products: none -> 3.79 us  [local(): jnp.dot(placing, proj_owned, preferred_element_type=jnp.float32)]
    all_to_all x1, starting transfers between devices: 4.99 us -> 3.5 us  [local(): lax.all_to_all(grad_both.reshape(seq_count, portion, 2 * depth), 'seq', s...]
  transfers between devices with their start and end apart: 8 -> 8, of which waited for: 6 -> 7; matrix products, arithmetic and copies ran while one was open for 19% -> 16% of each run, Pallas kernels for 16% -> 16%
where the time goes in v10:
time: 142 us
  waiting for transfers between devices  55.9 us (39%)
  starting transfers between devices  25.1 us (18%)
  Pallas kernels  22.4 us (16%)
  matrix products  18.1 us (13%)
  between operations  14.1 us (10%)
  local copies, waits for them, and re-layouts  5.95 us (4%)
    pallas_call x1, Pallas kernels, attend_group(): pl.pallas_call(attention_kernel, out_shape=(jax.ShapeDtypeStruct((total,...  22.4 us
    all_to_all x1, waiting for transfers between devices, local(): lax.all_to_all(grad_both.reshape(seq_count, portion, 2 * depth), 'seq', s...  15.3 us
    all_to_all x1, waiting for transfers between devices, local(): lax.all_to_all(proj_mine, 'seq', split_axis=0, concat_axis=0, tiled=True)  14.2 us
    dot_general x1, matrix products, local(): jnp.einsum('od,oc->dc', owned_all, head_grad, preferred_element_type=jnp....  9.52 us
    all_to_all x1, waiting for transfers between devices, local(): lax.all_to_all(upstream, 'seq', split_axis=0, concat_axis=0, tiled=True)  6.49 us
    all_to_all x1, starting transfers between devices, local(): lax.all_to_all(upstream, 'seq', split_axis=0, concat_axis=0, tiled=True)  6.47 us
    all_to_all x1, waiting for transfers between devices, local(): lax.all_to_all(summed.reshape(seq_count, rows_out, 2 * depth), 'seq', spl...  5.23 us
    all_to_all x1, waiting for transfers between devices, local(): lax.all_to_all(jnp.broadcast_to(targets[None], (seq_count, tokens_here)),...  4.95 us
  transfers between devices with their start and end apart: 8, of which 7 were waited for; matrix products, arithmetic and copies ran while one was open for 16% of the time, Pallas kernels for 16%

profile of v10, /device:TPU:0, one launch (start us, length us, event | category | flops | bytes accessed | tf_op | source)
XLA Modules:
  0.0 141.5 jit_solution(1876977374350713913)
XLA Ops:
  7.2 0.0 copy-start.1
  7.2 0.0 copy-start
  7.2 6.5 %all-to-all-start.2 = ((bf16[8,256,64]{1,2,0:T(8,128)(2,1)}), bf16[8,256,64]{1,2,0:T(8,128)(2,1)S(1)}, u32[]{:S(2)}, u32[]{:S(2)}) async-start(bf16[8,256,64]{1,2,0:T(8,128)(2,1)} %bitcast.36), calls=%async_computation.2 | async-start | bytes 524288 | tf_op jit(solution)/shard_map/all_to_all | solution.py:130
  13.7 3.2 %fusion.19 = bf16[8,256,128]{1,2,0:T(8,128)(2,1)} fusion(bf16[1024,8,128]{2,1,0:T(8,128)(2,1)} %param.8, bf16[1,256,1024]{2,1,0:T(8,128)(2,1)} %param.6), kind=kOutput, calls=%fused_computation.14 | convolution fusion | flops 537133056 | bytes 3145728 | tf_op jit(solution)/shard_map/td,dhc->htc/dot_general | solution.py:140
  16.9 6.5 %all-to-all-done.2 = bf16[8,256,64]{1,2,0:T(8,128)(2,1)S(1)} async-done(((bf16[8,256,64]{1,2,0:T(8,128)(2,1)}), bf16[8,256,64]{1,2,0:T(8,128)(2,1)S(1)}, u32[]{:S(2)}, u32[]{:S(2)}) %all-to-all-start.2) | async-done | bytes 262176 | tf_op jit(solution)/shard_map/all_to_all | solution.py:130
  23.4 3.5 %all-to-all-start.1 = ((bf16[8,256,128]{1,2,0:T(8,128)(2,1)}), bf16[8,256,128]{1,2,0:T(8,128)(2,1)S(1)}, u32[]{:S(2)}, u32[]{:S(2)}) async-start(bf16[8,256,128]{1,2,0:T(8,128)(2,1)} %fusion.19), calls=%async_computation.1 | async-start | bytes 1048576 | tf_op jit(solution)/shard_map/all_to_all | solution.py:143
  26.9 0.0 all-gather.2.cloned.1.call-start
  26.9 1.0 copy.24
  28.0 14.2 %all-to-all-done.1 = bf16[8,256,128]{1,2,0:T(8,128)(2,1)S(1)} async-done(((bf16[8,256,128]{1,2,0:T(8,128)(2,1)}), bf16[8,256,128]{1,2,0:T(8,128)(2,1)S(1)}, u32[]{:S(2)}, u32[]{:S(2)}) %all-to-all-start.1) | async-done | bytes 524320 | tf_op jit(solution)/shard_map/all_to_all | solution.py:143
  42.2 0.3 copy.23
  42.5 0.0 all-gather.2.cloned.1.call-update
  42.5 0.0 copy-done.1
  42.5 0.6 broadcast_in_dim.12
  43.1 3.3 %all-to-all-start = ((s32[8,1,256]{2,1,0:T(1,128)}), s32[8,1,256]{2,1,0:T(1,128)S(1)}, u32[]{:S(2)}, u32[]{:S(2)}) async-start(s32[8,1,256]{2,1,0:T(1,128)} %broadcast_in_dim.12), calls=%async_computation | async-start | bytes 16384 | tf_op jit(solution)/shard_map/all_to_all | solution.py:133
  46.4 0.0 copy-done
  46.5 0.7 copy.25.lists_ref
  47.1 4.9 %all-to-all-done = s32[8,1,256]{2,1,0:T(1,128)S(1)} async-done(((s32[8,1,256]{2,1,0:T(1,128)}), s32[8,1,256]{2,1,0:T(1,128)S(1)}, u32[]{:S(2)}, u32[]{:S(2)}) %all-to-all-start) | async-done | bytes 8224 | tf_op jit(solution)/shard_map/all_to_all | solution.py:133
  52.1 3.8 %fusion.4.both_ref = bf16[2048,128]{1,0:T(8,128)(2,1)} fusion(bf16[2048,128]{1,0:T(8,128)(2,1)S(1)} %bitcast.34, s32[2048]{0:T(1024)S(1)} %bitcast.38), kind=kOutput, calls=%fused_computation.5 | convolution fusion | flops 1078198272 | bytes 1056768 | tf_op jit(solution)/shard_map/dot_general | solution.py:152
  55.9 22.4 %shard_map.88 = (bf16[2048,64]{1,0:T(8,128)(2,1)}, bf16[2048,128]{1,0:T(8,128)(2,1)}) custom-call(s32[16,8]{1,0:T(8,128)} %copy.25.lists_ref, s32[16]{0:T(128)} %bitcast.42, bf16[2048,128]{1,0:T(8,128)(2,1)} %fusion.4.both_ref, bf16[2048,64]{1,0:T(8,128)(2,1)} %bitcast.30), custom_call_target="tpu_custom_call" | custom-call | tf_op jit(solution)/shard_map/pallas_call | solution.py:68
  78.3 1.9 %copy.26 = bf16[8,256,64]{1,2,0:T(8,128)(2,1)} copy(bf16[8,256,64]{2,1,0:T(8,128)(2,1)} %bitcast.32) | data formatting | bytes 524288 | tf_op jit(solution)/shard_map/reshape | solution.py:166
  80.2 3.4 %all-to-all-start.3 = ((bf16[8,256,64]{1,2,0:T(8,128)(2,1)}), bf16[8,256,64]{1,2,0:T(8,128)(2,1)S(1)}, u32[]{:S(2)}, u32[]{:S(2)}) async-start(bf16[8,256,64]{1,2,0:T(8,128)(2,1)} %copy.26), calls=%async_computation.3 | async-start | bytes 524288 | tf_op jit(solution)/shard_map/all_to_all | solution.py:165
  83.6 0.2 reduce-scatter.2.cloned.1.call-start
  83.9 4.8 %all-gather.2.cloned.1.call-done = bf16[2048,1024]{1,0:T(8,128)(2,1)} async-done(((bf16[256,1024]{1,0:T(8,128)(2,1)}), bf16[2048,1024]{1,0:T(8,128)(2,1)}) %all-gather.2.cloned.1.call-update) | async-done | bytes 4194320 | tf_op jit(solution)/shard_map/all_gather | solution.py:149
  88.7 0.0 copy-start.2
  88.7 9.5 %fusion.25 = f32[1024,128]{1,0:T(8,128)} fusion(bf16[2048,1024]{1,0:T(8,128)(2,1)} %all-gather.2.cloned.1.call-done, bf16[2048,128]{1,0:T(8,128)(2,1)} %get-tuple-element.11, s32[2048]{0:T(1024)S(1)} %bitcast.39), kind=kOutput, calls=%fused_computation.16 | convolution fusion | flops 1615069184 | bytes 5251072 | tf_op jit(solution)/shard_map/od,oc->dc/dot_general | solution.py:190
  98.2 0.0 reduce-scatter.2.cloned.1.call-update
  98.3 0.0 all-to-all-done.3
  98.3 3.5 %all-to-all-start.4 = ((bf16[8,256,128]{2,1,0:T(8,128)(2,1)}), bf16[8,256,128]{2,1,0:T(8,128)(2,1)S(1)}, u32[]{:S(2)}, u32[]{:S(2)}) async-start(bf16[8,256,128]{2,1,0:T(8,128)(2,1)} %bitcast.12), calls=%async_computation.4 | async-start | bytes 1048576 | tf_op jit(solution)/shard_map/all_to_all | solution.py:172
  101.8 15.3 %all-to-all-done.4 = bf16[8,256,128]{2,1,0:T(8,128)(2,1)S(1)} async-done(((bf16[8,256,128]{2,1,0:T(8,128)(2,1)}), bf16[8,256,128]{2,1,0:T(8,128)(2,1)S(1)}, u32[]{:S(2)}, u32[]{:S(2)}) %all-to-all-start.4) | async-done | bytes 524320 | tf_op jit(solution)/shard_map/all_to_all | solution.py:172
  117.1 4.8 %reduce-scatter.2.cloned.1.call-done = f32[256,128]{1,0:T(8,128)} async-done(((f32[1024,128]{1,0:T(8,128)}), f32[256,128]{1,0:T(8,128)}) %reduce-scatter.2.cloned.1.call-update) | async-done | bytes 131088 | tf_op jit(solution)/shard_map/reduce_scatter | solution.py:193
  121.9 4.6 %all-to-all-start.5 = ((f32[8,32,128]{2,1,0:T(8,128)}), f32[8,32,128]{2,1,0:T(8,128)S(1)}, u32[]{:S(2)}, u32[]{:S(2)}) async-start(f32[8,32,128]{2,1,0:T(8,128)} %bitcast.37), calls=%async_computation.6 | async-start | bytes 262144 | tf_op jit(solution)/shard_map/all_to_all | solution.py:194
  126.5 0.0 copy-done.2
  126.5 1.5 %fusion.22 = bf16[1,256,1024]{2,1,0:T(8,128)(2,1)} fusion(bf16[8,256,128]{2,1,0:T(8,128)(2,1)S(1)} %all-to-all-done.4, bf16[1024,8,128]{2,1,0:T(8,128)(2,1)S(1)} %copy-done.2), kind=kOutput, calls=%fused_computation.15 | convolution fusion | flops 537133056 | bytes 3145728 | tf_op jit(solution)/shard_map/htc,dhc->td/dot_general | solution.py:182
  128.0 5.2 %all-to-all-done.5 = f32[8,32,128]{2,1,0:T(8,128)S(1)} async-done(((f32[8,32,128]{2,1,0:T(8,128)}), f32[8,32,128]{2,1,0:T(8,128)S(1)}, u32[]{:S(2)}, u32[]{:S(2)}) %all-to-all-start.5) | async-done | bytes 131104 | tf_op jit(solution)/shard_map/all_to_all | solution.py:194
  133.3 0.7 copy.28
  134.0 0.7 copy.44
Async XLA Ops:
  7.2 35.3 %copy-start.1 = (s32[1,256]{1,0:T(1,128)S(1)}, s32[1,256]{1,0:T(1,128)}, u32[]{:S(2)}) copy-start(s32[1,256]{1,0:T(1,128)} %param.7) | copy-start | bytes 3076
  7.2 39.3 %copy-start = (s32[1,16,8]{1,2,0:T(8,128)S(1)}, s32[1,16,8]{1,2,0:T(8,128)}, u32[]{:S(2)}) copy-start(s32[1,16,8]{1,2,0:T(8,128)} %param.9) | copy-start | bytes 1540
  7.2 16.2 %all-to-all-start.2 = ((bf16[8,256,64]{1,2,0:T(8,128)(2,1)}), bf16[8,256,64]{1,2,0:T(8,128)(2,1)S(1)}, u32[]{:S(2)}, u32[]{:S(2)}) async-start(bf16[8,256,64]{1,2,0:T(8,128)(2,1)} %bitcast.36), calls=%async_computation.2 | async-start | bytes 524288 | tf_op jit(solution)/shard_map/all_to_all | solution.py:130
  23.4 18.8 %all-to-all-start.1 = ((bf16[8,256,128]{1,2,0:T(8,128)(2,1)}), bf16[8,256,128]{1,2,0:T(8,128)(2,1)S(1)}, u32[]{:S(2)}, u32[]{:S(2)}) async-start(bf16[8,256,128]{1,2,0:T(8,128)(2,1)} %fusion.19), calls=%async_computation.1 | async-start | bytes 1048576 | tf_op jit(solution)/shard_map/all_to_all | solution.py:143
  26.9 61.8 %all-gather.2.cloned.1.call-start = ((), (), s32[]{:S(2)}) async-start(), calls=%async_computation.7 | async-start | bytes 4718592 | tf_op jit(solution)/shard_map/all_gather | solution.py:149
  43.1 9.0 %all-to-all-start = ((s32[8,1,256]{2,1,0:T(1,128)}), s32[8,1,256]{2,1,0:T(1,128)S(1)}, u32[]{:S(2)}, u32[]{:S(2)}) async-start(s32[8,1,256]{2,1,0:T(1,128)} %broadcast_in_dim.12), calls=%async_computation | async-start | bytes 16384 | tf_op jit(solution)/shard_map/all_to_all | solution.py:133
  80.2 18.0 %all-to-all-start.3 = ((bf16[8,256,64]{1,2,0:T(8,128)(2,1)}), bf16[8,256,64]{1,2,0:T(8,128)(2,1)S(1)}, u32[]{:S(2)}, u32[]{:S(2)}) async-start(bf16[8,256,64]{1,2,0:T(8,128)(2,1)} %copy.26), calls=%async_computation.3 | async-start | bytes 524288 | tf_op jit(solution)/shard_map/all_to_all | solution.py:165
  83.6 38.2 %reduce-scatter.2.cloned.1.call-start = ((), (), s32[]{:S(2)}) async-start(), calls=%async_computation.8 | async-start | bytes 655360 | tf_op jit(solution)/shard_map/reduce_scatter | solution.py:193
  88.7 37.8 %copy-start.2 = (bf16[1024,8,128]{2,1,0:T(8,128)(2,1)S(1)}, bf16[1024,8,128]{2,1,0:T(8,128)(2,1)}, u32[]{:S(2)}) copy-start(bf16[1024,8,128]{2,1,0:T(8,128)(2,1)} %param.8) | copy-start | bytes 6291460
  98.3 18.8 %all-to-all-start.4 = ((bf16[8,256,128]{2,1,0:T(8,128)(2,1)}), bf16[8,256,128]{2,1,0:T(8,128)(2,1)S(1)}, u32[]{:S(2)}, u32[]{:S(2)}) async-start(bf16[8,256,128]{2,1,0:T(8,128)(2,1)} %bitcast.12), calls=%async_computation.4 | async-start | bytes 1048576 | tf_op jit(solution)/shard_map/all_to_all | solution.py:172
  121.9 11.4 %all-to-all-start.5 = ((f32[8,32,128]{2,1,0:T(8,128)}), f32[8,32,128]{2,1,0:T(8,128)S(1)}, u32[]{:S(2)}, u32[]{:S(2)}) async-start(f32[8,32,128]{2,1,0:T(8,128)} %bitcast.37), calls=%async_computation.6 | async-start | bytes 262144 | tf_op jit(solution)/shard_map/all_to_all | solution.py:194
Sparse Core Ops, SparseCore 0:
  42.6 46.0 all-gather.1
  98.4 23.4 reduce-scatter.1

commit v11 on v10

--- a/solution.py
+++ b/solution.py
@@ -127,16 +127,19 @@
     targets = seq_position[0]
     group = my_index % groups
     upstream = out_grad[0].reshape(seq_count, portion, depth)
-    got_grad = lax.all_to_all(upstream, "seq", split_axis=0, concat_axis=0, tiled=True)
-    grad_rows = got_grad.reshape(seq_count * portion, depth)
     if groups == 1:
-        places_all = lax.all_to_all(
-            jnp.broadcast_to(targets[None], (seq_count, tokens_here)),
-            "seq",
-            split_axis=0,
-            concat_axis=0,
-            tiled=True,
-        ).reshape(-1)
+        extra = ((2 * tokens_here + depth - 1) // depth + 15) // 16 * 16
+        coded = jnp.concatenate([targets // 256, targets % 256]).astype(jnp.bfloat16)
+        coded = jnp.pad(coded, (0, extra * depth - coded.shape[0])).reshape(extra, depth)
+        sent = jnp.concatenate(
+            [upstream, jnp.broadcast_to(coded[None], (seq_count, extra, depth))], axis=1
+        )
+        got_both = lax.all_to_all(sent, "seq", split_axis=0, concat_axis=0, tiled=True)
+        grad_rows = got_both[:, :portion].reshape(seq_count * portion, depth)
+        codes = got_both[:, portion:].reshape(seq_count, extra * depth).astype(jnp.float32)
+        places_all = (
+            codes[:, :tokens_here] * 256 + codes[:, tokens_here : 2 * tokens_here]
+        ).astype(jnp.int32).reshape(-1)
         proj_mine = jnp.einsum(
             "td,dhc->htc", rows_here, head_weights, preferred_element_type=jnp.float32
         ).astype(jnp.bfloat16)
@@ -153,6 +156,8 @@
             jnp.bfloat16
         )
     else:
+        got_grad = lax.all_to_all(upstream, "seq", split_axis=0, concat_axis=0, tiled=True)
+        grad_rows = got_grad.reshape(seq_count * portion, depth)
         tokens = route_tokens(rows_here, targets, seq_count, my_index)
         proj = jnp.einsum(
             "td,dhc->htc", tokens, head_weights, preferred_element_type=jnp.float32

time: 142 us -> 153 us (1.077)
  waiting for transfers between devices: 55.9 us -> 67.6 us
  starting transfers between devices: 25.1 us -> 21.6 us
  other arithmetic: 0 us -> 2.47 us
    all_gather x1, waiting for transfers between devices: 4.84 us -> 19.1 us  [local(): owned_all = lax.all_gather(later_rows, 'seq', axis=0, tiled=True)]
    all_to_all x2 -> x1, starting transfers between devices: 9.8 us -> 6.33 us  [local(): lax.all_to_all(sent, 'seq', split_axis=0, concat_axis=0, tiled=True)]
    all_to_all x2 -> x1, waiting for transfers between devices: 11.4 us -> 9.28 us  [local(): lax.all_to_all(sent, 'seq', split_axis=0, concat_axis=0, tiled=True)]
    concatenate x0 -> x2, other arithmetic: none -> 1.77 us  [the longest x1 1.76 us: local(): jnp.concatenate([upstream, jnp.broadcast_to(coded[None], (seq_count, extr...]
  transfers between devices with their start and end apart: 8 -> 7, of which waited for: 7 -> 6; matrix products, arithmetic and copies ran while one was open for 16% -> 14% of each run, Pallas kernels for 16% -> 15%
where the time goes in v11:
time: 153 us; the launch traced here: 152 us
  waiting for transfers between devices  67.6 us (44%)
  Pallas kernels  22.6 us (15%)
  starting transfers between devices  21.6 us (14%)
  matrix products  18.1 us (12%)
  between operations  14.1 us (9%)
  local copies, waits for them, and re-layouts  5.81 us (4%)
  other arithmetic  2.47 us (2%)
    pallas_call x1, Pallas kernels, attend_group(): pl.pallas_call(attention_kernel, out_shape=(jax.ShapeDtypeStruct((total,...  22.6 us
    all_gather x1, waiting for transfers between devices, local(): owned_all = lax.all_gather(later_rows, 'seq', axis=0, tiled=True)  19.1 us
    all_to_all x1, waiting for transfers between devices, local(): lax.all_to_all(grad_both.reshape(seq_count, portion, 2 * depth), 'seq', s...  15.3 us
    all_to_all x1, waiting for transfers between devices, local(): lax.all_to_all(proj_mine, 'seq', split_axis=0, concat_axis=0, tiled=True)  14.2 us
    dot_general x1, matrix products, local(): jnp.einsum('od,oc->dc', owned_all, head_grad, preferred_element_type=jnp....  9.52 us
    all_to_all x1, waiting for transfers between devices, local(): lax.all_to_all(sent, 'seq', split_axis=0, concat_axis=0, tiled=True)  9.28 us
    all_to_all x1, starting transfers between devices, local(): lax.all_to_all(sent, 'seq', split_axis=0, concat_axis=0, tiled=True)  6.33 us
    all_to_all x1, waiting for transfers between devices, local(): lax.all_to_all(summed.reshape(seq_count, rows_out, 2 * depth), 'seq', spl...  5.22 us
  transfers between devices with their start and end apart: 7, of which 6 were waited for; matrix products, arithmetic and copies ran while one was open for 14% of the time, Pallas kernels for 15%

profile of v11, /device:TPU:0, one launch (start us, length us, event | category | flops | bytes accessed | tf_op | source)
XLA Modules:
  0.0 152.4 jit_solution(2759631962171919710)
XLA Ops:
  7.2 0.7 fusion.33
  7.9 0.1 broadcast_in_dim.14
  7.9 0.1 copy.40
  8.1 1.8 %pad_maximum_fusion = bf16[8,272,64]{1,2,0:T(8,128)(2,1)} fusion(bf16[8,16,64]{1,2,0:T(8,128)(2,1)S(1)} %broadcast_in_dim.15, bf16[8,256,64]{1,2,0:T(8,128)(2,1)} %bitcast.38), kind=kLoop, calls=%fused_computation.18 | loop fusion | flops 557056 | bytes 557056 | tf_op jit(solution)/shard_map/concatenate | solution.py:134
  9.8 6.3 %all-to-all-start = ((bf16[8,272,64]{1,2,0:T(8,128)(2,1)}), bf16[8,272,64]{1,2,0:T(8,128)(2,1)S(1)}, u32[]{:S(2)}, u32[]{:S(2)}) async-start(bf16[8,272,64]{1,2,0:T(8,128)(2,1)} %pad_maximum_fusion), calls=%async_computation | async-start | bytes 786432 | tf_op jit(solution)/shard_map/all_to_all | solution.py:137
  16.2 0.0 copy-start
  16.2 3.3 %fusion.19 = bf16[8,256,128]{1,2,0:T(8,128)(2,1)} fusion(bf16[1024,8,128]{2,1,0:T(8,128)(2,1)} %param.8, bf16[1,256,1024]{2,1,0:T(8,128)(2,1)} %param.6), kind=kOutput, calls=%fused_computation.14 | convolution fusion | flops 537133056 | bytes 3145728 | tf_op jit(solution)/shard_map/td,dhc->htc/dot_general | solution.py:143
  19.4 9.3 %all-to-all-done = bf16[8,272,64]{1,2,0:T(8,128)(2,1)S(1)} async-done(((bf16[8,272,64]{1,2,0:T(8,128)(2,1)}), bf16[8,272,64]{1,2,0:T(8,128)(2,1)S(1)}, u32[]{:S(2)}, u32[]{:S(2)}) %all-to-all-start) | async-done | bytes 278560 | tf_op jit(solution)/shard_map/all_to_all | solution.py:137
  28.7 3.5 %all-to-all-start.1 = ((bf16[8,256,128]{1,2,0:T(8,128)(2,1)}), bf16[8,256,128]{1,2,0:T(8,128)(2,1)S(1)}, u32[]{:S(2)}, u32[]{:S(2)}) async-start(bf16[8,256,128]{1,2,0:T(8,128)(2,1)} %fusion.19), calls=%async_computation.1 | async-start | bytes 1048576 | tf_op jit(solution)/shard_map/all_to_all | solution.py:146
  32.2 0.0 all-gather.2.cloned.1.call-start
  32.3 1.0 copy.44
  33.3 14.2 %all-to-all-done.1 = bf16[8,256,128]{1,2,0:T(8,128)(2,1)S(1)} async-done(((bf16[8,256,128]{1,2,0:T(8,128)(2,1)}), bf16[8,256,128]{1,2,0:T(8,128)(2,1)S(1)}, u32[]{:S(2)}, u32[]{:S(2)}) %all-to-all-start.1) | async-done | bytes 524320 | tf_op jit(solution)/shard_map/all_to_all | solution.py:146
  47.5 0.3 copy.43
  47.8 0.0 all-gather.2.cloned.1.call-update
  47.8 0.0 copy-done
  47.8 0.7 copy.45.lists_ref
  48.5 0.1 copy.49
  48.6 0.1 reshape.31
  48.7 3.8 %fusion.4.both_ref = bf16[2048,128]{1,0:T(8,128)(2,1)} fusion(bf16[2048,128]{1,0:T(8,128)(2,1)S(1)} %bitcast.36, s32[2048]{0:T(1024)S(1)} %bitcast.40), kind=kOutput, calls=%fused_computation.5 | convolution fusion | flops 1078198272 | bytes 1056768 | tf_op jit(solution)/shard_map/dot_general | solution.py:155
  52.5 22.6 %shard_map.85 = (bf16[2048,64]{1,0:T(8,128)(2,1)}, bf16[2048,128]{1,0:T(8,128)(2,1)}) custom-call(s32[16,8]{1,0:T(8,128)} %copy.45.lists_ref, s32[16]{0:T(128)} %bitcast.44, bf16[2048,128]{1,0:T(8,128)(2,1)} %fusion.4.both_ref, bf16[2048,64]{1,0:T(8,128)(2,1)} %bitcast.32), custom_call_target="tpu_custom_call" | custom-call | tf_op jit(solution)/shard_map/pallas_call | solution.py:68
  75.2 1.9 %copy.46 = bf16[8,256,64]{1,2,0:T(8,128)(2,1)} copy(bf16[8,256,64]{2,1,0:T(8,128)(2,1)} %bitcast.34) | data formatting | bytes 524288 | tf_op jit(solution)/shard_map/reshape | solution.py:171
  77.1 3.4 %all-to-all-start.2 = ((bf16[8,256,64]{1,2,0:T(8,128)(2,1)}), bf16[8,256,64]{1,2,0:T(8,128)(2,1)S(1)}, u32[]{:S(2)}, u32[]{:S(2)}) async-start(bf16[8,256,64]{1,2,0:T(8,128)(2,1)} %copy.46), calls=%async_computation.2 | async-start | bytes 524288 | tf_op jit(solution)/shard_map/all_to_all | solution.py:170
  80.5 0.2 reduce-scatter.2.cloned.1.call-start
  80.7 19.1 %all-gather.2.cloned.1.call-done = bf16[2048,1024]{1,0:T(8,128)(2,1)} async-done(((bf16[256,1024]{1,0:T(8,128)(2,1)}), bf16[2048,1024]{1,0:T(8,128)(2,1)}) %all-gather.2.cloned.1.call-update) | async-done | bytes 4194320 | tf_op jit(solution)/shard_map/all_gather | solution.py:152
  99.8 0.0 copy-start.1
  99.8 9.5 %fusion.25 = f32[1024,128]{1,0:T(8,128)} fusion(bf16[2048,1024]{1,0:T(8,128)(2,1)} %all-gather.2.cloned.1.call-done, bf16[2048,128]{1,0:T(8,128)(2,1)} %get-tuple-element.11, s32[2048]{0:T(1024)S(1)} %bitcast.41), kind=kOutput, calls=%fused_computation.16 | convolution fusion | flops 1615069184 | bytes 5251072 | tf_op jit(solution)/shard_map/od,oc->dc/dot_general | solution.py:195
  109.3 0.0 reduce-scatter.2.cloned.1.call-update
  109.4 0.0 all-to-all-done.2
  109.4 3.5 %all-to-all-start.3 = ((bf16[8,256,128]{2,1,0:T(8,128)(2,1)}), bf16[8,256,128]{2,1,0:T(8,128)(2,1)S(1)}, u32[]{:S(2)}, u32[]{:S(2)}) async-start(bf16[8,256,128]{2,1,0:T(8,128)(2,1)} %bitcast.11), calls=%async_computation.3 | async-start | bytes 1048576 | tf_op jit(solution)/shard_map/all_to_all | solution.py:177
  112.9 15.3 %all-to-all-done.3 = bf16[8,256,128]{2,1,0:T(8,128)(2,1)S(1)} async-done(((bf16[8,256,128]{2,1,0:T(8,128)(2,1)}), bf16[8,256,128]{2,1,0:T(8,128)(2,1)S(1)}, u32[]{:S(2)}, u32[]{:S(2)}) %all-to-all-start.3) | async-done | bytes 524320 | tf_op jit(solution)/shard_map/all_to_all | solution.py:177
  128.2 4.5 %reduce-scatter.2.cloned.1.call-done = f32[256,128]{1,0:T(8,128)} async-done(((f32[1024,128]{1,0:T(8,128)}), f32[256,128]{1,0:T(8,128)}) %reduce-scatter.2.cloned.1.call-update) | async-done | bytes 131088 | tf_op jit(solution)/shard_map/reduce_scatter | solution.py:198
  132.7 4.6 %all-to-all-start.4 = ((f32[8,32,128]{2,1,0:T(8,128)}), f32[8,32,128]{2,1,0:T(8,128)S(1)}, u32[]{:S(2)}, u32[]{:S(2)}) async-start(f32[8,32,128]{2,1,0:T(8,128)} %bitcast.39), calls=%async_computation.5 | async-start | bytes 262144 | tf_op jit(solution)/shard_map/all_to_all | solution.py:199
  137.3 0.0 copy-done.1
  137.3 1.6 %fusion.22 = bf16[1,256,1024]{2,1,0:T(8,128)(2,1)} fusion(bf16[8,256,128]{2,1,0:T(8,128)(2,1)S(1)} %all-to-all-done.3, bf16[1024,8,128]{2,1,0:T(8,128)(2,1)S(1)} %copy-done.1), kind=kOutput, calls=%fused_computation.15 | convolution fusion | flops 537133056 | bytes 3145728 | tf_op jit(solution)/shard_map/htc,dhc->td/dot_general | solution.py:187
  138.9 5.2 %all-to-all-done.4 = f32[8,32,128]{2,1,0:T(8,128)S(1)} async-done(((f32[8,32,128]{2,1,0:T(8,128)}), f32[8,32,128]{2,1,0:T(8,128)S(1)}, u32[]{:S(2)}, u32[]{:S(2)}) %all-to-all-start.4) | async-done | bytes 131104 | tf_op jit(solution)/shard_map/all_to_all | solution.py:199
  144.1 0.7 copy.48
  144.8 0.7 copy.66
  (6 shorter events, 0.1 us)
Async XLA Ops:
  9.8 18.9 %all-to-all-start = ((bf16[8,272,64]{1,2,0:T(8,128)(2,1)}), bf16[8,272,64]{1,2,0:T(8,128)(2,1)S(1)}, u32[]{:S(2)}, u32[]{:S(2)}) async-start(bf16[8,272,64]{1,2,0:T(8,128)(2,1)} %pad_maximum_fusion), calls=%async_computation | async-start | bytes 786432 | tf_op jit(solution)/shard_map/all_to_all | solution.py:137
  16.2 31.7 %copy-start = (s32[1,16,8]{1,2,0:T(8,128)S(1)}, s32[1,16,8]{1,2,0:T(8,128)}, u32[]{:S(2)}) copy-start(s32[1,16,8]{1,2,0:T(8,128)} %param.9) | copy-start | bytes 1540
  28.7 18.8 %all-to-all-start.1 = ((bf16[8,256,128]{1,2,0:T(8,128)(2,1)}), bf16[8,256,128]{1,2,0:T(8,128)(2,1)S(1)}, u32[]{:S(2)}, u32[]{:S(2)}) async-start(bf16[8,256,128]{1,2,0:T(8,128)(2,1)} %fusion.19), calls=%async_computation.1 | async-start | bytes 1048576 | tf_op jit(solution)/shard_map/all_to_all | solution.py:146
  32.2 67.6 %all-gather.2.cloned.1.call-start = ((), (), s32[]{:S(2)}) async-start(), calls=%async_computation.6 | async-start | bytes 4718592 | tf_op jit(solution)/shard_map/all_gather | solution.py:152
  77.1 32.3 %all-to-all-start.2 = ((bf16[8,256,64]{1,2,0:T(8,128)(2,1)}), bf16[8,256,64]{1,2,0:T(8,128)(2,1)S(1)}, u32[]{:S(2)}, u32[]{:S(2)}) async-start(bf16[8,256,64]{1,2,0:T(8,128)(2,1)} %copy.46), calls=%async_computation.2 | async-start | bytes 524288 | tf_op jit(solution)/shard_map/all_to_all | solution.py:170
  80.5 52.2 %reduce-scatter.2.cloned.1.call-start = ((), (), s32[]{:S(2)}) async-start(), calls=%async_computation.7 | async-start | bytes 655360 | tf_op jit(solution)/shard_map/reduce_scatter | solution.py:198
  99.8 37.5 %copy-start.1 = (bf16[1024,8,128]{2,1,0:T(8,128)(2,1)S(1)}, bf16[1024,8,128]{2,1,0:T(8,128)(2,1)}, u32[]{:S(2)}) copy-start(bf16[1024,8,128]{2,1,0:T(8,128)(2,1)} %param.8) | copy-start | bytes 6291460
  109.4 18.8 %all-to-all-start.3 = ((bf16[8,256,128]{2,1,0:T(8,128)(2,1)}), bf16[8,256,128]{2,1,0:T(8,128)(2,1)S(1)}, u32[]{:S(2)}, u32[]{:S(2)}) async-start(bf16[8,256,128]{2,1,0:T(8,128)(2,1)} %bitcast.11), calls=%async_computation.3 | async-start | bytes 1048576 | tf_op jit(solution)/shard_map/all_to_all | solution.py:177
  132.7 11.4 %all-to-all-start.4 = ((f32[8,32,128]{2,1,0:T(8,128)}), f32[8,32,128]{2,1,0:T(8,128)S(1)}, u32[]{:S(2)}, u32[]{:S(2)}) async-start(f32[8,32,128]{2,1,0:T(8,128)} %bitcast.39), calls=%async_computation.5 | async-start | bytes 262144 | tf_op jit(solution)/shard_map/all_to_all | solution.py:199
Sparse Core Ops, SparseCore 0:
  47.9 51.8 all-gather.1
  109.5 23.1 reduce-scatter.1

commit v12 on v11

--- a/solution.py
+++ b/solution.py
@@ -182,6 +182,11 @@
             tiled=True,
         ),
     )
+    if groups == 1:
+        head_grad = lax.dot_general(
+            placing, grad_both, (((0,), (0,)), ((), ())), preferred_element_type=jnp.float32
+        ).astype(jnp.bfloat16)
+        head_grad, back_out, back_grad = lax.optimization_barrier((head_grad, back_out, back_grad))
     attention = back_out.reshape(heads, tokens_here, depth)[None]
     grad_proj = back_grad.reshape(heads, tokens_here, 2 * depth)
     seq_grad = jnp.einsum(
@@ -189,13 +194,17 @@
     ).astype(jnp.bfloat16)[None]
     if groups == 1:
         rows_out = width // (rec_count * seq_count)
-        head_grad = lax.dot_general(
-            placing, grad_both, (((0,), (0,)), ((), ())), preferred_element_type=jnp.float32
-        ).astype(jnp.bfloat16)
         partial = jnp.einsum(
             "od,oc->dc", owned_all, head_grad, preferred_element_type=jnp.float32
         )
-        summed = lax.psum_scatter(partial, "rec", scatter_dimension=0, tiled=True)
+        pieces = lax.all_to_all(
+            partial.reshape(rec_count, width // rec_count, 2 * depth),
+            "rec",
+            split_axis=0,
+            concat_axis=0,
+            tiled=True,
+        )
+        summed = jnp.sum(pieces, axis=0)
         spread = lax.all_to_all(
             summed.reshape(seq_count, rows_out, 2 * depth),
             "seq",

time: 153 us -> 150 us (0.980)
  waiting for transfers between devices: 67.6 us -> 46 us
  blocking collectives: 0 us -> 18.5 us
    all_gather x1, waiting for transfers between devices: 19.1 us -> 0.01 us  [local(): owned_all = lax.all_gather(later_rows, 'seq', axis=0, tiled=True)]
    all_to_all x0 -> x1, blocking collectives: none -> 18.5 us  [local(): lax.all_to_all(mixed.reshape(seq_count, portion, depth), 'seq', split_axi...]
    all_to_all x1, waiting for transfers between devices: 0.01 us -> 7.82 us  [local(): lax.all_to_all(partial.reshape(rec_count, width // rec_count, 2 * depth),...]
    all_to_all x1, waiting for transfers between devices: 15.3 us -> 9.49 us  [local(): lax.all_to_all(grad_both.reshape(seq_count, portion, 2 * depth), 'seq', s...]
    dot_general x0 -> x1, matrix products: none -> 5.6 us  [local(): lax.dot_general(placing, grad_both, (((0,), (0,)), ((), ())), preferred_e...]
    dot_general x1, matrix products: 9.52 us -> 4.26 us  [local(): jnp.einsum('od,oc->dc', owned_all, head_grad, preferred_element_type=jnp....]
    reduce_scatter x1 -> x0, waiting for transfers between devices: 4.54 us -> none  [local(): summed = lax.psum_scatter(partial, 'rec', scatter_dimension=0, tiled=True)]
  transfers between devices with their start and end apart: 7 -> 6, of which waited for: 6 -> 5; matrix products, arithmetic and copies ran while one was open for 14% -> 12% of each run, Pallas kernels for 15% -> 15%
where the time goes in v12:
time: 150 us; the launch traced here: 149 us
  waiting for transfers between devices  46 us (31%)
  Pallas kernels  22.6 us (15%)
  starting transfers between devices  21.6 us (14%)
  matrix products  18.5 us (12%)
  blocking collectives  18.5 us (12%)
  between operations  14.1 us (9%)
  local copies, waits for them, and re-layouts  5.08 us (3%)
  other arithmetic  3.14 us (2%)
    pallas_call x1, Pallas kernels, attend_group(): pl.pallas_call(attention_kernel, out_shape=(jax.ShapeDtypeStruct((total,...  22.6 us
    all_to_all x1, blocking collectives, local(): lax.all_to_all(mixed.reshape(seq_count, portion, depth), 'seq', split_axi...  18.5 us
    all_to_all x1, waiting for transfers between devices, local(): lax.all_to_all(proj_mine, 'seq', split_axis=0, concat_axis=0, tiled=True)  14.2 us
    all_to_all x1, waiting for transfers between devices, local(): lax.all_to_all(grad_both.reshape(seq_count, portion, 2 * depth), 'seq', s...  9.49 us
    all_to_all x1, waiting for transfers between devices, local(): lax.all_to_all(sent, 'seq', split_axis=0, concat_axis=0, tiled=True)  9.28 us
    all_to_all x1, waiting for transfers between devices, local(): lax.all_to_all(partial.reshape(rec_count, width // rec_count, 2 * depth),...  7.82 us
    all_to_all x1, starting transfers between devices, local(): lax.all_to_all(sent, 'seq', split_axis=0, concat_axis=0, tiled=True)  6.33 us
    dot_general x1, matrix products, local(): lax.dot_general(placing, grad_both, (((0,), (0,)), ((), ())), preferred_e...  5.6 us
  transfers between devices with their start and end apart: 6, of which 5 were waited for; matrix products, arithmetic and copies ran while one was open for 12% of the time, Pallas kernels for 15%

profile of v12, /device:TPU:0, one launch (start us, length us, event | category | flops | bytes accessed | tf_op | source)
XLA Modules:
  0.0 149.5 jit_solution(9488257560649861730)
XLA Ops:
  7.2 0.7 fusion.32
  7.9 0.1 broadcast_in_dim.14
  7.9 0.1 copy.30
  8.1 1.7 %pad_maximum_fusion = bf16[8,272,64]{1,2,0:T(8,128)(2,1)} fusion(bf16[8,16,64]{1,2,0:T(8,128)(2,1)S(1)} %broadcast_in_dim.15, bf16[8,256,64]{1,2,0:T(8,128)(2,1)} %bitcast.41), kind=kLoop, calls=%fused_computation.17 | loop fusion | flops 557056 | bytes 557056 | tf_op jit(solution)/shard_map/concatenate | solution.py:134
  9.8 6.3 %all-to-all-start = ((bf16[8,272,64]{1,2,0:T(8,128)(2,1)}), bf16[8,272,64]{1,2,0:T(8,128)(2,1)S(1)}, u32[]{:S(2)}, u32[]{:S(2)}) async-start(bf16[8,272,64]{1,2,0:T(8,128)(2,1)} %pad_maximum_fusion), calls=%async_computation | async-start | bytes 786432 | tf_op jit(solution)/shard_map/all_to_all | solution.py:137
  16.1 0.0 copy-start
  16.2 3.3 %fusion.19 = bf16[8,256,128]{1,2,0:T(8,128)(2,1)} fusion(bf16[1024,8,128]{2,1,0:T(8,128)(2,1)} %param.8, bf16[1,256,1024]{2,1,0:T(8,128)(2,1)} %param.6), kind=kOutput, calls=%fused_computation.14 | convolution fusion | flops 537133056 | bytes 3145728 | tf_op jit(solution)/shard_map/td,dhc->htc/dot_general | solution.py:143
  19.4 9.3 %all-to-all-done = bf16[8,272,64]{1,2,0:T(8,128)(2,1)S(1)} async-done(((bf16[8,272,64]{1,2,0:T(8,128)(2,1)}), bf16[8,272,64]{1,2,0:T(8,128)(2,1)S(1)}, u32[]{:S(2)}, u32[]{:S(2)}) %all-to-all-start) | async-done | bytes 278560 | tf_op jit(solution)/shard_map/all_to_all | solution.py:137
  28.7 3.5 %all-to-all-start.1 = ((bf16[8,256,128]{1,2,0:T(8,128)(2,1)}), bf16[8,256,128]{1,2,0:T(8,128)(2,1)S(1)}, u32[]{:S(2)}, u32[]{:S(2)}) async-start(bf16[8,256,128]{1,2,0:T(8,128)(2,1)} %fusion.19), calls=%async_computation.1 | async-start | bytes 1048576 | tf_op jit(solution)/shard_map/all_to_all | solution.py:146
  32.2 0.0 all-gather.2.cloned.1.call-start
  32.3 1.0 copy.34
  33.3 14.2 %all-to-all-done.1 = bf16[8,256,128]{1,2,0:T(8,128)(2,1)S(1)} async-done(((bf16[8,256,128]{1,2,0:T(8,128)(2,1)}), bf16[8,256,128]{1,2,0:T(8,128)(2,1)S(1)}, u32[]{:S(2)}, u32[]{:S(2)}) %all-to-all-start.1) | async-done | bytes 524320 | tf_op jit(solution)/shard_map/all_to_all | solution.py:146
  47.5 0.3 copy.33
  47.8 0.0 all-gather.2.cloned.1.call-update
  47.8 0.0 copy-done
  47.8 0.7 copy.35.lists_ref
  48.5 0.1 copy.39
  48.6 0.1 reshape.35
  48.7 3.8 %fusion.4.both_ref = bf16[2048,128]{1,0:T(8,128)(2,1)} fusion(bf16[2048,128]{1,0:T(8,128)(2,1)S(1)} %bitcast.38, s32[2048]{0:T(1024)S(1)} %bitcast.42), kind=kOutput, calls=%fused_computation.5 | convolution fusion | flops 1078198272 | bytes 1056768 | tf_op jit(solution)/shard_map/dot_general | solution.py:155
  52.5 22.6 %shard_map.85 = (bf16[2048,64]{1,0:T(8,128)(2,1)}, bf16[2048,128]{1,0:T(8,128)(2,1)}) custom-call(s32[16,8]{1,0:T(8,128)} %copy.35.lists_ref, s32[16]{0:T(128)} %bitcast.46, bf16[2048,128]{1,0:T(8,128)(2,1)} %fusion.4.both_ref, bf16[2048,64]{1,0:T(8,128)(2,1)} %bitcast.34), custom_call_target="tpu_custom_call" | custom-call | tf_op jit(solution)/shard_map/pallas_call | solution.py:68
  75.1 1.2 copy.36
  76.3 18.5 %all_to_all.30 = bf16[8,256,64]{1,2,0:T(8,128)(2,1)S(1)} all-to-all(bf16[8,256,64]{1,2,0:T(8,128)(2,1)S(1)} %copy.36), channel_id=1, replica_groups=mesh['rec'=4,'seq'=8] {'seq'}, dimensions={0} | all-to-all | bytes 524288 | tf_op jit(solution)/shard_map/all_to_all | solution.py:170
  94.8 3.7 %all-to-all-start.3 = ((bf16[8,256,128]{2,1,0:T(8,128)(2,1)}), bf16[8,256,128]{2,1,0:T(8,128)(2,1)S(1)}, u32[]{:S(2)}, u32[]{:S(2)}) async-start(bf16[8,256,128]{2,1,0:T(8,128)(2,1)} %bitcast.39), calls=%async_computation.3 | async-start | bytes 1048576 | tf_op jit(solution)/shard_map/all_to_all | solution.py:177
  98.5 5.6 %fusion.5 = bf16[2048,128]{1,0:T(8,128)(2,1)S(1)} fusion(bf16[2048,128]{1,0:T(8,128)(2,1)} %get-tuple-element.13, s32[2048]{0:T(1024)S(1)} %bitcast.43), kind=kOutput, calls=%fused_computation.6 | convolution fusion | flops 1078198272 | bytes 1056768 | tf_op jit(solution)/shard_map/dot_general | solution.py:186
  104.1 0.0 copy-start.1
  104.1 9.5 %all-to-all-done.3 = bf16[8,256,128]{2,1,0:T(8,128)(2,1)S(1)} async-done(((bf16[8,256,128]{2,1,0:T(8,128)(2,1)}), bf16[8,256,128]{2,1,0:T(8,128)(2,1)S(1)}, u32[]{:S(2)}, u32[]{:S(2)}) %all-to-all-start.3) | async-done | bytes 524320 | tf_op jit(solution)/shard_map/all_to_all | solution.py:177
  113.6 0.0 all-gather.2.cloned.1.call-done
  113.6 4.3 %fusion.33 = f32[1024,128]{1,0:T(8,128)} fusion(bf16[2048,1024]{1,0:T(8,128)(2,1)} %all-gather.2.cloned.1.call-done, bf16[2048,128]{1,0:T(8,128)(2,1)S(1)} %fusion.5), kind=kOutput, calls=%fused_computation.35 | convolution fusion | flops 536870912 | bytes 5242880 | tf_op jit(solution)/shard_map/od,oc->dc/dot_general | solution.py:197
  117.9 4.7 %all-to-all-start.4 = ((f32[4,256,128]{2,1,0:T(8,128)}), f32[4,256,128]{2,1,0:T(8,128)S(1)}, u32[]{:S(2)}, u32[]{:S(2)}) async-start(f32[4,256,128]{2,1,0:T(8,128)} %bitcast.14), calls=%async_computation.4 | async-start | bytes 1048576 | tf_op jit(solution)/shard_map/all_to_all | solution.py:200
  122.6 7.8 %all-to-all-done.4 = f32[4,256,128]{2,1,0:T(8,128)S(1)} async-done(((f32[4,256,128]{2,1,0:T(8,128)}), f32[4,256,128]{2,1,0:T(8,128)S(1)}, u32[]{:S(2)}, u32[]{:S(2)}) %all-to-all-start.4) | async-done | bytes 524320 | tf_op jit(solution)/shard_map/all_to_all | solution.py:200
  130.4 0.7 reduce_sum.9
  131.1 3.4 %all-to-all-start.5 = ((f32[8,32,128]{2,1,0:T(8,128)}), f32[8,32,128]{2,1,0:T(8,128)S(1)}, u32[]{:S(2)}, u32[]{:S(2)}) async-start(f32[8,32,128]{2,1,0:T(8,128)} %bitcast.15), calls=%async_computation.5 | async-start | bytes 262144 | tf_op jit(solution)/shard_map/all_to_all | solution.py:208
  134.5 0.0 copy-done.1
  134.5 1.6 %fusion.22 = bf16[1,256,1024]{2,1,0:T(8,128)(2,1)} fusion(bf16[8,256,128]{2,1,0:T(8,128)(2,1)S(1)} %all-to-all-done.3, bf16[1024,8,128]{2,1,0:T(8,128)(2,1)S(1)} %copy-done.1), kind=kOutput, calls=%fused_computation.15 | convolution fusion | flops 537133056 | bytes 3145728 | tf_op jit(solution)/shard_map/htc,dhc->td/dot_general | solution.py:192
  136.1 5.2 %all-to-all-done.5 = f32[8,32,128]{2,1,0:T(8,128)S(1)} async-done(((f32[8,32,128]{2,1,0:T(8,128)}), f32[8,32,128]{2,1,0:T(8,128)S(1)}, u32[]{:S(2)}, u32[]{:S(2)}) %all-to-all-start.5) | async-done | bytes 131104 | tf_op jit(solution)/shard_map/all_to_all | solution.py:208
  141.2 0.7 copy.38
  141.9 0.7 copy.56
  (6 shorter events, 0.1 us)
Async XLA Ops:
  9.8 18.9 %all-to-all-start = ((bf16[8,272,64]{1,2,0:T(8,128)(2,1)}), bf16[8,272,64]{1,2,0:T(8,128)(2,1)S(1)}, u32[]{:S(2)}, u32[]{:S(2)}) async-start(bf16[8,272,64]{1,2,0:T(8,128)(2,1)} %pad_maximum_fusion), calls=%async_computation | async-start | bytes 786432 | tf_op jit(solution)/shard_map/all_to_all | solution.py:137
  16.1 31.6 %copy-start = (s32[1,16,8]{1,2,0:T(8,128)S(1)}, s32[1,16,8]{1,2,0:T(8,128)}, u32[]{:S(2)}) copy-start(s32[1,16,8]{1,2,0:T(8,128)} %param.9) | copy-start | bytes 1540
  28.7 18.8 %all-to-all-start.1 = ((bf16[8,256,128]{1,2,0:T(8,128)(2,1)}), bf16[8,256,128]{1,2,0:T(8,128)(2,1)S(1)}, u32[]{:S(2)}, u32[]{:S(2)}) async-start(bf16[8,256,128]{1,2,0:T(8,128)(2,1)} %fusion.19), calls=%async_computation.1 | async-start | bytes 1048576 | tf_op jit(solution)/shard_map/all_to_all | solution.py:146
  32.2 81.4 %all-gather.2.cloned.1.call-start = ((), (), s32[]{:S(2)}) async-start(), calls=%async_computation.6 | async-start | bytes 4718592 | tf_op jit(solution)/shard_map/all_gather | solution.py:152
  94.8 18.8 %all-to-all-start.3 = ((bf16[8,256,128]{2,1,0:T(8,128)(2,1)}), bf16[8,256,128]{2,1,0:T(8,128)(2,1)S(1)}, u32[]{:S(2)}, u32[]{:S(2)}) async-start(bf16[8,256,128]{2,1,0:T(8,128)(2,1)} %bitcast.39), calls=%async_computation.3 | async-start | bytes 1048576 | tf_op jit(solution)/shard_map/all_to_all | solution.py:177
  104.1 30.4 %copy-start.1 = (bf16[1024,8,128]{2,1,0:T(8,128)(2,1)S(1)}, bf16[1024,8,128]{2,1,0:T(8,128)(2,1)}, u32[]{:S(2)}) copy-start(bf16[1024,8,128]{2,1,0:T(8,128)(2,1)} %param.8) | copy-start | bytes 6291460
  117.9 12.6 %all-to-all-start.4 = ((f32[4,256,128]{2,1,0:T(8,128)}), f32[4,256,128]{2,1,0:T(8,128)S(1)}, u32[]{:S(2)}, u32[]{:S(2)}) async-start(f32[4,256,128]{2,1,0:T(8,128)} %bitcast.14), calls=%async_computation.4 | async-start | bytes 1048576 | tf_op jit(solution)/shard_map/all_to_all | solution.py:200
  131.1 10.1 %all-to-all-start.5 = ((f32[8,32,128]{2,1,0:T(8,128)}), f32[8,32,128]{2,1,0:T(8,128)S(1)}, u32[]{:S(2)}, u32[]{:S(2)}) async-start(f32[8,32,128]{2,1,0:T(8,128)} %bitcast.15), calls=%async_computation.5 | async-start | bytes 262144 | tf_op jit(solution)/shard_map/all_to_all | solution.py:208
Sparse Core Ops, SparseCore 0:
  47.9 51.7 all-gather.1

commit v13 on v10

--- a/solution.py
+++ b/solution.py
@@ -184,9 +184,11 @@
     ).astype(jnp.bfloat16)[None]
     if groups == 1:
         rows_out = width // (rec_count * seq_count)
-        head_grad = lax.dot_general(
-            placing, grad_both, (((0,), (0,)), ((), ())), preferred_element_type=jnp.float32
-        ).astype(jnp.bfloat16)
+        head_grad = lax.optimization_barrier(
+            lax.dot_general(
+                placing, grad_both, (((0,), (0,)), ((), ())), preferred_element_type=jnp.float32
+            ).astype(jnp.bfloat16)
+        )
         partial = jnp.einsum(
             "od,oc->dc", owned_all, head_grad, preferred_element_type=jnp.float32
         )

time: 142 us -> 140 us (0.986)
  waiting for transfers between devices: 55.9 us -> 52.2 us
    dot_general x0 -> x1, matrix products: none -> 5.57 us  [local(): lax.dot_general(placing, grad_both, (((0,), (0,)), ((), ())), preferred_e...]
    dot_general x1, matrix products: 9.52 us -> 4.4 us  [local(): jnp.einsum('od,oc->dc', owned_all, head_grad, preferred_element_type=jnp....]
    all_gather x1, waiting for transfers between devices: 4.84 us -> 0.02 us  [local(): owned_all = lax.all_gather(later_rows, 'seq', axis=0, tiled=True)]
  transfers between devices with their start and end apart: 8 -> 8, of which waited for: 7 -> 6; matrix products, arithmetic and copies ran while one was open for 16% -> 16% of each run, Pallas kernels for 16% -> 16%
where the time goes in v13:
time: 140 us
  waiting for transfers between devices  52.2 us (37%)
  starting transfers between devices  26.4 us (19%)
  Pallas kernels  22.4 us (16%)
  matrix products  18.5 us (13%)
  between operations  14.1 us (10%)
  local copies, waits for them, and re-layouts  5.95 us (4%)
    pallas_call x1, Pallas kernels, attend_group(): pl.pallas_call(attention_kernel, out_shape=(jax.ShapeDtypeStruct((total,...  22.4 us
    all_to_all x1, waiting for transfers between devices, local(): lax.all_to_all(grad_both.reshape(seq_count, portion, 2 * depth), 'seq', s...  15.4 us
    all_to_all x1, waiting for transfers between devices, local(): lax.all_to_all(proj_mine, 'seq', split_axis=0, concat_axis=0, tiled=True)  14.2 us
    all_to_all x1, waiting for transfers between devices, local(): lax.all_to_all(upstream, 'seq', split_axis=0, concat_axis=0, tiled=True)  6.49 us
    all_to_all x1, starting transfers between devices, local(): lax.all_to_all(upstream, 'seq', split_axis=0, concat_axis=0, tiled=True)  6.47 us
    reduce_scatter x1, waiting for transfers between devices, local(): summed = lax.psum_scatter(partial, 'rec', scatter_dimension=0, tiled=True)  5.93 us
    dot_general x1, matrix products, local(): lax.dot_general(placing, grad_both, (((0,), (0,)), ((), ())), preferred_e...  5.57 us
    all_to_all x1, waiting for transfers between devices, local(): lax.all_to_all(summed.reshape(seq_count, rows_out, 2 * depth), 'seq', spl...  5.23 us
  transfers between devices with their start and end apart: 8, of which 6 were waited for; matrix products, arithmetic and copies ran while one was open for 16% of the time, Pallas kernels for 16%

profile of v13, /device:TPU:0, one launch (start us, length us, event | category | flops | bytes accessed | tf_op | source)
XLA Modules:
  0.0 139.7 jit_solution(3693408652799350671)
XLA Ops:
  7.2 0.0 copy-start.1
  7.2 0.0 copy-start
  7.2 6.5 %all-to-all-start.2 = ((bf16[8,256,64]{1,2,0:T(8,128)(2,1)}), bf16[8,256,64]{1,2,0:T(8,128)(2,1)S(1)}, u32[]{:S(2)}, u32[]{:S(2)}) async-start(bf16[8,256,64]{1,2,0:T(8,128)(2,1)} %bitcast.37), calls=%async_computation.2 | async-start | bytes 524288 | tf_op jit(solution)/shard_map/all_to_all | solution.py:130
  13.7 3.2 %fusion.19 = bf16[8,256,128]{1,2,0:T(8,128)(2,1)} fusion(bf16[1024,8,128]{2,1,0:T(8,128)(2,1)} %param.8, bf16[1,256,1024]{2,1,0:T(8,128)(2,1)} %param.6), kind=kOutput, calls=%fused_computation.14 | convolution fusion | flops 537133056 | bytes 3145728 | tf_op jit(solution)/shard_map/td,dhc->htc/dot_general | solution.py:140
  16.9 6.5 %all-to-all-done.2 = bf16[8,256,64]{1,2,0:T(8,128)(2,1)S(1)} async-done(((bf16[8,256,64]{1,2,0:T(8,128)(2,1)}), bf16[8,256,64]{1,2,0:T(8,128)(2,1)S(1)}, u32[]{:S(2)}, u32[]{:S(2)}) %all-to-all-start.2) | async-done | bytes 262176 | tf_op jit(solution)/shard_map/all_to_all | solution.py:130
  23.4 3.5 %all-to-all-start.1 = ((bf16[8,256,128]{1,2,0:T(8,128)(2,1)}), bf16[8,256,128]{1,2,0:T(8,128)(2,1)S(1)}, u32[]{:S(2)}, u32[]{:S(2)}) async-start(bf16[8,256,128]{1,2,0:T(8,128)(2,1)} %fusion.19), calls=%async_computation.1 | async-start | bytes 1048576 | tf_op jit(solution)/shard_map/all_to_all | solution.py:143
  26.9 0.0 all-gather.2.cloned.1.call-start
  26.9 1.0 copy.24
  28.0 14.2 %all-to-all-done.1 = bf16[8,256,128]{1,2,0:T(8,128)(2,1)S(1)} async-done(((bf16[8,256,128]{1,2,0:T(8,128)(2,1)}), bf16[8,256,128]{1,2,0:T(8,128)(2,1)S(1)}, u32[]{:S(2)}, u32[]{:S(2)}) %all-to-all-start.1) | async-done | bytes 524320 | tf_op jit(solution)/shard_map/all_to_all | solution.py:143
  42.2 0.3 copy.23
  42.5 0.0 all-gather.2.cloned.1.call-update
  42.5 0.0 copy-done.1
  42.5 0.6 broadcast_in_dim.12
  43.1 3.3 %all-to-all-start = ((s32[8,1,256]{2,1,0:T(1,128)}), s32[8,1,256]{2,1,0:T(1,128)S(1)}, u32[]{:S(2)}, u32[]{:S(2)}) async-start(s32[8,1,256]{2,1,0:T(1,128)} %broadcast_in_dim.12), calls=%async_computation | async-start | bytes 16384 | tf_op jit(solution)/shard_map/all_to_all | solution.py:133
  46.4 0.0 copy-done
  46.5 0.7 copy.25.lists_ref
  47.1 4.9 %all-to-all-done = s32[8,1,256]{2,1,0:T(1,128)S(1)} async-done(((s32[8,1,256]{2,1,0:T(1,128)}), s32[8,1,256]{2,1,0:T(1,128)S(1)}, u32[]{:S(2)}, u32[]{:S(2)}) %all-to-all-start) | async-done | bytes 8224 | tf_op jit(solution)/shard_map/all_to_all | solution.py:133
  52.1 3.8 %fusion.4.both_ref = bf16[2048,128]{1,0:T(8,128)(2,1)} fusion(bf16[2048,128]{1,0:T(8,128)(2,1)S(1)} %bitcast.35, s32[2048]{0:T(1024)S(1)} %bitcast.39), kind=kOutput, calls=%fused_computation.5 | convolution fusion | flops 1078198272 | bytes 1056768 | tf_op jit(solution)/shard_map/dot_general | solution.py:152
  55.8 22.4 %shard_map.88 = (bf16[2048,64]{1,0:T(8,128)(2,1)}, bf16[2048,128]{1,0:T(8,128)(2,1)}) custom-call(s32[16,8]{1,0:T(8,128)} %copy.25.lists_ref, s32[16]{0:T(128)} %bitcast.43, bf16[2048,128]{1,0:T(8,128)(2,1)} %fusion.4.both_ref, bf16[2048,64]{1,0:T(8,128)(2,1)} %bitcast.31), custom_call_target="tpu_custom_call" | custom-call | tf_op jit(solution)/shard_map/pallas_call | solution.py:68
  78.3 1.9 %copy.26 = bf16[8,256,64]{1,2,0:T(8,128)(2,1)} copy(bf16[8,256,64]{2,1,0:T(8,128)(2,1)} %bitcast.33) | data formatting | bytes 524288 | tf_op jit(solution)/shard_map/reshape | solution.py:166
  80.2 3.4 %all-to-all-start.3 = ((bf16[8,256,64]{1,2,0:T(8,128)(2,1)}), bf16[8,256,64]{1,2,0:T(8,128)(2,1)S(1)}, u32[]{:S(2)}, u32[]{:S(2)}) async-start(bf16[8,256,64]{1,2,0:T(8,128)(2,1)} %copy.26), calls=%async_computation.3 | async-start | bytes 524288 | tf_op jit(solution)/shard_map/all_to_all | solution.py:165
  83.6 0.2 reduce-scatter.2.cloned.1.call-start
  83.8 5.6 %fusion.5 = bf16[2048,128]{1,0:T(8,128)(2,1)S(1)} fusion(bf16[2048,128]{1,0:T(8,128)(2,1)} %get-tuple-element.11, s32[2048]{0:T(1024)S(1)} %bitcast.40), kind=kOutput, calls=%fused_computation.6 | convolution fusion | flops 1078198272 | bytes 1056768 | tf_op jit(solution)/shard_map/dot_general | solution.py:188
  89.4 0.0 copy-start.2
  89.4 0.0 all-gather.2.cloned.1.call-done
  89.5 4.4 %fusion.26 = f32[1024,128]{1,0:T(8,128)} fusion(bf16[2048,1024]{1,0:T(8,128)(2,1)} %all-gather.2.cloned.1.call-done, bf16[2048,128]{1,0:T(8,128)(2,1)S(1)} %fusion.5), kind=kOutput, calls=%fused_computation.17 | convolution fusion | flops 536870912 | bytes 5242880 | tf_op jit(solution)/shard_map/od,oc->dc/dot_general | solution.py:192
  93.9 0.0 reduce-scatter.2.cloned.1.call-update
  93.9 0.0 all-to-all-done.3
  93.9 4.8 %all-to-all-start.4 = ((bf16[8,256,128]{2,1,0:T(8,128)(2,1)}), bf16[8,256,128]{2,1,0:T(8,128)(2,1)S(1)}, u32[]{:S(2)}, u32[]{:S(2)}) async-start(bf16[8,256,128]{2,1,0:T(8,128)(2,1)} %bitcast.12), calls=%async_computation.4 | async-start | bytes 1048576 | tf_op jit(solution)/shard_map/all_to_all | solution.py:172
  98.7 15.4 %all-to-all-done.4 = bf16[8,256,128]{2,1,0:T(8,128)(2,1)S(1)} async-done(((bf16[8,256,128]{2,1,0:T(8,128)(2,1)}), bf16[8,256,128]{2,1,0:T(8,128)(2,1)S(1)}, u32[]{:S(2)}, u32[]{:S(2)}) %all-to-all-start.4) | async-done | bytes 524320 | tf_op jit(solution)/shard_map/all_to_all | solution.py:172
  114.1 5.9 %reduce-scatter.2.cloned.1.call-done = f32[256,128]{1,0:T(8,128)} async-done(((f32[1024,128]{1,0:T(8,128)}), f32[256,128]{1,0:T(8,128)}) %reduce-scatter.2.cloned.1.call-update) | async-done | bytes 131088 | tf_op jit(solution)/shard_map/reduce_scatter | solution.py:195
  120.0 4.6 %all-to-all-start.5 = ((f32[8,32,128]{2,1,0:T(8,128)}), f32[8,32,128]{2,1,0:T(8,128)S(1)}, u32[]{:S(2)}, u32[]{:S(2)}) async-start(f32[8,32,128]{2,1,0:T(8,128)} %bitcast.38), calls=%async_computation.6 | async-start | bytes 262144 | tf_op jit(solution)/shard_map/all_to_all | solution.py:196
  124.6 0.0 copy-done.2
  124.6 1.5 %fusion.22 = bf16[1,256,1024]{2,1,0:T(8,128)(2,1)} fusion(bf16[8,256,128]{2,1,0:T(8,128)(2,1)S(1)} %all-to-all-done.4, bf16[1024,8,128]{2,1,0:T(8,128)(2,1)S(1)} %copy-done.2), kind=kOutput, calls=%fused_computation.15 | convolution fusion | flops 537133056 | bytes 3145728 | tf_op jit(solution)/shard_map/htc,dhc->td/dot_general | solution.py:182
  126.1 5.2 %all-to-all-done.5 = f32[8,32,128]{2,1,0:T(8,128)S(1)} async-done(((f32[8,32,128]{2,1,0:T(8,128)}), f32[8,32,128]{2,1,0:T(8,128)S(1)}, u32[]{:S(2)}, u32[]{:S(2)}) %all-to-all-start.5) | async-done | bytes 131104 | tf_op jit(solution)/shard_map/all_to_all | solution.py:196
  131.4 0.7 copy.28
  132.1 0.7 copy.44
Async XLA Ops:
  7.2 35.3 %copy-start.1 = (s32[1,256]{1,0:T(1,128)S(1)}, s32[1,256]{1,0:T(1,128)}, u32[]{:S(2)}) copy-start(s32[1,256]{1,0:T(1,128)} %param.7) | copy-start | bytes 3076
  7.2 39.3 %copy-start = (s32[1,16,8]{1,2,0:T(8,128)S(1)}, s32[1,16,8]{1,2,0:T(8,128)}, u32[]{:S(2)}) copy-start(s32[1,16,8]{1,2,0:T(8,128)} %param.9) | copy-start | bytes 1540
  7.2 16.2 %all-to-all-start.2 = ((bf16[8,256,64]{1,2,0:T(8,128)(2,1)}), bf16[8,256,64]{1,2,0:T(8,128)(2,1)S(1)}, u32[]{:S(2)}, u32[]{:S(2)}) async-start(bf16[8,256,64]{1,2,0:T(8,128)(2,1)} %bitcast.37), calls=%async_computation.2 | async-start | bytes 524288 | tf_op jit(solution)/shard_map/all_to_all | solution.py:130
  23.4 18.8 %all-to-all-start.1 = ((bf16[8,256,128]{1,2,0:T(8,128)(2,1)}), bf16[8,256,128]{1,2,0:T(8,128)(2,1)S(1)}, u32[]{:S(2)}, u32[]{:S(2)}) async-start(bf16[8,256,128]{1,2,0:T(8,128)(2,1)} %fusion.19), calls=%async_computation.1 | async-start | bytes 1048576 | tf_op jit(solution)/shard_map/all_to_all | solution.py:143
  26.9 62.5 %all-gather.2.cloned.1.call-start = ((), (), s32[]{:S(2)}) async-start(), calls=%async_computation.7 | async-start | bytes 4718592 | tf_op jit(solution)/shard_map/all_gather | solution.py:149
  43.1 9.0 %all-to-all-start = ((s32[8,1,256]{2,1,0:T(1,128)}), s32[8,1,256]{2,1,0:T(1,128)S(1)}, u32[]{:S(2)}, u32[]{:S(2)}) async-start(s32[8,1,256]{2,1,0:T(1,128)} %broadcast_in_dim.12), calls=%async_computation | async-start | bytes 16384 | tf_op jit(solution)/shard_map/all_to_all | solution.py:133
  80.2 13.7 %all-to-all-start.3 = ((bf16[8,256,64]{1,2,0:T(8,128)(2,1)}), bf16[8,256,64]{1,2,0:T(8,128)(2,1)S(1)}, u32[]{:S(2)}, u32[]{:S(2)}) async-start(bf16[8,256,64]{1,2,0:T(8,128)(2,1)} %copy.26), calls=%async_computation.3 | async-start | bytes 524288 | tf_op jit(solution)/shard_map/all_to_all | solution.py:165
  83.6 36.4 %reduce-scatter.2.cloned.1.call-start = ((), (), s32[]{:S(2)}) async-start(), calls=%async_computation.8 | async-start | bytes 655360 | tf_op jit(solution)/shard_map/reduce_scatter | solution.py:195
  89.4 35.2 %copy-start.2 = (bf16[1024,8,128]{2,1,0:T(8,128)(2,1)S(1)}, bf16[1024,8,128]{2,1,0:T(8,128)(2,1)}, u32[]{:S(2)}) copy-start(bf16[1024,8,128]{2,1,0:T(8,128)(2,1)} %param.8) | copy-start | bytes 6291460
  93.9 20.2 %all-to-all-start.4 = ((bf16[8,256,128]{2,1,0:T(8,128)(2,1)}), bf16[8,256,128]{2,1,0:T(8,128)(2,1)S(1)}, u32[]{:S(2)}, u32[]{:S(2)}) async-start(bf16[8,256,128]{2,1,0:T(8,128)(2,1)} %bitcast.12), calls=%async_computation.4 | async-start | bytes 1048576 | tf_op jit(solution)/shard_map/all_to_all | solution.py:172
  120.0 11.4 %all-to-all-start.5 = ((f32[8,32,128]{2,1,0:T(8,128)}), f32[8,32,128]{2,1,0:T(8,128)S(1)}, u32[]{:S(2)}, u32[]{:S(2)}) async-start(f32[8,32,128]{2,1,0:T(8,128)} %bitcast.38), calls=%async_computation.6 | async-start | bytes 262144 | tf_op jit(solution)/shard_map/all_to_all | solution.py:196
Sparse Core Ops, SparseCore 0:
  42.6 46.0 all-gather.1
  94.0 25.9 reduce-scatter.1

commit v14 on v13

--- a/solution.py
+++ b/solution.py
@@ -1,3 +1,5 @@
+import functools
+
 import jax
 import jax.numpy as jnp
 from jax import lax
@@ -13,26 +15,21 @@
     depth = grad_ref.shape[1]
     scale = depth ** (-0.5)
     acc_ref[...] = jnp.zeros(acc_ref.shape, jnp.float32)
-    col_block = lax.broadcasted_iota(jnp.int32, (BLOCK, listed * BLOCK), 1) // BLOCK
     trans_a = (((0,), (0,)), ((), ()))
     trans_b = (((1,), (1,)), ((), ()))
 
-    def one_block(a, carry):
+    def attend(a, used):
         start = pl.multiple_of(a * BLOCK, BLOCK)
         query = both_ref[pl.ds(start, BLOCK), :][:, :depth]
         upstream = grad_ref[pl.ds(start, BLOCK), :]
-        active = counts_ref[a]
-        picks = [jnp.clip(lists_ref[a, j], 0, nblocks - 1) for j in range(listed)]
-        near = jnp.concatenate(
-            [both_ref[pl.ds(pl.multiple_of(b * BLOCK, BLOCK), BLOCK), :] for b in picks], axis=0
-        )
+        picks = [jnp.clip(lists_ref[a, j], 0, nblocks - 1) for j in range(used)]
+        tiles = [both_ref[pl.ds(pl.multiple_of(b * BLOCK, BLOCK), BLOCK), :] for b in picks]
+        near = tiles[0] if used == 1 else jnp.concatenate(tiles, axis=0)
         keys = near[:, :depth]
         values = near[:, depth:]
         scores = lax.dot_general(query, keys, trans_b, preferred_element_type=jnp.float32) * scale
-        usable = col_block < active
-        scores = jnp.where(usable, scores, -jnp.inf)
         peak = jnp.max(scores, axis=1, keepdims=True)
-        weights = jnp.where(usable, jnp.exp(scores - peak), 0.0)
+        weights = jnp.exp(scores - peak)
         probs = weights / jnp.sum(weights, axis=1, keepdims=True)
         probs_low = probs.astype(jnp.bfloat16)
         mixed = jnp.dot(probs_low, values, preferred_element_type=jnp.float32)
@@ -44,16 +41,16 @@
         dkeys = lax.dot_general(dscores, query, trans_a, preferred_element_type=jnp.float32)
         dvalues = lax.dot_general(probs_low, upstream, trans_a, preferred_element_type=jnp.float32)
         both_grads = jnp.concatenate([dkeys, dvalues], axis=1)
-        for j in range(listed):
+        for j in range(used):
             part = both_grads[j * BLOCK:(j + 1) * BLOCK]
             if j == 0:
                 part = part + jnp.concatenate([dquery, jnp.zeros_like(dquery)], axis=1)
-
-            @pl.when(j < active)
-            def _():
-                rows = pl.ds(pl.multiple_of(picks[j] * BLOCK, BLOCK), BLOCK)
-                acc_ref[rows, :] += part
-
+            rows = pl.ds(pl.multiple_of(picks[j] * BLOCK, BLOCK), BLOCK)
+            acc_ref[rows, :] += part
+
+    def one_block(a, carry):
+        active = jnp.clip(counts_ref[a], 1, listed)
+        lax.switch(active - 1, [functools.partial(attend, a, used) for used in range(1, listed + 1)])
         return carry
 
     lax.fori_loop(0, nblocks, one_block, 0)

time: 140 us -> 143 us (1.021)
  waiting for transfers between devices: 52.2 us -> 61.5 us
  Pallas kernels: 22.4 us -> 16.8 us
    all_gather x1, waiting for transfers between devices: 0.02 us -> 10.3 us  [local(): owned_all = lax.all_gather(later_rows, 'seq', axis=0, tiled=True)]
    pallas_call x1, Pallas kernels: 22.4 us -> 16.8 us  [attend_group(): pl.pallas_call(attention_kernel, out_shape=(jax.ShapeDtypeStruct((total,...]
  transfers between devices with their start and end apart: 8 -> 8, of which waited for: 6 -> 7; matrix products, arithmetic and copies ran while one was open for 16% -> 16% of each run, Pallas kernels for 16% -> 12%
where the time goes in v14:
time: 143 us; the launch traced here: 142 us
  waiting for transfers between devices  61.5 us (43%)
  starting transfers between devices  25.1 us (18%)
  matrix products  18.4 us (13%)
  Pallas kernels  16.8 us (12%)
  between operations  14.1 us (10%)
  local copies, waits for them, and re-layouts  5.95 us (4%)
    pallas_call x1, Pallas kernels, attend_group(): pl.pallas_call(attention_kernel, out_shape=(jax.ShapeDtypeStruct((total,...  16.8 us
    all_to_all x1, waiting for transfers between devices, local(): lax.all_to_all(grad_both.reshape(seq_count, portion, 2 * depth), 'seq', s...  15.3 us
    all_to_all x1, waiting for transfers between devices, local(): lax.all_to_all(proj_mine, 'seq', split_axis=0, concat_axis=0, tiled=True)  14.2 us
    all_gather x1, waiting for transfers between devices, local(): owned_all = lax.all_gather(later_rows, 'seq', axis=0, tiled=True)  10.3 us
    all_to_all x1, waiting for transfers between devices, local(): lax.all_to_all(upstream, 'seq', split_axis=0, concat_axis=0, tiled=True)  6.49 us
    all_to_all x1, starting transfers between devices, local(): lax.all_to_all(upstream, 'seq', split_axis=0, concat_axis=0, tiled=True)  6.47 us
    dot_general x1, matrix products, local(): lax.dot_general(placing, grad_both, (((0,), (0,)), ((), ())), preferred_e...  5.57 us
    all_to_all x1, waiting for transfers between devices, local(): lax.all_to_all(summed.reshape(seq_count, rows_out, 2 * depth), 'seq', spl...  5.22 us
  transfers between devices with their start and end apart: 8, of which 7 were waited for; matrix products, arithmetic and copies ran while one was open for 16% of the time, Pallas kernels for 12%

profile of v14, /device:TPU:0, one launch (start us, length us, event | category | flops | bytes accessed | tf_op | source)
XLA Modules:
  0.0 141.9 jit_solution(9928975739104462320)
XLA Ops:
  7.2 0.0 copy-start.1
  7.2 0.0 copy-start
  7.2 6.5 %all-to-all-start.2 = ((bf16[8,256,64]{1,2,0:T(8,128)(2,1)}), bf16[8,256,64]{1,2,0:T(8,128)(2,1)S(1)}, u32[]{:S(2)}, u32[]{:S(2)}) async-start(bf16[8,256,64]{1,2,0:T(8,128)(2,1)} %bitcast.37), calls=%async_computation.2 | async-start | bytes 524288 | tf_op jit(solution)/shard_map/all_to_all | solution.py:127
  13.7 3.2 %fusion.19 = bf16[8,256,128]{1,2,0:T(8,128)(2,1)} fusion(bf16[1024,8,128]{2,1,0:T(8,128)(2,1)} %param.8, bf16[1,256,1024]{2,1,0:T(8,128)(2,1)} %param.6), kind=kOutput, calls=%fused_computation.14 | convolution fusion | flops 537133056 | bytes 3145728 | tf_op jit(solution)/shard_map/td,dhc->htc/dot_general | solution.py:137
  16.9 6.5 %all-to-all-done.2 = bf16[8,256,64]{1,2,0:T(8,128)(2,1)S(1)} async-done(((bf16[8,256,64]{1,2,0:T(8,128)(2,1)}), bf16[8,256,64]{1,2,0:T(8,128)(2,1)S(1)}, u32[]{:S(2)}, u32[]{:S(2)}) %all-to-all-start.2) | async-done | bytes 262176 | tf_op jit(solution)/shard_map/all_to_all | solution.py:127
  23.4 3.5 %all-to-all-start.1 = ((bf16[8,256,128]{1,2,0:T(8,128)(2,1)}), bf16[8,256,128]{1,2,0:T(8,128)(2,1)S(1)}, u32[]{:S(2)}, u32[]{:S(2)}) async-start(bf16[8,256,128]{1,2,0:T(8,128)(2,1)} %fusion.19), calls=%async_computation.1 | async-start | bytes 1048576 | tf_op jit(solution)/shard_map/all_to_all | solution.py:140
  26.9 0.0 all-gather.2.cloned.1.call-start
  26.9 1.0 copy.24
  28.0 14.2 %all-to-all-done.1 = bf16[8,256,128]{1,2,0:T(8,128)(2,1)S(1)} async-done(((bf16[8,256,128]{1,2,0:T(8,128)(2,1)}), bf16[8,256,128]{1,2,0:T(8,128)(2,1)S(1)}, u32[]{:S(2)}, u32[]{:S(2)}) %all-to-all-start.1) | async-done | bytes 524320 | tf_op jit(solution)/shard_map/all_to_all | solution.py:140
  42.2 0.3 copy.23
  42.5 0.0 all-gather.2.cloned.1.call-update
  42.5 0.0 copy-done.1
  42.5 0.6 broadcast_in_dim.12
  43.1 3.3 %all-to-all-start = ((s32[8,1,256]{2,1,0:T(1,128)}), s32[8,1,256]{2,1,0:T(1,128)S(1)}, u32[]{:S(2)}, u32[]{:S(2)}) async-start(s32[8,1,256]{2,1,0:T(1,128)} %broadcast_in_dim.12), calls=%async_computation | async-start | bytes 16384 | tf_op jit(solution)/shard_map/all_to_all | solution.py:130
  46.4 0.0 copy-done
  46.5 0.7 copy.25.lists_ref
  47.1 4.9 %all-to-all-done = s32[8,1,256]{2,1,0:T(1,128)S(1)} async-done(((s32[8,1,256]{2,1,0:T(1,128)}), s32[8,1,256]{2,1,0:T(1,128)S(1)}, u32[]{:S(2)}, u32[]{:S(2)}) %all-to-all-start) | async-done | bytes 8224 | tf_op jit(solution)/shard_map/all_to_all | solution.py:130
  52.1 3.8 %fusion.4.both_ref = bf16[2048,128]{1,0:T(8,128)(2,1)} fusion(bf16[2048,128]{1,0:T(8,128)(2,1)S(1)} %bitcast.35, s32[2048]{0:T(1024)S(1)} %bitcast.39), kind=kOutput, calls=%fused_computation.5 | convolution fusion | flops 1078198272 | bytes 1056768 | tf_op jit(solution)/shard_map/dot_general | solution.py:149
  55.8 16.8 %shard_map.88 = (bf16[2048,64]{1,0:T(8,128)(2,1)}, bf16[2048,128]{1,0:T(8,128)(2,1)}) custom-call(s32[16,8]{1,0:T(8,128)} %copy.25.lists_ref, s32[16]{0:T(128)} %bitcast.43, bf16[2048,128]{1,0:T(8,128)(2,1)} %fusion.4.both_ref, bf16[2048,64]{1,0:T(8,128)(2,1)} %bitcast.31), custom_call_target="tpu_custom_call" | custom-call | tf_op jit(solution)/shard_map/pallas_call | solution.py:65
  72.7 1.9 %copy.26 = bf16[8,256,64]{1,2,0:T(8,128)(2,1)} copy(bf16[8,256,64]{2,1,0:T(8,128)(2,1)} %bitcast.33) | data formatting | bytes 524288 | tf_op jit(solution)/shard_map/reshape | solution.py:163
  74.6 3.4 %all-to-all-start.3 = ((bf16[8,256,64]{1,2,0:T(8,128)(2,1)}), bf16[8,256,64]{1,2,0:T(8,128)(2,1)S(1)}, u32[]{:S(2)}, u32[]{:S(2)}) async-start(bf16[8,256,64]{1,2,0:T(8,128)(2,1)} %copy.26), calls=%async_computation.3 | async-start | bytes 524288 | tf_op jit(solution)/shard_map/all_to_all | solution.py:162
  78.0 0.2 reduce-scatter.2.cloned.1.call-start
  78.2 5.6 %fusion.5 = bf16[2048,128]{1,0:T(8,128)(2,1)S(1)} fusion(bf16[2048,128]{1,0:T(8,128)(2,1)} %get-tuple-element.11, s32[2048]{0:T(1024)S(1)} %bitcast.40), kind=kOutput, calls=%fused_computation.6 | convolution fusion | flops 1078198272 | bytes 1056768 | tf_op jit(solution)/shard_map/dot_general | solution.py:185
  83.8 0.0 copy-start.2
  83.8 10.3 %all-gather.2.cloned.1.call-done = bf16[2048,1024]{1,0:T(8,128)(2,1)} async-done(((bf16[256,1024]{1,0:T(8,128)(2,1)}), bf16[2048,1024]{1,0:T(8,128)(2,1)}) %all-gather.2.cloned.1.call-update) | async-done | bytes 4194320 | tf_op jit(solution)/shard_map/all_gather | solution.py:146
  94.1 4.3 %fusion.26 = f32[1024,128]{1,0:T(8,128)} fusion(bf16[2048,1024]{1,0:T(8,128)(2,1)} %all-gather.2.cloned.1.call-done, bf16[2048,128]{1,0:T(8,128)(2,1)S(1)} %fusion.5), kind=kOutput, calls=%fused_computation.17 | convolution fusion | flops 536870912 | bytes 5242880 | tf_op jit(solution)/shard_map/od,oc->dc/dot_general | solution.py:189
  98.4 0.0 reduce-scatter.2.cloned.1.call-update
  98.4 0.0 all-to-all-done.3
  98.4 3.5 %all-to-all-start.4 = ((bf16[8,256,128]{2,1,0:T(8,128)(2,1)}), bf16[8,256,128]{2,1,0:T(8,128)(2,1)S(1)}, u32[]{:S(2)}, u32[]{:S(2)}) async-start(bf16[8,256,128]{2,1,0:T(8,128)(2,1)} %bitcast.12), calls=%async_computation.4 | async-start | bytes 1048576 | tf_op jit(solution)/shard_map/all_to_all | solution.py:169
  101.9 15.3 %all-to-all-done.4 = bf16[8,256,128]{2,1,0:T(8,128)(2,1)S(1)} async-done(((bf16[8,256,128]{2,1,0:T(8,128)(2,1)}), bf16[8,256,128]{2,1,0:T(8,128)(2,1)S(1)}, u32[]{:S(2)}, u32[]{:S(2)}) %all-to-all-start.4) | async-done | bytes 524320 | tf_op jit(solution)/shard_map/all_to_all | solution.py:169
  117.2 5.0 %reduce-scatter.2.cloned.1.call-done = f32[256,128]{1,0:T(8,128)} async-done(((f32[1024,128]{1,0:T(8,128)}), f32[256,128]{1,0:T(8,128)}) %reduce-scatter.2.cloned.1.call-update) | async-done | bytes 131088 | tf_op jit(solution)/shard_map/reduce_scatter | solution.py:192
  122.2 4.6 %all-to-all-start.5 = ((f32[8,32,128]{2,1,0:T(8,128)}), f32[8,32,128]{2,1,0:T(8,128)S(1)}, u32[]{:S(2)}, u32[]{:S(2)}) async-start(f32[8,32,128]{2,1,0:T(8,128)} %bitcast.38), calls=%async_computation.6 | async-start | bytes 262144 | tf_op jit(solution)/shard_map/all_to_all | solution.py:193
  126.8 0.0 copy-done.2
  126.8 1.6 %fusion.22 = bf16[1,256,1024]{2,1,0:T(8,128)(2,1)} fusion(bf16[8,256,128]{2,1,0:T(8,128)(2,1)S(1)} %all-to-all-done.4, bf16[1024,8,128]{2,1,0:T(8,128)(2,1)S(1)} %copy-done.2), kind=kOutput, calls=%fused_computation.15 | convolution fusion | flops 537133056 | bytes 3145728 | tf_op jit(solution)/shard_map/htc,dhc->td/dot_general | solution.py:179
  128.4 5.2 %all-to-all-done.5 = f32[8,32,128]{2,1,0:T(8,128)S(1)} async-done(((f32[8,32,128]{2,1,0:T(8,128)}), f32[8,32,128]{2,1,0:T(8,128)S(1)}, u32[]{:S(2)}, u32[]{:S(2)}) %all-to-all-start.5) | async-done | bytes 131104 | tf_op jit(solution)/shard_map/all_to_all | solution.py:193
  133.6 0.7 copy.28
  134.4 0.7 copy.44
Async XLA Ops:
  7.2 35.3 %copy-start.1 = (s32[1,256]{1,0:T(1,128)S(1)}, s32[1,256]{1,0:T(1,128)}, u32[]{:S(2)}) copy-start(s32[1,256]{1,0:T(1,128)} %param.7) | copy-start | bytes 3076
  7.2 39.3 %copy-start = (s32[1,16,8]{1,2,0:T(8,128)S(1)}, s32[1,16,8]{1,2,0:T(8,128)}, u32[]{:S(2)}) copy-start(s32[1,16,8]{1,2,0:T(8,128)} %param.9) | copy-start | bytes 1540
  7.2 16.2 %all-to-all-start.2 = ((bf16[8,256,64]{1,2,0:T(8,128)(2,1)}), bf16[8,256,64]{1,2,0:T(8,128)(2,1)S(1)}, u32[]{:S(2)}, u32[]{:S(2)}) async-start(bf16[8,256,64]{1,2,0:T(8,128)(2,1)} %bitcast.37), calls=%async_computation.2 | async-start | bytes 524288 | tf_op jit(solution)/shard_map/all_to_all | solution.py:127
  23.4 18.8 %all-to-all-start.1 = ((bf16[8,256,128]{1,2,0:T(8,128)(2,1)}), bf16[8,256,128]{1,2,0:T(8,128)(2,1)S(1)}, u32[]{:S(2)}, u32[]{:S(2)}) async-start(bf16[8,256,128]{1,2,0:T(8,128)(2,1)} %fusion.19), calls=%async_computation.1 | async-start | bytes 1048576 | tf_op jit(solution)/shard_map/all_to_all | solution.py:140
  26.9 67.2 %all-gather.2.cloned.1.call-start = ((), (), s32[]{:S(2)}) async-start(), calls=%async_computation.7 | async-start | bytes 4718592 | tf_op jit(solution)/shard_map/all_gather | solution.py:146
  43.1 9.0 %all-to-all-start = ((s32[8,1,256]{2,1,0:T(1,128)}), s32[8,1,256]{2,1,0:T(1,128)S(1)}, u32[]{:S(2)}, u32[]{:S(2)}) async-start(s32[8,1,256]{2,1,0:T(1,128)} %broadcast_in_dim.12), calls=%async_computation | async-start | bytes 16384 | tf_op jit(solution)/shard_map/all_to_all | solution.py:130
  74.6 23.8 %all-to-all-start.3 = ((bf16[8,256,64]{1,2,0:T(8,128)(2,1)}), bf16[8,256,64]{1,2,0:T(8,128)(2,1)S(1)}, u32[]{:S(2)}, u32[]{:S(2)}) async-start(bf16[8,256,64]{1,2,0:T(8,128)(2,1)} %copy.26), calls=%async_computation.3 | async-start | bytes 524288 | tf_op jit(solution)/shard_map/all_to_all | solution.py:162
  78.0 44.2 %reduce-scatter.2.cloned.1.call-start = ((), (), s32[]{:S(2)}) async-start(), calls=%async_computation.8 | async-start | bytes 655360 | tf_op jit(solution)/shard_map/reduce_scatter | solution.py:192
  83.8 43.0 %copy-start.2 = (bf16[1024,8,128]{2,1,0:T(8,128)(2,1)S(1)}, bf16[1024,8,128]{2,1,0:T(8,128)(2,1)}, u32[]{:S(2)}) copy-start(bf16[1024,8,128]{2,1,0:T(8,128)(2,1)} %param.8) | copy-start | bytes 6291460
  98.4 18.8 %all-to-all-start.4 = ((bf16[8,256,128]{2,1,0:T(8,128)(2,1)}), bf16[8,256,128]{2,1,0:T(8,128)(2,1)S(1)}, u32[]{:S(2)}, u32[]{:S(2)}) async-start(bf16[8,256,128]{2,1,0:T(8,128)(2,1)} %bitcast.12), calls=%async_computation.4 | async-start | bytes 1048576 | tf_op jit(solution)/shard_map/all_to_all | solution.py:169
  122.2 11.4 %all-to-all-start.5 = ((f32[8,32,128]{2,1,0:T(8,128)}), f32[8,32,128]{2,1,0:T(8,128)S(1)}, u32[]{:S(2)}, u32[]{:S(2)}) async-start(f32[8,32,128]{2,1,0:T(8,128)} %bitcast.38), calls=%async_computation.6 | async-start | bytes 262144 | tf_op jit(solution)/shard_map/all_to_all | solution.py:193
Sparse Core Ops, SparseCore 0:
  42.6 51.4 all-gather.1
  98.5 23.6 reduce-scatter.1

commit v15 on v14

--- a/solution.py
+++ b/solution.py
@@ -140,9 +140,7 @@
         proj_owned = lax.all_to_all(
             proj_mine, "seq", split_axis=0, concat_axis=0, tiled=True
         ).reshape(seq_count * tokens_here, 2 * depth)
-        later_rows, proj_owned, grad_rows = lax.optimization_barrier(
-            (rows_here, proj_owned, grad_rows)
-        )
+        later_rows, grad_rows = lax.optimization_barrier((rows_here, grad_rows))
         owned_all = lax.all_gather(later_rows, "seq", axis=0, tiled=True)
         slots = jnp.arange(places_all.shape[0], dtype=places_all.dtype)
         placing = (slots[:, None] == places_all[None, :]).astype(jnp.bfloat16)

time: 143 us -> 152 us (1.063)
  blocking collectives: 0 us -> 45.7 us
  waiting for transfers between devices: 61.5 us -> 31.4 us
  starting transfers between devices: 25.1 us -> 17.4 us
    all_to_all x0 -> x2, blocking collectives: none -> 45.7 us  [the longest x1 29.6 us: local(): lax.all_to_all(proj_mine, 'seq', split_axis=0, concat_axis=0, tiled=True)]
    all_to_all x2 -> x0, waiting for transfers between devices: 20.7 us -> none  [the longest x1 14.2 us: local(): lax.all_to_all(proj_mine, 'seq', split_axis=0, concat_axis=0, tiled=True)]
    all_gather x1, waiting for transfers between devices: 10.3 us -> 0.02 us  [local(): owned_all = lax.all_gather(later_rows, 'seq', axis=0, tiled=True)]
    all_to_all x2 -> x0, starting transfers between devices: 9.96 us -> none  [the longest x1 6.47 us: local(): lax.all_to_all(upstream, 'seq', split_axis=0, concat_axis=0, tiled=True)]
  transfers between devices with their start and end apart: 8 -> 6, of which waited for: 7 -> 4; matrix products, arithmetic and copies ran while one was open for 16% -> 14% of each run, Pallas kernels for 12% -> 12%
where the time goes in v15:
time: 152 us; the launch traced here: 150 us
  blocking collectives  45.7 us (30%)
  waiting for transfers between devices  31.4 us (21%)
  matrix products  17.8 us (12%)
  starting transfers between devices  17.4 us (11%)
  Pallas kernels  17.3 us (11%)
  between operations  14.1 us (9%)
  local copies, waits for them, and re-layouts  5.94 us (4%)
    all_to_all x1, blocking collectives, local(): lax.all_to_all(proj_mine, 'seq', split_axis=0, concat_axis=0, tiled=True)  29.6 us
    pallas_call x1, Pallas kernels, attend_group(): pl.pallas_call(attention_kernel, out_shape=(jax.ShapeDtypeStruct((total,...  17.3 us
    all_to_all x1, blocking collectives, local(): lax.all_to_all(upstream, 'seq', split_axis=0, concat_axis=0, tiled=True)  16.1 us
    all_to_all x1, waiting for transfers between devices, local(): lax.all_to_all(grad_both.reshape(seq_count, portion, 2 * depth), 'seq', s...  15.4 us
    reduce_scatter x1, waiting for transfers between devices, local(): summed = lax.psum_scatter(partial, 'rec', scatter_dimension=0, tiled=True)  5.9 us
    dot_general x1, matrix products, local(): lax.dot_general(placing, grad_both, (((0,), (0,)), ((), ())), preferred_e...  5.56 us
    all_to_all x1, waiting for transfers between devices, local(): lax.all_to_all(summed.reshape(seq_count, rows_out, 2 * depth), 'seq', spl...  5.22 us
    all_to_all x1, waiting for transfers between devices, local(): lax.all_to_all(jnp.broadcast_to(targets[None], (seq_count, tokens_here)),...  4.86 us
  transfers between devices with their start and end apart: 6, of which 4 were waited for; matrix products, arithmetic and copies ran while one was open for 14% of the time, Pallas kernels for 12%

profile of v15, /device:TPU:0, one launch (start us, length us, event | category | flops | bytes accessed | tf_op | source)
XLA Modules:
  0.0 149.6 jit_solution(244082214248709038)
XLA Ops:
  7.2 0.0 copy-start.1
  7.2 0.0 copy-start
  7.2 0.0 all-gather.2.cloned.1.call-start
  7.2 16.1 %all_to_all.31 = bf16[8,256,64]{1,2,0:T(8,128)(2,1)S(1)} all-to-all(bf16[8,256,64]{1,2,0:T(8,128)(2,1)} %bitcast.37), channel_id=1, replica_groups=mesh['rec'=4,'seq'=8] {'seq'}, dimensions={0} | all-to-all | bytes 524288 | tf_op jit(solution)/shard_map/all_to_all | solution.py:127
  23.3 1.0 copy.24
  24.3 0.0 all-gather.2.cloned.1.call-update
  24.3 2.5 %fusion.19 = bf16[8,256,128]{1,2,0:T(8,128)(2,1)S(1)} fusion(bf16[1024,8,128]{2,1,0:T(8,128)(2,1)} %param.8, bf16[1,256,1024]{2,1,0:T(8,128)(2,1)} %param.6), kind=kOutput, calls=%fused_computation.14 | convolution fusion | flops 537133056 | bytes 3145728 | tf_op jit(solution)/shard_map/td,dhc->htc/dot_general | solution.py:137
  26.8 29.6 %all_to_all.32 = bf16[8,256,128]{1,2,0:T(8,128)(2,1)S(1)} all-to-all(bf16[8,256,128]{1,2,0:T(8,128)(2,1)S(1)} %fusion.19), channel_id=1, replica_groups=mesh['rec'=4,'seq'=8] {'seq'}, dimensions={0} | all-to-all | bytes 1048576 | tf_op jit(solution)/shard_map/all_to_all | solution.py:140
  56.4 0.0 copy-done.1
  56.4 0.6 broadcast_in_dim.12
  57.0 4.3 %all-to-all-start = ((s32[8,1,256]{2,1,0:T(1,128)}), s32[8,1,256]{2,1,0:T(1,128)S(1)}, u32[]{:S(2)}, u32[]{:S(2)}) async-start(s32[8,1,256]{2,1,0:T(1,128)} %broadcast_in_dim.12), calls=%async_computation | async-start | bytes 16384 | tf_op jit(solution)/shard_map/all_to_all | solution.py:130
  61.3 0.0 copy-done
  61.3 0.7 copy.25.lists_ref
  62.0 0.3 copy.23
  62.3 4.9 %all-to-all-done = s32[8,1,256]{2,1,0:T(1,128)S(1)} async-done(((s32[8,1,256]{2,1,0:T(1,128)}), s32[8,1,256]{2,1,0:T(1,128)S(1)}, u32[]{:S(2)}, u32[]{:S(2)}) %all-to-all-start) | async-done | bytes 8224 | tf_op jit(solution)/shard_map/all_to_all | solution.py:130
  67.2 3.8 %fusion.4.both_ref = bf16[2048,128]{1,0:T(8,128)(2,1)} fusion(bf16[2048,128]{1,0:T(8,128)(2,1)S(1)} %bitcast.35, s32[2048]{0:T(1024)S(1)} %bitcast.39), kind=kOutput, calls=%fused_computation.5 | convolution fusion | flops 1078198272 | bytes 1056768 | tf_op jit(solution)/shard_map/dot_general | solution.py:147
  70.9 17.3 %shard_map.88 = (bf16[2048,64]{1,0:T(8,128)(2,1)}, bf16[2048,128]{1,0:T(8,128)(2,1)}) custom-call(s32[16,8]{1,0:T(8,128)} %copy.25.lists_ref, s32[16]{0:T(128)} %bitcast.43, bf16[2048,128]{1,0:T(8,128)(2,1)} %fusion.4.both_ref, bf16[2048,64]{1,0:T(8,128)(2,1)} %bitcast.31), custom_call_target="tpu_custom_call" | custom-call | tf_op jit(solution)/shard_map/pallas_call | solution.py:65
  88.2 1.9 %copy.26 = bf16[8,256,64]{1,2,0:T(8,128)(2,1)} copy(bf16[8,256,64]{2,1,0:T(8,128)(2,1)} %bitcast.33) | data formatting | bytes 524288 | tf_op jit(solution)/shard_map/reshape | solution.py:161
  90.2 3.4 %all-to-all-start.3 = ((bf16[8,256,64]{1,2,0:T(8,128)(2,1)}), bf16[8,256,64]{1,2,0:T(8,128)(2,1)S(1)}, u32[]{:S(2)}, u32[]{:S(2)}) async-start(bf16[8,256,64]{1,2,0:T(8,128)(2,1)} %copy.26), calls=%async_computation.3 | async-start | bytes 524288 | tf_op jit(solution)/shard_map/all_to_all | solution.py:160
  93.6 0.2 reduce-scatter.2.cloned.1.call-start
  93.8 5.6 %fusion.5 = bf16[2048,128]{1,0:T(8,128)(2,1)S(1)} fusion(bf16[2048,128]{1,0:T(8,128)(2,1)} %get-tuple-element.9, s32[2048]{0:T(1024)S(1)} %bitcast.40), kind=kOutput, calls=%fused_computation.6 | convolution fusion | flops 1078198272 | bytes 1056768 | tf_op jit(solution)/shard_map/dot_general | solution.py:183
  99.4 0.0 copy-start.2
  99.4 0.0 all-gather.2.cloned.1.call-done
  99.4 4.4 %fusion.26 = f32[1024,128]{1,0:T(8,128)} fusion(bf16[2048,1024]{1,0:T(8,128)(2,1)} %all-gather.2.cloned.1.call-done, bf16[2048,128]{1,0:T(8,128)(2,1)S(1)} %fusion.5), kind=kOutput, calls=%fused_computation.17 | convolution fusion | flops 536870912 | bytes 5242880 | tf_op jit(solution)/shard_map/od,oc->dc/dot_general | solution.py:187
  103.8 0.0 reduce-scatter.2.cloned.1.call-update
  103.9 0.0 all-to-all-done.3
  103.9 4.8 %all-to-all-start.4 = ((bf16[8,256,128]{2,1,0:T(8,128)(2,1)}), bf16[8,256,128]{2,1,0:T(8,128)(2,1)S(1)}, u32[]{:S(2)}, u32[]{:S(2)}) async-start(bf16[8,256,128]{2,1,0:T(8,128)(2,1)} %bitcast.12), calls=%async_computation.4 | async-start | bytes 1048576 | tf_op jit(solution)/shard_map/all_to_all | solution.py:167
  108.7 15.4 %all-to-all-done.4 = bf16[8,256,128]{2,1,0:T(8,128)(2,1)S(1)} async-done(((bf16[8,256,128]{2,1,0:T(8,128)(2,1)}), bf16[8,256,128]{2,1,0:T(8,128)(2,1)S(1)}, u32[]{:S(2)}, u32[]{:S(2)}) %all-to-all-start.4) | async-done | bytes 524320 | tf_op jit(solution)/shard_map/all_to_all | solution.py:167
  124.0 5.9 %reduce-scatter.2.cloned.1.call-done = f32[256,128]{1,0:T(8,128)} async-done(((f32[1024,128]{1,0:T(8,128)}), f32[256,128]{1,0:T(8,128)}) %reduce-scatter.2.cloned.1.call-update) | async-done | bytes 131088 | tf_op jit(solution)/shard_map/reduce_scatter | solution.py:190
  130.0 4.6 %all-to-all-start.5 = ((f32[8,32,128]{2,1,0:T(8,128)}), f32[8,32,128]{2,1,0:T(8,128)S(1)}, u32[]{:S(2)}, u32[]{:S(2)}) async-start(f32[8,32,128]{2,1,0:T(8,128)} %bitcast.38), calls=%async_computation.6 | async-start | bytes 262144 | tf_op jit(solution)/shard_map/all_to_all | solution.py:191
  134.6 0.0 copy-done.2
  134.6 1.6 %fusion.22 = bf16[1,256,1024]{2,1,0:T(8,128)(2,1)} fusion(bf16[8,256,128]{2,1,0:T(8,128)(2,1)S(1)} %all-to-all-done.4, bf16[1024,8,128]{2,1,0:T(8,128)(2,1)S(1)} %copy-done.2), kind=kOutput, calls=%fused_computation.15 | convolution fusion | flops 537133056 | bytes 3145728 | tf_op jit(solution)/shard_map/htc,dhc->td/dot_general | solution.py:177
  136.1 5.2 %all-to-all-done.5 = f32[8,32,128]{2,1,0:T(8,128)S(1)} async-done(((f32[8,32,128]{2,1,0:T(8,128)}), f32[8,32,128]{2,1,0:T(8,128)S(1)}, u32[]{:S(2)}, u32[]{:S(2)}) %all-to-all-start.5) | async-done | bytes 131104 | tf_op jit(solution)/shard_map/all_to_all | solution.py:191
  141.3 0.7 copy.28
  142.1 0.7 copy.44
Async XLA Ops:
  7.2 49.3 %copy-start.1 = (s32[1,256]{1,0:T(1,128)S(1)}, s32[1,256]{1,0:T(1,128)}, u32[]{:S(2)}) copy-start(s32[1,256]{1,0:T(1,128)} %param.7) | copy-start | bytes 3076
  7.2 54.2 %copy-start = (s32[1,16,8]{1,2,0:T(8,128)S(1)}, s32[1,16,8]{1,2,0:T(8,128)}, u32[]{:S(2)}) copy-start(s32[1,16,8]{1,2,0:T(8,128)} %param.9) | copy-start | bytes 1540
  7.2 92.2 %all-gather.2.cloned.1.call-start = ((), (), s32[]{:S(2)}) async-start(), calls=%async_computation.7 | async-start | bytes 4718592 | tf_op jit(solution)/shard_map/all_gather | solution.py:144
  57.0 10.1 %all-to-all-start = ((s32[8,1,256]{2,1,0:T(1,128)}), s32[8,1,256]{2,1,0:T(1,128)S(1)}, u32[]{:S(2)}, u32[]{:S(2)}) async-start(s32[8,1,256]{2,1,0:T(1,128)} %broadcast_in_dim.12), calls=%async_computation | async-start | bytes 16384 | tf_op jit(solution)/shard_map/all_to_all | solution.py:130
  90.2 13.7 %all-to-all-start.3 = ((bf16[8,256,64]{1,2,0:T(8,128)(2,1)}), bf16[8,256,64]{1,2,0:T(8,128)(2,1)S(1)}, u32[]{:S(2)}, u32[]{:S(2)}) async-start(bf16[8,256,64]{1,2,0:T(8,128)(2,1)} %copy.26), calls=%async_computation.3 | async-start | bytes 524288 | tf_op jit(solution)/shard_map/all_to_all | solution.py:160
  93.6 36.4 %reduce-scatter.2.cloned.1.call-start = ((), (), s32[]{:S(2)}) async-start(), calls=%async_computation.8 | async-start | bytes 655360 | tf_op jit(solution)/shard_map/reduce_scatter | solution.py:190
  99.4 35.2 %copy-start.2 = (bf16[1024,8,128]{2,1,0:T(8,128)(2,1)S(1)}, bf16[1024,8,128]{2,1,0:T(8,128)(2,1)}, u32[]{:S(2)}) copy-start(bf16[1024,8,128]{2,1,0:T(8,128)(2,1)} %param.8) | copy-start | bytes 6291460
  103.9 20.2 %all-to-all-start.4 = ((bf16[8,256,128]{2,1,0:T(8,128)(2,1)}), bf16[8,256,128]{2,1,0:T(8,128)(2,1)S(1)}, u32[]{:S(2)}, u32[]{:S(2)}) async-start(bf16[8,256,128]{2,1,0:T(8,128)(2,1)} %bitcast.12), calls=%async_computation.4 | async-start | bytes 1048576 | tf_op jit(solution)/shard_map/all_to_all | solution.py:167
  130.0 11.4 %all-to-all-start.5 = ((f32[8,32,128]{2,1,0:T(8,128)}), f32[8,32,128]{2,1,0:T(8,128)S(1)}, u32[]{:S(2)}, u32[]{:S(2)}) async-start(f32[8,32,128]{2,1,0:T(8,128)} %bitcast.38), calls=%async_computation.6 | async-start | bytes 262144 | tf_op jit(solution)/shard_map/all_to_all | solution.py:191
Sparse Core Ops, SparseCore 0:
  24.5 55.7 all-gather.1
  104.0 25.9 reduce-scatter.1

commit v16 on v14

--- a/solution.py
+++ b/solution.py
@@ -158,22 +158,15 @@
         got = lax.all_to_all(sending, "seq", split_axis=0, concat_axis=0, tiled=True)
         gathered = got.reshape(seq_count * portion, 2 * depth)
     mixed, grad_both = attend_group(gathered, grad_rows, key_blocks[group], key_counts[group])
-    back_out, back_grad = (
-        lax.all_to_all(
-            mixed.reshape(seq_count, portion, depth),
-            "seq",
-            split_axis=0,
-            concat_axis=0,
-            tiled=True,
-        ),
-        lax.all_to_all(
-            grad_both.reshape(seq_count, portion, 2 * depth),
-            "seq",
-            split_axis=0,
-            concat_axis=0,
-            tiled=True,
-        ),
-    )
+    back = lax.all_to_all(
+        jnp.concatenate([mixed, grad_both], axis=1).reshape(seq_count, portion, 3 * depth),
+        "seq",
+        split_axis=0,
+        concat_axis=0,
+        tiled=True,
+    )
+    back_out = back[:, :, :depth]
+    back_grad = back[:, :, depth:]
     attention = back_out.reshape(heads, tokens_here, depth)[None]
     grad_proj = back_grad.reshape(heads, tokens_here, 2 * depth)
     seq_grad = jnp.einsum(
@@ -189,7 +182,14 @@
         partial = jnp.einsum(
             "od,oc->dc", owned_all, head_grad, preferred_element_type=jnp.float32
         )
-        summed = lax.psum_scatter(partial, "rec", scatter_dimension=0, tiled=True)
+        pieces = lax.all_to_all(
+            partial.reshape(rec_count, width // rec_count, 2 * depth),
+            "rec",
+            split_axis=0,
+            concat_axis=0,
+            tiled=True,
+        )
+        summed = jnp.sum(pieces, axis=0)
         spread = lax.all_to_all(
             summed.reshape(seq_count, rows_out, 2 * depth),
             "seq",

time: 143 us -> 135 us (0.944)
  waiting for transfers between devices: 61.5 us -> 52.9 us
  other arithmetic: 0 us -> 2.4 us
    reduce_scatter x1 -> x0, waiting for transfers between devices: 5.02 us -> none  [local(): summed = lax.psum_scatter(partial, 'rec', scatter_dimension=0, tiled=True)]
    all_to_all x2, waiting for transfers between devices: 15.3 us -> 11.3 us  [the longest x1 6.1 us: local(): lax.all_to_all(jnp.concatenate([mixed, grad_both], axis=1).reshape(seq_co...]
    concatenate x0 -> x1, other arithmetic: none -> 1.72 us  [local(): jnp.concatenate([mixed, grad_both], axis=1)]
    dot_general x1, matrix products: 1.55 us -> 3.15 us  [local(): jnp.einsum('htc,dhc->td', grad_proj, head_weights, preferred_element_type...]
  transfers between devices with their start and end apart: 8 -> 7, of which waited for: 7 -> 7; matrix products, arithmetic and copies ran while one was open for 16% -> 19% of each run, Pallas kernels for 12% -> 12%
where the time goes in v16:
time: 135 us; the launch traced here: 134 us
  waiting for transfers between devices  52.9 us (39%)
  starting transfers between devices  24.1 us (18%)
  matrix products  19 us (14%)
  Pallas kernels  16.5 us (12%)
  between operations  14.1 us (10%)
  local copies, waits for them, and re-layouts  5.33 us (4%)
  other arithmetic  2.4 us (2%)
    pallas_call x1, Pallas kernels, attend_group(): pl.pallas_call(attention_kernel, out_shape=(jax.ShapeDtypeStruct((total,...  16.5 us
    all_to_all x1, waiting for transfers between devices, local(): lax.all_to_all(proj_mine, 'seq', split_axis=0, concat_axis=0, tiled=True)  14.2 us
    all_gather x1, waiting for transfers between devices, local(): owned_all = lax.all_gather(later_rows, 'seq', axis=0, tiled=True)  9.97 us
    all_to_all x1, waiting for transfers between devices, local(): lax.all_to_all(upstream, 'seq', split_axis=0, concat_axis=0, tiled=True)  6.49 us
    all_to_all x1, starting transfers between devices, local(): lax.all_to_all(upstream, 'seq', split_axis=0, concat_axis=0, tiled=True)  6.47 us
    all_to_all x1, waiting for transfers between devices, local(): lax.all_to_all(jnp.concatenate([mixed, grad_both], axis=1).reshape(seq_co...  6.1 us
    all_to_all x1, waiting for transfers between devices, local(): lax.all_to_all(summed.reshape(seq_count, rows_out, 2 * depth), 'seq', spl...  5.99 us
    all_to_all x1, waiting for transfers between devices, local(): lax.all_to_all(partial.reshape(rec_count, width // rec_count, 2 * depth),...  5.16 us
  transfers between devices with their start and end apart: 7, of which 7 were waited for; matrix products, arithmetic and copies ran while one was open for 19% of the time, Pallas kernels for 12%

profile of v16, /device:TPU:0, one launch (start us, length us, event | category | flops | bytes accessed | tf_op | source)
XLA Modules:
  0.0 134.3 jit_solution(7359459265624342723)
XLA Ops:
  7.2 0.0 copy-start.2
  7.2 0.0 copy-start.1
  7.2 6.5 %all-to-all-start.2 = ((bf16[8,256,64]{1,2,0:T(8,128)(2,1)}), bf16[8,256,64]{1,2,0:T(8,128)(2,1)S(1)}, u32[]{:S(2)}, u32[]{:S(2)}) async-start(bf16[8,256,64]{1,2,0:T(8,128)(2,1)} %bitcast.36), calls=%async_computation.2 | async-start | bytes 524288 | tf_op jit(solution)/shard_map/all_to_all | solution.py:127
  13.7 3.2 %fusion.19 = bf16[8,256,128]{1,2,0:T(8,128)(2,1)} fusion(bf16[1024,8,128]{2,1,0:T(8,128)(2,1)} %param.8, bf16[1,256,1024]{2,1,0:T(8,128)(2,1)} %param.6), kind=kOutput, calls=%fused_computation.14 | convolution fusion | flops 537133056 | bytes 3145728 | tf_op jit(solution)/shard_map/td,dhc->htc/dot_general | solution.py:137
  16.9 6.5 %all-to-all-done.2 = bf16[8,256,64]{1,2,0:T(8,128)(2,1)S(1)} async-done(((bf16[8,256,64]{1,2,0:T(8,128)(2,1)}), bf16[8,256,64]{1,2,0:T(8,128)(2,1)S(1)}, u32[]{:S(2)}, u32[]{:S(2)}) %all-to-all-start.2) | async-done | bytes 262176 | tf_op jit(solution)/shard_map/all_to_all | solution.py:127
  23.4 3.5 %all-to-all-start.1 = ((bf16[8,256,128]{1,2,0:T(8,128)(2,1)}), bf16[8,256,128]{1,2,0:T(8,128)(2,1)S(1)}, u32[]{:S(2)}, u32[]{:S(2)}) async-start(bf16[8,256,128]{1,2,0:T(8,128)(2,1)} %fusion.19), calls=%async_computation.1 | async-start | bytes 1048576 | tf_op jit(solution)/shard_map/all_to_all | solution.py:140
  26.9 0.0 all-gather.2.cloned.1.call-start
  26.9 1.0 copy.23
  28.0 14.2 %all-to-all-done.1 = bf16[8,256,128]{1,2,0:T(8,128)(2,1)S(1)} async-done(((bf16[8,256,128]{1,2,0:T(8,128)(2,1)}), bf16[8,256,128]{1,2,0:T(8,128)(2,1)S(1)}, u32[]{:S(2)}, u32[]{:S(2)}) %all-to-all-start.1) | async-done | bytes 524320 | tf_op jit(solution)/shard_map/all_to_all | solution.py:140
  42.2 0.3 copy.22
  42.5 0.0 all-gather.2.cloned.1.call-update
  42.5 0.0 copy-done.2
  42.5 0.6 broadcast_in_dim.12
  43.1 3.3 %all-to-all-start = ((s32[8,1,256]{2,1,0:T(1,128)}), s32[8,1,256]{2,1,0:T(1,128)S(1)}, u32[]{:S(2)}, u32[]{:S(2)}) async-start(s32[8,1,256]{2,1,0:T(1,128)} %broadcast_in_dim.12), calls=%async_computation | async-start | bytes 16384 | tf_op jit(solution)/shard_map/all_to_all | solution.py:130
  46.4 0.0 copy-done.1
  46.5 0.7 copy.24.lists_ref
  47.1 4.9 %all-to-all-done = s32[8,1,256]{2,1,0:T(1,128)S(1)} async-done(((s32[8,1,256]{2,1,0:T(1,128)}), s32[8,1,256]{2,1,0:T(1,128)S(1)}, u32[]{:S(2)}, u32[]{:S(2)}) %all-to-all-start) | async-done | bytes 8224 | tf_op jit(solution)/shard_map/all_to_all | solution.py:130
  52.1 3.8 %fusion.4.both_ref = bf16[2048,128]{1,0:T(8,128)(2,1)} fusion(bf16[2048,128]{1,0:T(8,128)(2,1)S(1)} %bitcast.34, s32[2048]{0:T(1024)S(1)} %bitcast.37), kind=kOutput, calls=%fused_computation.5 | convolution fusion | flops 1078198272 | bytes 1056768 | tf_op jit(solution)/shard_map/dot_general | solution.py:149
  55.9 16.5 %shard_map.88 = (bf16[2048,64]{1,0:T(8,128)(2,1)}, bf16[2048,128]{1,0:T(8,128)(2,1)}) custom-call(s32[16,8]{1,0:T(8,128)} %copy.24.lists_ref, s32[16]{0:T(128)} %bitcast.41, bf16[2048,128]{1,0:T(8,128)(2,1)} %fusion.4.both_ref, bf16[2048,64]{1,0:T(8,128)(2,1)} %bitcast.32), custom_call_target="tpu_custom_call" | custom-call | tf_op jit(solution)/shard_map/pallas_call | solution.py:65
  72.3 0.0 copy-start
  72.3 1.7 %pad_maximum_fusion = bf16[2048,192]{1,0:T(8,128)(2,1)S(1)} fusion(bf16[2048,128]{1,0:T(8,128)(2,1)} %get-tuple-element.11, bf16[2048,64]{1,0:T(8,128)(2,1)} %get-tuple-element.10), kind=kLoop, calls=%fused_computation.16 | loop fusion | flops 1572864 | bytes 1572864 | tf_op jit(solution)/shard_map/concatenate | solution.py:162
  74.0 1.3 copy.25
  75.3 3.7 %all-to-all-start.3 = ((bf16[8,256,192]{1,2,0:T(8,128)(2,1)}), bf16[8,256,192]{1,2,0:T(8,128)(2,1)S(1)}, u32[]{:S(2)}, u32[]{:S(2)}) async-start(bf16[8,256,192]{1,2,0:T(8,128)(2,1)} %copy.25), calls=%async_computation.3 | async-start | bytes 1572864 | tf_op jit(solution)/shard_map/all_to_all | solution.py:161
  79.1 0.0 copy-done
  79.1 4.5 %fusion.5 = bf16[2048,128]{1,0:T(8,128)(2,1)S(1)} fusion(bf16[2048,128]{1,0:T(8,128)(2,1)S(1)} %copy-done, s32[2048]{0:T(1024)S(1)} %bitcast.38), kind=kOutput, calls=%fused_computation.6 | convolution fusion | flops 1078198272 | bytes 1056768 | tf_op jit(solution)/shard_map/dot_general | solution.py:178
  83.6 10.0 %all-gather.2.cloned.1.call-done = bf16[2048,1024]{1,0:T(8,128)(2,1)} async-done(((bf16[256,1024]{1,0:T(8,128)(2,1)}), bf16[2048,1024]{1,0:T(8,128)(2,1)}) %all-gather.2.cloned.1.call-update) | async-done | bytes 4194320 | tf_op jit(solution)/shard_map/all_gather | solution.py:146
  93.6 4.3 %fusion.27 = f32[1024,128]{1,0:T(8,128)} fusion(bf16[2048,1024]{1,0:T(8,128)(2,1)} %all-gather.2.cloned.1.call-done, bf16[2048,128]{1,0:T(8,128)(2,1)S(1)} %fusion.5), kind=kOutput, calls=%fused_computation.20 | convolution fusion | flops 536870912 | bytes 5242880 | tf_op jit(solution)/shard_map/od,oc->dc/dot_general | solution.py:182
  97.8 6.1 %all-to-all-done.3 = bf16[8,256,192]{1,2,0:T(8,128)(2,1)S(1)} async-done(((bf16[8,256,192]{1,2,0:T(8,128)(2,1)}), bf16[8,256,192]{1,2,0:T(8,128)(2,1)S(1)}, u32[]{:S(2)}, u32[]{:S(2)}) %all-to-all-start.3) | async-done | bytes 786464 | tf_op jit(solution)/shard_map/all_to_all | solution.py:161
  103.9 3.6 %all-to-all-start.4 = ((f32[4,256,128]{2,1,0:T(8,128)}), f32[4,256,128]{2,1,0:T(8,128)S(1)}, u32[]{:S(2)}, u32[]{:S(2)}) async-start(f32[4,256,128]{2,1,0:T(8,128)} %bitcast.14), calls=%async_computation.4 | async-start | bytes 1048576 | tf_op jit(solution)/shard_map/all_to_all | solution.py:185
  107.6 3.1 %fusion.22 = bf16[1,256,1024]{2,1,0:T(8,128)(2,1)} fusion(bf16[1024,8,128]{2,1,0:T(8,128)(2,1)} %param.8, bf16[8,256,192]{1,2,0:T(8,128)(2,1)S(1)} %all-to-all-done.3), kind=kOutput, calls=%fused_computation.15 | convolution fusion | flops 537133056 | bytes 3145728 | tf_op jit(solution)/shard_map/htc,dhc->td/dot_general | solution.py:172
  110.7 5.2 %all-to-all-done.4 = f32[4,256,128]{2,1,0:T(8,128)S(1)} async-done(((f32[4,256,128]{2,1,0:T(8,128)}), f32[4,256,128]{2,1,0:T(8,128)S(1)}, u32[]{:S(2)}, u32[]{:S(2)}) %all-to-all-start.4) | async-done | bytes 524320 | tf_op jit(solution)/shard_map/all_to_all | solution.py:185
  115.9 0.7 reduce_sum.9
  116.6 3.4 %all-to-all-start.5 = ((f32[8,32,128]{2,1,0:T(8,128)}), f32[8,32,128]{2,1,0:T(8,128)S(1)}, u32[]{:S(2)}, u32[]{:S(2)}) async-start(f32[8,32,128]{2,1,0:T(8,128)} %bitcast.15), calls=%async_computation.5 | async-start | bytes 262144 | tf_op jit(solution)/shard_map/all_to_all | solution.py:193
  120.0 0.7 slice_bitcast_fusion
  120.7 6.0 %all-to-all-done.5 = f32[8,32,128]{2,1,0:T(8,128)S(1)} async-done(((f32[8,32,128]{2,1,0:T(8,128)}), f32[8,32,128]{2,1,0:T(8,128)S(1)}, u32[]{:S(2)}, u32[]{:S(2)}) %all-to-all-start.5) | async-done | bytes 131104 | tf_op jit(solution)/shard_map/all_to_all | solution.py:193
  126.7 0.7 copy.28
Async XLA Ops:
  7.2 35.3 %copy-start.2 = (s32[1,256]{1,0:T(1,128)S(1)}, s32[1,256]{1,0:T(1,128)}, u32[]{:S(2)}) copy-start(s32[1,256]{1,0:T(1,128)} %param.7) | copy-start | bytes 3076
  7.2 39.3 %copy-start.1 = (s32[1,16,8]{1,2,0:T(8,128)S(1)}, s32[1,16,8]{1,2,0:T(8,128)}, u32[]{:S(2)}) copy-start(s32[1,16,8]{1,2,0:T(8,128)} %param.9) | copy-start | bytes 1540
  7.2 16.2 %all-to-all-start.2 = ((bf16[8,256,64]{1,2,0:T(8,128)(2,1)}), bf16[8,256,64]{1,2,0:T(8,128)(2,1)S(1)}, u32[]{:S(2)}, u32[]{:S(2)}) async-start(bf16[8,256,64]{1,2,0:T(8,128)(2,1)} %bitcast.36), calls=%async_computation.2 | async-start | bytes 524288 | tf_op jit(solution)/shard_map/all_to_all | solution.py:127
  23.4 18.8 %all-to-all-start.1 = ((bf16[8,256,128]{1,2,0:T(8,128)(2,1)}), bf16[8,256,128]{1,2,0:T(8,128)(2,1)S(1)}, u32[]{:S(2)}, u32[]{:S(2)}) async-start(bf16[8,256,128]{1,2,0:T(8,128)(2,1)} %fusion.19), calls=%async_computation.1 | async-start | bytes 1048576 | tf_op jit(solution)/shard_map/all_to_all | solution.py:140
  26.9 66.7 %all-gather.2.cloned.1.call-start = ((), (), s32[]{:S(2)}) async-start(), calls=%async_computation.6 | async-start | bytes 4718592 | tf_op jit(solution)/shard_map/all_gather | solution.py:146
  43.1 9.0 %all-to-all-start = ((s32[8,1,256]{2,1,0:T(1,128)}), s32[8,1,256]{2,1,0:T(1,128)S(1)}, u32[]{:S(2)}, u32[]{:S(2)}) async-start(s32[8,1,256]{2,1,0:T(1,128)} %broadcast_in_dim.12), calls=%async_computation | async-start | bytes 16384 | tf_op jit(solution)/shard_map/all_to_all | solution.py:130
  72.3 6.8 %copy-start = (bf16[2048,128]{1,0:T(8,128)(2,1)S(1)}, bf16[2048,128]{1,0:T(8,128)(2,1)}, u32[]{:S(2)}) copy-start(bf16[2048,128]{1,0:T(8,128)(2,1)} %get-tuple-element.11) | copy-start | bytes 1572868
  75.3 28.6 %all-to-all-start.3 = ((bf16[8,256,192]{1,2,0:T(8,128)(2,1)}), bf16[8,256,192]{1,2,0:T(8,128)(2,1)S(1)}, u32[]{:S(2)}, u32[]{:S(2)}) async-start(bf16[8,256,192]{1,2,0:T(8,128)(2,1)} %copy.25), calls=%async_computation.3 | async-start | bytes 1572864 | tf_op jit(solution)/shard_map/all_to_all | solution.py:161
  103.9 12.0 %all-to-all-start.4 = ((f32[4,256,128]{2,1,0:T(8,128)}), f32[4,256,128]{2,1,0:T(8,128)S(1)}, u32[]{:S(2)}, u32[]{:S(2)}) async-start(f32[4,256,128]{2,1,0:T(8,128)} %bitcast.14), calls=%async_computation.4 | async-start | bytes 1048576 | tf_op jit(solution)/shard_map/all_to_all | solution.py:185
  116.6 10.1 %all-to-all-start.5 = ((f32[8,32,128]{2,1,0:T(8,128)}), f32[8,32,128]{2,1,0:T(8,128)S(1)}, u32[]{:S(2)}, u32[]{:S(2)}) async-start(f32[8,32,128]{2,1,0:T(8,128)} %bitcast.15), calls=%async_computation.5 | async-start | bytes 262144 | tf_op jit(solution)/shard_map/all_to_all | solution.py:193
Sparse Core Ops, SparseCore 0:
  42.6 50.9 all-gather.1

commit v17 on v16

--- a/solution.py
+++ b/solution.py
@@ -124,16 +124,19 @@
     targets = seq_position[0]
     group = my_index % groups
     upstream = out_grad[0].reshape(seq_count, portion, depth)
-    got_grad = lax.all_to_all(upstream, "seq", split_axis=0, concat_axis=0, tiled=True)
-    grad_rows = got_grad.reshape(seq_count * portion, depth)
     if groups == 1:
-        places_all = lax.all_to_all(
-            jnp.broadcast_to(targets[None], (seq_count, tokens_here)),
-            "seq",
-            split_axis=0,
-            concat_axis=0,
-            tiled=True,
-        ).reshape(-1)
+        extra = ((2 * tokens_here + depth - 1) // depth + 15) // 16 * 16
+        coded = jnp.concatenate([targets // 256, targets % 256]).astype(jnp.bfloat16)
+        coded = jnp.pad(coded, (0, extra * depth - coded.shape[0])).reshape(extra, depth)
+        sent = jnp.concatenate(
+            [upstream, jnp.broadcast_to(coded[None], (seq_count, extra, depth))], axis=1
+        )
+        got_both = lax.all_to_all(sent, "seq", split_axis=0, concat_axis=0, tiled=True)
+        grad_rows = got_both[:, :portion].reshape(seq_count * portion, depth)
+        codes = got_both[:, portion:].reshape(seq_count, extra * depth).astype(jnp.float32)
+        places_all = (
+            codes[:, :tokens_here] * 256 + codes[:, tokens_here : 2 * tokens_here]
+        ).astype(jnp.int32).reshape(-1)
         proj_mine = jnp.einsum(
             "td,dhc->htc", rows_here, head_weights, preferred_element_type=jnp.float32
         ).astype(jnp.bfloat16)
@@ -150,6 +153,8 @@
             jnp.bfloat16
         )
     else:
+        got_grad = lax.all_to_all(upstream, "seq", split_axis=0, concat_axis=0, tiled=True)
+        grad_rows = got_grad.reshape(seq_count * portion, depth)
         tokens = route_tokens(rows_here, targets, seq_count, my_index)
         proj = jnp.einsum(
             "td,dhc->htc", tokens, head_weights, preferred_element_type=jnp.float32

time: 135 us -> 143 us (1.059)
  waiting for transfers between devices: 52.9 us -> 64.1 us
  starting transfers between devices: 24.1 us -> 20.8 us
  other arithmetic: 2.4 us -> 4.86 us
  matrix products: 19 us -> 17.4 us
    all_gather x1, waiting for transfers between devices: 9.97 us -> 27.7 us  [local(): owned_all = lax.all_gather(later_rows, 'seq', axis=0, tiled=True)]
    all_to_all x1, waiting for transfers between devices: 6.1 us -> 0.01 us  [local(): lax.all_to_all(jnp.concatenate([mixed, grad_both], axis=1).reshape(seq_co...]
    all_to_all x2 -> x1, starting transfers between devices: 9.8 us -> 6.33 us  [local(): lax.all_to_all(sent, 'seq', split_axis=0, concat_axis=0, tiled=True)]
    all_to_all x2 -> x1, waiting for transfers between devices: 11.4 us -> 9.28 us  [local(): lax.all_to_all(sent, 'seq', split_axis=0, concat_axis=0, tiled=True)]
    concatenate x0 -> x2, other arithmetic: none -> 1.76 us  [the longest x1 1.75 us: local(): jnp.concatenate([upstream, jnp.broadcast_to(coded[None], (seq_count, extr...]
    all_to_all x1, waiting for transfers between devices: 5.16 us -> 6.86 us  [local(): lax.all_to_all(partial.reshape(rec_count, width // rec_count, 2 * depth),...]
    dot_general x1, matrix products: 3.15 us -> 1.55 us  [local(): jnp.einsum('htc,dhc->td', grad_proj, head_weights, preferred_element_type...]
  transfers between devices with their start and end apart: 7 -> 6, of which waited for: 7 -> 5; matrix products, arithmetic and copies ran while one was open for 19% -> 16% of each run, Pallas kernels for 12% -> 12%
where the time goes in v17:
time: 143 us; the launch traced here: 144 us
  waiting for transfers between devices  64.1 us (45%)
  starting transfers between devices  20.8 us (15%)
  matrix products  17.4 us (12%)
  Pallas kernels  17.2 us (12%)
  between operations  14.1 us (10%)
  local copies, waits for them, and re-layouts  5.17 us (4%)
  other arithmetic  4.86 us (3%)
    all_gather x1, waiting for transfers between devices, local(): owned_all = lax.all_gather(later_rows, 'seq', axis=0, tiled=True)  27.7 us
    pallas_call x1, Pallas kernels, attend_group(): pl.pallas_call(attention_kernel, out_shape=(jax.ShapeDtypeStruct((total,...  17.2 us
    all_to_all x1, waiting for transfers between devices, local(): lax.all_to_all(proj_mine, 'seq', split_axis=0, concat_axis=0, tiled=True)  14.2 us
    all_to_all x1, waiting for transfers between devices, local(): lax.all_to_all(sent, 'seq', split_axis=0, concat_axis=0, tiled=True)  9.28 us
    all_to_all x1, waiting for transfers between devices, local(): lax.all_to_all(partial.reshape(rec_count, width // rec_count, 2 * depth),...  6.86 us
    all_to_all x1, starting transfers between devices, local(): lax.all_to_all(sent, 'seq', split_axis=0, concat_axis=0, tiled=True)  6.33 us
    all_to_all x1, waiting for transfers between devices, local(): lax.all_to_all(summed.reshape(seq_count, rows_out, 2 * depth), 'seq', spl...  5.99 us
    dot_general x1, matrix products, local(): lax.dot_general(placing, grad_both, (((0,), (0,)), ((), ())), preferred_e...  4.52 us
  transfers between devices with their start and end apart: 6, of which 5 were waited for; matrix products, arithmetic and copies ran while one was open for 16% of the time, Pallas kernels for 12%

profile of v17, /device:TPU:0, one launch (start us, length us, event | category | flops | bytes accessed | tf_op | source)
XLA Modules:
  0.0 143.7 jit_solution(14209246192630532368)
XLA Ops:
  7.2 0.7 fusion.33
  7.9 0.1 broadcast_in_dim.14
  7.9 0.1 copy.41
  8.1 1.7 %pad_maximum_fusion.1 = bf16[8,272,64]{1,2,0:T(8,128)(2,1)} fusion(bf16[8,16,64]{1,2,0:T(8,128)(2,1)S(1)} %broadcast_in_dim.15, bf16[8,256,64]{1,2,0:T(8,128)(2,1)} %bitcast.38), kind=kLoop, calls=%fused_computation.19 | loop fusion | flops 557056 | bytes 557056 | tf_op jit(solution)/shard_map/concatenate | solution.py:131
  9.8 6.3 %all-to-all-start = ((bf16[8,272,64]{1,2,0:T(8,128)(2,1)}), bf16[8,272,64]{1,2,0:T(8,128)(2,1)S(1)}, u32[]{:S(2)}, u32[]{:S(2)}) async-start(bf16[8,272,64]{1,2,0:T(8,128)(2,1)} %pad_maximum_fusion.1), calls=%async_computation | async-start | bytes 786432 | tf_op jit(solution)/shard_map/all_to_all | solution.py:134
  16.2 0.0 copy-start.1
  16.2 3.3 %fusion.19 = bf16[8,256,128]{1,2,0:T(8,128)(2,1)} fusion(bf16[1024,8,128]{2,1,0:T(8,128)(2,1)} %param.8, bf16[1,256,1024]{2,1,0:T(8,128)(2,1)} %param.6), kind=kOutput, calls=%fused_computation.14 | convolution fusion | flops 537133056 | bytes 3145728 | tf_op jit(solution)/shard_map/td,dhc->htc/dot_general | solution.py:140
  19.4 9.3 %all-to-all-done = bf16[8,272,64]{1,2,0:T(8,128)(2,1)S(1)} async-done(((bf16[8,272,64]{1,2,0:T(8,128)(2,1)}), bf16[8,272,64]{1,2,0:T(8,128)(2,1)S(1)}, u32[]{:S(2)}, u32[]{:S(2)}) %all-to-all-start) | async-done | bytes 278560 | tf_op jit(solution)/shard_map/all_to_all | solution.py:134
  28.7 3.5 %all-to-all-start.1 = ((bf16[8,256,128]{1,2,0:T(8,128)(2,1)}), bf16[8,256,128]{1,2,0:T(8,128)(2,1)S(1)}, u32[]{:S(2)}, u32[]{:S(2)}) async-start(bf16[8,256,128]{1,2,0:T(8,128)(2,1)} %fusion.19), calls=%async_computation.1 | async-start | bytes 1048576 | tf_op jit(solution)/shard_map/all_to_all | solution.py:143
  32.2 0.0 all-gather.2.cloned.1.call-start
  32.3 1.0 copy.45
  33.3 14.2 %all-to-all-done.1 = bf16[8,256,128]{1,2,0:T(8,128)(2,1)S(1)} async-done(((bf16[8,256,128]{1,2,0:T(8,128)(2,1)}), bf16[8,256,128]{1,2,0:T(8,128)(2,1)S(1)}, u32[]{:S(2)}, u32[]{:S(2)}) %all-to-all-start.1) | async-done | bytes 524320 | tf_op jit(solution)/shard_map/all_to_all | solution.py:143
  47.5 0.3 copy.44
  47.8 0.0 all-gather.2.cloned.1.call-update
  47.8 0.0 copy-done.1
  47.8 0.7 copy.46.lists_ref
  48.5 0.1 copy.51
  48.6 0.1 reshape.31
  48.7 3.8 %fusion.4.both_ref = bf16[2048,128]{1,0:T(8,128)(2,1)} fusion(bf16[2048,128]{1,0:T(8,128)(2,1)S(1)} %bitcast.36, s32[2048]{0:T(1024)S(1)} %bitcast.39), kind=kOutput, calls=%fused_computation.5 | convolution fusion | flops 1078198272 | bytes 1056768 | tf_op jit(solution)/shard_map/dot_general | solution.py:152
  52.5 17.2 %shard_map.85 = (bf16[2048,64]{1,0:T(8,128)(2,1)}, bf16[2048,128]{1,0:T(8,128)(2,1)}) custom-call(s32[16,8]{1,0:T(8,128)} %copy.46.lists_ref, s32[16]{0:T(128)} %bitcast.43, bf16[2048,128]{1,0:T(8,128)(2,1)} %fusion.4.both_ref, bf16[2048,64]{1,0:T(8,128)(2,1)} %bitcast.34), custom_call_target="tpu_custom_call" | custom-call | tf_op jit(solution)/shard_map/pallas_call | solution.py:65
  69.7 0.0 copy-start
  69.7 1.7 %pad_maximum_fusion = bf16[2048,192]{1,0:T(8,128)(2,1)S(1)} fusion(bf16[2048,128]{1,0:T(8,128)(2,1)} %get-tuple-element.11, bf16[2048,64]{1,0:T(8,128)(2,1)} %get-tuple-element.10), kind=kLoop, calls=%fused_computation.16 | loop fusion | flops 1572864 | bytes 1572864 | tf_op jit(solution)/shard_map/concatenate | solution.py:167
  71.4 1.3 copy.47
  72.7 3.7 %all-to-all-start.2 = ((bf16[8,256,192]{1,2,0:T(8,128)(2,1)}), bf16[8,256,192]{1,2,0:T(8,128)(2,1)S(1)}, u32[]{:S(2)}, u32[]{:S(2)}) async-start(bf16[8,256,192]{1,2,0:T(8,128)(2,1)} %copy.47), calls=%async_computation.2 | async-start | bytes 1572864 | tf_op jit(solution)/shard_map/all_to_all | solution.py:166
  76.5 0.0 copy-done
  76.5 4.5 %fusion.5 = bf16[2048,128]{1,0:T(8,128)(2,1)S(1)} fusion(bf16[2048,128]{1,0:T(8,128)(2,1)S(1)} %copy-done, s32[2048]{0:T(1024)S(1)} %bitcast.40), kind=kOutput, calls=%fused_computation.6 | convolution fusion | flops 1078198272 | bytes 1056768 | tf_op jit(solution)/shard_map/dot_general | solution.py:183
  81.0 0.0 copy-start.2
  81.0 27.7 %all-gather.2.cloned.1.call-done = bf16[2048,1024]{1,0:T(8,128)(2,1)} async-done(((bf16[256,1024]{1,0:T(8,128)(2,1)}), bf16[2048,1024]{1,0:T(8,128)(2,1)}) %all-gather.2.cloned.1.call-update) | async-done | bytes 4194320 | tf_op jit(solution)/shard_map/all_gather | solution.py:149
  108.7 4.3 %fusion.34 = f32[1024,128]{1,0:T(8,128)} fusion(bf16[2048,1024]{1,0:T(8,128)(2,1)} %all-gather.2.cloned.1.call-done, bf16[2048,128]{1,0:T(8,128)(2,1)S(1)} %fusion.5), kind=kOutput, calls=%fused_computation.38 | convolution fusion | flops 536870912 | bytes 5242880 | tf_op jit(solution)/shard_map/od,oc->dc/dot_general | solution.py:187
  113.0 0.0 all-to-all-done.2
  113.0 3.9 %all-to-all-start.3 = ((f32[4,256,128]{2,1,0:T(8,128)}), f32[4,256,128]{2,1,0:T(8,128)S(1)}, u32[]{:S(2)}, u32[]{:S(2)}) async-start(f32[4,256,128]{2,1,0:T(8,128)} %bitcast.13), calls=%async_computation.3 | async-start | bytes 1048576 | tf_op jit(solution)/shard_map/all_to_all | solution.py:190
  116.9 0.0 copy-done.2
  116.9 1.6 %fusion.22 = bf16[1,256,1024]{2,1,0:T(8,128)(2,1)} fusion(bf16[1024,8,128]{2,1,0:T(8,128)(2,1)S(1)} %copy-done.2, bf16[8,256,192]{1,2,0:T(8,128)(2,1)S(1)} %all-to-all-done.2), kind=kOutput, calls=%fused_computation.15 | convolution fusion | flops 537133056 | bytes 3145728 | tf_op jit(solution)/shard_map/htc,dhc->td/dot_general | solution.py:177
  118.5 6.9 %all-to-all-done.3 = f32[4,256,128]{2,1,0:T(8,128)S(1)} async-done(((f32[4,256,128]{2,1,0:T(8,128)}), f32[4,256,128]{2,1,0:T(8,128)S(1)}, u32[]{:S(2)}, u32[]{:S(2)}) %all-to-all-start.3) | async-done | bytes 524320 | tf_op jit(solution)/shard_map/all_to_all | solution.py:190
  125.3 0.7 reduce_sum.9
  126.0 3.4 %all-to-all-start.4 = ((f32[8,32,128]{2,1,0:T(8,128)}), f32[8,32,128]{2,1,0:T(8,128)S(1)}, u32[]{:S(2)}, u32[]{:S(2)}) async-start(f32[8,32,128]{2,1,0:T(8,128)} %bitcast.14), calls=%async_computation.4 | async-start | bytes 262144 | tf_op jit(solution)/shard_map/all_to_all | solution.py:198
  129.4 0.7 slice_bitcast_fusion
  130.1 6.0 %all-to-all-done.4 = f32[8,32,128]{2,1,0:T(8,128)S(1)} async-done(((f32[8,32,128]{2,1,0:T(8,128)}), f32[8,32,128]{2,1,0:T(8,128)S(1)}, u32[]{:S(2)}, u32[]{:S(2)}) %all-to-all-start.4) | async-done | bytes 131104 | tf_op jit(solution)/shard_map/all_to_all | solution.py:198
  136.1 0.7 copy.50
  (6 shorter events, 0.1 us)
Async XLA Ops:
  9.8 18.9 %all-to-all-start = ((bf16[8,272,64]{1,2,0:T(8,128)(2,1)}), bf16[8,272,64]{1,2,0:T(8,128)(2,1)S(1)}, u32[]{:S(2)}, u32[]{:S(2)}) async-start(bf16[8,272,64]{1,2,0:T(8,128)(2,1)} %pad_maximum_fusion.1), calls=%async_computation | async-start | bytes 786432 | tf_op jit(solution)/shard_map/all_to_all | solution.py:134
  16.2 31.6 %copy-start.1 = (s32[1,16,8]{1,2,0:T(8,128)S(1)}, s32[1,16,8]{1,2,0:T(8,128)}, u32[]{:S(2)}) copy-start(s32[1,16,8]{1,2,0:T(8,128)} %param.9) | copy-start | bytes 1540
  28.7 18.8 %all-to-all-start.1 = ((bf16[8,256,128]{1,2,0:T(8,128)(2,1)}), bf16[8,256,128]{1,2,0:T(8,128)(2,1)S(1)}, u32[]{:S(2)}, u32[]{:S(2)}) async-start(bf16[8,256,128]{1,2,0:T(8,128)(2,1)} %fusion.19), calls=%async_computation.1 | async-start | bytes 1048576 | tf_op jit(solution)/shard_map/all_to_all | solution.py:143
  32.2 76.5 %all-gather.2.cloned.1.call-start = ((), (), s32[]{:S(2)}) async-start(), calls=%async_computation.5 | async-start | bytes 4718592 | tf_op jit(solution)/shard_map/all_gather | solution.py:149
  69.7 6.8 %copy-start = (bf16[2048,128]{1,0:T(8,128)(2,1)S(1)}, bf16[2048,128]{1,0:T(8,128)(2,1)}, u32[]{:S(2)}) copy-start(bf16[2048,128]{1,0:T(8,128)(2,1)} %get-tuple-element.11) | copy-start | bytes 1572868
  72.7 40.3 %all-to-all-start.2 = ((bf16[8,256,192]{1,2,0:T(8,128)(2,1)}), bf16[8,256,192]{1,2,0:T(8,128)(2,1)S(1)}, u32[]{:S(2)}, u32[]{:S(2)}) async-start(bf16[8,256,192]{1,2,0:T(8,128)(2,1)} %copy.47), calls=%async_computation.2 | async-start | bytes 1572864 | tf_op jit(solution)/shard_map/all_to_all | solution.py:166
  81.0 35.9 %copy-start.2 = (bf16[1024,8,128]{2,1,0:T(8,128)(2,1)S(1)}, bf16[1024,8,128]{2,1,0:T(8,128)(2,1)}, u32[]{:S(2)}) copy-start(bf16[1024,8,128]{2,1,0:T(8,128)(2,1)} %param.8) | copy-start | bytes 6291460
  113.0 12.3 %all-to-all-start.3 = ((f32[4,256,128]{2,1,0:T(8,128)}), f32[4,256,128]{2,1,0:T(8,128)S(1)}, u32[]{:S(2)}, u32[]{:S(2)}) async-start(f32[4,256,128]{2,1,0:T(8,128)} %bitcast.13), calls=%async_computation.3 | async-start | bytes 1048576 | tf_op jit(solution)/shard_map/all_to_all | solution.py:190
  126.0 10.1 %all-to-all-start.4 = ((f32[8,32,128]{2,1,0:T(8,128)}), f32[8,32,128]{2,1,0:T(8,128)S(1)}, u32[]{:S(2)}, u32[]{:S(2)}) async-start(f32[8,32,128]{2,1,0:T(8,128)} %bitcast.14), calls=%async_computation.4 | async-start | bytes 262144 | tf_op jit(solution)/shard_map/all_to_all | solution.py:198
Sparse Core Ops, SparseCore 0:
  47.9 60.7 all-gather.1

commit v18 on v16

--- a/solution.py
+++ b/solution.py
@@ -183,21 +183,14 @@
             "od,oc->dc", owned_all, head_grad, preferred_element_type=jnp.float32
         )
         pieces = lax.all_to_all(
-            partial.reshape(rec_count, width // rec_count, 2 * depth),
-            "rec",
+            partial.reshape(rec_count * seq_count, rows_out, 2 * depth),
+            ("rec", "seq"),
             split_axis=0,
             concat_axis=0,
             tiled=True,
         )
-        summed = jnp.sum(pieces, axis=0)
-        spread = lax.all_to_all(
-            summed.reshape(seq_count, rows_out, 2 * depth),
-            "seq",
-            split_axis=0,
-            concat_axis=0,
-            tiled=True,
-        )
-        weight_grad = jnp.transpose(spread, (1, 0, 2))
+        summed = jnp.sum(pieces.reshape(rec_count, heads, rows_out, 2 * depth), axis=0)
+        weight_grad = jnp.transpose(summed, (1, 0, 2))
     else:
         weight_grad = lax.psum_scatter(
             jnp.einsum("td,htc->dhc", tokens, grad_proj, preferred_element_type=jnp.float32),

time: 135 us -> 132 us (0.978)
  starting transfers between devices: 24.1 us -> 20.4 us
  Pallas kernels: 16.5 us -> 19 us
    all_gather x1, waiting for transfers between devices: 9.97 us -> 4.4 us  [local(): owned_all = lax.all_gather(later_rows, 'seq', axis=0, tiled=True)]
    all_to_all x2 -> x1, starting transfers between devices: 7.02 us -> 3.32 us  [local(): lax.all_to_all(partial.reshape(rec_count * seq_count, rows_out, 2 * depth...]
    all_to_all x1, waiting for transfers between devices: 6.1 us -> 9.06 us  [local(): lax.all_to_all(jnp.concatenate([mixed, grad_both], axis=1).reshape(seq_co...]
    pallas_call x1, Pallas kernels: 16.5 us -> 19 us  [attend_group(): pl.pallas_call(attention_kernel, out_shape=(jax.ShapeDtypeStruct((total,...]
    all_to_all x2 -> x1, waiting for transfers between devices: 11.2 us -> 12.5 us  [local(): lax.all_to_all(partial.reshape(rec_count * seq_count, rows_out, 2 * depth...]
  transfers between devices with their start and end apart: 7 -> 6, of which waited for: 7 -> 6; matrix products, arithmetic and copies ran while one was open for 19% -> 19% of each run, Pallas kernels for 12% -> 15%
where the time goes in v18:
time: 132 us; the launch traced here: 131 us
  waiting for transfers between devices  51.6 us (39%)
  starting transfers between devices  20.4 us (15%)
  matrix products  19 us (14%)
  Pallas kernels  19 us (14%)
  between operations  14.1 us (11%)
  local copies, waits for them, and re-layouts  5.33 us (4%)
  other arithmetic  1.75 us (1%)
    pallas_call x1, Pallas kernels, attend_group(): pl.pallas_call(attention_kernel, out_shape=(jax.ShapeDtypeStruct((total,...  19 us
    all_to_all x1, waiting for transfers between devices, local(): lax.all_to_all(proj_mine, 'seq', split_axis=0, concat_axis=0, tiled=True)  14.2 us
    all_to_all x1, waiting for transfers between devices, local(): lax.all_to_all(partial.reshape(rec_count * seq_count, rows_out, 2 * depth...  12.5 us
    all_to_all x1, waiting for transfers between devices, local(): lax.all_to_all(jnp.concatenate([mixed, grad_both], axis=1).reshape(seq_co...  9.06 us
    all_to_all x1, waiting for transfers between devices, local(): lax.all_to_all(upstream, 'seq', split_axis=0, concat_axis=0, tiled=True)  6.49 us
    all_to_all x1, starting transfers between devices, local(): lax.all_to_all(upstream, 'seq', split_axis=0, concat_axis=0, tiled=True)  6.47 us
    all_to_all x1, waiting for transfers between devices, local(): lax.all_to_all(jnp.broadcast_to(targets[None], (seq_count, tokens_here)),...  4.95 us
    dot_general x1, matrix products, local(): lax.dot_general(placing, grad_both, (((0,), (0,)), ((), ())), preferred_e...  4.53 us
  transfers between devices with their start and end apart: 6, of which 6 were waited for; matrix products, arithmetic and copies ran while one was open for 19% of the time, Pallas kernels for 15%

profile of v18, /device:TPU:0, one launch (start us, length us, event | category | flops | bytes accessed | tf_op | source)
XLA Modules:
  0.0 131.2 jit_solution(9918573429765299188)
XLA Ops:
  7.2 0.0 copy-start.2
  7.2 0.0 copy-start.1
  7.2 6.5 %all-to-all-start.2 = ((bf16[8,256,64]{1,2,0:T(8,128)(2,1)}), bf16[8,256,64]{1,2,0:T(8,128)(2,1)S(1)}, u32[]{:S(2)}, u32[]{:S(2)}) async-start(bf16[8,256,64]{1,2,0:T(8,128)(2,1)} %bitcast.37), calls=%async_computation.2 | async-start | bytes 524288 | tf_op jit(solution)/shard_map/all_to_all | solution.py:127
  13.7 3.2 %fusion.19 = bf16[8,256,128]{1,2,0:T(8,128)(2,1)} fusion(bf16[1024,8,128]{2,1,0:T(8,128)(2,1)} %param.8, bf16[1,256,1024]{2,1,0:T(8,128)(2,1)} %param.6), kind=kOutput, calls=%fused_computation.14 | convolution fusion | flops 537133056 | bytes 3145728 | tf_op jit(solution)/shard_map/td,dhc->htc/dot_general | solution.py:137
  16.9 6.5 %all-to-all-done.2 = bf16[8,256,64]{1,2,0:T(8,128)(2,1)S(1)} async-done(((bf16[8,256,64]{1,2,0:T(8,128)(2,1)}), bf16[8,256,64]{1,2,0:T(8,128)(2,1)S(1)}, u32[]{:S(2)}, u32[]{:S(2)}) %all-to-all-start.2) | async-done | bytes 262176 | tf_op jit(solution)/shard_map/all_to_all | solution.py:127
  23.4 3.5 %all-to-all-start.1 = ((bf16[8,256,128]{1,2,0:T(8,128)(2,1)}), bf16[8,256,128]{1,2,0:T(8,128)(2,1)S(1)}, u32[]{:S(2)}, u32[]{:S(2)}) async-start(bf16[8,256,128]{1,2,0:T(8,128)(2,1)} %fusion.19), calls=%async_computation.1 | async-start | bytes 1048576 | tf_op jit(solution)/shard_map/all_to_all | solution.py:140
  26.9 0.0 all-gather.2.cloned.1.call-start
  26.9 1.0 copy.22
  28.0 14.2 %all-to-all-done.1 = bf16[8,256,128]{1,2,0:T(8,128)(2,1)S(1)} async-done(((bf16[8,256,128]{1,2,0:T(8,128)(2,1)}), bf16[8,256,128]{1,2,0:T(8,128)(2,1)S(1)}, u32[]{:S(2)}, u32[]{:S(2)}) %all-to-all-start.1) | async-done | bytes 524320 | tf_op jit(solution)/shard_map/all_to_all | solution.py:140
  42.2 0.3 copy.21
  42.5 0.0 all-gather.2.cloned.1.call-update
  42.5 0.0 copy-done.2
  42.5 0.6 broadcast_in_dim.12
  43.1 3.3 %all-to-all-start = ((s32[8,1,256]{2,1,0:T(1,128)}), s32[8,1,256]{2,1,0:T(1,128)S(1)}, u32[]{:S(2)}, u32[]{:S(2)}) async-start(s32[8,1,256]{2,1,0:T(1,128)} %broadcast_in_dim.12), calls=%async_computation | async-start | bytes 16384 | tf_op jit(solution)/shard_map/all_to_all | solution.py:130
  46.4 0.0 copy-done.1
  46.5 0.7 copy.23.lists_ref
  47.1 4.9 %all-to-all-done = s32[8,1,256]{2,1,0:T(1,128)S(1)} async-done(((s32[8,1,256]{2,1,0:T(1,128)}), s32[8,1,256]{2,1,0:T(1,128)S(1)}, u32[]{:S(2)}, u32[]{:S(2)}) %all-to-all-start) | async-done | bytes 8224 | tf_op jit(solution)/shard_map/all_to_all | solution.py:130
  52.1 3.8 %fusion.4.both_ref = bf16[2048,128]{1,0:T(8,128)(2,1)} fusion(bf16[2048,128]{1,0:T(8,128)(2,1)S(1)} %bitcast.35, s32[2048]{0:T(1024)S(1)} %bitcast.38), kind=kOutput, calls=%fused_computation.5 | convolution fusion | flops 1078198272 | bytes 1056768 | tf_op jit(solution)/shard_map/dot_general | solution.py:149
  55.9 19.0 %shard_map.88 = (bf16[2048,64]{1,0:T(8,128)(2,1)}, bf16[2048,128]{1,0:T(8,128)(2,1)}) custom-call(s32[16,8]{1,0:T(8,128)} %copy.23.lists_ref, s32[16]{0:T(128)} %bitcast.42, bf16[2048,128]{1,0:T(8,128)(2,1)} %fusion.4.both_ref, bf16[2048,64]{1,0:T(8,128)(2,1)} %bitcast.32), custom_call_target="tpu_custom_call" | custom-call | tf_op jit(solution)/shard_map/pallas_call | solution.py:65
  74.9 0.0 copy-start
  74.9 1.7 %pad_maximum_fusion = bf16[2048,192]{1,0:T(8,128)(2,1)S(1)} fusion(bf16[2048,128]{1,0:T(8,128)(2,1)} %get-tuple-element.11, bf16[2048,64]{1,0:T(8,128)(2,1)} %get-tuple-element.10), kind=kLoop, calls=%fused_computation.16 | loop fusion | flops 1572864 | bytes 1572864 | tf_op jit(solution)/shard_map/concatenate | solution.py:162
  76.6 1.3 copy.24
  77.9 3.7 %all-to-all-start.3 = ((bf16[8,256,192]{1,2,0:T(8,128)(2,1)}), bf16[8,256,192]{1,2,0:T(8,128)(2,1)S(1)}, u32[]{:S(2)}, u32[]{:S(2)}) async-start(bf16[8,256,192]{1,2,0:T(8,128)(2,1)} %copy.24), calls=%async_computation.3 | async-start | bytes 1572864 | tf_op jit(solution)/shard_map/all_to_all | solution.py:161
  81.6 0.0 copy-done
  81.7 4.5 %fusion.5 = bf16[2048,128]{1,0:T(8,128)(2,1)S(1)} fusion(bf16[2048,128]{1,0:T(8,128)(2,1)S(1)} %copy-done, s32[2048]{0:T(1024)S(1)} %bitcast.39), kind=kOutput, calls=%fused_computation.6 | convolution fusion | flops 1078198272 | bytes 1056768 | tf_op jit(solution)/shard_map/dot_general | solution.py:178
  86.2 4.4 %all-gather.2.cloned.1.call-done = bf16[2048,1024]{1,0:T(8,128)(2,1)} async-done(((bf16[256,1024]{1,0:T(8,128)(2,1)}), bf16[2048,1024]{1,0:T(8,128)(2,1)}) %all-gather.2.cloned.1.call-update) | async-done | bytes 4194320 | tf_op jit(solution)/shard_map/all_gather | solution.py:146
  90.6 4.3 %fusion.27 = f32[1024,128]{1,0:T(8,128)} fusion(bf16[2048,1024]{1,0:T(8,128)(2,1)} %all-gather.2.cloned.1.call-done, bf16[2048,128]{1,0:T(8,128)(2,1)S(1)} %fusion.5), kind=kOutput, calls=%fused_computation.20 | convolution fusion | flops 536870912 | bytes 5242880 | tf_op jit(solution)/shard_map/od,oc->dc/dot_general | solution.py:182
  94.9 9.1 %all-to-all-done.3 = bf16[8,256,192]{1,2,0:T(8,128)(2,1)S(1)} async-done(((bf16[8,256,192]{1,2,0:T(8,128)(2,1)}), bf16[8,256,192]{1,2,0:T(8,128)(2,1)S(1)}, u32[]{:S(2)}, u32[]{:S(2)}) %all-to-all-start.3) | async-done | bytes 786464 | tf_op jit(solution)/shard_map/all_to_all | solution.py:161
  103.9 3.3 %all-to-all-start.4 = ((f32[32,32,128]{2,1,0:T(8,128)}), f32[32,32,128]{2,1,0:T(8,128)S(1)}, u32[]{:S(2)}, u32[]{:S(2)}) async-start(f32[32,32,128]{2,1,0:T(8,128)} %bitcast.14), calls=%async_computation.4 | async-start | bytes 1048576 | tf_op jit(solution)/shard_map/all_to_all | solution.py:185
  107.3 0.7 slice_bitcast_fusion
  108.0 3.1 %fusion.22 = bf16[1,256,1024]{2,1,0:T(8,128)(2,1)} fusion(bf16[1024,8,128]{2,1,0:T(8,128)(2,1)} %param.8, bf16[8,256,192]{1,2,0:T(8,128)(2,1)S(1)} %all-to-all-done.3), kind=kOutput, calls=%fused_computation.15 | convolution fusion | flops 537133056 | bytes 3145728 | tf_op jit(solution)/shard_map/htc,dhc->td/dot_general | solution.py:172
  111.1 12.5 %all-to-all-done.4 = f32[32,32,128]{2,1,0:T(8,128)S(1)} async-done(((f32[32,32,128]{2,1,0:T(8,128)}), f32[32,32,128]{2,1,0:T(8,128)S(1)}, u32[]{:S(2)}, u32[]{:S(2)}) %all-to-all-start.4) | async-done | bytes 524320 | tf_op jit(solution)/shard_map/all_to_all | solution.py:185
  123.7 0.7 copy.27
  (1 shorter events, 0.0 us)
Async XLA Ops:
  7.2 35.3 %copy-start.2 = (s32[1,256]{1,0:T(1,128)S(1)}, s32[1,256]{1,0:T(1,128)}, u32[]{:S(2)}) copy-start(s32[1,256]{1,0:T(1,128)} %param.7) | copy-start | bytes 3076
  7.2 39.3 %copy-start.1 = (s32[1,16,8]{1,2,0:T(8,128)S(1)}, s32[1,16,8]{1,2,0:T(8,128)}, u32[]{:S(2)}) copy-start(s32[1,16,8]{1,2,0:T(8,128)} %param.9) | copy-start | bytes 1540
  7.2 16.2 %all-to-all-start.2 = ((bf16[8,256,64]{1,2,0:T(8,128)(2,1)}), bf16[8,256,64]{1,2,0:T(8,128)(2,1)S(1)}, u32[]{:S(2)}, u32[]{:S(2)}) async-start(bf16[8,256,64]{1,2,0:T(8,128)(2,1)} %bitcast.37), calls=%async_computation.2 | async-start | bytes 524288 | tf_op jit(solution)/shard_map/all_to_all | solution.py:127
  23.4 18.8 %all-to-all-start.1 = ((bf16[8,256,128]{1,2,0:T(8,128)(2,1)}), bf16[8,256,128]{1,2,0:T(8,128)(2,1)S(1)}, u32[]{:S(2)}, u32[]{:S(2)}) async-start(bf16[8,256,128]{1,2,0:T(8,128)(2,1)} %fusion.19), calls=%async_computation.1 | async-start | bytes 1048576 | tf_op jit(solution)/shard_map/all_to_all | solution.py:140
  26.9 63.7 %all-gather.2.cloned.1.call-start = ((), (), s32[]{:S(2)}) async-start(), calls=%async_computation.5 | async-start | bytes 4718592 | tf_op jit(solution)/shard_map/all_gather | solution.py:146
  43.1 9.0 %all-to-all-start = ((s32[8,1,256]{2,1,0:T(1,128)}), s32[8,1,256]{2,1,0:T(1,128)S(1)}, u32[]{:S(2)}, u32[]{:S(2)}) async-start(s32[8,1,256]{2,1,0:T(1,128)} %broadcast_in_dim.12), calls=%async_computation | async-start | bytes 16384 | tf_op jit(solution)/shard_map/all_to_all | solution.py:130
  74.9 6.8 %copy-start = (bf16[2048,128]{1,0:T(8,128)(2,1)S(1)}, bf16[2048,128]{1,0:T(8,128)(2,1)}, u32[]{:S(2)}) copy-start(bf16[2048,128]{1,0:T(8,128)(2,1)} %get-tuple-element.11) | copy-start | bytes 1572868
  77.9 26.0 %all-to-all-start.3 = ((bf16[8,256,192]{1,2,0:T(8,128)(2,1)}), bf16[8,256,192]{1,2,0:T(8,128)(2,1)S(1)}, u32[]{:S(2)}, u32[]{:S(2)}) async-start(bf16[8,256,192]{1,2,0:T(8,128)(2,1)} %copy.24), calls=%async_computation.3 | async-start | bytes 1572864 | tf_op jit(solution)/shard_map/all_to_all | solution.py:161
  103.9 19.7 %all-to-all-start.4 = ((f32[32,32,128]{2,1,0:T(8,128)}), f32[32,32,128]{2,1,0:T(8,128)S(1)}, u32[]{:S(2)}, u32[]{:S(2)}) async-start(f32[32,32,128]{2,1,0:T(8,128)} %bitcast.14), calls=%async_computation.4 | async-start | bytes 1048576 | tf_op jit(solution)/shard_map/all_to_all | solution.py:185
Sparse Core Ops, SparseCore 0:
  42.6 47.9 all-gather.1

commit v19 on v18

--- a/solution.py
+++ b/solution.py
@@ -107,6 +107,32 @@
         jnp.zeros((tokens_here, width), rows_here.dtype)
         .at[local_ids]
         .set(arrived.reshape(-1, width), mode="drop")
+    )
+
+
+def gather_pairs(rows, seq_count, my_index):
+    if seq_count % 2:
+        return lax.all_gather(rows, "seq", axis=0, tiled=True)
+    chips = seq_count // 2
+    core = my_index % 2
+    chip = my_index // 2
+    half = rows.shape[1] // 2
+    swap = [(i, i ^ 1) for i in range(seq_count)]
+    sibling = lax.ppermute(rows, "seq", swap)
+    pair = jnp.where(core == 0, jnp.stack([rows, sibling]), jnp.stack([sibling, rows]))
+    mine = lax.dynamic_slice_in_dim(pair, core * half, half, axis=2)
+    held = [mine]
+    for shift in range(1, chips):
+        ring = [(i, (i + 2 * shift) % seq_count) for i in range(seq_count)]
+        held.append(lax.ppermute(mine, "seq", ring))
+    held = jnp.stack(held)
+    order = (chip - jnp.arange(chips)) % chips
+    cols = jnp.take(held, order, axis=0).reshape(-1, half)
+    other = lax.ppermute(cols, "seq", swap)
+    return jnp.where(
+        core == 0,
+        jnp.concatenate([cols, other], axis=1),
+        jnp.concatenate([other, cols], axis=1),
     )
 
 
@@ -143,7 +169,7 @@
         later_rows, proj_owned, grad_rows = lax.optimization_barrier(
             (rows_here, proj_owned, grad_rows)
         )
-        owned_all = lax.all_gather(later_rows, "seq", axis=0, tiled=True)
+        owned_all = gather_pairs(later_rows, seq_count, my_index)
         slots = jnp.arange(places_all.shape[0], dtype=places_all.dtype)
         placing = (slots[:, None] == places_all[None, :]).astype(jnp.bfloat16)
         gathered = jnp.dot(placing, proj_owned, preferred_element_type=jnp.float32).astype(

time: 132 us -> 170 us (1.29)
  waiting for transfers between devices: 51.6 us -> 84.9 us
  between operations: 14.1 us -> 0.78 us
  starting transfers between devices: 20.4 us -> 32.8 us
  other arithmetic: 1.75 us -> 5.23 us
  local copies, waits for them, and re-layouts: 5.33 us -> 8.23 us
  Pallas kernels: 19 us -> 16.3 us
    ppermute x0 -> x5, waiting for transfers between devices: none -> 36 us  [the longest x3 34.2 us: gather_pairs(): held.append(lax.ppermute(mine, 'seq', ring))]
    all_to_all x1, starting transfers between devices: 3.33 us -> 11.7 us  [local(): lax.all_to_all(jnp.broadcast_to(targets[None], (seq_count, tokens_here)),...]
    all_gather x1 -> x0, waiting for transfers between devices: 4.4 us -> none  [local(): owned_all = lax.all_gather(later_rows, 'seq', axis=0, tiled=True)]
    ppermute x0 -> x5, starting transfers between devices: none -> 4.01 us  [the longest x3 3.87 us: gather_pairs(): held.append(lax.ppermute(mine, 'seq', ring))]
    pallas_call x1, Pallas kernels: 19 us -> 16.3 us  [attend_group(): pl.pallas_call(attention_kernel, out_shape=(jax.ShapeDtypeStruct((total,...]
    gather x0 -> x1, local copies, waits for them, and re-layouts: none -> 2.02 us  [gather_pairs(): cols = jnp.take(held, order, axis=0).reshape(-1, half)]
    select_n x0 -> x3, other arithmetic: none -> 1.92 us  [the longest x2 1.81 us: gather_pairs(): cols = jnp.take(held, order, axis=0).reshape(-1, half)]
  transfers between devices with their start and end apart: 6 -> 10, of which waited for: 6 -> 8; matrix products, arithmetic and copies ran while one was open for 19% -> 16% of each run, Pallas kernels for 15% -> 10%
where the time goes in v19:
time: 170 us; the launch traced here: 168 us
  waiting for transfers between devices  84.9 us (50%)
  starting transfers between devices  32.8 us (19%)
  matrix products  20.1 us (12%)
  Pallas kernels  16.3 us (10%)
  local copies, waits for them, and re-layouts  8.23 us (5%)
  other arithmetic  5.23 us (3%)
    ppermute x3, waiting for transfers between devices, gather_pairs(): held.append(lax.ppermute(mine, 'seq', ring))  34.2 us
    pallas_call x1, Pallas kernels, attend_group(): pl.pallas_call(attention_kernel, out_shape=(jax.ShapeDtypeStruct((total,...  16.3 us
    all_to_all x1, waiting for transfers between devices, local(): lax.all_to_all(proj_mine, 'seq', split_axis=0, concat_axis=0, tiled=True)  14.3 us
    all_to_all x1, waiting for transfers between devices, local(): lax.all_to_all(partial.reshape(rec_count * seq_count, rows_out, 2 * depth...  12.5 us
    all_to_all x1, starting transfers between devices, local(): lax.all_to_all(jnp.broadcast_to(targets[None], (seq_count, tokens_here)),...  11.7 us
    all_to_all x1, waiting for transfers between devices, local(): lax.all_to_all(jnp.concatenate([mixed, grad_both], axis=1).reshape(seq_co...  10.7 us
    all_to_all x1, waiting for transfers between devices, local(): lax.all_to_all(upstream, 'seq', split_axis=0, concat_axis=0, tiled=True)  6.49 us
    all_to_all x1, starting transfers between devices, local(): lax.all_to_all(upstream, 'seq', split_axis=0, concat_axis=0, tiled=True)  6.34 us
  transfers between devices with their start and end apart: 10, of which 8 were waited for; matrix products, arithmetic and copies ran while one was open for 16% of the time, Pallas kernels for 10%

profile of v19, /device:TPU:0, one launch (start us, length us, event | category | flops | bytes accessed | tf_op | source)
XLA Modules:
  0.0 168.4 jit_solution(8865535471414490382)
XLA Ops:
  0.6 6.3 %all-to-all-start.2 = ((bf16[8,256,64]{1,2,0:T(8,128)(2,1)}), bf16[8,256,64]{1,2,0:T(8,128)(2,1)S(1)}, u32[]{:S(2)}, u32[]{:S(2)}) async-start(bf16[8,256,64]{1,2,0:T(8,128)(2,1)} %bitcast.51), calls=%async_computation.2 | async-start | bytes 524288 | tf_op jit(solution)/shard_map/all_to_all | solution.py:153
  7.0 3.3 %fusion.26 = bf16[8,256,128]{1,2,0:T(8,128)(2,1)} fusion(bf16[1024,8,128]{2,1,0:T(8,128)(2,1)} %param.8, bf16[1,256,1024]{2,1,0:T(8,128)(2,1)} %param.6), kind=kOutput, calls=%fused_computation.25 | convolution fusion | flops 537133056 | bytes 3145728 | tf_op jit(solution)/shard_map/td,dhc->htc/dot_general | solution.py:163
  10.2 0.0 copy-start
  10.2 6.5 %all-to-all-done.2 = bf16[8,256,64]{1,2,0:T(8,128)(2,1)S(1)} async-done(((bf16[8,256,64]{1,2,0:T(8,128)(2,1)}), bf16[8,256,64]{1,2,0:T(8,128)(2,1)S(1)}, u32[]{:S(2)}, u32[]{:S(2)}) %all-to-all-start.2) | async-done | bytes 262176 | tf_op jit(solution)/shard_map/all_to_all | solution.py:153
  16.7 3.5 %all-to-all-start.1 = ((bf16[8,256,128]{1,2,0:T(8,128)(2,1)}), bf16[8,256,128]{1,2,0:T(8,128)(2,1)S(1)}, u32[]{:S(2)}, u32[]{:S(2)}) async-start(bf16[8,256,128]{1,2,0:T(8,128)(2,1)} %fusion.26), calls=%async_computation.1 | async-start | bytes 1048576 | tf_op jit(solution)/shard_map/all_to_all | solution.py:166
  20.2 1.0 copy.22
  21.2 14.3 %all-to-all-done.1 = bf16[8,256,128]{1,2,0:T(8,128)(2,1)S(1)} async-done(((bf16[8,256,128]{1,2,0:T(8,128)(2,1)}), bf16[8,256,128]{1,2,0:T(8,128)(2,1)S(1)}, u32[]{:S(2)}, u32[]{:S(2)}) %all-to-all-start.1) | async-done | bytes 524320 | tf_op jit(solution)/shard_map/all_to_all | solution.py:166
  35.5 0.3 copy.21
  35.8 0.0 copy-done
  35.8 0.1 collective-permute-start
  35.9 1.9 %collective-permute-done = bf16[256,1024]{1,0:T(8,128)(2,1)S(1)} collective-permute-done((bf16[256,1024]{1,0:T(8,128)(2,1)S(1)}, bf16[256,1024]{1,0:T(8,128)(2,1)S(1)}, u32[]{:S(2)}, u32[]{:S(2)}) %collective-permute-start) | collective-permute-done | bytes 524320 | tf_op jit(solution)/shard_map/ppermute | solution.py:121
  37.8 0.1 fusion.33
  37.9 0.1 collective-permute-start.1
  37.9 1.8 %collective-permute-start.2 = (bf16[2,256,512]{2,1,0:T(8,128)(2,1)S(1)}, bf16[2,256,512]{2,1,0:T(8,128)(2,1)S(1)}, u32[]{:S(2)}, u32[]{:S(2)}) collective-permute-start(bf16[2,256,512]{2,1,0:T(8,128)(2,1)S(1)} %fusion.33), channel_id=1, source_target_pairs={{0,4},{1,5},{2,6},{3,7},{4,0},{5,1},{6,2},{7,3},{8,12},{9,13},{10,... | collective-permute-start | bytes 1572872 | tf_op jit(solution)/shard_map/ppermute | solution.py:127
  39.7 2.0 %collective-permute-start.3 = (bf16[2,256,512]{2,1,0:T(8,128)(2,1)S(1)}, bf16[2,256,512]{2,1,0:T(8,128)(2,1)}, u32[]{:S(2)}, u32[]{:S(2)}) collective-permute-start(bf16[2,256,512]{2,1,0:T(8,128)(2,1)S(1)} %fusion.33), channel_id=1, source_target_pairs={{0,6},{1,7},{2,0},{3,1},{4,2},{5,3},{6,4},{7,5},{8,14},{9,15},{10,... | collective-permute-start | bytes 1572872 | tf_op jit(solution)/shard_map/ppermute | solution.py:127
  41.8 0.1 broadcast_in_dim.29
  41.9 0.1 fusion.44
  42.0 12.6 %collective-permute-done.1 = bf16[2,256,512]{2,1,0:T(8,128)(2,1)S(1)} collective-permute-done((bf16[2,256,512]{2,1,0:T(8,128)(2,1)S(1)}, bf16[2,256,512]{2,1,0:T(8,128)(2,1)S(1)}, u32[]{:S(2)}, u32[]{:S(2)}) %collective-permute-start.1) | collective-permute-done | bytes 524320 | tf_op jit(solution)/shard_map/ppermute | solution.py:127
  54.6 21.5 %collective-permute-done.2 = bf16[2,256,512]{2,1,0:T(8,128)(2,1)S(1)} collective-permute-done((bf16[2,256,512]{2,1,0:T(8,128)(2,1)S(1)}, bf16[2,256,512]{2,1,0:T(8,128)(2,1)S(1)}, u32[]{:S(2)}, u32[]{:S(2)}) %collective-permute-start.2) | collective-permute-done | bytes 524320 | tf_op jit(solution)/shard_map/ppermute | solution.py:127
  76.2 0.0 copy-start.1
  76.2 0.0 collective-permute-done.3
  76.2 0.8 copy-done.1
  77.0 1.5 pad_maximum_fusion
  78.4 2.0 %gather_fusion = bf16[4,2,256,512]{3,2,1,0:T(8,128)(2,1)} fusion(bf16[4,2,256,512]{3,2,1,0:T(8,128)(2,1)S(1)} %pad_maximum_fusion, s32[1024]{0:T(1024)S(1)} %pad_clamp_fusion), kind=kCustom, calls=%fused_computation | custom fusion | bytes 4194320 | tf_op jit(solution)/shard_map/jit(_take)/gather | solution.py:130
  80.5 0.0 copy-start.3
  80.5 0.0 copy-start.2
  80.5 1.8 %bitcast_select_fusion = bf16[2048,512]{1,0:T(8,128)(2,1)S(1)} fusion(bf16[4,2,256,512]{3,2,1,0:T(8,128)(2,1)} %gather_fusion, pred[2048]{0:T(1024)(128)(4,1)S(1)} %broadcast_in_dim.30), kind=kLoop, calls=%fused_computation.17 | loop fusion | flops 1048576 | bytes 4196352 | tf_op jit(solution)/shard_map/jit(_take)/select_n | solution.py:130
  82.3 0.1 collective-permute-start.4
  82.3 0.0 copy-done.3
  82.4 0.6 broadcast_in_dim.26
  83.0 11.7 %all-to-all-start = ((s32[8,1,256]{2,1,0:T(1,128)}), s32[8,1,256]{2,1,0:T(1,128)S(1)}, u32[]{:S(2)}, u32[]{:S(2)}) async-start(s32[8,1,256]{2,1,0:T(1,128)} %broadcast_in_dim.26), calls=%async_computation | async-start | bytes 16384 | tf_op jit(solution)/shard_map/all_to_all | solution.py:156
  94.7 0.0 copy-done.2
  94.7 0.7 copy.23.lists_ref
  95.3 4.9 %all-to-all-done = s32[8,1,256]{2,1,0:T(1,128)S(1)} async-done(((s32[8,1,256]{2,1,0:T(1,128)}), s32[8,1,256]{2,1,0:T(1,128)S(1)}, u32[]{:S(2)}, u32[]{:S(2)}) %all-to-all-start) | async-done | bytes 8224 | tf_op jit(solution)/shard_map/all_to_all | solution.py:156
  100.3 3.8 %fusion.11.both_ref = bf16[2048,128]{1,0:T(8,128)(2,1)} fusion(bf16[2048,128]{1,0:T(8,128)(2,1)S(1)} %bitcast.47, s32[2048]{0:T(1024)S(1)} %bitcast.52), kind=kOutput, calls=%fused_computation.14 | convolution fusion | flops 1078198272 | bytes 1056768 | tf_op jit(solution)/shard_map/dot_general | solution.py:175
  104.0 16.3 %shard_map.88 = (bf16[2048,64]{1,0:T(8,128)(2,1)}, bf16[2048,128]{1,0:T(8,128)(2,1)}) custom-call(s32[16,8]{1,0:T(8,128)} %copy.23.lists_ref, s32[16]{0:T(128)} %bitcast.56, bf16[2048,128]{1,0:T(8,128)(2,1)} %fusion.11.both_ref, bf16[2048,64]{1,0:T(8,128)(2,1)} %bitcast.42), custom_call_target="tpu_custom_call" | custom-call | tf_op jit(solution)/shard_map/pallas_call | solution.py:65
  120.3 1.7 pad_maximum_fusion.1
  122.0 1.3 copy.24
  123.3 3.8 %all-to-all-start.3 = ((bf16[8,256,192]{1,2,0:T(8,128)(2,1)}), bf16[8,256,192]{1,2,0:T(8,128)(2,1)S(1)}, u32[]{:S(2)}, u32[]{:S(2)}) async-start(bf16[8,256,192]{1,2,0:T(8,128)(2,1)} %copy.24), calls=%async_computation.3 | async-start | bytes 1572864 | tf_op jit(solution)/shard_map/all_to_all | solution.py:187
  127.1 5.6 %fusion.12 = bf16[2048,128]{1,0:T(8,128)(2,1)S(1)} fusion(bf16[2048,128]{1,0:T(8,128)(2,1)} %get-tuple-element.11, s32[2048]{0:T(1024)S(1)} %bitcast.53), kind=kOutput, calls=%fused_computation.15 | convolution fusion | flops 1078198272 | bytes 1056768 | tf_op jit(solution)/shard_map/dot_general | solution.py:204
  132.6 0.0 collective-permute-done.4
  132.6 4.4 %fusion.4 = f32[1024,128]{1,0:T(8,128)} fusion(bf16[2048,128]{1,0:T(8,128)(2,1)S(1)} %fusion.12, bf16[2048,512]{1,0:T(8,128)(2,1)} %collective-permute-done.4, bf16[2048,512]{1,0:T(8,128)(2,1)S(1)} %bitcast_select_fusion, pred[]{:T(512)S(6)} %eq.28), kind=kOutput, calls=%fused_computation.7 | convolution fusion | flops 555745280 | bytes 5242881 | tf_op jit(solution)/shard_map/od,oc->dc/dot_general | solution.py:208
  137.0 10.7 %all-to-all-done.3 = bf16[8,256,192]{1,2,0:T(8,128)(2,1)S(1)} async-done(((bf16[8,256,192]{1,2,0:T(8,128)(2,1)}), bf16[8,256,192]{1,2,0:T(8,128)(2,1)S(1)}, u32[]{:S(2)}, u32[]{:S(2)}) %all-to-all-start.3) | async-done | bytes 786464 | tf_op jit(solution)/shard_map/all_to_all | solution.py:187
  147.7 3.5 %all-to-all-start.4 = ((f32[32,32,128]{2,1,0:T(8,128)}), f32[32,32,128]{2,1,0:T(8,128)S(1)}, u32[]{:S(2)}, u32[]{:S(2)}) async-start(f32[32,32,128]{2,1,0:T(8,128)} %bitcast.22), calls=%async_computation.4 | async-start | bytes 1048576 | tf_op jit(solution)/shard_map/all_to_all | solution.py:211
  151.2 0.7 slice_bitcast_fusion
  152.0 3.1 %fusion.29 = bf16[1,256,1024]{2,1,0:T(8,128)(2,1)} fusion(bf16[1024,8,128]{2,1,0:T(8,128)(2,1)} %param.8, bf16[8,256,192]{1,2,0:T(8,128)(2,1)S(1)} %all-to-all-done.3), kind=kOutput, calls=%fused_computation.26 | convolution fusion | flops 537133056 | bytes 3145728 | tf_op jit(solution)/shard_map/htc,dhc->td/dot_general | solution.py:198
  155.1 12.5 %all-to-all-done.4 = f32[32,32,128]{2,1,0:T(8,128)S(1)} async-done(((f32[32,32,128]{2,1,0:T(8,128)}), f32[32,32,128]{2,1,0:T(8,128)S(1)}, u32[]{:S(2)}, u32[]{:S(2)}) %all-to-all-start.4) | async-done | bytes 524320 | tf_op jit(solution)/shard_map/all_to_all | solution.py:211
  167.6 0.7 copy.27
  (5 shorter events, 0.1 us)
Async XLA Ops:
  0.6 16.1 %all-to-all-start.2 = ((bf16[8,256,64]{1,2,0:T(8,128)(2,1)}), bf16[8,256,64]{1,2,0:T(8,128)(2,1)S(1)}, u32[]{:S(2)}, u32[]{:S(2)}) async-start(bf16[8,256,64]{1,2,0:T(8,128)(2,1)} %bitcast.51), calls=%async_computation.2 | async-start | bytes 524288 | tf_op jit(solution)/shard_map/all_to_all | solution.py:153
  10.2 25.6 %copy-start = (bf16[1,256,1024]{2,1,0:T(8,128)(2,1)S(1)}, bf16[1,256,1024]{2,1,0:T(8,128)(2,1)}, u32[]{:S(2)}) copy-start(bf16[1,256,1024]{2,1,0:T(8,128)(2,1)} %param.6) | copy-start | bytes 1572868
  16.7 18.8 %all-to-all-start.1 = ((bf16[8,256,128]{1,2,0:T(8,128)(2,1)}), bf16[8,256,128]{1,2,0:T(8,128)(2,1)S(1)}, u32[]{:S(2)}, u32[]{:S(2)}) async-start(bf16[8,256,128]{1,2,0:T(8,128)(2,1)} %fusion.26), calls=%async_computation.1 | async-start | bytes 1048576 | tf_op jit(solution)/shard_map/all_to_all | solution.py:166
  35.8 2.0 %collective-permute-start = (bf16[256,1024]{1,0:T(8,128)(2,1)S(1)}, bf16[256,1024]{1,0:T(8,128)(2,1)S(1)}, u32[]{:S(2)}, u32[]{:S(2)}) collective-permute-start(bf16[256,1024]{1,0:T(8,128)(2,1)S(1)} %bitcast.44), channel_id=1, source_target_pairs={{0,1},{1,0},{2,3},{3,2},{4,5},{5,4},{6,7},{7,6},{8,9},{9,8},{10,11... | collective-permute-start | bytes 1572872 | tf_op jit(solution)/shard_map/ppermute | solution.py:121
  37.9 16.8 %collective-permute-start.1 = (bf16[2,256,512]{2,1,0:T(8,128)(2,1)S(1)}, bf16[2,256,512]{2,1,0:T(8,128)(2,1)S(1)}, u32[]{:S(2)}, u32[]{:S(2)}) collective-permute-start(bf16[2,256,512]{2,1,0:T(8,128)(2,1)S(1)} %fusion.33), channel_id=1, source_target_pairs={{0,2},{1,3},{2,4},{3,5},{4,6},{5,7},{6,0},{7,1},{8,10},{9,11},{10,... | collective-permute-start | bytes 1572872 | tf_op jit(solution)/shard_map/ppermute | solution.py:127
  37.9 38.2 %collective-permute-start.2 = (bf16[2,256,512]{2,1,0:T(8,128)(2,1)S(1)}, bf16[2,256,512]{2,1,0:T(8,128)(2,1)S(1)}, u32[]{:S(2)}, u32[]{:S(2)}) collective-permute-start(bf16[2,256,512]{2,1,0:T(8,128)(2,1)S(1)} %fusion.33), channel_id=1, source_target_pairs={{0,4},{1,5},{2,6},{3,7},{4,0},{5,1},{6,2},{7,3},{8,12},{9,13},{10,... | collective-permute-start | bytes 1572872 | tf_op jit(solution)/shard_map/ppermute | solution.py:127
  39.7 36.5 %collective-permute-start.3 = (bf16[2,256,512]{2,1,0:T(8,128)(2,1)S(1)}, bf16[2,256,512]{2,1,0:T(8,128)(2,1)}, u32[]{:S(2)}, u32[]{:S(2)}) collective-permute-start(bf16[2,256,512]{2,1,0:T(8,128)(2,1)S(1)} %fusion.33), channel_id=1, source_target_pairs={{0,6},{1,7},{2,0},{3,1},{4,2},{5,3},{6,4},{7,5},{8,14},{9,15},{10,... | collective-permute-start | bytes 1572872 | tf_op jit(solution)/shard_map/ppermute | solution.py:127
  76.2 0.8 copy-start.1
  80.5 1.9 %copy-start.3 = (s32[1,256]{1,0:T(1,128)S(1)}, s32[1,256]{1,0:T(1,128)}, u32[]{:S(2)}) copy-start(s32[1,256]{1,0:T(1,128)} %param.7) | copy-start | bytes 3076
  80.5 14.2 %copy-start.2 = (s32[1,16,8]{1,2,0:T(8,128)S(1)}, s32[1,16,8]{1,2,0:T(8,128)}, u32[]{:S(2)}) copy-start(s32[1,16,8]{1,2,0:T(8,128)} %param.9) | copy-start | bytes 1540
  82.3 50.4 %collective-permute-start.4 = (bf16[2048,512]{1,0:T(8,128)(2,1)S(1)}, bf16[2048,512]{1,0:T(8,128)(2,1)}, u32[]{:S(2)}, u32[]{:S(2)}) collective-permute-start(bf16[2048,512]{1,0:T(8,128)(2,1)S(1)} %bitcast_select_fusion), channel_id=1, source_target_pairs={{0,1},{1,0},{2,3},{3,2},{4,5},{5,4},{6,7},{7,6},{8,9},{9,8},{10,11... | collective-permute-start | bytes 6291464 | tf_op jit(solution)/shard_map/ppermute | solution.py:131
  83.0 17.3 %all-to-all-start = ((s32[8,1,256]{2,1,0:T(1,128)}), s32[8,1,256]{2,1,0:T(1,128)S(1)}, u32[]{:S(2)}, u32[]{:S(2)}) async-start(s32[8,1,256]{2,1,0:T(1,128)} %broadcast_in_dim.26), calls=%async_computation | async-start | bytes 16384 | tf_op jit(solution)/shard_map/all_to_all | solution.py:156
  123.3 24.5 %all-to-all-start.3 = ((bf16[8,256,192]{1,2,0:T(8,128)(2,1)}), bf16[8,256,192]{1,2,0:T(8,128)(2,1)S(1)}, u32[]{:S(2)}, u32[]{:S(2)}) async-start(bf16[8,256,192]{1,2,0:T(8,128)(2,1)} %copy.24), calls=%async_computation.3 | async-start | bytes 1572864 | tf_op jit(solution)/shard_map/all_to_all | solution.py:187
  147.7 19.9 %all-to-all-start.4 = ((f32[32,32,128]{2,1,0:T(8,128)}), f32[32,32,128]{2,1,0:T(8,128)S(1)}, u32[]{:S(2)}, u32[]{:S(2)}) async-start(f32[32,32,128]{2,1,0:T(8,128)} %bitcast.22), calls=%async_computation.4 | async-start | bytes 1048576 | tf_op jit(solution)/shard_map/all_to_all | solution.py:211

commit v20 on v18

--- a/solution.py
+++ b/solution.py
@@ -158,8 +158,11 @@
         got = lax.all_to_all(sending, "seq", split_axis=0, concat_axis=0, tiled=True)
         gathered = got.reshape(seq_count * portion, 2 * depth)
     mixed, grad_both = attend_group(gathered, grad_rows, key_blocks[group], key_counts[group])
+    leaving = jnp.concatenate([mixed, grad_both], axis=1)
+    if groups == 1:
+        leaving, owned_all = lax.optimization_barrier((leaving, owned_all))
     back = lax.all_to_all(
-        jnp.concatenate([mixed, grad_both], axis=1).reshape(seq_count, portion, 3 * depth),
+        leaving.reshape(seq_count, portion, 3 * depth),
         "seq",
         split_axis=0,
         concat_axis=0,
@@ -182,6 +185,7 @@
         partial = jnp.einsum(
             "od,oc->dc", owned_all, head_grad, preferred_element_type=jnp.float32
         )
+        partial, back = lax.optimization_barrier((partial, back))
         pieces = lax.all_to_all(
             partial.reshape(rec_count * seq_count, rows_out, 2 * depth),
             ("rec", "seq"),

time: 132 us -> 142 us (1.076)
  waiting for transfers between devices: 51.6 us -> 67.1 us
  matrix products: 19 us -> 15.2 us
    all_gather x1, waiting for transfers between devices: 4.4 us -> 13.3 us  [local(): owned_all = lax.all_gather(later_rows, 'seq', axis=0, tiled=True)]
    all_to_all x1, waiting for transfers between devices: 9.06 us -> 14.1 us  [local(): lax.all_to_all(leaving.reshape(seq_count, portion, 3 * depth), 'seq', spl...]
    dot_general x1, matrix products: 4.28 us -> 2.07 us  [local(): jnp.einsum('od,oc->dc', owned_all, head_grad, preferred_element_type=jnp....]
    dot_general x1, matrix products: 3.14 us -> 1.55 us  [local(): jnp.einsum('htc,dhc->td', grad_proj, head_weights, preferred_element_type...]
    all_to_all x1, waiting for transfers between devices: 12.5 us -> 14.1 us  [local(): lax.all_to_all(partial.reshape(rec_count * seq_count, rows_out, 2 * depth...]
  transfers between devices with their start and end apart: 6 -> 6, of which waited for: 6 -> 6; matrix products, arithmetic and copies ran while one was open for 19% -> 14% of each run, Pallas kernels for 15% -> 13%
where the time goes in v20:
time: 142 us
  waiting for transfers between devices  67.1 us (47%)
  starting transfers between devices  20.5 us (14%)
  Pallas kernels  17.8 us (13%)
  matrix products  15.2 us (11%)
  between operations  14.1 us (10%)
  local copies, waits for them, and re-layouts  5.33 us (4%)
  other arithmetic  1.79 us (1%)
    pallas_call x1, Pallas kernels, attend_group(): pl.pallas_call(attention_kernel, out_shape=(jax.ShapeDtypeStruct((total,...  17.8 us
    all_to_all x1, waiting for transfers between devices, local(): lax.all_to_all(proj_mine, 'seq', split_axis=0, concat_axis=0, tiled=True)  14.2 us
    all_to_all x1, waiting for transfers between devices, local(): lax.all_to_all(partial.reshape(rec_count * seq_count, rows_out, 2 * depth...  14.1 us
    all_to_all x1, waiting for transfers between devices, local(): lax.all_to_all(leaving.reshape(seq_count, portion, 3 * depth), 'seq', spl...  14.1 us
    all_gather x1, waiting for transfers between devices, local(): owned_all = lax.all_gather(later_rows, 'seq', axis=0, tiled=True)  13.3 us
    all_to_all x1, waiting for transfers between devices, local(): lax.all_to_all(upstream, 'seq', split_axis=0, concat_axis=0, tiled=True)  6.49 us
    all_to_all x1, starting transfers between devices, local(): lax.all_to_all(upstream, 'seq', split_axis=0, concat_axis=0, tiled=True)  6.47 us
    all_to_all x1, waiting for transfers between devices, local(): lax.all_to_all(jnp.broadcast_to(targets[None], (seq_count, tokens_here)),...  4.95 us
  transfers between devices with their start and end apart: 6, of which 6 were waited for; matrix products, arithmetic and copies ran while one was open for 14% of the time, Pallas kernels for 13%

profile of v20, /device:TPU:0, one launch (start us, length us, event | category | flops | bytes accessed | tf_op | source)
XLA Modules:
  0.0 141.8 jit_solution(5562687999604108829)
XLA Ops:
  7.2 0.0 copy-start.3
  7.2 0.0 copy-start.2
  7.2 6.5 %all-to-all-start.2 = ((bf16[8,256,64]{1,2,0:T(8,128)(2,1)}), bf16[8,256,64]{1,2,0:T(8,128)(2,1)S(1)}, u32[]{:S(2)}, u32[]{:S(2)}) async-start(bf16[8,256,64]{1,2,0:T(8,128)(2,1)} %bitcast.37), calls=%async_computation.2 | async-start | bytes 524288 | tf_op jit(solution)/shard_map/all_to_all | solution.py:127
  13.7 3.2 %fusion.19 = bf16[8,256,128]{1,2,0:T(8,128)(2,1)} fusion(bf16[1024,8,128]{2,1,0:T(8,128)(2,1)} %param.8, bf16[1,256,1024]{2,1,0:T(8,128)(2,1)} %param.6), kind=kOutput, calls=%fused_computation.14 | convolution fusion | flops 537133056 | bytes 3145728 | tf_op jit(solution)/shard_map/td,dhc->htc/dot_general | solution.py:137
  16.9 6.5 %all-to-all-done.2 = bf16[8,256,64]{1,2,0:T(8,128)(2,1)S(1)} async-done(((bf16[8,256,64]{1,2,0:T(8,128)(2,1)}), bf16[8,256,64]{1,2,0:T(8,128)(2,1)S(1)}, u32[]{:S(2)}, u32[]{:S(2)}) %all-to-all-start.2) | async-done | bytes 262176 | tf_op jit(solution)/shard_map/all_to_all | solution.py:127
  23.4 3.5 %all-to-all-start.1 = ((bf16[8,256,128]{1,2,0:T(8,128)(2,1)}), bf16[8,256,128]{1,2,0:T(8,128)(2,1)S(1)}, u32[]{:S(2)}, u32[]{:S(2)}) async-start(bf16[8,256,128]{1,2,0:T(8,128)(2,1)} %fusion.19), calls=%async_computation.1 | async-start | bytes 1048576 | tf_op jit(solution)/shard_map/all_to_all | solution.py:140
  26.9 0.0 all-gather.2.cloned.1.call-start
  26.9 1.0 copy.22
  28.0 14.2 %all-to-all-done.1 = bf16[8,256,128]{1,2,0:T(8,128)(2,1)S(1)} async-done(((bf16[8,256,128]{1,2,0:T(8,128)(2,1)}), bf16[8,256,128]{1,2,0:T(8,128)(2,1)S(1)}, u32[]{:S(2)}, u32[]{:S(2)}) %all-to-all-start.1) | async-done | bytes 524320 | tf_op jit(solution)/shard_map/all_to_all | solution.py:140
  42.2 0.3 copy.21
  42.5 0.0 all-gather.2.cloned.1.call-update
  42.5 0.0 copy-done.3
  42.5 0.6 broadcast_in_dim.12
  43.1 3.3 %all-to-all-start = ((s32[8,1,256]{2,1,0:T(1,128)}), s32[8,1,256]{2,1,0:T(1,128)S(1)}, u32[]{:S(2)}, u32[]{:S(2)}) async-start(s32[8,1,256]{2,1,0:T(1,128)} %broadcast_in_dim.12), calls=%async_computation | async-start | bytes 16384 | tf_op jit(solution)/shard_map/all_to_all | solution.py:130
  46.4 0.0 copy-done.2
  46.5 0.7 copy.23.lists_ref
  47.1 4.9 %all-to-all-done = s32[8,1,256]{2,1,0:T(1,128)S(1)} async-done(((s32[8,1,256]{2,1,0:T(1,128)}), s32[8,1,256]{2,1,0:T(1,128)S(1)}, u32[]{:S(2)}, u32[]{:S(2)}) %all-to-all-start) | async-done | bytes 8224 | tf_op jit(solution)/shard_map/all_to_all | solution.py:130
  52.1 3.8 %fusion.4.both_ref = bf16[2048,128]{1,0:T(8,128)(2,1)} fusion(bf16[2048,128]{1,0:T(8,128)(2,1)S(1)} %bitcast.35, s32[2048]{0:T(1024)S(1)} %bitcast.38), kind=kOutput, calls=%fused_computation.5 | convolution fusion | flops 1078198272 | bytes 1056768 | tf_op jit(solution)/shard_map/dot_general | solution.py:149
  55.8 17.8 %shard_map.88 = (bf16[2048,64]{1,0:T(8,128)(2,1)}, bf16[2048,128]{1,0:T(8,128)(2,1)}) custom-call(s32[16,8]{1,0:T(8,128)} %copy.23.lists_ref, s32[16]{0:T(128)} %bitcast.42, bf16[2048,128]{1,0:T(8,128)(2,1)} %fusion.4.both_ref, bf16[2048,64]{1,0:T(8,128)(2,1)} %bitcast.32), custom_call_target="tpu_custom_call" | custom-call | tf_op jit(solution)/shard_map/pallas_call | solution.py:65
  73.6 0.0 copy-start.1
  73.6 1.7 %pad_maximum_fusion = bf16[2048,192]{1,0:T(8,128)(2,1)S(1)} fusion(bf16[2048,128]{1,0:T(8,128)(2,1)} %get-tuple-element.14, bf16[2048,64]{1,0:T(8,128)(2,1)} %get-tuple-element.13), kind=kLoop, calls=%fused_computation.16 | loop fusion | flops 1572864 | bytes 1572864 | tf_op jit(solution)/shard_map/concatenate | solution.py:161
  75.4 13.3 %all-gather.2.cloned.1.call-done = bf16[2048,1024]{1,0:T(8,128)(2,1)} async-done(((bf16[256,1024]{1,0:T(8,128)(2,1)}), bf16[2048,1024]{1,0:T(8,128)(2,1)}) %all-gather.2.cloned.1.call-update) | async-done | bytes 4194320 | tf_op jit(solution)/shard_map/all_gather | solution.py:146
  88.7 1.3 copy.24
  90.0 3.7 %all-to-all-start.3 = ((bf16[8,256,192]{1,2,0:T(8,128)(2,1)}), bf16[8,256,192]{1,2,0:T(8,128)(2,1)S(1)}, u32[]{:S(2)}, u32[]{:S(2)}) async-start(bf16[8,256,192]{1,2,0:T(8,128)(2,1)} %copy.24), calls=%async_computation.3 | async-start | bytes 1572864 | tf_op jit(solution)/shard_map/all_to_all | solution.py:164
  93.7 0.0 copy-done.1
  93.7 0.0 copy-start
  93.7 4.5 %fusion.5 = bf16[2048,128]{1,0:T(8,128)(2,1)S(1)} fusion(bf16[2048,128]{1,0:T(8,128)(2,1)S(1)} %copy-done.1, s32[2048]{0:T(1024)S(1)} %bitcast.39), kind=kOutput, calls=%fused_computation.6 | convolution fusion | flops 1078198272 | bytes 1056768 | tf_op jit(solution)/shard_map/dot_general | solution.py:181
  98.2 0.0 copy-done
  98.3 0.0 copy-start.4
  98.3 2.1 %fusion.27 = f32[1024,128]{1,0:T(8,128)} fusion(bf16[2048,1024]{1,0:T(8,128)(2,1)S(1)} %copy-done, bf16[2048,128]{1,0:T(8,128)(2,1)S(1)} %fusion.5), kind=kOutput, calls=%fused_computation.20 | convolution fusion | flops 536870912 | bytes 5242880 | tf_op jit(solution)/shard_map/od,oc->dc/dot_general | solution.py:185
  100.3 14.1 %all-to-all-done.3 = bf16[8,256,192]{1,2,0:T(8,128)(2,1)S(1)} async-done(((bf16[8,256,192]{1,2,0:T(8,128)(2,1)}), bf16[8,256,192]{1,2,0:T(8,128)(2,1)S(1)}, u32[]{:S(2)}, u32[]{:S(2)}) %all-to-all-start.3) | async-done | bytes 786464 | tf_op jit(solution)/shard_map/all_to_all | solution.py:164
  114.4 3.4 %all-to-all-start.4 = ((f32[32,32,128]{2,1,0:T(8,128)}), f32[32,32,128]{2,1,0:T(8,128)S(1)}, u32[]{:S(2)}, u32[]{:S(2)}) async-start(f32[32,32,128]{2,1,0:T(8,128)} %bitcast.14), calls=%async_computation.4 | async-start | bytes 1048576 | tf_op jit(solution)/shard_map/all_to_all | solution.py:189
  117.8 0.7 slice_bitcast_fusion
  118.6 0.0 copy-done.4
  118.6 1.6 %fusion.22 = bf16[1,256,1024]{2,1,0:T(8,128)(2,1)} fusion(bf16[1024,8,128]{2,1,0:T(8,128)(2,1)S(1)} %copy-done.4, bf16[8,256,192]{1,2,0:T(8,128)(2,1)S(1)} %all-to-all-done.3), kind=kOutput, calls=%fused_computation.15 | convolution fusion | flops 537133056 | bytes 3145728 | tf_op jit(solution)/shard_map/htc,dhc->td/dot_general | solution.py:175
  120.1 14.1 %all-to-all-done.4 = f32[32,32,128]{2,1,0:T(8,128)S(1)} async-done(((f32[32,32,128]{2,1,0:T(8,128)}), f32[32,32,128]{2,1,0:T(8,128)S(1)}, u32[]{:S(2)}, u32[]{:S(2)}) %all-to-all-start.4) | async-done | bytes 524320 | tf_op jit(solution)/shard_map/all_to_all | solution.py:189
  134.2 0.7 copy.27
  (1 shorter events, 0.0 us)
Async XLA Ops:
  7.2 35.3 %copy-start.3 = (s32[1,256]{1,0:T(1,128)S(1)}, s32[1,256]{1,0:T(1,128)}, u32[]{:S(2)}) copy-start(s32[1,256]{1,0:T(1,128)} %param.7) | copy-start | bytes 3076
  7.2 39.3 %copy-start.2 = (s32[1,16,8]{1,2,0:T(8,128)S(1)}, s32[1,16,8]{1,2,0:T(8,128)}, u32[]{:S(2)}) copy-start(s32[1,16,8]{1,2,0:T(8,128)} %param.9) | copy-start | bytes 1540
  7.2 16.2 %all-to-all-start.2 = ((bf16[8,256,64]{1,2,0:T(8,128)(2,1)}), bf16[8,256,64]{1,2,0:T(8,128)(2,1)S(1)}, u32[]{:S(2)}, u32[]{:S(2)}) async-start(bf16[8,256,64]{1,2,0:T(8,128)(2,1)} %bitcast.37), calls=%async_computation.2 | async-start | bytes 524288 | tf_op jit(solution)/shard_map/all_to_all | solution.py:127
  23.4 18.8 %all-to-all-start.1 = ((bf16[8,256,128]{1,2,0:T(8,128)(2,1)}), bf16[8,256,128]{1,2,0:T(8,128)(2,1)S(1)}, u32[]{:S(2)}, u32[]{:S(2)}) async-start(bf16[8,256,128]{1,2,0:T(8,128)(2,1)} %fusion.19), calls=%async_computation.1 | async-start | bytes 1048576 | tf_op jit(solution)/shard_map/all_to_all | solution.py:140
  26.9 61.8 %all-gather.2.cloned.1.call-start = ((), (), s32[]{:S(2)}) async-start(), calls=%async_computation.5 | async-start | bytes 4718592 | tf_op jit(solution)/shard_map/all_gather | solution.py:146
  43.1 9.0 %all-to-all-start = ((s32[8,1,256]{2,1,0:T(1,128)}), s32[8,1,256]{2,1,0:T(1,128)S(1)}, u32[]{:S(2)}, u32[]{:S(2)}) async-start(s32[8,1,256]{2,1,0:T(1,128)} %broadcast_in_dim.12), calls=%async_computation | async-start | bytes 16384 | tf_op jit(solution)/shard_map/all_to_all | solution.py:130
  73.6 20.1 %copy-start.1 = (bf16[2048,128]{1,0:T(8,128)(2,1)S(1)}, bf16[2048,128]{1,0:T(8,128)(2,1)}, u32[]{:S(2)}) copy-start(bf16[2048,128]{1,0:T(8,128)(2,1)} %get-tuple-element.14) | copy-start | bytes 1572868
  90.0 24.5 %all-to-all-start.3 = ((bf16[8,256,192]{1,2,0:T(8,128)(2,1)}), bf16[8,256,192]{1,2,0:T(8,128)(2,1)S(1)}, u32[]{:S(2)}, u32[]{:S(2)}) async-start(bf16[8,256,192]{1,2,0:T(8,128)(2,1)} %copy.24), calls=%async_computation.3 | async-start | bytes 1572864 | tf_op jit(solution)/shard_map/all_to_all | solution.py:164
  93.7 4.5 %copy-start = (bf16[2048,1024]{1,0:T(8,128)(2,1)S(1)}, bf16[2048,1024]{1,0:T(8,128)(2,1)}, u32[]{:S(2)}) copy-start(bf16[2048,1024]{1,0:T(8,128)(2,1)} %all-gather.2.cloned.1.call-done) | copy-start | bytes 12582916
  98.3 20.3 %copy-start.4 = (bf16[1024,8,128]{2,1,0:T(8,128)(2,1)S(1)}, bf16[1024,8,128]{2,1,0:T(8,128)(2,1)}, u32[]{:S(2)}) copy-start(bf16[1024,8,128]{2,1,0:T(8,128)(2,1)} %param.8) | copy-start | bytes 6291460
  114.4 19.8 %all-to-all-start.4 = ((f32[32,32,128]{2,1,0:T(8,128)}), f32[32,32,128]{2,1,0:T(8,128)S(1)}, u32[]{:S(2)}, u32[]{:S(2)}) async-start(f32[32,32,128]{2,1,0:T(8,128)} %bitcast.14), calls=%async_computation.4 | async-start | bytes 1048576 | tf_op jit(solution)/shard_map/all_to_all | solution.py:189
Sparse Core Ops, SparseCore 0:
  42.6 46.0 all-gather.1

commit v21 on v18

--- a/solution.py
+++ b/solution.py
@@ -10,7 +10,7 @@
 BLOCK = 128
 
 
-def attention_kernel(lists_ref, counts_ref, both_ref, grad_ref, out_ref, back_ref, acc_ref):
+def attention_kernel(lists_ref, counts_ref, both_ref, grad_ref, out_ref, acc_ref):
     nblocks, listed = lists_ref.shape
     depth = grad_ref.shape[1]
     scale = depth ** (-0.5)
@@ -33,7 +33,7 @@
         probs = weights / jnp.sum(weights, axis=1, keepdims=True)
         probs_low = probs.astype(jnp.bfloat16)
         mixed = jnp.dot(probs_low, values, preferred_element_type=jnp.float32)
-        out_ref[pl.ds(start, BLOCK), :] = mixed.astype(out_ref.dtype)
+        out_ref[pl.ds(start, BLOCK), :depth] = mixed.astype(out_ref.dtype)
         dprobs = lax.dot_general(upstream, values, trans_b, preferred_element_type=jnp.float32)
         inner = jnp.sum(probs * dprobs, axis=1, keepdims=True)
         dscores = (scale * probs * (dprobs - inner)).astype(jnp.bfloat16)
@@ -54,7 +54,7 @@
         return carry
 
     lax.fori_loop(0, nblocks, one_block, 0)
-    back_ref[...] = acc_ref[...].astype(back_ref.dtype)
+    out_ref[:, depth:] = acc_ref[...].astype(out_ref.dtype)
 
 
 def attend_group(both, grad_rows, lists, counts):
@@ -64,17 +64,14 @@
     vmem = pltpu.MemorySpace.VMEM
     return pl.pallas_call(
         attention_kernel,
-        out_shape=(
-            jax.ShapeDtypeStruct((total, depth), jnp.bfloat16),
-            jax.ShapeDtypeStruct((total, width), jnp.bfloat16),
-        ),
+        out_shape=jax.ShapeDtypeStruct((total, depth + width), jnp.bfloat16),
         in_specs=[
             pl.BlockSpec(memory_space=smem),
             pl.BlockSpec(memory_space=smem),
             pl.BlockSpec(memory_space=vmem),
             pl.BlockSpec(memory_space=vmem),
         ],
-        out_specs=(pl.BlockSpec(memory_space=vmem), pl.BlockSpec(memory_space=vmem)),
+        out_specs=pl.BlockSpec(memory_space=vmem),
         scratch_shapes=[pltpu.VMEM((total, width), jnp.float32)],
     )(lists, counts, both, grad_rows)
 
@@ -157,9 +154,10 @@
         sending = proj.reshape(seq_count, portion * 2 * depth)
         got = lax.all_to_all(sending, "seq", split_axis=0, concat_axis=0, tiled=True)
         gathered = got.reshape(seq_count * portion, 2 * depth)
-    mixed, grad_both = attend_group(gathered, grad_rows, key_blocks[group], key_counts[group])
+    leaving = attend_group(gathered, grad_rows, key_blocks[group], key_counts[group])
+    grad_both = leaving[:, depth:]
     back = lax.all_to_all(
-        jnp.concatenate([mixed, grad_both], axis=1).reshape(seq_count, portion, 3 * depth),
+        leaving.reshape(seq_count, portion, 3 * depth),
         "seq",
         split_axis=0,
         concat_axis=0,

time: 132 us -> 132 us (level)
  other arithmetic: 1.75 us -> 0.04 us
    concatenate x1 -> x0, other arithmetic: 1.72 us -> none  [local(): jnp.concatenate([mixed, grad_both], axis=1)]
    dot_general x1, matrix products: 3.14 us -> 1.55 us  [local(): jnp.einsum('htc,dhc->td', grad_proj, head_weights, preferred_element_type...]
    all_to_all x1, waiting for transfers between devices: 12.5 us -> 14.1 us  [local(): lax.all_to_all(partial.reshape(rec_count * seq_count, rows_out, 2 * depth...]
    dot_general x1, matrix products: 4.53 us -> 5.95 us  [local(): lax.dot_general(placing, grad_both, (((0,), (0,)), ((), ())), preferred_e...]
  transfers between devices with their start and end apart: 6 -> 6, of which waited for: 6 -> 6; matrix products, arithmetic and copies ran while one was open for 19% -> 18% of each run, Pallas kernels for 15% -> 15%
where the time goes in v21:
time: 132 us; the launch traced here: 131 us
  waiting for transfers between devices  52.5 us (40%)
  starting transfers between devices  20.4 us (15%)
  Pallas kernels  19.2 us (15%)
  matrix products  18.8 us (14%)
  between operations  14.1 us (11%)
  local copies, waits for them, and re-layouts  6.29 us (5%)
    pallas_call x1, Pallas kernels, attend_group(): pl.pallas_call(attention_kernel, out_shape=jax.ShapeDtypeStruct((total, d...  19.2 us
    all_to_all x1, waiting for transfers between devices, local(): lax.all_to_all(proj_mine, 'seq', split_axis=0, concat_axis=0, tiled=True)  14.2 us
    all_to_all x1, waiting for transfers between devices, local(): lax.all_to_all(partial.reshape(rec_count * seq_count, rows_out, 2 * depth...  14.1 us
    all_to_all x1, waiting for transfers between devices, local(): lax.all_to_all(leaving.reshape(seq_count, portion, 3 * depth), 'seq', spl...  8.85 us
    all_to_all x1, waiting for transfers between devices, local(): lax.all_to_all(upstream, 'seq', split_axis=0, concat_axis=0, tiled=True)  6.49 us
    all_to_all x1, starting transfers between devices, local(): lax.all_to_all(upstream, 'seq', split_axis=0, concat_axis=0, tiled=True)  6.47 us
    dot_general x1, matrix products, local(): lax.dot_general(placing, grad_both, (((0,), (0,)), ((), ())), preferred_e...  5.95 us
    all_to_all x1, waiting for transfers between devices, local(): lax.all_to_all(jnp.broadcast_to(targets[None], (seq_count, tokens_here)),...  4.95 us
  transfers between devices with their start and end apart: 6, of which 6 were waited for; matrix products, arithmetic and copies ran while one was open for 18% of the time, Pallas kernels for 15%

profile of v21, /device:TPU:0, one launch (start us, length us, event | category | flops | bytes accessed | tf_op | source)
XLA Modules:
  0.0 131.2 jit_solution(13124185771327412014)
XLA Ops:
  7.2 0.0 copy-start.1
  7.2 0.0 copy-start
  7.2 6.5 %all-to-all-start.2 = ((bf16[8,256,64]{1,2,0:T(8,128)(2,1)}), bf16[8,256,64]{1,2,0:T(8,128)(2,1)S(1)}, u32[]{:S(2)}, u32[]{:S(2)}) async-start(bf16[8,256,64]{1,2,0:T(8,128)(2,1)} %bitcast.36), calls=%async_computation.2 | async-start | bytes 524288 | tf_op jit(solution)/shard_map/all_to_all | solution.py:124
  13.7 3.2 %fusion.19 = bf16[8,256,128]{1,2,0:T(8,128)(2,1)} fusion(bf16[1024,8,128]{2,1,0:T(8,128)(2,1)} %param.8, bf16[1,256,1024]{2,1,0:T(8,128)(2,1)} %param.6), kind=kOutput, calls=%fused_computation.14 | convolution fusion | flops 537133056 | bytes 3145728 | tf_op jit(solution)/shard_map/td,dhc->htc/dot_general | solution.py:134
  16.9 6.5 %all-to-all-done.2 = bf16[8,256,64]{1,2,0:T(8,128)(2,1)S(1)} async-done(((bf16[8,256,64]{1,2,0:T(8,128)(2,1)}), bf16[8,256,64]{1,2,0:T(8,128)(2,1)S(1)}, u32[]{:S(2)}, u32[]{:S(2)}) %all-to-all-start.2) | async-done | bytes 262176 | tf_op jit(solution)/shard_map/all_to_all | solution.py:124
  23.4 3.5 %all-to-all-start.1 = ((bf16[8,256,128]{1,2,0:T(8,128)(2,1)}), bf16[8,256,128]{1,2,0:T(8,128)(2,1)S(1)}, u32[]{:S(2)}, u32[]{:S(2)}) async-start(bf16[8,256,128]{1,2,0:T(8,128)(2,1)} %fusion.19), calls=%async_computation.1 | async-start | bytes 1048576 | tf_op jit(solution)/shard_map/all_to_all | solution.py:137
  26.9 0.0 all-gather.2.cloned.1.call-start
  26.9 1.1 copy.22
  28.0 14.2 %all-to-all-done.1 = bf16[8,256,128]{1,2,0:T(8,128)(2,1)S(1)} async-done(((bf16[8,256,128]{1,2,0:T(8,128)(2,1)}), bf16[8,256,128]{1,2,0:T(8,128)(2,1)S(1)}, u32[]{:S(2)}, u32[]{:S(2)}) %all-to-all-start.1) | async-done | bytes 524320 | tf_op jit(solution)/shard_map/all_to_all | solution.py:137
  42.2 0.3 copy.21
  42.5 0.0 all-gather.2.cloned.1.call-update
  42.5 0.0 copy-done.1
  42.5 0.6 broadcast_in_dim.12
  43.1 3.3 %all-to-all-start = ((s32[8,1,256]{2,1,0:T(1,128)}), s32[8,1,256]{2,1,0:T(1,128)S(1)}, u32[]{:S(2)}, u32[]{:S(2)}) async-start(s32[8,1,256]{2,1,0:T(1,128)} %broadcast_in_dim.12), calls=%async_computation | async-start | bytes 16384 | tf_op jit(solution)/shard_map/all_to_all | solution.py:127
  46.4 0.0 copy-done
  46.5 0.7 copy.23.lists_ref
  47.1 4.9 %all-to-all-done = s32[8,1,256]{2,1,0:T(1,128)S(1)} async-done(((s32[8,1,256]{2,1,0:T(1,128)}), s32[8,1,256]{2,1,0:T(1,128)S(1)}, u32[]{:S(2)}, u32[]{:S(2)}) %all-to-all-start) | async-done | bytes 8224 | tf_op jit(solution)/shard_map/all_to_all | solution.py:127
  52.1 3.8 %fusion.4.both_ref = bf16[2048,128]{1,0:T(8,128)(2,1)} fusion(bf16[2048,128]{1,0:T(8,128)(2,1)S(1)} %bitcast.34, s32[2048]{0:T(1024)S(1)} %bitcast.37), kind=kOutput, calls=%fused_computation.5 | convolution fusion | flops 1078198272 | bytes 1056768 | tf_op jit(solution)/shard_map/dot_general | solution.py:146
  55.8 19.2 %shard_map.88 = bf16[2048,192]{1,0:T(8,128)(2,1)} custom-call(s32[16,8]{1,0:T(8,128)} %copy.23.lists_ref, s32[16]{0:T(128)} %bitcast.41, bf16[2048,128]{1,0:T(8,128)(2,1)} %fusion.4.both_ref, bf16[2048,64]{1,0:T(8,128)(2,1)} %bitcast.31), custom_call_target="tpu_custom_call" | custom-call | tf_op jit(solution)/shard_map/pallas_call | solution.py:65
  75.0 2.2 %copy.24 = bf16[8,256,192]{1,2,0:T(8,128)(2,1)} copy(bf16[8,256,192]{2,1,0:T(8,128)(2,1)} %bitcast.30) | data formatting | bytes 1572864 | tf_op jit(solution)/shard_map/reshape | solution.py:160
  77.2 3.7 %all-to-all-start.3 = ((bf16[8,256,192]{1,2,0:T(8,128)(2,1)}), bf16[8,256,192]{1,2,0:T(8,128)(2,1)S(1)}, u32[]{:S(2)}, u32[]{:S(2)}) async-start(bf16[8,256,192]{1,2,0:T(8,128)(2,1)} %copy.24), calls=%async_computation.3 | async-start | bytes 1572864 | tf_op jit(solution)/shard_map/all_to_all | solution.py:159
  81.0 6.0 %fusion.5 = bf16[2048,128]{1,0:T(8,128)(2,1)S(1)} fusion(s32[2048]{0:T(1024)S(1)} %bitcast.38, bf16[2048,192]{1,0:T(8,128)(2,1)} %shard_map.88), kind=kOutput, calls=%fused_computation.6 | convolution fusion | flops 1078198272 | bytes 1056768 | tf_op jit(solution)/shard_map/dot_general | solution.py:176
  86.9 0.0 copy-start.2
  86.9 3.9 %all-gather.2.cloned.1.call-done = bf16[2048,1024]{1,0:T(8,128)(2,1)} async-done(((bf16[256,1024]{1,0:T(8,128)(2,1)}), bf16[2048,1024]{1,0:T(8,128)(2,1)}) %all-gather.2.cloned.1.call-update) | async-done | bytes 4194320 | tf_op jit(solution)/shard_map/all_gather | solution.py:143
  90.8 4.3 %fusion.28 = f32[1024,128]{1,0:T(8,128)} fusion(bf16[2048,1024]{1,0:T(8,128)(2,1)} %all-gather.2.cloned.1.call-done, bf16[2048,128]{1,0:T(8,128)(2,1)S(1)} %fusion.5), kind=kOutput, calls=%fused_computation.20 | convolution fusion | flops 536870912 | bytes 5242880 | tf_op jit(solution)/shard_map/od,oc->dc/dot_general | solution.py:180
  95.1 8.8 %all-to-all-done.3 = bf16[8,256,192]{1,2,0:T(8,128)(2,1)S(1)} async-done(((bf16[8,256,192]{1,2,0:T(8,128)(2,1)}), bf16[8,256,192]{1,2,0:T(8,128)(2,1)S(1)}, u32[]{:S(2)}, u32[]{:S(2)}) %all-to-all-start.3) | async-done | bytes 786464 | tf_op jit(solution)/shard_map/all_to_all | solution.py:159
  103.9 3.3 %all-to-all-start.4 = ((f32[32,32,128]{2,1,0:T(8,128)}), f32[32,32,128]{2,1,0:T(8,128)S(1)}, u32[]{:S(2)}, u32[]{:S(2)}) async-start(f32[32,32,128]{2,1,0:T(8,128)} %bitcast.14), calls=%async_computation.4 | async-start | bytes 1048576 | tf_op jit(solution)/shard_map/all_to_all | solution.py:183
  107.3 0.7 slice_bitcast_fusion
  108.0 0.0 copy-done.2
  108.0 1.6 %fusion.22 = bf16[1,256,1024]{2,1,0:T(8,128)(2,1)} fusion(bf16[1024,8,128]{2,1,0:T(8,128)(2,1)S(1)} %copy-done.2, bf16[8,256,192]{1,2,0:T(8,128)(2,1)S(1)} %all-to-all-done.3), kind=kOutput, calls=%fused_computation.15 | convolution fusion | flops 537133056 | bytes 3145728 | tf_op jit(solution)/shard_map/htc,dhc->td/dot_general | solution.py:170
  109.5 14.1 %all-to-all-done.4 = f32[32,32,128]{2,1,0:T(8,128)S(1)} async-done(((f32[32,32,128]{2,1,0:T(8,128)}), f32[32,32,128]{2,1,0:T(8,128)S(1)}, u32[]{:S(2)}, u32[]{:S(2)}) %all-to-all-start.4) | async-done | bytes 524320 | tf_op jit(solution)/shard_map/all_to_all | solution.py:183
  123.7 0.7 copy.27
  (1 shorter events, 0.0 us)
Async XLA Ops:
  7.2 35.3 %copy-start.1 = (s32[1,256]{1,0:T(1,128)S(1)}, s32[1,256]{1,0:T(1,128)}, u32[]{:S(2)}) copy-start(s32[1,256]{1,0:T(1,128)} %param.7) | copy-start | bytes 3076
  7.2 39.3 %copy-start = (s32[1,16,8]{1,2,0:T(8,128)S(1)}, s32[1,16,8]{1,2,0:T(8,128)}, u32[]{:S(2)}) copy-start(s32[1,16,8]{1,2,0:T(8,128)} %param.9) | copy-start | bytes 1540
  7.2 16.2 %all-to-all-start.2 = ((bf16[8,256,64]{1,2,0:T(8,128)(2,1)}), bf16[8,256,64]{1,2,0:T(8,128)(2,1)S(1)}, u32[]{:S(2)}, u32[]{:S(2)}) async-start(bf16[8,256,64]{1,2,0:T(8,128)(2,1)} %bitcast.36), calls=%async_computation.2 | async-start | bytes 524288 | tf_op jit(solution)/shard_map/all_to_all | solution.py:124
  23.4 18.8 %all-to-all-start.1 = ((bf16[8,256,128]{1,2,0:T(8,128)(2,1)}), bf16[8,256,128]{1,2,0:T(8,128)(2,1)S(1)}, u32[]{:S(2)}, u32[]{:S(2)}) async-start(bf16[8,256,128]{1,2,0:T(8,128)(2,1)} %fusion.19), calls=%async_computation.1 | async-start | bytes 1048576 | tf_op jit(solution)/shard_map/all_to_all | solution.py:137
  26.9 63.9 %all-gather.2.cloned.1.call-start = ((), (), s32[]{:S(2)}) async-start(), calls=%async_computation.5 | async-start | bytes 4718592 | tf_op jit(solution)/shard_map/all_gather | solution.py:143
  43.1 9.0 %all-to-all-start = ((s32[8,1,256]{2,1,0:T(1,128)}), s32[8,1,256]{2,1,0:T(1,128)S(1)}, u32[]{:S(2)}, u32[]{:S(2)}) async-start(s32[8,1,256]{2,1,0:T(1,128)} %broadcast_in_dim.12), calls=%async_computation | async-start | bytes 16384 | tf_op jit(solution)/shard_map/all_to_all | solution.py:127
  77.2 26.7 %all-to-all-start.3 = ((bf16[8,256,192]{1,2,0:T(8,128)(2,1)}), bf16[8,256,192]{1,2,0:T(8,128)(2,1)S(1)}, u32[]{:S(2)}, u32[]{:S(2)}) async-start(bf16[8,256,192]{1,2,0:T(8,128)(2,1)} %copy.24), calls=%async_computation.3 | async-start | bytes 1572864 | tf_op jit(solution)/shard_map/all_to_all | solution.py:159
  86.9 21.1 %copy-start.2 = (bf16[1024,8,128]{2,1,0:T(8,128)(2,1)S(1)}, bf16[1024,8,128]{2,1,0:T(8,128)(2,1)}, u32[]{:S(2)}) copy-start(bf16[1024,8,128]{2,1,0:T(8,128)(2,1)} %param.8) | copy-start | bytes 6291460
  103.9 19.7 %all-to-all-start.4 = ((f32[32,32,128]{2,1,0:T(8,128)}), f32[32,32,128]{2,1,0:T(8,128)S(1)}, u32[]{:S(2)}, u32[]{:S(2)}) async-start(f32[32,32,128]{2,1,0:T(8,128)} %bitcast.14), calls=%async_computation.4 | async-start | bytes 1048576 | tf_op jit(solution)/shard_map/all_to_all | solution.py:183
Sparse Core Ops, SparseCore 0:
  42.6 48.1 all-gather.1

commit v22 on v18

--- a/solution.py
+++ b/solution.py
@@ -180,8 +180,8 @@
             ).astype(jnp.bfloat16)
         )
         partial = jnp.einsum(
-            "od,oc->dc", owned_all, head_grad, preferred_element_type=jnp.float32
-        )
+            "oc,od->cd", head_grad, owned_all, preferred_element_type=jnp.float32
+        ).T
         pieces = lax.all_to_all(
             partial.reshape(rec_count * seq_count, rows_out, 2 * depth),
             ("rec", "seq"),

time: 132 us -> 132 us (level)
  Pallas kernels: 19 us -> 16.3 us
  waiting for transfers between devices: 51.6 us -> 54.3 us
    all_gather x1, waiting for transfers between devices: 4.4 us -> 10.1 us  [local(): owned_all = lax.all_gather(later_rows, 'seq', axis=0, tiled=True)]
    all_to_all x1, waiting for transfers between devices: 9.06 us -> 6.07 us  [local(): lax.all_to_all(jnp.concatenate([mixed, grad_both], axis=1).reshape(seq_co...]
    pallas_call x1, Pallas kernels: 19 us -> 16.3 us  [attend_group(): pl.pallas_call(attention_kernel, out_shape=(jax.ShapeDtypeStruct((total,...]
  transfers between devices with their start and end apart: 6 -> 6, of which waited for: 6 -> 6; matrix products, arithmetic and copies ran while one was open for 19% -> 19% of each run, Pallas kernels for 15% -> 12%
where the time goes in v22:
time: 132 us; the launch traced here: 131 us
  waiting for transfers between devices  54.3 us (41%)
  starting transfers between devices  20.4 us (15%)
  matrix products  19 us (14%)
  Pallas kernels  16.3 us (12%)
  between operations  14.1 us (11%)
  local copies, waits for them, and re-layouts  5.33 us (4%)
  other arithmetic  1.75 us (1%)
    pallas_call x1, Pallas kernels, attend_group(): pl.pallas_call(attention_kernel, out_shape=(jax.ShapeDtypeStruct((total,...  16.3 us
    all_to_all x1, waiting for transfers between devices, local(): lax.all_to_all(proj_mine, 'seq', split_axis=0, concat_axis=0, tiled=True)  14.2 us
    all_to_all x1, waiting for transfers between devices, local(): lax.all_to_all(partial.reshape(rec_count * seq_count, rows_out, 2 * depth...  12.5 us
    all_gather x1, waiting for transfers between devices, local(): owned_all = lax.all_gather(later_rows, 'seq', axis=0, tiled=True)  10.1 us
    all_to_all x1, waiting for transfers between devices, local(): lax.all_to_all(upstream, 'seq', split_axis=0, concat_axis=0, tiled=True)  6.49 us
    all_to_all x1, starting transfers between devices, local(): lax.all_to_all(upstream, 'seq', split_axis=0, concat_axis=0, tiled=True)  6.47 us
    all_to_all x1, waiting for transfers between devices, local(): lax.all_to_all(jnp.concatenate([mixed, grad_both], axis=1).reshape(seq_co...  6.07 us
    all_to_all x1, waiting for transfers between devices, local(): lax.all_to_all(jnp.broadcast_to(targets[None], (seq_count, tokens_here)),...  4.95 us
  transfers between devices with their start and end apart: 6, of which 6 were waited for; matrix products, arithmetic and copies ran while one was open for 19% of the time, Pallas kernels for 12%

profile of v22, /device:TPU:0, one launch (start us, length us, event | category | flops | bytes accessed | tf_op | source)
XLA Modules:
  0.0 131.2 jit_solution(9918573429765299188)
XLA Ops:
  7.2 0.0 copy-start.2
  7.2 0.0 copy-start.1
  7.2 6.5 %all-to-all-start.2 = ((bf16[8,256,64]{1,2,0:T(8,128)(2,1)}), bf16[8,256,64]{1,2,0:T(8,128)(2,1)S(1)}, u32[]{:S(2)}, u32[]{:S(2)}) async-start(bf16[8,256,64]{1,2,0:T(8,128)(2,1)} %bitcast.37), calls=%async_computation.2 | async-start | bytes 524288 | tf_op jit(solution)/shard_map/all_to_all | solution.py:127
  13.7 3.2 %fusion.19 = bf16[8,256,128]{1,2,0:T(8,128)(2,1)} fusion(bf16[1024,8,128]{2,1,0:T(8,128)(2,1)} %param.8, bf16[1,256,1024]{2,1,0:T(8,128)(2,1)} %param.6), kind=kOutput, calls=%fused_computation.14 | convolution fusion | flops 537133056 | bytes 3145728 | tf_op jit(solution)/shard_map/td,dhc->htc/dot_general | solution.py:137
  16.9 6.5 %all-to-all-done.2 = bf16[8,256,64]{1,2,0:T(8,128)(2,1)S(1)} async-done(((bf16[8,256,64]{1,2,0:T(8,128)(2,1)}), bf16[8,256,64]{1,2,0:T(8,128)(2,1)S(1)}, u32[]{:S(2)}, u32[]{:S(2)}) %all-to-all-start.2) | async-done | bytes 262176 | tf_op jit(solution)/shard_map/all_to_all | solution.py:127
  23.4 3.5 %all-to-all-start.1 = ((bf16[8,256,128]{1,2,0:T(8,128)(2,1)}), bf16[8,256,128]{1,2,0:T(8,128)(2,1)S(1)}, u32[]{:S(2)}, u32[]{:S(2)}) async-start(bf16[8,256,128]{1,2,0:T(8,128)(2,1)} %fusion.19), calls=%async_computation.1 | async-start | bytes 1048576 | tf_op jit(solution)/shard_map/all_to_all | solution.py:140
  26.9 0.0 all-gather.2.cloned.1.call-start
  26.9 1.0 copy.22
  28.0 14.2 %all-to-all-done.1 = bf16[8,256,128]{1,2,0:T(8,128)(2,1)S(1)} async-done(((bf16[8,256,128]{1,2,0:T(8,128)(2,1)}), bf16[8,256,128]{1,2,0:T(8,128)(2,1)S(1)}, u32[]{:S(2)}, u32[]{:S(2)}) %all-to-all-start.1) | async-done | bytes 524320 | tf_op jit(solution)/shard_map/all_to_all | solution.py:140
  42.2 0.3 copy.21
  42.5 0.0 all-gather.2.cloned.1.call-update
  42.5 0.0 copy-done.2
  42.5 0.6 broadcast_in_dim.12
  43.1 3.3 %all-to-all-start = ((s32[8,1,256]{2,1,0:T(1,128)}), s32[8,1,256]{2,1,0:T(1,128)S(1)}, u32[]{:S(2)}, u32[]{:S(2)}) async-start(s32[8,1,256]{2,1,0:T(1,128)} %broadcast_in_dim.12), calls=%async_computation | async-start | bytes 16384 | tf_op jit(solution)/shard_map/all_to_all | solution.py:130
  46.4 0.0 copy-done.1
  46.5 0.7 copy.23.lists_ref
  47.1 4.9 %all-to-all-done = s32[8,1,256]{2,1,0:T(1,128)S(1)} async-done(((s32[8,1,256]{2,1,0:T(1,128)}), s32[8,1,256]{2,1,0:T(1,128)S(1)}, u32[]{:S(2)}, u32[]{:S(2)}) %all-to-all-start) | async-done | bytes 8224 | tf_op jit(solution)/shard_map/all_to_all | solution.py:130
  52.1 3.8 %fusion.4.both_ref = bf16[2048,128]{1,0:T(8,128)(2,1)} fusion(bf16[2048,128]{1,0:T(8,128)(2,1)S(1)} %bitcast.35, s32[2048]{0:T(1024)S(1)} %bitcast.38), kind=kOutput, calls=%fused_computation.5 | convolution fusion | flops 1078198272 | bytes 1056768 | tf_op jit(solution)/shard_map/dot_general | solution.py:149
  55.9 16.3 %shard_map.88 = (bf16[2048,64]{1,0:T(8,128)(2,1)}, bf16[2048,128]{1,0:T(8,128)(2,1)}) custom-call(s32[16,8]{1,0:T(8,128)} %copy.23.lists_ref, s32[16]{0:T(128)} %bitcast.42, bf16[2048,128]{1,0:T(8,128)(2,1)} %fusion.4.both_ref, bf16[2048,64]{1,0:T(8,128)(2,1)} %bitcast.32), custom_call_target="tpu_custom_call" | custom-call | tf_op jit(solution)/shard_map/pallas_call | solution.py:65
  72.2 0.0 copy-start
  72.2 1.7 %pad_maximum_fusion = bf16[2048,192]{1,0:T(8,128)(2,1)S(1)} fusion(bf16[2048,128]{1,0:T(8,128)(2,1)} %get-tuple-element.11, bf16[2048,64]{1,0:T(8,128)(2,1)} %get-tuple-element.10), kind=kLoop, calls=%fused_computation.16 | loop fusion | flops 1572864 | bytes 1572864 | tf_op jit(solution)/shard_map/concatenate | solution.py:162
  73.9 1.3 copy.24
  75.2 3.7 %all-to-all-start.3 = ((bf16[8,256,192]{1,2,0:T(8,128)(2,1)}), bf16[8,256,192]{1,2,0:T(8,128)(2,1)S(1)}, u32[]{:S(2)}, u32[]{:S(2)}) async-start(bf16[8,256,192]{1,2,0:T(8,128)(2,1)} %copy.24), calls=%async_computation.3 | async-start | bytes 1572864 | tf_op jit(solution)/shard_map/all_to_all | solution.py:161
  79.0 0.0 copy-done
  79.0 4.5 %fusion.5 = bf16[2048,128]{1,0:T(8,128)(2,1)S(1)} fusion(bf16[2048,128]{1,0:T(8,128)(2,1)S(1)} %copy-done, s32[2048]{0:T(1024)S(1)} %bitcast.39), kind=kOutput, calls=%fused_computation.6 | convolution fusion | flops 1078198272 | bytes 1056768 | tf_op jit(solution)/shard_map/dot_general | solution.py:178
  83.5 10.1 %all-gather.2.cloned.1.call-done = bf16[2048,1024]{1,0:T(8,128)(2,1)} async-done(((bf16[256,1024]{1,0:T(8,128)(2,1)}), bf16[2048,1024]{1,0:T(8,128)(2,1)}) %all-gather.2.cloned.1.call-update) | async-done | bytes 4194320 | tf_op jit(solution)/shard_map/all_gather | solution.py:146
  93.6 4.3 %fusion.27 = f32[1024,128]{1,0:T(8,128)} fusion(bf16[2048,1024]{1,0:T(8,128)(2,1)} %all-gather.2.cloned.1.call-done, bf16[2048,128]{1,0:T(8,128)(2,1)S(1)} %fusion.5), kind=kOutput, calls=%fused_computation.20 | convolution fusion | flops 536870912 | bytes 5242880 | tf_op jit(solution)/shard_map/oc,od->cd/dot_general | solution.py:182
  97.9 6.1 %all-to-all-done.3 = bf16[8,256,192]{1,2,0:T(8,128)(2,1)S(1)} async-done(((bf16[8,256,192]{1,2,0:T(8,128)(2,1)}), bf16[8,256,192]{1,2,0:T(8,128)(2,1)S(1)}, u32[]{:S(2)}, u32[]{:S(2)}) %all-to-all-start.3) | async-done | bytes 786464 | tf_op jit(solution)/shard_map/all_to_all | solution.py:161
  103.9 3.3 %all-to-all-start.4 = ((f32[32,32,128]{2,1,0:T(8,128)}), f32[32,32,128]{2,1,0:T(8,128)S(1)}, u32[]{:S(2)}, u32[]{:S(2)}) async-start(f32[32,32,128]{2,1,0:T(8,128)} %bitcast.14), calls=%async_computation.4 | async-start | bytes 1048576 | tf_op jit(solution)/shard_map/all_to_all | solution.py:185
  107.2 0.7 slice_bitcast_fusion
  108.0 3.1 %fusion.22 = bf16[1,256,1024]{2,1,0:T(8,128)(2,1)} fusion(bf16[1024,8,128]{2,1,0:T(8,128)(2,1)} %param.8, bf16[8,256,192]{1,2,0:T(8,128)(2,1)S(1)} %all-to-all-done.3), kind=kOutput, calls=%fused_computation.15 | convolution fusion | flops 537133056 | bytes 3145728 | tf_op jit(solution)/shard_map/htc,dhc->td/dot_general | solution.py:172
  111.1 12.5 %all-to-all-done.4 = f32[32,32,128]{2,1,0:T(8,128)S(1)} async-done(((f32[32,32,128]{2,1,0:T(8,128)}), f32[32,32,128]{2,1,0:T(8,128)S(1)}, u32[]{:S(2)}, u32[]{:S(2)}) %all-to-all-start.4) | async-done | bytes 524320 | tf_op jit(solution)/shard_map/all_to_all | solution.py:185
  123.6 0.7 copy.27
  (1 shorter events, 0.0 us)
Async XLA Ops:
  7.2 35.3 %copy-start.2 = (s32[1,256]{1,0:T(1,128)S(1)}, s32[1,256]{1,0:T(1,128)}, u32[]{:S(2)}) copy-start(s32[1,256]{1,0:T(1,128)} %param.7) | copy-start | bytes 3076
  7.2 39.3 %copy-start.1 = (s32[1,16,8]{1,2,0:T(8,128)S(1)}, s32[1,16,8]{1,2,0:T(8,128)}, u32[]{:S(2)}) copy-start(s32[1,16,8]{1,2,0:T(8,128)} %param.9) | copy-start | bytes 1540
  7.2 16.2 %all-to-all-start.2 = ((bf16[8,256,64]{1,2,0:T(8,128)(2,1)}), bf16[8,256,64]{1,2,0:T(8,128)(2,1)S(1)}, u32[]{:S(2)}, u32[]{:S(2)}) async-start(bf16[8,256,64]{1,2,0:T(8,128)(2,1)} %bitcast.37), calls=%async_computation.2 | async-start | bytes 524288 | tf_op jit(solution)/shard_map/all_to_all | solution.py:127
  23.4 18.8 %all-to-all-start.1 = ((bf16[8,256,128]{1,2,0:T(8,128)(2,1)}), bf16[8,256,128]{1,2,0:T(8,128)(2,1)S(1)}, u32[]{:S(2)}, u32[]{:S(2)}) async-start(bf16[8,256,128]{1,2,0:T(8,128)(2,1)} %fusion.19), calls=%async_computation.1 | async-start | bytes 1048576 | tf_op jit(solution)/shard_map/all_to_all | solution.py:140
  26.9 66.7 %all-gather.2.cloned.1.call-start = ((), (), s32[]{:S(2)}) async-start(), calls=%async_computation.5 | async-start | bytes 4718592 | tf_op jit(solution)/shard_map/all_gather | solution.py:146
  43.1 9.0 %all-to-all-start = ((s32[8,1,256]{2,1,0:T(1,128)}), s32[8,1,256]{2,1,0:T(1,128)S(1)}, u32[]{:S(2)}, u32[]{:S(2)}) async-start(s32[8,1,256]{2,1,0:T(1,128)} %broadcast_in_dim.12), calls=%async_computation | async-start | bytes 16384 | tf_op jit(solution)/shard_map/all_to_all | solution.py:130
  72.2 6.8 %copy-start = (bf16[2048,128]{1,0:T(8,128)(2,1)S(1)}, bf16[2048,128]{1,0:T(8,128)(2,1)}, u32[]{:S(2)}) copy-start(bf16[2048,128]{1,0:T(8,128)(2,1)} %get-tuple-element.11) | copy-start | bytes 1572868
  75.2 28.7 %all-to-all-start.3 = ((bf16[8,256,192]{1,2,0:T(8,128)(2,1)}), bf16[8,256,192]{1,2,0:T(8,128)(2,1)S(1)}, u32[]{:S(2)}, u32[]{:S(2)}) async-start(bf16[8,256,192]{1,2,0:T(8,128)(2,1)} %copy.24), calls=%async_computation.3 | async-start | bytes 1572864 | tf_op jit(solution)/shard_map/all_to_all | solution.py:161
  103.9 19.7 %all-to-all-start.4 = ((f32[32,32,128]{2,1,0:T(8,128)}), f32[32,32,128]{2,1,0:T(8,128)S(1)}, u32[]{:S(2)}, u32[]{:S(2)}) async-start(f32[32,32,128]{2,1,0:T(8,128)} %bitcast.14), calls=%async_computation.4 | async-start | bytes 1048576 | tf_op jit(solution)/shard_map/all_to_all | solution.py:185
Sparse Core Ops, SparseCore 0:
  42.6 50.9 all-gather.1
